TPU v7x, 256 devices: a whole 4x4x8 slice. The times are simulated.
256 devices in a mesh: chan: 64 (over x, z, core), tm: 4 (over y).
Axes of the slice: x: 4, y: 4, z: 8, core: 2. Of those that a mesh axis runs over, the one named last changes fastest.
Arguments:
- recorded: bfloat16 [8192, 512], P(('tm', 'chan')), may hold values from -6 to 6
- partners: int32 [64], replicated, may hold values from 0 to 63, as said below
- offsets: int32 [64], P('chan'), may hold values from 3 to 4
- first_weight: bfloat16 [16, 1, 7, 7], replicated, may hold values from -1.25 to 1.25
- first_bias: float32 [16], replicated, may hold values from -3 to 3
- second_weight: bfloat16 [32, 16, 7, 7], replicated, may hold values from -0.3125 to 0.3125
- second_bias: float32 [32], replicated, may hold values from -3 to 3
- loop_weight: bfloat16 [7, 32, 32], replicated, may hold values from -1 to 1
- third_weight: bfloat16 [32, 32, 7, 7], replicated, may hold values from -0.21875 to 0.21875
- third_bias: float32 [32], replicated, may hold values from -3 to 3
- fourth_weight: bfloat16 [64, 32, 7, 7], replicated, may hold values from -0.21875 to 0.21875
- fourth_bias: float32 [64], replicated, may hold values from -3 to 3
Outputs:
- features: bfloat16 [64, 512, 512], P(None, 'chan', 'tm')
Inputs may be any that keep to these rules, and one draw needn't show every extreme that they name: partners pairs the 64 blocks: partners[partners[b]] = b and partners[b] != b for every block b.
All inputs are finite; a program needn't handle non-finite values.
Results may differ from a plain program's by a relative error of at most 0.014.
Values may be sent and summed in bfloat16 or wider, within the bound.
No kernel may reach another device: no remote copies, remote signals or barrier semaphores. Data moves between devices by JAX's collectives and lax.ppermute only.
A program may use at most 64 MiB of HBM per device.

v0:
```python
import jax
import jax.numpy as jnp
from jax import lax
from jax.sharding import PartitionSpec as P

F2 = 32
C_DEV = 8
REACH = 6
LEFT = 25
RIGHT = 24
LEAD = 5


def conv_valid(values, weight, stride):
    return lax.conv_general_dilated(
        values[None],
        weight,
        (1, stride),
        "VALID",
        dimension_numbers=("NCHW", "OIHW", "NCHW"),
        preferred_element_type=jnp.float32,
    )[0]


def edge_mask(rows, length, row0, col0, span):
    c = lax.axis_index("chan")
    t = lax.axis_index("tm")
    total_rows = lax.axis_size("chan") * C_DEV
    last = lax.axis_size("tm") - 1
    row = c * C_DEV + row0 + lax.broadcasted_iota(jnp.int32, (rows, length), 0)
    col = col0 + lax.broadcasted_iota(jnp.int32, (rows, length), 1)
    ok = (row >= 0) & (row < total_rows)
    ok = ok & ((t > 0) | (col >= 0)) & ((t < last) | (col < span))
    return ok[None]


def activate(values, bias, mask):
    return jnp.where(mask, jnp.maximum(values + bias[:, None, None], 0.0), 0.0).astype(jnp.bfloat16)


def on_device(
    recorded,
    partners,
    offsets,
    first_weight,
    first_bias,
    second_weight,
    second_bias,
    loop_weight,
    third_weight,
    third_bias,
    fourth_weight,
    fourth_bias,
):
    blocks = lax.axis_size("chan")
    times_here, nc = recorded.shape
    wide = C_DEV + 2 * REACH
    padded = jnp.pad(recorded, ((0, 0), (REACH, 3 * C_DEV - REACH)))
    windows = jnp.concatenate(
        [padded[:, k * C_DEV : k * C_DEV + nc].reshape(times_here, blocks, C_DEV) for k in range(3)], axis=2
    )[:, :, :wide]
    outgoing = jnp.transpose(windows, (1, 0, 2))
    arrived = lax.all_to_all(outgoing, "chan", split_axis=0, concat_axis=0, tiled=True)
    times = blocks * times_here
    strain = jnp.transpose(arrived.reshape(times, wide))
    tms = lax.axis_size("tm")
    up = [(i, i + 1) for i in range(tms - 1)]
    down = [(j, i) for i, j in up]
    before = lax.ppermute(strain[:, times - LEFT :], "tm", up)
    after = lax.ppermute(strain[:, :RIGHT], "tm", down)
    strain_wide = jnp.concatenate([before, strain, after], axis=1)

    first_pre = conv_valid(strain_wide[None], first_weight, 1)
    first = activate(first_pre, first_bias, edge_mask(wide - 6, first_pre.shape[2], 3 - REACH, 3 - LEFT, times))

    quarter = times // 4
    length = quarter + 2 * LEAD
    start = (3 - LEFT) + 4 * LEAD + 2
    first_cut = first[:, :, -start : -start + 4 * (length - 1) + 7]
    pre_second = (conv_valid(first_cut, second_weight, 4) + second_bias[:, None, None]).astype(jnp.bfloat16)

    own_offset = offsets[0]
    crossing = lax.dynamic_slice(pre_second, (0, own_offset - 3, 0), (F2, 7, length))
    packed = crossing.reshape(blocks, 1, -1)
    moved = jnp.take(
        lax.all_to_all(packed, "chan", split_axis=0, concat_axis=1, tiled=True), partners, axis=1
    )
    came = lax.all_to_all(moved, "chan", split_axis=1, concat_axis=0, tiled=True).reshape(F2, 7, length)
    flipped = came[:, ::-1, :]
    coupling = jnp.einsum("kof,fkt->okt", loop_weight, flipped, preferred_element_type=jnp.float32)
    extra = lax.dynamic_update_slice(
        jnp.zeros((F2, C_DEV, length), jnp.float32), coupling, (0, own_offset - 3, 0)
    )
    second_mask = edge_mask(C_DEV, length, 0, -LEAD, quarter)
    second = jnp.where(second_mask, jnp.maximum(pre_second.astype(jnp.float32) + extra, 0.0), 0.0).astype(
        jnp.bfloat16
    )

    ring_up = [(i, i + 1) for i in range(blocks - 1)]
    ring_down = [(j, i) for i, j in ring_up]
    above = lax.ppermute(second[:, C_DEV - REACH :, :], "chan", ring_up)
    below = lax.ppermute(second[:, :REACH, :], "chan", ring_down)
    second_wide = jnp.concatenate([above, second, below], axis=1)

    third_pre = conv_valid(second_wide, third_weight, 1)
    third = activate(third_pre, third_bias, edge_mask(wide - 6, third_pre.shape[2], 3 - REACH, 3 - LEAD, quarter))
    cut = 4 * (quarter // 4 - 1) + 7
    third_cut = third[:, :, LEAD - 5 : LEAD - 5 + cut]
    return activate(conv_valid(third_cut, fourth_weight, 4), fourth_bias, True)


def solution(mesh):
    return jax.shard_map(
        on_device,
        mesh=mesh,
        in_specs=(
            P(("tm", "chan"), None),
            P(),
            P("chan"),
            P(),
            P(),
            P(),
            P(),
            P(),
            P(),
            P(),
            P(),
            P(),
        ),
        out_specs=P(None, "chan", "tm"),
        check_vma=False,
    )
```

profile of v0, /device:TPU:1, one launch (start us, length us, event | category | flops | bytes accessed | tf_op | source)
XLA Modules:
  0.0 206.3 jit_solution(7758732325334072656)
XLA Ops:
  2.4 13.1 %all-to-all-start = ((bf16[64,2,320]{2,1,0:T(2,128)(2,1)}), bf16[64,2,320]{2,1,0:T(2,128)(2,1)S(1)}, u32[]{:S(2)}, u32[]{:S(2)}) async-start(bf16[64,2,320]{2,1,0:T(2,128)(2,1)} %reshape.253), calls=%async_computation | async-start | bytes 196608 | tf_op jit(solution)/shard_map/all_to_all | solution.py:63
  15.7 10.0 %all-to-all-done = bf16[64,2,320]{2,1,0:T(2,128)(2,1)S(1)} async-done(((bf16[64,2,320]{2,1,0:T(2,128)(2,1)}), bf16[64,2,320]{2,1,0:T(2,128)(2,1)S(1)}, u32[]{:S(2)}, u32[]{:S(2)}) %all-to-all-start) | async-done | bytes 81952 | tf_op jit(solution)/shard_map/all_to_all | solution.py:63
  26.5 3.2 %collective-permute-start = (bf16[20,25]{1,0:T(8,128)(2,1)S(1)}, bf16[20,25]{1,0:T(8,128)(2,1)S(1)}, u32[]{:S(2)}, u32[]{:S(2)}) collective-permute-start(bf16[20,25]{1,0:T(8,128)(2,1)S(1)} %slice.46), channel_id=1, source_target_pairs={{0,1},{1,2},{2,3},{4,5},{5,6},{6,7},{8,9},{9,10},{10,11},{12,13},{... | collective-permute-start | bytes 3008 | tf_op jit(solution)/shard_map/ppermute | solution.py:69
  29.7 1.3 collective-permute-start.1
  31.7 2.4 %collective-permute-done.1 = bf16[20,24]{1,0:T(8,128)(2,1)S(1)} collective-permute-done((bf16[20,24]{1,0:T(8,128)(2,1)S(1)}, bf16[20,24]{1,0:T(8,128)(2,1)S(1)}, u32[]{:S(2)}, u32[]{:S(2)}) %collective-permute-start.1) | collective-permute-done | bytes 992 | tf_op jit(solution)/shard_map/ppermute | solution.py:70
  34.5 2.3 %copy.88 = bf16[1,20,8,269]{2,0,3,1:T(2,128)(2,1)S(1)} copy(bf16[1,20,8,269]{3,2,1,0:T(8,128)(2,1)S(1)} %fusion.52) | data formatting | bytes 172160 | tf_op jit(solution)/shard_map/conv_general_dilated | solution.py:15
  36.9 42.6 %add_maximum_fusion = bf16[14,8,263,16]{3,1,2,0:T(8,128)(2,1)} fusion(bf16[1,20,8,269]{2,0,3,1:T(2,128)(2,1)S(1)} %copy.88, f32[16]{0:T(128)S(1)} %copy-done.7, pred[8,263]{0,1:T(8,128)(4,1)S(1)} %copy-done.9, bf16[16,1,7,7]{0,3,2,1:T(8,128)(2,1)S(1)} %copy-done.6), kind=kOutput, calls=%fused_computation.3 | convolution fusion | flops 48072192 | bytes 1032408 | tf_op jit(solution)/shard_map/conv_general_dilated | solution.py:15
  79.5 7.4 %copy.90 = bf16[14,8,263,16]{2,1,3,0:T(8,128)(2,1)S(1)} copy(bf16[14,8,263,16]{3,1,2,0:T(8,128)(2,1)} %add_maximum_fusion) | data formatting | bytes 1885184 | tf_op jit(solution)/shard_map/max | solution.py:38
  86.9 1.1 reshape.198
  88.3 1.6 reshape.201
  89.9 6.4 %copy.92 = bf16[16,14,1,8,264]{0,3,4,1,2:T(8,128)(2,1)} copy(bf16[16,14,1,8,264]{4,3,0,1,2:T(8,128)(2,1)S(1)} %reshape.201) | data formatting | bytes 1892352 | tf_op jit(solution)/shard_map/conv_general_dilated | solution.py:15
  96.3 1.0 slice.50
  97.3 12.9 %fusion.28 = f32[8,8,66,32]{3,1,2,0:T(8,128)} fusion(bf16[32,16,7,7]{0,1,3,2:T(8,128)(2,1)S(1)} %copy-done.5, bf16[16,14,1,7,6]{0,3,4,1,2:T(8,128)(2,1)S(1)} %slice.50, bf16[16,14,1,8,264]{0,3,4,1,2:T(8,128)(2,1)} %copy.92, pred[8,66]{0,1:T(8,128)(4,1)S(1)} %copy-done.11), kind=kOutput, calls=%fused_computation.30 | convolution fusion | flops 214981632 | bytes 1556368 | tf_op jit(solution)/shard_map/conv_general_dilated | solution.py:15
  110.2 2.1 %copy.93 = f32[8,8,66,32]{2,1,3,0:T(8,128)S(1)} copy(f32[8,8,66,32]{3,1,2,0:T(8,128)} %fusion.28) | data formatting | bytes 1081344 | tf_op jit(solution)/shard_map/conv_general_dilated | solution.py:15
  112.9 1.3 reshape.251
  114.2 5.9 %all-to-all-start.1 = ((bf16[64,1,1827]{2,1,0:T(2,128)(2,1)}), bf16[64,1,1827]{2,1,0:T(2,128)(2,1)S(1)}, u32[]{:S(2)}, u32[]{:S(2)}) async-start(bf16[64,1,1827]{2,1,0:T(2,128)(2,1)} %reshape.251), calls=%async_computation.1 | async-start | bytes 983040 | tf_op jit(solution)/shard_map/all_to_all | solution.py:86
  120.2 16.6 %all-to-all-done.1 = bf16[64,1,1827]{2,1,0:T(2,128)(2,1)S(1)} async-done(((bf16[64,1,1827]{2,1,0:T(2,128)(2,1)}), bf16[64,1,1827]{2,1,0:T(2,128)(2,1)S(1)}, u32[]{:S(2)}, u32[]{:S(2)}) %all-to-all-start.1) | async-done | bytes 233888 | tf_op jit(solution)/shard_map/all_to_all | solution.py:86
  137.7 1.2 copy.96
  138.8 6.6 %all-to-all-start.2 = ((bf16[1,64,1827]{2,0,1:T(2,128)(2,1)}), bf16[1,64,1827]{2,0,1:T(2,128)(2,1)S(1)}, u32[]{:S(2)}, u32[]{:S(2)}) async-start(bf16[1,64,1827]{2,0,1:T(2,128)(2,1)} %copy.96), calls=%async_computation.2 | async-start | bytes 983040 | tf_op jit(solution)/shard_map/all_to_all | solution.py:88
  145.6 16.3 %all-to-all-done.2 = bf16[1,64,1827]{2,0,1:T(2,128)(2,1)S(1)} async-done(((bf16[1,64,1827]{2,0,1:T(2,128)(2,1)}), bf16[1,64,1827]{2,0,1:T(2,128)(2,1)S(1)}, u32[]{:S(2)}, u32[]{:S(2)}) %all-to-all-start.2) | async-done | bytes 233888 | tf_op jit(solution)/shard_map/all_to_all | solution.py:88
  162.0 1.6 reduce
  164.8 3.3 %collective-permute-start.2 = (bf16[32,6,522]{2,0,1:T(8,128)(2,1)S(1)}, bf16[32,6,522]{2,0,1:T(8,128)(2,1)S(1)}, u32[]{:S(2)}, u32[]{:S(2)}) collective-permute-start(bf16[32,6,522]{2,0,1:T(8,128)(2,1)S(1)} %get-tuple-element.7), channel_id=1, source_target_pairs={{0,4},{4,8},{8,12},{12,16},{16,20},{20,24},{24,28},{28,32},{32,36}... | collective-permute-start | bytes 601352 | tf_op jit(solution)/shard_map/ppermute | solution.py:101
  168.1 1.9 collective-permute-start.3
  170.2 1.1 collective-permute-done.2
  171.3 4.4 %collective-permute-done.3 = bf16[32,6,522]{2,0,1:T(8,128)(2,1)S(1)} collective-permute-done((bf16[32,6,522]{2,0,1:T(8,128)(2,1)S(1)}, bf16[32,6,522]{2,0,1:T(8,128)(2,1)S(1)}, u32[]{:S(2)}, u32[]{:S(2)}) %collective-permute-start.3) | collective-permute-done | bytes 200480 | tf_op jit(solution)/shard_map/ppermute | solution.py:102
  175.9 1.4 reshape.208
  177.3 3.6 %copy.99 = bf16[32,20,1,8,66]{0,3,4,1,2:T(8,128)(2,1)} copy(bf16[32,20,1,8,66]{4,3,0,1,2:T(8,128)(2,1)S(1)} %reshape.208) | data formatting | bytes 1351680 | tf_op jit(solution)/shard_map/conv_general_dilated | solution.py:15
  180.8 1.0 slice.54
  181.9 14.1 %broadcast_select_fusion = f32[14,8,66,32]{3,1,2,0:T(8,128)} fusion(pred[8,66]{0,1:T(8,128)(4,1)S(1)} %copy-done.10, bf16[32,32,7,7]{1,0,3,2:T(8,128)(2,1)S(1)} %copy-done, bf16[32,20,1,7,6]{0,3,4,1,2:T(8,128)(2,1)S(1)} %slice.54, bf16[32,20,1,8,66]{0,3,4,1,2:T(8,128)(2,1)} %copy.99), kind=kOutput, calls=%fused_computation.29 | convolution fusion | flops 744250368 | bytes 1776656 | tf_op jit(solution)/shard_map/conv_general_dilated | solution.py:15
  196.0 2.9 %copy.100 = f32[14,8,66,32]{2,1,3,0:T(8,128)S(1)} copy(f32[14,8,66,32]{3,1,2,0:T(8,128)} %broadcast_select_fusion) | data formatting | bytes 1892352 | tf_op jit(solution)/shard_map/conv_general_dilated | solution.py:15
  200.8 1.4 copy.102
  202.3 2.7 %fusion.34 = f32[8,8,17,64]{3,1,2,0:T(8,128)S(1)} fusion(bf16[64,32,7,7]{0,1,3,2:T(8,128)(2,1)} %param.22, bf16[32,14,1,7,6]{0,3,4,1,2:T(8,128)(2,1)S(1)} %slice.58, bf16[32,14,1,8,68]{0,3,4,1,2:T(8,128)(2,1)S(1)} %copy.102, pred[8,17]{0,1:T(8,128)(4,1)S(1)} %copy-done.12), kind=kOutput, calls=%fused_computation.35 | convolution fusion | flops 220026880 | bytes 1004424 | tf_op jit(solution)/shard_map/conv_general_dilated | solution.py:15
  (81 shorter events, 10.1 us)
Async XLA Ops:
  0.0 181.9 %copy-start = (bf16[32,32,7,7]{1,0,3,2:T(8,128)(2,1)S(1)}, bf16[32,32,7,7]{1,0,3,2:T(8,128)(2,1)}, u32[]{:S(2)}) copy-start(bf16[32,32,7,7]{1,0,3,2:T(8,128)(2,1)} %param.20) | copy-start | bytes 301060
  0.0 31.0 %copy-start.8 = (s32[64]{0:T(128)S(1)}, s32[64]{0:T(128)}, u32[]{:S(2)}) copy-start(s32[64]{0:T(128)} %param.13) | copy-start | bytes 772
  2.4 34.4 %copy-start.6 = (bf16[16,1,7,7]{0,3,2,1:T(8,128)(2,1)S(1)}, bf16[16,1,7,7]{0,3,2,1:T(8,128)(2,1)}, u32[]{:S(2)}) copy-start(bf16[16,1,7,7]{0,3,2,1:T(8,128)(2,1)} %param.15) | copy-start | bytes 4708
  2.4 34.5 %copy-start.7 = (f32[16]{0:T(128)S(1)}, f32[16]{0:T(128)}, u32[]{:S(2)}) copy-start(f32[16]{0:T(128)} %param.16) | copy-start | bytes 196
  2.4 34.5 %copy-start.9 = (pred[8,263]{0,1:T(8,128)(4,1)S(1)}, pred[8,263]{0,1:T(8,128)(4,1)}, u32[]{:S(2)}) copy-start(pred[8,263]{0,1:T(8,128)(4,1)} %constant.85) | copy-start | bytes 6316
  2.4 23.3 %all-to-all-start = ((bf16[64,2,320]{2,1,0:T(2,128)(2,1)}), bf16[64,2,320]{2,1,0:T(2,128)(2,1)S(1)}, u32[]{:S(2)}, u32[]{:S(2)}) async-start(bf16[64,2,320]{2,1,0:T(2,128)(2,1)} %reshape.253), calls=%async_computation | async-start | bytes 196608 | tf_op jit(solution)/shard_map/all_to_all | solution.py:63
  26.5 7.6 %collective-permute-start = (bf16[20,25]{1,0:T(8,128)(2,1)S(1)}, bf16[20,25]{1,0:T(8,128)(2,1)S(1)}, u32[]{:S(2)}, u32[]{:S(2)}) collective-permute-start(bf16[20,25]{1,0:T(8,128)(2,1)S(1)} %slice.46), channel_id=1, source_target_pairs={{0,1},{1,2},{2,3},{4,5},{5,6},{6,7},{8,9},{9,10},{10,11},{12,13},{... | collective-permute-start | bytes 3008 | tf_op jit(solution)/shard_map/ppermute | solution.py:69
  29.7 4.4 %collective-permute-start.1 = (bf16[20,24]{1,0:T(8,128)(2,1)S(1)}, bf16[20,24]{1,0:T(8,128)(2,1)S(1)}, u32[]{:S(2)}, u32[]{:S(2)}) collective-permute-start(bf16[20,24]{1,0:T(8,128)(2,1)S(1)} %slice.47), channel_id=1, source_target_pairs={{1,0},{2,1},{3,2},{5,4},{6,5},{7,6},{9,8},{10,9},{11,10},{13,12},{... | collective-permute-start | bytes 2888 | tf_op jit(solution)/shard_map/ppermute | solution.py:70
  89.9 7.4 %copy-start.5 = (bf16[32,16,7,7]{0,1,3,2:T(8,128)(2,1)S(1)}, bf16[32,16,7,7]{0,1,3,2:T(8,128)(2,1)}, u32[]{:S(2)}) copy-start(bf16[32,16,7,7]{0,1,3,2:T(8,128)(2,1)} %param.17) | copy-start | bytes 150532
  89.9 7.4 %copy-start.11 = (pred[8,66]{0,1:T(8,128)(4,1)S(1)}, pred[8,66]{0,1:T(8,128)(4,1)}, u32[]{:S(2)}) copy-start(pred[8,66]{0,1:T(8,128)(4,1)} %constant.84) | copy-start | bytes 1588
  110.2 2.4 %copy-start.3 = (f32[32]{0:T(128)S(1)}, f32[32]{0:T(128)}, u32[]{:S(2)}) copy-start(f32[32]{0:T(128)} %param.18) | copy-start | bytes 388
  114.2 22.5 %all-to-all-start.1 = ((bf16[64,1,1827]{2,1,0:T(2,128)(2,1)}), bf16[64,1,1827]{2,1,0:T(2,128)(2,1)S(1)}, u32[]{:S(2)}, u32[]{:S(2)}) async-start(bf16[64,1,1827]{2,1,0:T(2,128)(2,1)} %reshape.251), calls=%async_computation.1 | async-start | bytes 983040 | tf_op jit(solution)/shard_map/all_to_all | solution.py:86
  136.8 27.6 %copy-start.1 = (bf16[7,32,32]{2,1,0:T(8,128)(2,1)S(1)}, bf16[7,32,32]{2,1,0:T(8,128)(2,1)}, u32[]{:S(2)}) copy-start(bf16[7,32,32]{2,1,0:T(8,128)(2,1)} %param.19) | copy-start | bytes 43012
  138.8 23.1 %all-to-all-start.2 = ((bf16[1,64,1827]{2,0,1:T(2,128)(2,1)}), bf16[1,64,1827]{2,0,1:T(2,128)(2,1)S(1)}, u32[]{:S(2)}, u32[]{:S(2)}) async-start(bf16[1,64,1827]{2,0,1:T(2,128)(2,1)} %copy.96), calls=%async_computation.2 | async-start | bytes 983040 | tf_op jit(solution)/shard_map/all_to_all | solution.py:88
  164.8 6.5 %collective-permute-start.2 = (bf16[32,6,522]{2,0,1:T(8,128)(2,1)S(1)}, bf16[32,6,522]{2,0,1:T(8,128)(2,1)S(1)}, u32[]{:S(2)}, u32[]{:S(2)}) collective-permute-start(bf16[32,6,522]{2,0,1:T(8,128)(2,1)S(1)} %get-tuple-element.7), channel_id=1, source_target_pairs={{0,4},{4,8},{8,12},{12,16},{16,20},{20,24},{24,28},{28,32},{32,36}... | collective-permute-start | bytes 601352 | tf_op jit(solution)/shard_map/ppermute | solution.py:101
  168.1 7.5 %collective-permute-start.3 = (bf16[32,6,522]{2,0,1:T(8,128)(2,1)S(1)}, bf16[32,6,522]{2,0,1:T(8,128)(2,1)S(1)}, u32[]{:S(2)}, u32[]{:S(2)}) collective-permute-start(bf16[32,6,522]{2,0,1:T(8,128)(2,1)S(1)} %get-tuple-element.8), channel_id=1, source_target_pairs={{4,0},{8,4},{12,8},{16,12},{20,16},{24,20},{28,24},{32,28},{36,32}... | collective-permute-start | bytes 601352 | tf_op jit(solution)/shard_map/ppermute | solution.py:102
  175.9 6.0 %copy-start.10 = (pred[8,66]{0,1:T(8,128)(4,1)S(1)}, pred[8,66]{0,1:T(8,128)(4,1)}, u32[]{:S(2)}) copy-start(pred[8,66]{0,1:T(8,128)(4,1)} %constant.83) | copy-start | bytes 1588
  198.9 0.7 copy-start.2
  199.8 2.4 %copy-start.12 = (pred[8,17]{0,1:T(8,128)(4,1)S(1)}, pred[8,17]{0,1:T(8,128)(4,1)}, u32[]{:S(2)}) copy-start(pred[8,17]{0,1:T(8,128)(4,1)} %constant.82) | copy-start | bytes 412
  202.3 2.9 %copy-start.4 = (f32[64]{0:T(128)S(1)}, f32[64]{0:T(128)}, u32[]{:S(2)}) copy-start(f32[64]{0:T(128)} %param.23) | copy-start | bytes 772
where the time goes:
time: 210 us; the launch traced here: 206 us
  matrix products  72.6 us (35%)
  waiting for transfers between devices  50.8 us (24%)
  local copies, waits for them, and re-layouts  42.9 us (20%)
  starting transfers between devices  35.4 us (17%)
  other arithmetic  3.07 us (1%)
    conv_general_dilated x4, matrix products, conv_valid(): lax.conv_general_dilated(values[None], weight, (1, stride), 'VALID', dime...  72.3 us
    conv_general_dilated x17, local copies, waits for them, and re-layouts, conv_valid(): lax.conv_general_dilated(values[None], weight, (1, stride), 'VALID', dime...  25.8 us
    all_to_all x1, waiting for transfers between devices, on_device(): lax.all_to_all(packed, 'chan', split_axis=0, concat_axis=1, tiled=True)  16.6 us
    all_to_all x1, waiting for transfers between devices, on_device(): lax.all_to_all(moved, 'chan', split_axis=1, concat_axis=0, tiled=True)  16.3 us
    all_to_all x1, starting transfers between devices, on_device(): lax.all_to_all(outgoing, 'chan', split_axis=0, concat_axis=0, tiled=True)  13.1 us
    all_to_all x1, waiting for transfers between devices, on_device(): lax.all_to_all(outgoing, 'chan', split_axis=0, concat_axis=0, tiled=True)  10 us
    max x2, local copies, waits for them, and re-layouts, activate(): jnp.maximum(values + bias[:, None, None], 0.0)  8.46 us
    all_to_all x1, starting transfers between devices, on_device(): lax.all_to_all(moved, 'chan', split_axis=1, concat_axis=0, tiled=True)  6.65 us
  transfers between devices with their start and end apart: 7, of which 6 were waited for; matrix products, arithmetic and copies ran while one was open for 0% of the time, Pallas kernels for 0%

commit v1 on v0

v1 whole, which is shorter than its diff:
```python
import numpy as np
import jax
import jax.numpy as jnp
from jax import lax
from jax.experimental import pallas as pl
from jax.sharding import PartitionSpec as P

F2 = 32
C_DEV = 8
REACH = 6
PH = 4
WL = 7
WR = 8
LEAD = 5
LANE_BLOCK = 256


def banded(x, w_all, bias, mask, *, groups, shifts, n_out, relu, select=None, n_sel=0):
    flat = x.ndim == 2
    k_all = w_all.shape[1]
    row_step = k_all // 7
    r_out = (x.shape[0] // row_step if flat else x.shape[0]) - 6
    n_in = x.shape[-1]
    fout = w_all.shape[0] // (groups * shifts)
    if select is None:
        out_shape = (r_out, groups * fout, n_out)
    else:
        out_shape = (r_out, PH * fout, n_sel)

    def kernel(x_ref, w_ref, b_ref, m_ref, *rest):
        if select is None:
            (o_ref,) = rest
        else:
            s_ref, o_ref = rest

        def row(r, carry):
            if flat:
                xs = x_ref[r * row_step : r * row_step + k_all, :]
            else:
                xs = x_ref[pl.ds(r, 7), :, :].reshape(k_all, n_in)
            z = jnp.dot(w_ref[...], xs, preferred_element_type=jnp.float32)
            m_row = m_ref[r]
            for g in range(groups):
                base = g * shifts * fout
                acc = z[base : base + fout, 0:n_out]
                for s in range(1, shifts):
                    acc = acc + z[base + s * fout : base + (s + 1) * fout, s : s + n_out]
                acc = acc + b_ref[...]
                if relu:
                    acc = jnp.maximum(acc, 0.0)
                acc = (acc * m_row[g : g + 1, :]).astype(jnp.bfloat16)
                if select is None:
                    o_ref[r, g * fout : (g + 1) * fout, :] = acc
                else:
                    y = jnp.dot(acc, s_ref[...], preferred_element_type=jnp.float32)
                    for p in range(PH):
                        o_ref[r, p * fout : (p + 1) * fout, :] = y[
                            :, p * LANE_BLOCK : p * LANE_BLOCK + n_sel
                        ].astype(jnp.bfloat16)
            return carry

        if flat:
            for r in range(r_out):
                row(r, 0)
        else:
            lax.fori_loop(0, r_out, row, 0)

    args = [x, w_all, bias.reshape(fout, 1).astype(jnp.float32), mask]
    if select is not None:
        args.append(select)
    return pl.pallas_call(kernel, out_shape=jax.ShapeDtypeStruct(out_shape, jnp.bfloat16))(*args)


def weights_stride1(w):
    fout, fin = w.shape[:2]
    return jnp.transpose(w, (3, 0, 2, 1)).reshape(7 * fout, 7 * fin)


def weights_stride4(w, shifts, lag):
    fout, fin = w.shape[:2]
    s = np.arange(shifts)[:, None]
    p = np.arange(PH)[None, :]
    b = 4 * s + p - lag
    ok = (b >= 0) & (b <= 6)
    taps = jnp.take(w, np.clip(b, 0, 6).reshape(-1), axis=3).reshape(fout, fin, 7, shifts, PH)
    taps = jnp.where(ok[None, None, None], taps, jnp.zeros((), w.dtype))
    return jnp.transpose(taps, (3, 0, 2, 4, 1)).reshape(shifts * fout, 7 * PH * fin)


def weights_first(w):
    fout = w.shape[0]
    p = np.arange(PH)[:, None, None]
    dd = np.arange(4)[None, :, None]
    q = np.arange(PH)[None, None, :]
    b = 4 * (dd - 1) + q - p + 3
    ok = (b >= 0) & (b <= 6)
    taps = jnp.take(w[:, 0], np.clip(b, 0, 6).reshape(-1), axis=2).reshape(fout, 7, PH, 4, PH)
    taps = jnp.where(ok[None, None], taps, jnp.zeros((), w.dtype))
    return jnp.transpose(taps, (2, 3, 0, 1, 4)).reshape(PH * 4 * fout, 7 * PH)


def phase_select(n_in, n_sel):
    sel = np.zeros((n_in, PH * LANE_BLOCK), np.float32)
    for p in range(PH):
        for u in range(n_sel):
            if PH * u + p < n_in:
                sel[PH * u + p, p * LANE_BLOCK + u] = 1.0
    return jnp.asarray(sel, jnp.bfloat16)


def edge_mask(rows, groups, length, row0, time_of):
    c = lax.axis_index("chan")
    t = lax.axis_index("tm")
    total_rows = lax.axis_size("chan") * C_DEV
    last = lax.axis_size("tm") - 1
    shape = (rows, groups, length)
    row = c * C_DEV + row0 + lax.broadcasted_iota(jnp.int32, shape, 0)
    tau, span = time_of(lax.broadcasted_iota(jnp.int32, shape, 1), lax.broadcasted_iota(jnp.int32, shape, 2))
    ok = (row >= 0) & (row < total_rows)
    ok = ok & ((t > 0) | (tau >= 0)) & ((t < last) | (tau < span))
    return ok.astype(jnp.float32)


def on_device(
    recorded,
    partners,
    offsets,
    first_weight,
    first_bias,
    second_weight,
    second_bias,
    loop_weight,
    third_weight,
    third_bias,
    fourth_weight,
    fourth_bias,
):
    blocks = lax.axis_size("chan")
    times_here, nc = recorded.shape
    wide = C_DEV + 2 * REACH
    padded = jnp.pad(recorded, ((0, 0), (REACH, 3 * C_DEV - REACH)))
    windows = jnp.concatenate(
        [padded[:, k * C_DEV : k * C_DEV + nc].reshape(times_here, blocks, C_DEV) for k in range(3)], axis=2
    )[:, :, :wide]
    outgoing = jnp.transpose(windows, (1, 0, 2))
    arrived = lax.all_to_all(outgoing, "chan", split_axis=0, concat_axis=0, tiled=True)
    times = blocks * times_here
    cols = times // PH
    strain = jnp.transpose(arrived.reshape(blocks, times_here // PH, PH, wide), (3, 2, 0, 1)).reshape(wide, PH, cols)
    tms = lax.axis_size("tm")
    up = [(i, i + 1) for i in range(tms - 1)]
    down = [(j, i) for i, j in up]
    before = lax.ppermute(strain[:, :, cols - WL :], "tm", up)
    after = lax.ppermute(strain[:, :, :WR], "tm", down)
    strain_wide = jnp.concatenate([before, strain, after], axis=2)
    n_s = strain_wide.shape[2]

    n_f = n_s - 3
    first_mask = edge_mask(wide - 6, PH, n_f, 3 - REACH, lambda p, v: (PH * (v - (WL - 1)) + p, times))
    first = banded(
        strain_wide.reshape(wide * PH, n_s),
        weights_first(first_weight),
        first_bias,
        first_mask,
        groups=PH,
        shifts=4,
        n_out=n_f,
        relu=True,
    )

    quarter = times // 4
    length = quarter + 2 * LEAD
    pre_second = banded(
        first,
        weights_stride4(second_weight, 3, 2),
        second_bias,
        jnp.ones((C_DEV, 1, length), jnp.float32),
        groups=1,
        shifts=3,
        n_out=length,
        relu=False,
    )

    own_offset = offsets[0]
    crossing = lax.dynamic_slice(pre_second, (own_offset - 3, 0, 0), (7, F2, length))
    packed = crossing.reshape(blocks, 1, -1)
    moved = jnp.take(
        lax.all_to_all(packed, "chan", split_axis=0, concat_axis=1, tiled=True), partners, axis=1
    )
    came = lax.all_to_all(moved, "chan", split_axis=1, concat_axis=0, tiled=True).reshape(7, F2, length)
    flipped = came[::-1]
    coupling = jnp.einsum("kof,kft->kot", loop_weight, flipped, preferred_element_type=jnp.float32)
    extra = lax.dynamic_update_slice(
        jnp.zeros((C_DEV, F2, length), jnp.float32), coupling, (own_offset - 3, 0, 0)
    )
    second_mask = edge_mask(C_DEV, 1, length, 0, lambda p, j: (j - LEAD, quarter))
    second = (jnp.maximum(pre_second.astype(jnp.float32) + extra, 0.0) * second_mask).astype(jnp.bfloat16)

    ring_up = [(i, i + 1) for i in range(blocks - 1)]
    ring_down = [(j, i) for i, j in ring_up]
    above = lax.ppermute(second[C_DEV - REACH :], "chan", ring_up)
    below = lax.ppermute(second[:REACH], "chan", ring_down)
    second_wide = jnp.concatenate([above, second, below], axis=0)

    n_t = length - 6
    n_sel = quarter // 4 + 1
    third_mask = edge_mask(wide - 6, 1, n_t, 3 - REACH, lambda p, j: (j - (LEAD - 3), quarter))
    third = banded(
        second_wide,
        weights_stride1(third_weight),
        third_bias,
        third_mask,
        groups=1,
        shifts=7,
        n_out=n_t,
        relu=True,
        select=phase_select(n_t, n_sel),
        n_sel=n_sel,
    )
    features = banded(
        third,
        weights_stride4(fourth_weight, 2, 0),
        fourth_bias,
        jnp.ones((C_DEV, 1, quarter // 4), jnp.float32),
        groups=1,
        shifts=2,
        n_out=quarter // 4,
        relu=True,
    )
    return jnp.transpose(features, (1, 0, 2))


def solution(mesh):
    return jax.shard_map(
        on_device,
        mesh=mesh,
        in_specs=(
            P(("tm", "chan"), None),
            P(),
            P("chan"),
            P(),
            P(),
            P(),
            P(),
            P(),
            P(),
            P(),
            P(),
            P(),
        ),
        out_specs=P(None, "chan", "tm"),
        check_vma=False,
    )
```

time: 210 us -> 131 us (0.62); the launches traced: 206 us -> 130 us
  matrix products: 72.6 us -> 0.22 us
  Pallas kernels: 0 us -> 24.2 us
  local copies, waits for them, and re-layouts: 42.9 us -> 22.7 us
  waiting for transfers between devices: 50.8 us -> 40.3 us
  other arithmetic: 3.07 us -> 6.34 us
    conv_general_dilated x4 -> x0, matrix products: 72.3 us -> none  [conv_valid(): lax.conv_general_dilated(values[None], weight, (1, stride), 'VALID', dime...]
    conv_general_dilated x17 -> x0, local copies, waits for them, and re-layouts: 25.8 us -> none  [conv_valid(): lax.conv_general_dilated(values[None], weight, (1, stride), 'VALID', dime...]
    pallas_call x0 -> x4, Pallas kernels: none -> 24.2 us  [banded(): pl.pallas_call(kernel, out_shape=jax.ShapeDtypeStruct(out_shape, jnp.bflo...]
    max x2 -> x0, local copies, waits for them, and re-layouts: 8.46 us -> none  [activate(): jnp.maximum(values + bias[:, None, None], 0.0)]
    reshape x1 -> x11, local copies, waits for them, and re-layouts: 0.34 us -> 6.61 us  [the longest x4 2.75 us: banded(): args = [x, w_all, bias.reshape(fout, 1).astype(jnp.float32), mask]]
    all_to_all x1, waiting for transfers between devices: 16.3 us -> 12.8 us  [on_device(): lax.all_to_all(moved, 'chan', split_axis=1, concat_axis=0, tiled=True)]
    all_to_all x1, waiting for transfers between devices: 10 us -> 6.57 us  [on_device(): lax.all_to_all(outgoing, 'chan', split_axis=0, concat_axis=0, tiled=True)]
    ppermute x4, waiting for transfers between devices: 7.91 us -> 4.88 us  [the longest x1 4.4 us: on_device(): below = lax.ppermute(second[:REACH], 'chan', ring_down)]
  transfers between devices with their start and end apart: 7 -> 7, of which waited for: 6 -> 5; matrix products, arithmetic and copies ran while one was open for 0% -> 11% of each run, Pallas kernels for 0% -> 0%
where the time goes in v1:
time: 131 us; the launch traced here: 130 us
  waiting for transfers between devices  40.3 us (31%)
  starting transfers between devices  35.1 us (27%)
  Pallas kernels  24.2 us (18%)
  local copies, waits for them, and re-layouts  22.7 us (17%)
  other arithmetic  6.34 us (5%)
    pallas_call x4, Pallas kernels, banded(): pl.pallas_call(kernel, out_shape=jax.ShapeDtypeStruct(out_shape, jnp.bflo...  24.2 us
    all_to_all x1, waiting for transfers between devices, on_device(): lax.all_to_all(packed, 'chan', split_axis=0, concat_axis=1, tiled=True)  16 us
    all_to_all x1, starting transfers between devices, on_device(): lax.all_to_all(outgoing, 'chan', split_axis=0, concat_axis=0, tiled=True)  13.1 us
    all_to_all x1, waiting for transfers between devices, on_device(): lax.all_to_all(moved, 'chan', split_axis=1, concat_axis=0, tiled=True)  12.8 us
    all_to_all x1, waiting for transfers between devices, on_device(): lax.all_to_all(outgoing, 'chan', split_axis=0, concat_axis=0, tiled=True)  6.57 us
    all_to_all x1, starting transfers between devices, on_device(): lax.all_to_all(moved, 'chan', split_axis=1, concat_axis=0, tiled=True)  6.5 us
    all_to_all x1, starting transfers between devices, on_device(): lax.all_to_all(packed, 'chan', split_axis=0, concat_axis=1, tiled=True)  5.02 us
    ppermute x1, waiting for transfers between devices, on_device(): below = lax.ppermute(second[:REACH], 'chan', ring_down)  4.4 us
  transfers between devices with their start and end apart: 7, of which 5 were waited for; matrix products, arithmetic and copies ran while one was open for 11% of the time, Pallas kernels for 0%

profile of v1, /device:TPU:1, one launch (start us, length us, event | category | flops | bytes accessed | tf_op | source)
XLA Modules:
  0.0 130.1 jit_solution(17739061156763749226)
XLA Ops:
  0.1 1.0 pad_slice_fusion.2
  1.6 0.9 reshape.278
  2.5 13.1 %all-to-all-start = ((bf16[64,2,320]{2,1,0:T(2,128)(2,1)}), bf16[64,2,320]{2,1,0:T(2,128)(2,1)S(1)}, u32[]{:S(2)}, u32[]{:S(2)}) async-start(bf16[64,2,320]{2,1,0:T(2,128)(2,1)} %reshape.278), calls=%async_computation | async-start | bytes 196608 | tf_op jit(solution)/shard_map/all_to_all | solution.py:146
  17.5 0.8 fusion.10.m_ref
  18.5 0.7 copy.82.w_ref
  19.2 6.6 %all-to-all-done = bf16[64,2,320]{2,1,0:T(2,128)(2,1)S(1)} async-done(((bf16[64,2,320]{2,1,0:T(2,128)(2,1)}), bf16[64,2,320]{2,1,0:T(2,128)(2,1)S(1)}, u32[]{:S(2)}, u32[]{:S(2)}) %all-to-all-start) | async-done | bytes 81952 | tf_op jit(solution)/shard_map/all_to_all | solution.py:146
  26.8 1.3 collective-permute-start.1
  28.1 4.0 %collective-permute-start = (bf16[20,4,7]{0,2,1:T(8,128)(2,1)S(1)}, bf16[20,4,7]{0,2,1:T(8,128)(2,1)S(1)}, u32[]{:S(2)}, u32[]{:S(2)}) collective-permute-start(bf16[20,4,7]{0,2,1:T(8,128)(2,1)S(1)} %slice.40), channel_id=1, source_target_pairs={{0,1},{1,2},{2,3},{4,5},{5,6},{6,7},{8,9},{9,10},{10,11},{12,13},{... | collective-permute-start | bytes 3368 | tf_op jit(solution)/shard_map/ppermute | solution.py:153
  33.0 0.8 copy.85.w_ref
  35.8 0.7 copy.78
  36.5 2.1 %concatenate.18 = bf16[80,512]{1,0:T(8,128)(2,1)S(1)} reshape(bf16[20,4,64,8]{3,2,1,0:T(8,128)(2,1)S(1)} %copy.78) | data formatting | bytes 163840 | tf_op jit(solution)/shard_map/concatenate | solution.py:155
  38.8 0.8 pad_maximum_fusion.3.x_ref
  39.6 4.2 %shard_map.181.x_ref = bf16[14,64,524]{2,1,0:T(8,128)(2,1)} custom-call(bf16[80,527]{1,0:T(8,128)(2,1)} %pad_maximum_fusion.3.x_ref, bf16[256,28]{1,0:T(8,128)(2,1)} %copy.82.w_ref, f32[16,1]{1,0:T(8,128)} %copy.83.b_ref, f32[14,4,524]{2,1,0:T(4,128)} %fusion.10.m_ref), custom_call_target="tpu_custom_call" | custom-call | tf_op jit(solution)/shard_map/pallas_call | solution.py:71
  44.4 4.6 %shard_map.182 = bf16[8,32,522]{2,1,0:T(8,128)(2,1)} custom-call(bf16[14,64,524]{2,1,0:T(8,128)(2,1)} %shard_map.181.x_ref, bf16[96,448]{1,0:T(8,128)(2,1)} %copy.85.w_ref, f32[32,1]{1,0:T(8,128)} %copy.86.b_ref, f32[8,1,522]{2,1,0:T(1,128)} %broadcast_in_dim.116.m_ref), custom_call_target="tpu_custom_call" | custom-call | tf_op jit(solution)/shard_map/pallas_call | solution.py:71
  49.0 1.0 constant_dynamic-slice_fusion
  50.0 1.3 %reshape.276 = bf16[64,1,1827]{2,1,0:T(2,128)(2,1)} reshape(bf16[7,32,522]{2,1,0:T(8,128)(2,1)S(1)} %constant_dynamic-slice_fusion) | data formatting | bytes 467712 | tf_op jit(solution)/shard_map/reshape | solution.py:186
  51.3 5.0 %all-to-all-start.1 = ((bf16[64,1,1827]{2,1,0:T(2,128)(2,1)}), bf16[64,1,1827]{2,1,0:T(2,128)(2,1)S(1)}, u32[]{:S(2)}, u32[]{:S(2)}) async-start(bf16[64,1,1827]{2,1,0:T(2,128)(2,1)} %reshape.276), calls=%async_computation.1 | async-start | bytes 983040 | tf_op jit(solution)/shard_map/all_to_all | solution.py:188
  56.9 16.0 %all-to-all-done.1 = bf16[64,1,1827]{2,1,0:T(2,128)(2,1)S(1)} async-done(((bf16[64,1,1827]{2,1,0:T(2,128)(2,1)}), bf16[64,1,1827]{2,1,0:T(2,128)(2,1)S(1)}, u32[]{:S(2)}, u32[]{:S(2)}) %all-to-all-start.1) | async-done | bytes 233888 | tf_op jit(solution)/shard_map/all_to_all | solution.py:188
  73.0 0.8 gather_fusion.2
  73.9 1.2 copy.88
  75.1 6.5 %all-to-all-start.2 = ((bf16[1,64,1827]{2,0,1:T(2,128)(2,1)}), bf16[1,64,1827]{2,0,1:T(2,128)(2,1)S(1)}, u32[]{:S(2)}, u32[]{:S(2)}) async-start(bf16[1,64,1827]{2,0,1:T(2,128)(2,1)} %copy.88), calls=%async_computation.2 | async-start | bytes 983040 | tf_op jit(solution)/shard_map/all_to_all | solution.py:190
  81.8 0.9 reshape.236.w_ref
  83.7 0.8 copy.92.w_ref
  85.4 12.8 %all-to-all-done.2 = bf16[1,64,1827]{2,0,1:T(2,128)(2,1)S(1)} async-done(((bf16[1,64,1827]{2,0,1:T(2,128)(2,1)}), bf16[1,64,1827]{2,0,1:T(2,128)(2,1)S(1)}, u32[]{:S(2)}, u32[]{:S(2)}) %all-to-all-start.2) | async-done | bytes 233888 | tf_op jit(solution)/shard_map/all_to_all | solution.py:190
  98.2 1.6 %reduce = bf16[64,1827]{1,0:T(8,128)(2,1)S(1)} reduce(bf16[1,64,1827]{2,0,1:T(2,128)(2,1)S(1)} %all-to-all-done.2, bf16[]{:T(256)} %constant.162), dimensions={0}, to_apply=%all_to_all.22.reduce_sub_computation | reduce | bytes 467714 | tf_op jit(solution)/shard_map/all_to_all | solution.py:190
  100.6 3.3 %collective-permute-start.2 = (bf16[6,32,522]{2,1,0:T(8,128)(2,1)S(1)}, bf16[6,32,522]{2,1,0:T(8,128)(2,1)S(1)}, u32[]{:S(2)}, u32[]{:S(2)}) collective-permute-start(bf16[6,32,522]{2,1,0:T(8,128)(2,1)S(1)} %get-tuple-element.5), channel_id=1, source_target_pairs={{0,4},{4,8},{8,12},{12,16},{16,20},{20,24},{24,28},{28,32},{32,36}... | collective-permute-start | bytes 601352 | tf_op jit(solution)/shard_map/ppermute | solution.py:201
  103.9 1.9 %collective-permute-start.3 = (bf16[6,32,522]{2,1,0:T(8,128)(2,1)S(1)}, bf16[6,32,522]{2,1,0:T(8,128)(2,1)S(1)}, u32[]{:S(2)}, u32[]{:S(2)}) collective-permute-start(bf16[6,32,522]{2,1,0:T(8,128)(2,1)S(1)} %get-tuple-element.6), channel_id=1, source_target_pairs={{4,0},{8,4},{12,8},{16,12},{20,16},{24,20},{28,24},{32,28},{36,32}... | collective-permute-start | bytes 601352 | tf_op jit(solution)/shard_map/ppermute | solution.py:202
  107.1 4.4 %collective-permute-done.3 = bf16[6,32,522]{2,1,0:T(8,128)(2,1)S(1)} collective-permute-done((bf16[6,32,522]{2,1,0:T(8,128)(2,1)S(1)}, bf16[6,32,522]{2,1,0:T(8,128)(2,1)S(1)}, u32[]{:S(2)}, u32[]{:S(2)}) %collective-permute-start.3) | collective-permute-done | bytes 200480 | tf_op jit(solution)/shard_map/ppermute | solution.py:202
  111.4 1.1 pad_maximum_fusion.x_ref
  112.5 10.9 %shard_map.183.x_ref = bf16[14,128,129]{2,1,0:T(8,128)(2,1)} custom-call(bf16[20,32,522]{2,1,0:T(8,128)(2,1)} %pad_maximum_fusion.x_ref, bf16[224,224]{1,0:T(8,128)(2,1)} %reshape.236.w_ref, f32[32,1]{1,0:T(8,128)} %copy.90.b_ref, f32[14,1,516]{2,1,0:T(1,128)} %and_convert_fusion.m_ref, bf16[516,1024]{1,0:T(8,128)(2,1)} %constant.122.clone.rest_0_), custom_call_target="tpu_custom_call" | custom-call | tf_op jit(solution)/shard_map/pallas_call | solution.py:71
  124.0 4.5 %shard_map.184 = bf16[8,64,128]{2,1,0:T(8,128)(2,1)} custom-call(bf16[14,128,129]{2,1,0:T(8,128)(2,1)} %shard_map.183.x_ref, bf16[128,896]{1,0:T(8,128)(2,1)} %copy.92.w_ref, f32[64,1]{1,0:T(8,128)} %copy.93.b_ref, f32[8,1,128]{2,1,0:T(1,128)} %broadcast_in_dim.127.m_ref), custom_call_target="tpu_custom_call" | custom-call | tf_op jit(solution)/shard_map/pallas_call | solution.py:71
  128.5 1.6 %copy.94 = bf16[64,8,128]{2,1,0:T(8,128)(2,1)} copy(bf16[64,8,128]{2,0,1:T(8,128)(2,1)} %bitcast.71) | data formatting | bytes 262144 | tf_op jit(solution)/shard_map/transpose | solution.py:230
  (88 shorter events, 11.8 us)
Async XLA Ops:
  0.0 35.1 %copy-start = (bf16[64,32,7,7]{0,1,3,2:T(8,128)(2,1)S(1)}, bf16[64,32,7,7]{0,1,3,2:T(8,128)(2,1)}, u32[]{:S(2)}) copy-start(bf16[64,32,7,7]{0,1,3,2:T(8,128)(2,1)} %param.29) | copy-start | bytes 602116
  0.0 15.7 %copy-start.14 = (s32[64]{0:T(128)S(1)}, s32[64]{0:T(128)}, u32[]{:S(2)}) copy-start(s32[64]{0:T(128)} %constant.159) | copy-start | bytes 772
  0.0 15.7 %copy-start.13 = (s32[12]{0:T(128)S(1)}, s32[12]{0:T(128)}, u32[]{:S(2)}) copy-start(s32[12]{0:T(128)} %constant.160) | copy-start | bytes 148
  0.0 16.4 %copy-start.6 = (pred[4,4,4]{1,0,2:T(4,128)(4,1)S(1)}, pred[4,4,4]{1,0,2:T(4,128)(4,1)}, u32[]{:S(2)}) copy-start(pred[4,4,4]{1,0,2:T(4,128)(4,1)} %constant.129) | copy-start | bytes 196
  0.0 15.6 %copy-start.5 = (bf16[16,1,7,7]{0,3,2,1:T(8,128)(2,1)S(1)}, bf16[16,1,7,7]{0,3,2,1:T(8,128)(2,1)}, u32[]{:S(2)}) copy-start(bf16[16,1,7,7]{0,3,2,1:T(8,128)(2,1)} %param.22) | copy-start | bytes 4708
  0.0 15.7 %copy-start.16 = (s32[64]{0:T(128)S(1)}, s32[64]{0:T(128)}, u32[]{:S(2)}) copy-start(s32[64]{0:T(128)} %param.20) | copy-start | bytes 772
  0.0 16.5 %copy-start.1 = (bf16[32,16,7,7]{0,1,3,2:T(8,128)(2,1)S(1)}, bf16[32,16,7,7]{0,1,3,2:T(8,128)(2,1)}, u32[]{:S(2)}) copy-start(bf16[32,16,7,7]{0,1,3,2:T(8,128)(2,1)} %param.24) | copy-start | bytes 150532
  2.5 14.7 %copy-start.15 = (pred[3,4]{0,1:T(4,128)(4,1)S(1)}, pred[3,4]{0,1:T(4,128)(4,1)}, u32[]{:S(2)}) copy-start(pred[3,4]{0,1:T(4,128)(4,1)} %constant.138) | copy-start | bytes 40
  2.5 23.3 %all-to-all-start = ((bf16[64,2,320]{2,1,0:T(2,128)(2,1)}), bf16[64,2,320]{2,1,0:T(2,128)(2,1)S(1)}, u32[]{:S(2)}, u32[]{:S(2)}) async-start(bf16[64,2,320]{2,1,0:T(2,128)(2,1)} %reshape.278), calls=%async_computation | async-start | bytes 196608 | tf_op jit(solution)/shard_map/all_to_all | solution.py:146
  16.5 2.7 %copy-start.12 = (s32[8]{0:T(128)S(1)}, s32[8]{0:T(128)}, u32[]{:S(2)}) copy-start(s32[8]{0:T(128)} %constant.161) | copy-start | bytes 100
  17.2 14.9 %copy-start.9 = (f32[16]{0:T(128)S(1)}, f32[16]{0:T(128)}, u32[]{:S(2)}) copy-start(f32[16]{0:T(128)} %param.23) | copy-start | bytes 196
  18.5 15.3 %copy-start.10 = (f32[32]{0:T(128)S(1)}, f32[32]{0:T(128)}, u32[]{:S(2)}) copy-start(f32[32]{0:T(128)} %param.25) | copy-start | bytes 388
  26.8 11.9 %collective-permute-start.1 = (bf16[20,4,8]{0,2,1:T(8,128)(2,1)S(1)}, bf16[20,4,8]{0,2,1:T(8,128)(2,1)S(1)}, u32[]{:S(2)}, u32[]{:S(2)}) collective-permute-start(bf16[20,4,8]{0,2,1:T(8,128)(2,1)S(1)} %slice.41), channel_id=1, source_target_pairs={{1,0},{2,1},{3,2},{5,4},{6,5},{7,6},{9,8},{10,9},{11,10},{13,12},{... | collective-permute-start | bytes 3848 | tf_op jit(solution)/shard_map/ppermute | solution.py:154
  28.1 10.5 %collective-permute-start = (bf16[20,4,7]{0,2,1:T(8,128)(2,1)S(1)}, bf16[20,4,7]{0,2,1:T(8,128)(2,1)S(1)}, u32[]{:S(2)}, u32[]{:S(2)}) collective-permute-start(bf16[20,4,7]{0,2,1:T(8,128)(2,1)S(1)} %slice.40), channel_id=1, source_target_pairs={{0,1},{1,2},{2,3},{4,5},{5,6},{6,7},{8,9},{9,10},{10,11},{12,13},{... | collective-permute-start | bytes 3368 | tf_op jit(solution)/shard_map/ppermute | solution.py:153
  49.0 7.4 %copy-start.8 = (pred[2,4]{0,1:T(4,128)(4,1)S(1)}, pred[2,4]{0,1:T(4,128)(4,1)}, u32[]{:S(2)}) copy-start(pred[2,4]{0,1:T(4,128)(4,1)} %constant.147) | copy-start | bytes 28
  51.3 21.7 %all-to-all-start.1 = ((bf16[64,1,1827]{2,1,0:T(2,128)(2,1)}), bf16[64,1,1827]{2,1,0:T(2,128)(2,1)S(1)}, u32[]{:S(2)}, u32[]{:S(2)}) async-start(bf16[64,1,1827]{2,1,0:T(2,128)(2,1)} %reshape.276), calls=%async_computation.1 | async-start | bytes 983040 | tf_op jit(solution)/shard_map/all_to_all | solution.py:188
  73.8 7.8 %copy-start.3 = (bf16[32,32,7,7]{1,0,3,2:T(8,128)(2,1)S(1)}, bf16[32,32,7,7]{1,0,3,2:T(8,128)(2,1)}, u32[]{:S(2)}) copy-start(bf16[32,32,7,7]{1,0,3,2:T(8,128)(2,1)} %param.27) | copy-start | bytes 301060
  75.1 7.7 %copy-start.11 = (f32[32]{0:T(128)S(1)}, f32[32]{0:T(128)}, u32[]{:S(2)}) copy-start(f32[32]{0:T(128)} %param.28) | copy-start | bytes 388
  75.1 23.1 %all-to-all-start.2 = ((bf16[1,64,1827]{2,0,1:T(2,128)(2,1)}), bf16[1,64,1827]{2,0,1:T(2,128)(2,1)S(1)}, u32[]{:S(2)}, u32[]{:S(2)}) async-start(bf16[1,64,1827]{2,0,1:T(2,128)(2,1)} %copy.88), calls=%async_computation.2 | async-start | bytes 983040 | tf_op jit(solution)/shard_map/all_to_all | solution.py:190
  81.6 2.9 %copy-start.7 = (f32[64]{0:T(128)S(1)}, f32[64]{0:T(128)}, u32[]{:S(2)}) copy-start(f32[64]{0:T(128)} %param.30) | copy-start | bytes 772
  81.6 3.7 %copy-start.2 = (bf16[8,32,522]{2,1,0:T(8,128)(2,1)S(1)}, bf16[8,32,522]{2,1,0:T(8,128)(2,1)}, u32[]{:S(2)}) copy-start(bf16[8,32,522]{2,1,0:T(8,128)(2,1)} %shard_map.182) | copy-start | bytes 801796
  85.3 14.9 %copy-start.4 = (bf16[7,32,32]{2,1,0:T(8,128)(2,1)S(1)}, bf16[7,32,32]{2,1,0:T(8,128)(2,1)}, u32[]{:S(2)}) copy-start(bf16[7,32,32]{2,1,0:T(8,128)(2,1)} %param.26) | copy-start | bytes 43012
  100.6 6.4 %collective-permute-start.2 = (bf16[6,32,522]{2,1,0:T(8,128)(2,1)S(1)}, bf16[6,32,522]{2,1,0:T(8,128)(2,1)S(1)}, u32[]{:S(2)}, u32[]{:S(2)}) collective-permute-start(bf16[6,32,522]{2,1,0:T(8,128)(2,1)S(1)} %get-tuple-element.5), channel_id=1, source_target_pairs={{0,4},{4,8},{8,12},{12,16},{16,20},{20,24},{24,28},{28,32},{32,36}... | collective-permute-start | bytes 601352 | tf_op jit(solution)/shard_map/ppermute | solution.py:201
  103.9 7.5 %collective-permute-start.3 = (bf16[6,32,522]{2,1,0:T(8,128)(2,1)S(1)}, bf16[6,32,522]{2,1,0:T(8,128)(2,1)S(1)}, u32[]{:S(2)}, u32[]{:S(2)}) collective-permute-start(bf16[6,32,522]{2,1,0:T(8,128)(2,1)S(1)} %get-tuple-element.6), channel_id=1, source_target_pairs={{4,0},{8,4},{12,8},{16,12},{20,16},{24,20},{28,24},{32,28},{36,32}... | collective-permute-start | bytes 601352 | tf_op jit(solution)/shard_map/ppermute | solution.py:202

commit v2 on v1

--- a/solution.py
+++ b/solution.py
@@ -108,17 +108,43 @@
     return jnp.asarray(sel, jnp.bfloat16)
 
 
-def edge_mask(rows, groups, length, row0, time_of):
-    c = lax.axis_index("chan")
+def edge_mask(rows, groups, length, row0, time_of, block):
     t = lax.axis_index("tm")
     total_rows = lax.axis_size("chan") * C_DEV
     last = lax.axis_size("tm") - 1
     shape = (rows, groups, length)
-    row = c * C_DEV + row0 + lax.broadcasted_iota(jnp.int32, shape, 0)
+    row = block * C_DEV + row0 + lax.broadcasted_iota(jnp.int32, shape, 0)
     tau, span = time_of(lax.broadcasted_iota(jnp.int32, shape, 1), lax.broadcasted_iota(jnp.int32, shape, 2))
     ok = (row >= 0) & (row < total_rows)
     ok = ok & ((t > 0) | (tau >= 0)) & ((t < last) | (tau < span))
     return ok.astype(jnp.float32)
+
+
+def lower_layers(strain_wide, block, first_weight, first_bias, second_weight, second_bias, times, length):
+    wide = C_DEV + 2 * REACH
+    n_s = strain_wide.shape[2]
+    n_f = n_s - 3
+    first_mask = edge_mask(wide - 6, PH, n_f, 3 - REACH, lambda p, v: (PH * (v - (WL - 1)) + p, times), block)
+    first = banded(
+        strain_wide.reshape(wide * PH, n_s),
+        weights_first(first_weight),
+        first_bias,
+        first_mask,
+        groups=PH,
+        shifts=4,
+        n_out=n_f,
+        relu=True,
+    )
+    return banded(
+        first,
+        weights_stride4(second_weight, 3, 2),
+        second_bias,
+        jnp.ones((C_DEV, 1, length), jnp.float32),
+        groups=1,
+        shifts=3,
+        n_out=length,
+        relu=False,
+    )
 
 
 def on_device(
@@ -136,64 +162,45 @@
     fourth_bias,
 ):
     blocks = lax.axis_size("chan")
+    me = lax.axis_index("chan")
+    mate = partners[me]
     times_here, nc = recorded.shape
     wide = C_DEV + 2 * REACH
     padded = jnp.pad(recorded, ((0, 0), (REACH, 3 * C_DEV - REACH)))
     windows = jnp.concatenate(
         [padded[:, k * C_DEV : k * C_DEV + nc].reshape(times_here, blocks, C_DEV) for k in range(3)], axis=2
     )[:, :, :wide]
-    outgoing = jnp.transpose(windows, (1, 0, 2))
+    tag = jnp.zeros((times_here, blocks, 1), recorded.dtype).at[0].set(offsets[0].astype(recorded.dtype))
+    both = jnp.concatenate([windows, jnp.take(windows, partners, axis=1), tag], axis=2)
+    outgoing = jnp.transpose(both, (1, 0, 2))
     arrived = lax.all_to_all(outgoing, "chan", split_axis=0, concat_axis=0, tiled=True)
+    mate_offset = arrived[:, 0, 2 * wide].astype(jnp.int32)[mate]
     times = blocks * times_here
     cols = times // PH
-    strain = jnp.transpose(arrived.reshape(blocks, times_here // PH, PH, wide), (3, 2, 0, 1)).reshape(wide, PH, cols)
+    strain = jnp.transpose(
+        arrived[:, :, : 2 * wide].reshape(blocks, times_here // PH, PH, 2 * wide), (3, 2, 0, 1)
+    ).reshape(2 * wide, PH, cols)
     tms = lax.axis_size("tm")
     up = [(i, i + 1) for i in range(tms - 1)]
     down = [(j, i) for i, j in up]
     before = lax.ppermute(strain[:, :, cols - WL :], "tm", up)
     after = lax.ppermute(strain[:, :, :WR], "tm", down)
     strain_wide = jnp.concatenate([before, strain, after], axis=2)
-    n_s = strain_wide.shape[2]
-
-    n_f = n_s - 3
-    first_mask = edge_mask(wide - 6, PH, n_f, 3 - REACH, lambda p, v: (PH * (v - (WL - 1)) + p, times))
-    first = banded(
-        strain_wide.reshape(wide * PH, n_s),
-        weights_first(first_weight),
-        first_bias,
-        first_mask,
-        groups=PH,
-        shifts=4,
-        n_out=n_f,
-        relu=True,
-    )
 
     quarter = times // 4
     length = quarter + 2 * LEAD
-    pre_second = banded(
-        first,
-        weights_stride4(second_weight, 3, 2),
-        second_bias,
-        jnp.ones((C_DEV, 1, length), jnp.float32),
-        groups=1,
-        shifts=3,
-        n_out=length,
-        relu=False,
-    )
+    weights = (first_weight, first_bias, second_weight, second_bias, times, length)
+    pre_second = lower_layers(strain_wide[:wide], me, *weights)
+    mate_second = lower_layers(strain_wide[wide:], mate, *weights)
 
     own_offset = offsets[0]
-    crossing = lax.dynamic_slice(pre_second, (own_offset - 3, 0, 0), (7, F2, length))
-    packed = crossing.reshape(blocks, 1, -1)
-    moved = jnp.take(
-        lax.all_to_all(packed, "chan", split_axis=0, concat_axis=1, tiled=True), partners, axis=1
-    )
-    came = lax.all_to_all(moved, "chan", split_axis=1, concat_axis=0, tiled=True).reshape(7, F2, length)
-    flipped = came[::-1]
+    crossing = lax.dynamic_slice(mate_second, (mate_offset - 3, 0, 0), (7, F2, length))
+    flipped = crossing[::-1]
     coupling = jnp.einsum("kof,kft->kot", loop_weight, flipped, preferred_element_type=jnp.float32)
     extra = lax.dynamic_update_slice(
         jnp.zeros((C_DEV, F2, length), jnp.float32), coupling, (own_offset - 3, 0, 0)
     )
-    second_mask = edge_mask(C_DEV, 1, length, 0, lambda p, j: (j - LEAD, quarter))
+    second_mask = edge_mask(C_DEV, 1, length, 0, lambda p, j: (j - LEAD, quarter), me)
     second = (jnp.maximum(pre_second.astype(jnp.float32) + extra, 0.0) * second_mask).astype(jnp.bfloat16)
 
     ring_up = [(i, i + 1) for i in range(blocks - 1)]
@@ -204,7 +211,7 @@
 
     n_t = length - 6
     n_sel = quarter // 4 + 1
-    third_mask = edge_mask(wide - 6, 1, n_t, 3 - REACH, lambda p, j: (j - (LEAD - 3), quarter))
+    third_mask = edge_mask(wide - 6, 1, n_t, 3 - REACH, lambda p, j: (j - (LEAD - 3), quarter), me)
     third = banded(
         second_wide,
         weights_stride1(third_weight),

time: 131 us -> 101 us (0.77)
  waiting for transfers between devices: 40.3 us -> 10.4 us
  starting transfers between devices: 35.1 us -> 23.2 us
  Pallas kernels: 24.2 us -> 33.1 us
  between operations: 1.2 us -> 4.92 us
  local copies, waits for them, and re-layouts: 22.7 us -> 21.1 us
    all_to_all x2 -> x0, waiting for transfers between devices: 28.8 us -> none  [the longest x1 16 us: on_device(): lax.all_to_all(packed, 'chan', split_axis=0, concat_axis=1, tiled=True)]
    all_to_all x2 -> x0, starting transfers between devices: 11.5 us -> none  [the longest x1 6.5 us: on_device(): lax.all_to_all(moved, 'chan', split_axis=1, concat_axis=0, tiled=True)]
    pallas_call x4 -> x6, Pallas kernels: 24.2 us -> 33.1 us  [banded(): pl.pallas_call(kernel, out_shape=jax.ShapeDtypeStruct(out_shape, jnp.bflo...]
    concatenate x1 -> x0, local copies, waits for them, and re-layouts: 2.07 us -> none  [on_device(): strain_wide = jnp.concatenate([before, strain, after], axis=2)]
    unnamed x38 -> x36, local copies, waits for them, and re-layouts: 1.35 us -> 2.99 us
    all_to_all x1 -> x0, other arithmetic: 1.58 us -> none  [on_device(): lax.all_to_all(moved, 'chan', split_axis=1, concat_axis=0, tiled=True)]
  transfers between devices with their start and end apart: 7 -> 5, of which waited for: 5 -> 3; matrix products, arithmetic and copies ran while one was open for 11% -> 13% of each run, Pallas kernels for 0% -> 0%
where the time goes in v2:
time: 101 us; the launch traced here: 100 us
  Pallas kernels  33.1 us (33%)
  starting transfers between devices  23.2 us (23%)
  local copies, waits for them, and re-layouts  21.1 us (21%)
  waiting for transfers between devices  10.4 us (10%)
  other arithmetic  7.46 us (7%)
  between operations  4.92 us (5%)
    pallas_call x6, Pallas kernels, banded(): pl.pallas_call(kernel, out_shape=jax.ShapeDtypeStruct(out_shape, jnp.bflo...  33.1 us
    all_to_all x1, starting transfers between devices, on_device(): lax.all_to_all(outgoing, 'chan', split_axis=0, concat_axis=0, tiled=True)  13 us
    all_to_all x1, waiting for transfers between devices, on_device(): lax.all_to_all(outgoing, 'chan', split_axis=0, concat_axis=0, tiled=True)  5.52 us
    ppermute x1, waiting for transfers between devices, on_device(): below = lax.ppermute(second[:REACH], 'chan', ring_down)  4.4 us
    ppermute x1, starting transfers between devices, on_device(): above = lax.ppermute(second[C_DEV - REACH:], 'chan', ring_up)  3.61 us
    ppermute x1, starting transfers between devices, on_device(): before = lax.ppermute(strain[:, :, cols - WL:], 'tm', up)  3.2 us
    unnamed x36, local copies, waits for them, and re-layouts  2.99 us
    reshape x4, local copies, waits for them, and re-layouts, banded(): args = [x, w_all, bias.reshape(fout, 1).astype(jnp.float32), mask]  2.75 us
  transfers between devices with their start and end apart: 5, of which 3 were waited for; matrix products, arithmetic and copies ran while one was open for 13% of the time, Pallas kernels for 0%

profile of v2, /device:TPU:1, one launch (start us, length us, event | category | flops | bytes accessed | tf_op | source)
XLA Modules:
  0.0 100.3 jit_solution(1280577689387845134)
XLA Ops:
  0.0 0.7 compare_select_fusion
  1.4 1.0 pad_slice_fusion.2
  5.2 1.5 %reshape.301 = bf16[64,2,656]{2,1,0:T(2,128)(2,1)} reshape(bf16[64,32,41]{2,1,0:T(8,128)(2,1)S(1)} %copy.116) | data formatting | bytes 335872
  6.7 13.0 %all-to-all-start = ((bf16[64,2,656]{2,1,0:T(2,128)(2,1)}), bf16[64,2,656]{2,1,0:T(2,128)(2,1)S(1)}, u32[]{:S(2)}, u32[]{:S(2)}) async-start(bf16[64,2,656]{2,1,0:T(2,128)(2,1)} %reshape.301), calls=%async_computation | async-start | bytes 393216 | tf_op jit(solution)/shard_map/all_to_all | solution.py:176
  22.9 0.9 and_convert_fusion.1
  25.1 5.5 %all-to-all-done = bf16[64,2,656]{2,1,0:T(2,128)(2,1)S(1)} async-done(((bf16[64,2,656]{2,1,0:T(2,128)(2,1)}), bf16[64,2,656]{2,1,0:T(2,128)(2,1)S(1)}, u32[]{:S(2)}, u32[]{:S(2)}) %all-to-all-start) | async-done | bytes 167968 | tf_op jit(solution)/shard_map/all_to_all | solution.py:176
  30.6 0.8 reshape.302
  32.5 3.2 %collective-permute-start = (bf16[40,4,7]{0,2,1:T(8,128)(2,1)S(1)}, bf16[40,4,7]{0,2,1:T(8,128)(2,1)S(1)}, u32[]{:S(2)}, u32[]{:S(2)}) collective-permute-start(bf16[40,4,7]{0,2,1:T(8,128)(2,1)S(1)} %slice.76), channel_id=1, source_target_pairs={{0,1},{1,2},{2,3},{4,5},{5,6},{6,7},{8,9},{9,10},{10,11},{12,13},{... | collective-permute-start | bytes 6728 | tf_op jit(solution)/shard_map/ppermute | solution.py:186
  35.7 1.5 %collective-permute-start.1 = (bf16[40,4,8]{0,2,1:T(8,128)(2,1)S(1)}, bf16[40,4,8]{0,2,1:T(8,128)(2,1)S(1)}, u32[]{:S(2)}, u32[]{:S(2)}) collective-permute-start(bf16[40,4,8]{0,2,1:T(8,128)(2,1)S(1)} %slice.77), channel_id=1, source_target_pairs={{1,0},{2,1},{3,2},{5,4},{6,5},{7,6},{9,8},{10,9},{11,10},{13,12},{... | collective-permute-start | bytes 7688 | tf_op jit(solution)/shard_map/ppermute | solution.py:187
  38.6 0.8 copy.125.w_ref
  40.2 0.7 copy.128.w_ref
  41.0 0.7 copy.129.b_ref
  41.9 0.9 reshape.260.w_ref
  42.8 0.7 copy.136.b_ref
  43.7 0.8 copy.138.w_ref
  44.6 0.7 copy.139.b_ref
  48.4 0.7 reshape.255.x_ref
  49.1 4.2 %shard_map.219.x_ref = bf16[14,64,524]{2,1,0:T(8,128)(2,1)} custom-call(bf16[80,527]{1,0:T(8,128)(2,1)} %reshape.255.x_ref, bf16[256,28]{1,0:T(8,128)(2,1)} %copy.125.w_ref, f32[16,1]{1,0:T(8,128)} %copy.126.b_ref, f32[14,4,524]{2,1,0:T(4,128)} %get-tuple-element.26.m_ref), custom_call_target="tpu_custom_call" | custom-call | tf_op jit(solution)/shard_map/pallas_call | solution.py:71
  53.9 4.6 %shard_map.220 = bf16[8,32,522]{2,1,0:T(8,128)(2,1)} custom-call(bf16[14,64,524]{2,1,0:T(8,128)(2,1)} %shard_map.219.x_ref, bf16[96,448]{1,0:T(8,128)(2,1)} %copy.128.w_ref, f32[32,1]{1,0:T(8,128)} %copy.129.b_ref, f32[8,1,522]{2,1,0:T(1,128)} %broadcast_32_m_ref.2.m_ref), custom_call_target="tpu_custom_call" | custom-call | tf_op jit(solution)/shard_map/pallas_call | solution.py:71
  58.5 1.0 constant_dynamic-slice_fusion
  59.6 0.7 reshape.248.x_ref
  60.3 4.2 %shard_map.217.x_ref = bf16[14,64,524]{2,1,0:T(8,128)(2,1)} custom-call(bf16[80,527]{1,0:T(8,128)(2,1)} %reshape.248.x_ref, bf16[256,28]{1,0:T(8,128)(2,1)} %copy.125.w_ref, f32[16,1]{1,0:T(8,128)} %copy.126.b_ref, f32[14,4,524]{2,1,0:T(4,128)} %get-tuple-element.27.m_ref), custom_call_target="tpu_custom_call" | custom-call | tf_op jit(solution)/shard_map/pallas_call | solution.py:71
  64.5 4.6 %shard_map.218 = bf16[8,32,522]{2,1,0:T(8,128)(2,1)} custom-call(bf16[14,64,524]{2,1,0:T(8,128)(2,1)} %shard_map.217.x_ref, bf16[96,448]{1,0:T(8,128)(2,1)} %copy.128.w_ref, f32[32,1]{1,0:T(8,128)} %copy.129.b_ref, f32[8,1,522]{2,1,0:T(1,128)} %broadcast_32_m_ref.2.m_ref), custom_call_target="tpu_custom_call" | custom-call | tf_op jit(solution)/shard_map/pallas_call | solution.py:71
  69.1 1.0 %convert_element_type.37 = f32[8,32,522]{2,1,0:T(8,128)S(1)} convert(bf16[8,32,522]{2,1,0:T(8,128)(2,1)} %shard_map.218) | non-fusion elementwise | flops 133632 | bytes 801792 | tf_op jit(solution)/shard_map/convert_element_type | solution.py:204
  70.5 3.6 %collective-permute-start.2 = (bf16[6,32,522]{2,1,0:T(8,128)(2,1)S(1)}, bf16[6,32,522]{2,1,0:T(8,128)(2,1)S(1)}, u32[]{:S(2)}, u32[]{:S(2)}) collective-permute-start(bf16[6,32,522]{2,1,0:T(8,128)(2,1)S(1)} %get-tuple-element.19), channel_id=1, source_target_pairs={{0,4},{4,8},{8,12},{12,16},{16,20},{20,24},{24,28},{28,32},{32,36}... | collective-permute-start | bytes 601352 | tf_op jit(solution)/shard_map/ppermute | solution.py:208
  74.1 1.9 %collective-permute-start.3 = (bf16[6,32,522]{2,1,0:T(8,128)(2,1)S(1)}, bf16[6,32,522]{2,1,0:T(8,128)(2,1)S(1)}, u32[]{:S(2)}, u32[]{:S(2)}) collective-permute-start(bf16[6,32,522]{2,1,0:T(8,128)(2,1)S(1)} %get-tuple-element.20), channel_id=1, source_target_pairs={{4,0},{8,4},{12,8},{16,12},{20,16},{24,20},{28,24},{32,28},{36,32}... | collective-permute-start | bytes 601352 | tf_op jit(solution)/shard_map/ppermute | solution.py:209
  76.0 0.7 and_convert_fusion.m_ref
  77.2 4.4 %collective-permute-done.3 = bf16[6,32,522]{2,1,0:T(8,128)(2,1)S(1)} collective-permute-done((bf16[6,32,522]{2,1,0:T(8,128)(2,1)S(1)}, bf16[6,32,522]{2,1,0:T(8,128)(2,1)S(1)}, u32[]{:S(2)}, u32[]{:S(2)}) %collective-permute-start.3) | collective-permute-done | bytes 200480 | tf_op jit(solution)/shard_map/ppermute | solution.py:209
  81.6 1.1 %pad_maximum_fusion.x_ref = bf16[20,32,522]{2,1,0:T(8,128)(2,1)} fusion(bf16[6,32,522]{2,1,0:T(8,128)(2,1)S(1)} %collective-permute-done.3, bf16[8,32,522]{2,1,0:T(8,128)(2,1)S(1)} %multiply_convert_fusion, bf16[6,32,522]{2,1,0:T(8,128)(2,1)S(1)} %collective-permute-done.2), kind=kLoop, calls=%fused_computation.8 | loop fusion | flops 668160 | bytes 1336320 | tf_op jit(solution)/shard_map/concatenate | solution.py:210
  82.7 10.9 %shard_map.221.x_ref = bf16[14,128,129]{2,1,0:T(8,128)(2,1)} custom-call(bf16[20,32,522]{2,1,0:T(8,128)(2,1)} %pad_maximum_fusion.x_ref, bf16[224,224]{1,0:T(8,128)(2,1)} %reshape.260.w_ref, f32[32,1]{1,0:T(8,128)} %copy.136.b_ref, f32[14,1,516]{2,1,0:T(1,128)} %and_convert_fusion.m_ref, bf16[516,1024]{1,0:T(8,128)(2,1)} %constant.154.clone.rest_0_), custom_call_target="tpu_custom_call" | custom-call | tf_op jit(solution)/shard_map/pallas_call | solution.py:71
  94.2 4.5 %shard_map.222 = bf16[8,64,128]{2,1,0:T(8,128)(2,1)} custom-call(bf16[14,128,129]{2,1,0:T(8,128)(2,1)} %shard_map.221.x_ref, bf16[128,896]{1,0:T(8,128)(2,1)} %copy.138.w_ref, f32[64,1]{1,0:T(8,128)} %copy.139.b_ref, f32[8,1,128]{2,1,0:T(1,128)} %broadcast_in_dim.127.m_ref), custom_call_target="tpu_custom_call" | custom-call | tf_op jit(solution)/shard_map/pallas_call | solution.py:71
  98.7 1.6 %copy.140 = bf16[64,8,128]{2,1,0:T(8,128)(2,1)} copy(bf16[64,8,128]{2,0,1:T(8,128)(2,1)} %bitcast.62) | data formatting | bytes 262144 | tf_op jit(solution)/shard_map/transpose | solution.py:237
  (88 shorter events, 12.3 us)
Async XLA Ops:
  0.0 23.9 %copy-start = (bf16[64,32,7,7]{0,1,3,2:T(8,128)(2,1)S(1)}, bf16[64,32,7,7]{0,1,3,2:T(8,128)(2,1)}, u32[]{:S(2)}) copy-start(bf16[64,32,7,7]{0,1,3,2:T(8,128)(2,1)} %param.39) | copy-start | bytes 602116
  4.7 15.1 %copy-start.15 = (s32[64]{0:T(128)S(1)}, s32[64]{0:T(128)}, u32[]{:S(2)}) copy-start(s32[64]{0:T(128)} %param.30) | copy-start | bytes 772
  4.7 16.4 %copy-start.4 = (bf16[16,1,7,7]{0,3,2,1:T(8,128)(2,1)S(1)}, bf16[16,1,7,7]{0,3,2,1:T(8,128)(2,1)}, u32[]{:S(2)}) copy-start(bf16[16,1,7,7]{0,3,2,1:T(8,128)(2,1)} %param.32) | copy-start | bytes 4708
  4.7 16.4 %copy-start.13 = (s32[64]{0:T(128)S(1)}, s32[64]{0:T(128)}, u32[]{:S(2)}) copy-start(s32[64]{0:T(128)} %constant.194) | copy-start | bytes 772
  4.7 16.4 %copy-start.12 = (s32[12]{0:T(128)S(1)}, s32[12]{0:T(128)}, u32[]{:S(2)}) copy-start(s32[12]{0:T(128)} %constant.195) | copy-start | bytes 148
  4.7 17.1 %copy-start.5 = (pred[4,4,4]{1,0,2:T(4,128)(4,1)S(1)}, pred[4,4,4]{1,0,2:T(4,128)(4,1)}, u32[]{:S(2)}) copy-start(pred[4,4,4]{1,0,2:T(4,128)(4,1)} %constant.163) | copy-start | bytes 196
  4.7 17.2 %copy-start.1 = (bf16[32,16,7,7]{0,1,3,2:T(8,128)(2,1)S(1)}, bf16[32,16,7,7]{0,1,3,2:T(8,128)(2,1)}, u32[]{:S(2)}) copy-start(bf16[32,16,7,7]{0,1,3,2:T(8,128)(2,1)} %param.34) | copy-start | bytes 150532
  6.7 23.9 %all-to-all-start = ((bf16[64,2,656]{2,1,0:T(2,128)(2,1)}), bf16[64,2,656]{2,1,0:T(2,128)(2,1)S(1)}, u32[]{:S(2)}, u32[]{:S(2)}) async-start(bf16[64,2,656]{2,1,0:T(2,128)(2,1)} %reshape.301), calls=%async_computation | async-start | bytes 393216 | tf_op jit(solution)/shard_map/all_to_all | solution.py:176
  21.8 0.8 copy-start.14
  21.9 2.0 %copy-start.11 = (s32[8]{0:T(128)S(1)}, s32[8]{0:T(128)}, u32[]{:S(2)}) copy-start(s32[8]{0:T(128)} %constant.191) | copy-start | bytes 100
  23.9 0.7 copy-start.7
  31.5 7.9 %copy-start.8 = (f32[16]{0:T(128)S(1)}, f32[16]{0:T(128)}, u32[]{:S(2)}) copy-start(f32[16]{0:T(128)} %param.33) | copy-start | bytes 196
  32.1 8.9 %copy-start.9 = (f32[32]{0:T(128)S(1)}, f32[32]{0:T(128)}, u32[]{:S(2)}) copy-start(f32[32]{0:T(128)} %param.35) | copy-start | bytes 388
  32.1 9.6 %copy-start.2 = (bf16[32,32,7,7]{1,0,3,2:T(8,128)(2,1)S(1)}, bf16[32,32,7,7]{1,0,3,2:T(8,128)(2,1)}, u32[]{:S(2)}) copy-start(bf16[32,32,7,7]{1,0,3,2:T(8,128)(2,1)} %param.37) | copy-start | bytes 301060
  32.5 15.4 %collective-permute-start = (bf16[40,4,7]{0,2,1:T(8,128)(2,1)S(1)}, bf16[40,4,7]{0,2,1:T(8,128)(2,1)S(1)}, u32[]{:S(2)}, u32[]{:S(2)}) collective-permute-start(bf16[40,4,7]{0,2,1:T(8,128)(2,1)S(1)} %slice.76), channel_id=1, source_target_pairs={{0,1},{1,2},{2,3},{4,5},{5,6},{6,7},{8,9},{9,10},{10,11},{12,13},{... | collective-permute-start | bytes 6728 | tf_op jit(solution)/shard_map/ppermute | solution.py:186
  35.7 12.4 %collective-permute-start.1 = (bf16[40,4,8]{0,2,1:T(8,128)(2,1)S(1)}, bf16[40,4,8]{0,2,1:T(8,128)(2,1)S(1)}, u32[]{:S(2)}, u32[]{:S(2)}) collective-permute-start(bf16[40,4,8]{0,2,1:T(8,128)(2,1)S(1)} %slice.77), channel_id=1, source_target_pairs={{1,0},{2,1},{3,2},{5,4},{6,5},{7,6},{9,8},{10,9},{11,10},{13,12},{... | collective-permute-start | bytes 7688 | tf_op jit(solution)/shard_map/ppermute | solution.py:187
  39.3 3.5 %copy-start.10 = (f32[32]{0:T(128)S(1)}, f32[32]{0:T(128)}, u32[]{:S(2)}) copy-start(f32[32]{0:T(128)} %param.38) | copy-start | bytes 388
  41.7 2.9 %copy-start.6 = (f32[64]{0:T(128)S(1)}, f32[64]{0:T(128)}, u32[]{:S(2)}) copy-start(f32[64]{0:T(128)} %param.40) | copy-start | bytes 772
  64.5 5.6 %copy-start.3 = (bf16[7,32,32]{2,1,0:T(8,128)(2,1)S(1)}, bf16[7,32,32]{2,1,0:T(8,128)(2,1)}, u32[]{:S(2)}) copy-start(bf16[7,32,32]{2,1,0:T(8,128)(2,1)} %param.36) | copy-start | bytes 43012
  70.5 6.7 %collective-permute-start.2 = (bf16[6,32,522]{2,1,0:T(8,128)(2,1)S(1)}, bf16[6,32,522]{2,1,0:T(8,128)(2,1)S(1)}, u32[]{:S(2)}, u32[]{:S(2)}) collective-permute-start(bf16[6,32,522]{2,1,0:T(8,128)(2,1)S(1)} %get-tuple-element.19), channel_id=1, source_target_pairs={{0,4},{4,8},{8,12},{12,16},{16,20},{20,24},{24,28},{28,32},{32,36}... | collective-permute-start | bytes 601352 | tf_op jit(solution)/shard_map/ppermute | solution.py:208
  74.1 7.5 %collective-permute-start.3 = (bf16[6,32,522]{2,1,0:T(8,128)(2,1)S(1)}, bf16[6,32,522]{2,1,0:T(8,128)(2,1)S(1)}, u32[]{:S(2)}, u32[]{:S(2)}) collective-permute-start(bf16[6,32,522]{2,1,0:T(8,128)(2,1)S(1)} %get-tuple-element.20), channel_id=1, source_target_pairs={{4,0},{8,4},{12,8},{16,12},{20,16},{24,20},{28,24},{32,28},{36,32}... | collective-permute-start | bytes 601352 | tf_op jit(solution)/shard_map/ppermute | solution.py:209

commit v3 on v2

--- a/solution.py
+++ b/solution.py
@@ -15,23 +15,25 @@
 LANE_BLOCK = 256
 
 
-def banded(x, w_all, bias, mask, *, groups, shifts, n_out, relu, select=None, n_sel=0):
-    flat = x.ndim == 2
+def banded(x, w_all, bias, b_row, mask, *, groups, shifts, n_out, relu, select=None, n_sel=0):
+    windows = x.shape[0]
+    flat = x.ndim == 3
     k_all = w_all.shape[1]
     row_step = k_all // 7
-    r_out = (x.shape[0] // row_step if flat else x.shape[0]) - 6
+    r_out = (x.shape[1] // row_step if flat else x.shape[1]) - 6
     n_in = x.shape[-1]
     fout = w_all.shape[0] // (groups * shifts)
     if select is None:
-        out_shape = (r_out, groups * fout, n_out)
+        out_shape = (windows, r_out, groups * fout, n_out)
     else:
-        out_shape = (r_out, PH * fout, n_sel)
+        out_shape = (windows, r_out, PH * fout, n_sel)
 
     def kernel(x_ref, w_ref, b_ref, m_ref, *rest):
         if select is None:
             (o_ref,) = rest
         else:
             s_ref, o_ref = rest
+        b_val = b_ref[b_row : b_row + fout, :]
 
         def row(r, carry):
             if flat:
@@ -45,17 +47,22 @@
                 acc = z[base : base + fout, 0:n_out]
                 for s in range(1, shifts):
                     acc = acc + z[base + s * fout : base + (s + 1) * fout, s : s + n_out]
-                acc = acc + b_ref[...]
+                acc = acc + b_val
                 if relu:
                     acc = jnp.maximum(acc, 0.0)
                 acc = (acc * m_row[g : g + 1, :]).astype(jnp.bfloat16)
                 if select is None:
                     o_ref[r, g * fout : (g + 1) * fout, :] = acc
-                else:
-                    y = jnp.dot(acc, s_ref[...], preferred_element_type=jnp.float32)
+                    continue
+                for k in range(pl.cdiv(n_out, LANE_BLOCK // 2)):
+                    lo = k * (LANE_BLOCK // 2)
+                    width = min(LANE_BLOCK // 2, n_out - lo)
+                    n_u = pl.cdiv(width, PH)
+                    y = jnp.dot(acc[:, lo : lo + width], s_ref[0:width, :], preferred_element_type=jnp.float32)
+                    seg = LANE_BLOCK // 2 // PH
                     for p in range(PH):
-                        o_ref[r, p * fout : (p + 1) * fout, :] = y[
-                            :, p * LANE_BLOCK : p * LANE_BLOCK + n_sel
+                        o_ref[r, p * fout : (p + 1) * fout, lo // PH : lo // PH + n_u] = y[
+                            :, p * seg : p * seg + n_u
                         ].astype(jnp.bfloat16)
             return carry
 
@@ -65,10 +72,24 @@
         else:
             lax.fori_loop(0, r_out, row, 0)
 
-    args = [x, w_all, bias.reshape(fout, 1).astype(jnp.float32), mask]
+    def per_window(a):
+        return pl.BlockSpec((None,) + a.shape[1:], lambda w, n=a.ndim - 1: (w,) + (0,) * n)
+
+    def whole(a):
+        return pl.BlockSpec(a.shape, lambda w, n=a.ndim: (0,) * n)
+
+    args = [x, w_all, bias, mask]
+    specs = [per_window(x), whole(w_all), whole(bias), per_window(mask)]
     if select is not None:
         args.append(select)
-    return pl.pallas_call(kernel, out_shape=jax.ShapeDtypeStruct(out_shape, jnp.bfloat16))(*args)
+        specs.append(whole(select))
+    return pl.pallas_call(
+        kernel,
+        grid=(windows,),
+        in_specs=specs,
+        out_specs=pl.BlockSpec((None,) + out_shape[1:], lambda w: (w, 0, 0, 0)),
+        out_shape=jax.ShapeDtypeStruct(out_shape, jnp.bfloat16),
+    )(*args)
 
 
 def weights_stride1(w):
@@ -99,12 +120,13 @@
     return jnp.transpose(taps, (2, 3, 0, 1, 4)).reshape(PH * 4 * fout, 7 * PH)
 
 
-def phase_select(n_in, n_sel):
-    sel = np.zeros((n_in, PH * LANE_BLOCK), np.float32)
+def phase_select():
+    block = LANE_BLOCK // 2
+    seg = block // PH
+    sel = np.zeros((block, block), np.float32)
     for p in range(PH):
-        for u in range(n_sel):
-            if PH * u + p < n_in:
-                sel[PH * u + p, p * LANE_BLOCK + u] = 1.0
+        for u in range(seg):
+            sel[PH * u + p, p * seg + u] = 1.0
     return jnp.asarray(sel, jnp.bfloat16)
 
 
@@ -120,15 +142,21 @@
     return ok.astype(jnp.float32)
 
 
-def lower_layers(strain_wide, block, first_weight, first_bias, second_weight, second_bias, times, length):
+def lower_layers(strain_wide, blocks_of, first_weight, biases, second_weight, times, length):
     wide = C_DEV + 2 * REACH
-    n_s = strain_wide.shape[2]
+    n_win, n_s = strain_wide.shape[0], strain_wide.shape[-1]
     n_f = n_s - 3
-    first_mask = edge_mask(wide - 6, PH, n_f, 3 - REACH, lambda p, v: (PH * (v - (WL - 1)) + p, times), block)
+    first_mask = jnp.stack(
+        [
+            edge_mask(wide - 6, PH, n_f, 3 - REACH, lambda p, v: (PH * (v - (WL - 1)) + p, times), b)
+            for b in blocks_of
+        ]
+    )
     first = banded(
-        strain_wide.reshape(wide * PH, n_s),
+        strain_wide.reshape(n_win, wide * PH, n_s),
         weights_first(first_weight),
-        first_bias,
+        biases,
+        0,
         first_mask,
         groups=PH,
         shifts=4,
@@ -138,8 +166,9 @@
     return banded(
         first,
         weights_stride4(second_weight, 3, 2),
-        second_bias,
-        jnp.ones((C_DEV, 1, length), jnp.float32),
+        biases,
+        16,
+        jnp.ones((n_win, C_DEV, 1, length), jnp.float32),
         groups=1,
         shifts=3,
         n_out=length,
@@ -189,9 +218,11 @@
 
     quarter = times // 4
     length = quarter + 2 * LEAD
-    weights = (first_weight, first_bias, second_weight, second_bias, times, length)
-    pre_second = lower_layers(strain_wide[:wide], me, *weights)
-    mate_second = lower_layers(strain_wide[wide:], mate, *weights)
+    biases = jnp.concatenate([first_bias, second_bias, third_bias, fourth_bias]).reshape(-1, 1)
+    lower = lower_layers(
+        strain_wide.reshape(2, wide, PH, -1), (me, mate), first_weight, biases, second_weight, times, length
+    )
+    pre_second, mate_second = lower[0], lower[1]
 
     own_offset = offsets[0]
     crossing = lax.dynamic_slice(mate_second, (mate_offset - 3, 0, 0), (7, F2, length))
@@ -213,28 +244,30 @@
     n_sel = quarter // 4 + 1
     third_mask = edge_mask(wide - 6, 1, n_t, 3 - REACH, lambda p, j: (j - (LEAD - 3), quarter), me)
     third = banded(
-        second_wide,
+        second_wide[None],
         weights_stride1(third_weight),
-        third_bias,
-        third_mask,
+        biases,
+        48,
+        third_mask[None],
         groups=1,
         shifts=7,
         n_out=n_t,
         relu=True,
-        select=phase_select(n_t, n_sel),
+        select=phase_select(),
         n_sel=n_sel,
     )
     features = banded(
         third,
         weights_stride4(fourth_weight, 2, 0),
-        fourth_bias,
-        jnp.ones((C_DEV, 1, quarter // 4), jnp.float32),
+        biases,
+        80,
+        jnp.ones((1, C_DEV, 1, quarter // 4), jnp.float32),
         groups=1,
         shifts=2,
         n_out=quarter // 4,
         relu=True,
     )
-    return jnp.transpose(features, (1, 0, 2))
+    return jnp.transpose(features[0], (1, 0, 2))
 
 
 def solution(mesh):

time: 101 us -> 99 us (0.980)
  Pallas kernels: 33.1 us -> 28.1 us
  starting transfers between devices: 23.2 us -> 24.4 us
  other arithmetic: 7.46 us -> 8.52 us
    pallas_call x6 -> x4, Pallas kernels: 33.1 us -> 28.1 us  [banded(): pl.pallas_call(kernel, grid=(windows,), in_specs=specs, out_specs=pl.Bloc...]
    concatenate x0 -> x1, local copies, waits for them, and re-layouts: none -> 4.18 us  [on_device(): strain_wide = jnp.concatenate([before, strain, after], axis=2)]
    reshape x7 -> x1, local copies, waits for them, and re-layouts: 4.32 us -> 0.74 us  [on_device(): jnp.concatenate([first_bias, second_bias, third_bias, fourth_bias])]
    transpose x1 -> x2, local copies, waits for them, and re-layouts: 0.33 us -> 1.54 us  [on_device(): jnp.transpose(arrived[:, :, :2 * wide].reshape(blocks, times_here // PH,...]
    broadcast_in_dim x0 -> x1, other arithmetic: none -> 1.06 us  [on_device(): second_wide[None]]
  transfers between devices with their start and end apart: 5 -> 5, of which waited for: 3 -> 3; matrix products, arithmetic and copies ran while one was open for 13% -> 17% of each run, Pallas kernels for 0% -> 0%
where the time goes in v3:
time: 99 us; the launch traced here: 98.4 us
  Pallas kernels  28.1 us (28%)
  starting transfers between devices  24.4 us (25%)
  local copies, waits for them, and re-layouts  21.8 us (22%)
  waiting for transfers between devices  10.3 us (10%)
  other arithmetic  8.52 us (9%)
  between operations  5.1 us (5%)
    pallas_call x4, Pallas kernels, banded(): pl.pallas_call(kernel, grid=(windows,), in_specs=specs, out_specs=pl.Bloc...  28.1 us
    all_to_all x1, starting transfers between devices, on_device(): lax.all_to_all(outgoing, 'chan', split_axis=0, concat_axis=0, tiled=True)  13.1 us
    all_to_all x1, waiting for transfers between devices, on_device(): lax.all_to_all(outgoing, 'chan', split_axis=0, concat_axis=0, tiled=True)  5.41 us
    ppermute x1, waiting for transfers between devices, on_device(): below = lax.ppermute(second[:REACH], 'chan', ring_down)  4.4 us
    concatenate x1, local copies, waits for them, and re-layouts, on_device(): strain_wide = jnp.concatenate([before, strain, after], axis=2)  4.18 us
    ppermute x1, starting transfers between devices, on_device(): before = lax.ppermute(strain[:, :, cols - WL:], 'tm', up)  4.17 us
    ppermute x1, starting transfers between devices, on_device(): above = lax.ppermute(second[C_DEV - REACH:], 'chan', ring_up)  3.89 us
    unnamed x36, local copies, waits for them, and re-layouts  3 us
  transfers between devices with their start and end apart: 5, of which 3 were waited for; matrix products, arithmetic and copies ran while one was open for 17% of the time, Pallas kernels for 0%

profile of v3, /device:TPU:1, one launch (start us, length us, event | category | flops | bytes accessed | tf_op | source)
XLA Modules:
  0.0 98.4 jit_solution(380338180681796058)
XLA Ops:
  0.0 0.7 compare_select_fusion
  0.7 0.7 compare_and_fusion.3
  1.4 1.0 pad_slice_fusion.2
  3.5 0.7 gather_fusion
  5.2 1.5 %reshape.314 = bf16[64,2,656]{2,1,0:T(2,128)(2,1)} reshape(bf16[64,32,41]{2,1,0:T(8,128)(2,1)S(1)} %copy.73) | data formatting | bytes 335872
  6.7 13.1 %all-to-all-start = ((bf16[64,2,656]{2,1,0:T(2,128)(2,1)}), bf16[64,2,656]{2,1,0:T(2,128)(2,1)S(1)}, u32[]{:S(2)}, u32[]{:S(2)}) async-start(bf16[64,2,656]{2,1,0:T(2,128)(2,1)} %reshape.314), calls=%async_computation | async-start | bytes 393216 | tf_op jit(solution)/shard_map/all_to_all | solution.py:205
  19.9 0.7 dynamic_slice.11
  21.5 0.8 add_convert_fusion.m_ref
  24.0 0.6 gather_fusion.3
  25.4 5.4 %all-to-all-done = bf16[64,2,656]{2,1,0:T(2,128)(2,1)S(1)} async-done(((bf16[64,2,656]{2,1,0:T(2,128)(2,1)}), bf16[64,2,656]{2,1,0:T(2,128)(2,1)S(1)}, u32[]{:S(2)}, u32[]{:S(2)}) %all-to-all-start) | async-done | bytes 167968 | tf_op jit(solution)/shard_map/all_to_all | solution.py:205
  30.8 0.8 reshape.315
  32.6 1.3 %collective-permute-start.1 = (bf16[40,4,8]{0,2,1:T(8,128)(2,1)S(1)}, bf16[40,4,8]{0,2,1:T(8,128)(2,1)S(1)}, u32[]{:S(2)}, u32[]{:S(2)}) collective-permute-start(bf16[40,4,8]{0,2,1:T(8,128)(2,1)S(1)} %slice.77), channel_id=1, source_target_pairs={{1,0},{2,1},{3,2},{5,4},{6,5},{7,6},{9,8},{10,9},{11,10},{13,12},{... | collective-permute-start | bytes 7688 | tf_op jit(solution)/shard_map/ppermute | solution.py:216
  33.9 4.2 %collective-permute-start = (bf16[40,4,7]{0,2,1:T(8,128)(2,1)S(1)}, bf16[40,4,7]{0,2,1:T(8,128)(2,1)S(1)}, u32[]{:S(2)}, u32[]{:S(2)}) collective-permute-start(bf16[40,4,7]{0,2,1:T(8,128)(2,1)S(1)} %slice.76), channel_id=1, source_target_pairs={{0,1},{1,2},{2,3},{4,5},{5,6},{6,7},{8,9},{9,10},{10,11},{12,13},{... | collective-permute-start | bytes 6728 | tf_op jit(solution)/shard_map/ppermute | solution.py:215
  39.5 0.7 copy.82.b_ref
  40.3 0.7 copy.81.w_ref
  41.3 0.7 copy.84.w_ref
  42.2 0.9 reshape.279.w_ref
  43.4 0.8 copy.89.w_ref
  45.0 1.2 %copy.77 = bf16[40,4,64,8]{3,2,1,0:T(8,128)(2,1)S(1)} copy(bf16[40,4,64,8]{2,0,1,3:T(8,128)(2,1)S(1)} %bitcast.69) | data formatting | bytes 327680 | tf_op jit(solution)/shard_map/transpose | solution.py:209
  48.0 4.2 %concatenate.27 = bf16[2,80,512]{2,1,0:T(8,128)(2,1)S(1)} reshape(bf16[40,4,64,8]{3,2,1,0:T(8,128)(2,1)S(1)} %copy.77) | data formatting | bytes 327680 | tf_op jit(solution)/shard_map/concatenate | solution.py:217
  52.5 0.8 pad_maximum_fusion.2.x_ref
  53.3 6.2 %shard_map.181.x_ref = bf16[2,14,64,524]{3,2,1,0:T(8,128)(2,1)} custom-call(bf16[2,80,527]{2,1,0:T(8,128)(2,1)} %pad_maximum_fusion.2.x_ref, bf16[256,28]{1,0:T(8,128)(2,1)} %copy.81.w_ref, f32[144,1]{1,0:T(8,128)} %copy.82.b_ref, f32[2,14,4,524]{3,2,1,0:T(4,128)} %add_convert_fusion.m_ref), custom_call_target="tpu_custom_call" | custom-call | tf_op jit(solution)/shard_map/pallas_call | solution.py:86
  60.1 7.2 %shard_map.182 = bf16[2,8,32,522]{3,2,1,0:T(8,128)(2,1)} custom-call(bf16[2,14,64,524]{3,2,1,0:T(8,128)(2,1)} %shard_map.181.x_ref, bf16[96,448]{1,0:T(8,128)(2,1)} %copy.84.w_ref, f32[144,1]{1,0:T(8,128)} %copy.82.b_ref, f32[2,8,1,522]{3,2,1,0:T(1,128)} %broadcast_in_dim.125.m_ref), custom_call_target="tpu_custom_call" | custom-call | tf_op jit(solution)/shard_map/pallas_call | solution.py:86
  67.3 1.2 %slice_convert_fusion = (f32[1,8,32,522]{3,2,1,0:T(8,128)S(1)}, f32[8,32,522]{2,1,0:T(8,128)S(1)}, bf16[1,8,32,522]{3,2,1,0:T(8,128)(2,1)S(1)}) fusion(bf16[2,8,32,522]{3,2,1,0:T(8,128)(2,1)} %shard_map.182), kind=kLoop, calls=%fused_computation.17 | loop fusion | flops 133632 | bytes 1870848 | tf_op jit(solution)/shard_map/convert_element_type | solution.py:235
  69.0 3.9 %collective-permute-start.2 = (bf16[6,32,522]{2,1,0:T(8,128)(2,1)S(1)}, bf16[6,32,522]{2,1,0:T(8,128)(2,1)S(1)}, u32[]{:S(2)}, u32[]{:S(2)}) collective-permute-start(bf16[6,32,522]{2,1,0:T(8,128)(2,1)S(1)} %get-tuple-element.20), channel_id=1, source_target_pairs={{0,4},{4,8},{8,12},{12,16},{16,20},{20,24},{24,28},{28,32},{32,36}... | collective-permute-start | bytes 601352 | tf_op jit(solution)/shard_map/ppermute | solution.py:239
  72.9 1.9 %collective-permute-start.3 = (bf16[6,32,522]{2,1,0:T(8,128)(2,1)S(1)}, bf16[6,32,522]{2,1,0:T(8,128)(2,1)S(1)}, u32[]{:S(2)}, u32[]{:S(2)}) collective-permute-start(bf16[6,32,522]{2,1,0:T(8,128)(2,1)S(1)} %get-tuple-element.21), channel_id=1, source_target_pairs={{4,0},{8,4},{12,8},{16,12},{20,16},{24,20},{28,24},{32,28},{36,32}... | collective-permute-start | bytes 601352 | tf_op jit(solution)/shard_map/ppermute | solution.py:240
  74.8 0.7 and_convert_fusion.m_ref
  76.0 4.4 %collective-permute-done.3 = bf16[6,32,522]{2,1,0:T(8,128)(2,1)S(1)} collective-permute-done((bf16[6,32,522]{2,1,0:T(8,128)(2,1)S(1)}, bf16[6,32,522]{2,1,0:T(8,128)(2,1)S(1)}, u32[]{:S(2)}, u32[]{:S(2)}) %collective-permute-start.3) | collective-permute-done | bytes 200480 | tf_op jit(solution)/shard_map/ppermute | solution.py:240
  80.4 1.1 %maximum_bitcast_fusion.x_ref = bf16[1,20,32,522]{3,2,1,0:T(8,128)(2,1)} fusion(bf16[6,32,522]{2,1,0:T(8,128)(2,1)S(1)} %collective-permute-done.3, bf16[8,32,522]{2,1,0:T(8,128)(2,1)S(1)} %multiply_convert_fusion, bf16[6,32,522]{2,1,0:T(8,128)(2,1)S(1)} %collective-permute-done.2), kind=kLoop, calls=%fused_computation.8 | loop fusion | flops 668160 | bytes 1336320 | tf_op jit(solution)/shard_map/broadcast_in_dim | solution.py:247
  81.5 10.3 %shard_map.183.x_ref = bf16[1,14,128,129]{3,2,1,0:T(8,128)(2,1)} custom-call(bf16[1,20,32,522]{3,2,1,0:T(8,128)(2,1)} %maximum_bitcast_fusion.x_ref, bf16[224,224]{1,0:T(8,128)(2,1)} %reshape.279.w_ref, f32[144,1]{1,0:T(8,128)} %copy.82.b_ref, f32[1,14,1,516]{3,2,1,0:T(1,128)} %and_convert_fusion.m_ref, bf16[128,128]{1,0:T(8,128)(2,1)} %constant.160.clone.rest_0_), custom_call_target="tpu_custom_call" | custom-call | tf_op jit(solution)/shard_map/pallas_call | solution.py:86
  92.3 4.5 %shard_map.184 = bf16[1,8,64,128]{3,2,1,0:T(8,128)(2,1)} custom-call(bf16[1,14,128,129]{3,2,1,0:T(8,128)(2,1)} %shard_map.183.x_ref, bf16[128,896]{1,0:T(8,128)(2,1)} %copy.89.w_ref, f32[144,1]{1,0:T(8,128)} %copy.82.b_ref, f32[1,8,1,128]{3,2,1,0:T(1,128)} %broadcast_in_dim.134.m_ref), custom_call_target="tpu_custom_call" | custom-call | tf_op jit(solution)/shard_map/pallas_call | solution.py:86
  96.8 1.6 %copy.91 = bf16[64,8,128]{2,1,0:T(8,128)(2,1)} copy(bf16[64,8,128]{2,0,1:T(8,128)(2,1)} %bitcast.76) | data formatting | bytes 262144 | tf_op jit(solution)/shard_map/transpose | solution.py:270
  (81 shorter events, 8.9 us)
Async XLA Ops:
  0.0 24.0 %copy-start = (bf16[64,32,7,7]{0,1,3,2:T(8,128)(2,1)S(1)}, bf16[64,32,7,7]{0,1,3,2:T(8,128)(2,1)}, u32[]{:S(2)}) copy-start(bf16[64,32,7,7]{0,1,3,2:T(8,128)(2,1)} %param.31) | copy-start | bytes 602116
  4.7 15.2 %copy-start.15 = (s32[64]{0:T(128)S(1)}, s32[64]{0:T(128)}, u32[]{:S(2)}) copy-start(s32[64]{0:T(128)} %param.22) | copy-start | bytes 772
  4.7 16.5 %copy-start.4 = (bf16[16,1,7,7]{0,3,2,1:T(8,128)(2,1)S(1)}, bf16[16,1,7,7]{0,3,2,1:T(8,128)(2,1)}, u32[]{:S(2)}) copy-start(bf16[16,1,7,7]{0,3,2,1:T(8,128)(2,1)} %param.24) | copy-start | bytes 4708
  4.7 16.5 %copy-start.9 = (s32[64]{0:T(128)S(1)}, s32[64]{0:T(128)}, u32[]{:S(2)}) copy-start(s32[64]{0:T(128)} %constant.199) | copy-start | bytes 772
  4.7 16.5 %copy-start.8 = (s32[12]{0:T(128)S(1)}, s32[12]{0:T(128)}, u32[]{:S(2)}) copy-start(s32[12]{0:T(128)} %constant.200) | copy-start | bytes 148
  4.7 16.5 %copy-start.7 = (s32[8]{0:T(128)S(1)}, s32[8]{0:T(128)}, u32[]{:S(2)}) copy-start(s32[8]{0:T(128)} %constant.201) | copy-start | bytes 100
  4.7 18.2 %copy-start.5 = (pred[4,4,4]{1,0,2:T(4,128)(4,1)S(1)}, pred[4,4,4]{1,0,2:T(4,128)(4,1)}, u32[]{:S(2)}) copy-start(pred[4,4,4]{1,0,2:T(4,128)(4,1)} %constant.169) | copy-start | bytes 196
  4.7 18.3 %copy-start.1 = (bf16[32,16,7,7]{0,1,3,2:T(8,128)(2,1)S(1)}, bf16[32,16,7,7]{0,1,3,2:T(8,128)(2,1)}, u32[]{:S(2)}) copy-start(bf16[32,16,7,7]{0,1,3,2:T(8,128)(2,1)} %param.26) | copy-start | bytes 150532
  6.7 16.9 %copy-start.14 = (pred[3,4]{0,1:T(4,128)(4,1)S(1)}, pred[3,4]{0,1:T(4,128)(4,1)}, u32[]{:S(2)}) copy-start(pred[3,4]{0,1:T(4,128)(4,1)} %constant.178) | copy-start | bytes 40
  6.7 24.1 %all-to-all-start = ((bf16[64,2,656]{2,1,0:T(2,128)(2,1)}), bf16[64,2,656]{2,1,0:T(2,128)(2,1)S(1)}, u32[]{:S(2)}, u32[]{:S(2)}) async-start(bf16[64,2,656]{2,1,0:T(2,128)(2,1)} %reshape.314), calls=%async_computation | async-start | bytes 393216 | tf_op jit(solution)/shard_map/all_to_all | solution.py:205
  24.0 0.7 copy-start.6
  24.8 13.3 %copy-start.10 = (f32[64]{0:T(128)S(1)}, f32[64]{0:T(128)}, u32[]{:S(2)}) copy-start(f32[64]{0:T(128)} %param.32) | copy-start | bytes 772
  24.8 13.3 %copy-start.11 = (f32[32]{0:T(128)S(1)}, f32[32]{0:T(128)}, u32[]{:S(2)}) copy-start(f32[32]{0:T(128)} %param.30) | copy-start | bytes 388
  24.8 13.3 %copy-start.12 = (f32[32]{0:T(128)S(1)}, f32[32]{0:T(128)}, u32[]{:S(2)}) copy-start(f32[32]{0:T(128)} %param.27) | copy-start | bytes 388
  24.8 13.3 %copy-start.13 = (f32[16]{0:T(128)S(1)}, f32[16]{0:T(128)}, u32[]{:S(2)}) copy-start(f32[16]{0:T(128)} %param.25) | copy-start | bytes 196
  31.6 10.4 %copy-start.2 = (bf16[32,32,7,7]{1,0,3,2:T(8,128)(2,1)S(1)}, bf16[32,32,7,7]{1,0,3,2:T(8,128)(2,1)}, u32[]{:S(2)}) copy-start(bf16[32,32,7,7]{1,0,3,2:T(8,128)(2,1)} %param.29) | copy-start | bytes 301060
  32.6 19.8 %collective-permute-start.1 = (bf16[40,4,8]{0,2,1:T(8,128)(2,1)S(1)}, bf16[40,4,8]{0,2,1:T(8,128)(2,1)S(1)}, u32[]{:S(2)}, u32[]{:S(2)}) collective-permute-start(bf16[40,4,8]{0,2,1:T(8,128)(2,1)S(1)} %slice.77), channel_id=1, source_target_pairs={{1,0},{2,1},{3,2},{5,4},{6,5},{7,6},{9,8},{10,9},{11,10},{13,12},{... | collective-permute-start | bytes 7688 | tf_op jit(solution)/shard_map/ppermute | solution.py:216
  33.9 18.4 %collective-permute-start = (bf16[40,4,7]{0,2,1:T(8,128)(2,1)S(1)}, bf16[40,4,7]{0,2,1:T(8,128)(2,1)S(1)}, u32[]{:S(2)}, u32[]{:S(2)}) collective-permute-start(bf16[40,4,7]{0,2,1:T(8,128)(2,1)S(1)} %slice.76), channel_id=1, source_target_pairs={{0,1},{1,2},{2,3},{4,5},{5,6},{6,7},{8,9},{9,10},{10,11},{12,13},{... | collective-permute-start | bytes 6728 | tf_op jit(solution)/shard_map/ppermute | solution.py:215
  67.3 1.3 %copy-start.3 = (bf16[7,32,32]{2,1,0:T(8,128)(2,1)S(1)}, bf16[7,32,32]{2,1,0:T(8,128)(2,1)}, u32[]{:S(2)}) copy-start(bf16[7,32,32]{2,1,0:T(8,128)(2,1)} %param.28) | copy-start | bytes 43012
  69.0 7.0 %collective-permute-start.2 = (bf16[6,32,522]{2,1,0:T(8,128)(2,1)S(1)}, bf16[6,32,522]{2,1,0:T(8,128)(2,1)S(1)}, u32[]{:S(2)}, u32[]{:S(2)}) collective-permute-start(bf16[6,32,522]{2,1,0:T(8,128)(2,1)S(1)} %get-tuple-element.20), channel_id=1, source_target_pairs={{0,4},{4,8},{8,12},{12,16},{16,20},{20,24},{24,28},{28,32},{32,36}... | collective-permute-start | bytes 601352 | tf_op jit(solution)/shard_map/ppermute | solution.py:239
  72.9 7.5 %collective-permute-start.3 = (bf16[6,32,522]{2,1,0:T(8,128)(2,1)S(1)}, bf16[6,32,522]{2,1,0:T(8,128)(2,1)S(1)}, u32[]{:S(2)}, u32[]{:S(2)}) collective-permute-start(bf16[6,32,522]{2,1,0:T(8,128)(2,1)S(1)} %get-tuple-element.21), channel_id=1, source_target_pairs={{4,0},{8,4},{12,8},{16,12},{20,16},{24,20},{28,24},{32,28},{36,32}... | collective-permute-start | bytes 601352 | tf_op jit(solution)/shard_map/ppermute | solution.py:240

commit v4 on v3

--- a/solution.py
+++ b/solution.py
@@ -195,20 +195,18 @@
     mate = partners[me]
     times_here, nc = recorded.shape
     wide = C_DEV + 2 * REACH
-    padded = jnp.pad(recorded, ((0, 0), (REACH, 3 * C_DEV - REACH)))
+    by_channel = jnp.pad(jnp.transpose(recorded), ((REACH, 3 * C_DEV - REACH), (0, 0)))
     windows = jnp.concatenate(
-        [padded[:, k * C_DEV : k * C_DEV + nc].reshape(times_here, blocks, C_DEV) for k in range(3)], axis=2
-    )[:, :, :wide]
-    tag = jnp.zeros((times_here, blocks, 1), recorded.dtype).at[0].set(offsets[0].astype(recorded.dtype))
-    both = jnp.concatenate([windows, jnp.take(windows, partners, axis=1), tag], axis=2)
-    outgoing = jnp.transpose(both, (1, 0, 2))
-    arrived = lax.all_to_all(outgoing, "chan", split_axis=0, concat_axis=0, tiled=True)
-    mate_offset = arrived[:, 0, 2 * wide].astype(jnp.int32)[mate]
+        [by_channel[k * C_DEV : k * C_DEV + nc].reshape(blocks, C_DEV, times_here) for k in range(3)], axis=1
+    )[:, :wide]
+    tag = jnp.zeros((blocks, 1, times_here), recorded.dtype).at[:, 0, 0].set(offsets[0].astype(recorded.dtype))
+    both = jnp.concatenate([windows, jnp.take(windows, partners, axis=0), tag], axis=1)
+    outgoing = jnp.transpose(both.reshape(blocks, 2 * wide + 1, times_here // PH, PH), (0, 1, 3, 2))
+    arrived = lax.all_to_all(outgoing, "chan", split_axis=0, concat_axis=3, tiled=True)[0]
     times = blocks * times_here
     cols = times // PH
-    strain = jnp.transpose(
-        arrived[:, :, : 2 * wide].reshape(blocks, times_here // PH, PH, 2 * wide), (3, 2, 0, 1)
-    ).reshape(2 * wide, PH, cols)
+    mate_offset = arrived[2 * wide, 0].reshape(blocks, times_here // PH)[:, 0].astype(jnp.int32)[mate]
+    strain = arrived[: 2 * wide]
     tms = lax.axis_size("tm")
     up = [(i, i + 1) for i in range(tms - 1)]
     down = [(j, i) for i, j in up]

time: 99 us -> 101 us (1.020)
  local copies, waits for them, and re-layouts: 21.8 us -> 27.3 us
  waiting for transfers between devices: 10.3 us -> 4.85 us
    all_to_all x1, waiting for transfers between devices: 5.41 us -> 0.01 us  [on_device(): lax.all_to_all(outgoing, 'chan', split_axis=0, concat_axis=3, tiled=True)[0]]
    slice x5 -> x8, local copies, waits for them, and re-layouts: 1.42 us -> 6.03 us  [the longest x2 4.24 us: on_device(): strain = arrived[:2 * wide]]
    transpose x3 -> x1, local copies, waits for them, and re-layouts: 2.04 us -> 0.99 us  [on_device(): jnp.transpose(both.reshape(blocks, 2 * wide + 1, times_here // PH, PH), (...]
    unnamed x36 -> x45, local copies, waits for them, and re-layouts: 3 us -> 2.41 us
  transfers between devices with their start and end apart: 5 -> 5, of which waited for: 3 -> 2; matrix products, arithmetic and copies ran while one was open for 17% -> 21% of each run, Pallas kernels for 0% -> 0%
where the time goes in v4:
time: 101 us; the launch traced here: 99.6 us
  Pallas kernels  28 us (28%)
  local copies, waits for them, and re-layouts  27.3 us (27%)
  starting transfers between devices  24.8 us (25%)
  other arithmetic  9.41 us (9%)
  between operations  4.92 us (5%)
  waiting for transfers between devices  4.85 us (5%)
    pallas_call x4, Pallas kernels, banded(): pl.pallas_call(kernel, grid=(windows,), in_specs=specs, out_specs=pl.Bloc...  28 us
    all_to_all x1, starting transfers between devices, on_device(): lax.all_to_all(outgoing, 'chan', split_axis=0, concat_axis=3, tiled=True)[0]  13 us
    ppermute x1, starting transfers between devices, on_device(): before = lax.ppermute(strain[:, :, cols - WL:], 'tm', up)  4.58 us
    ppermute x1, waiting for transfers between devices, on_device(): below = lax.ppermute(second[:REACH], 'chan', ring_down)  4.4 us
    slice x2, local copies, waits for them, and re-layouts, on_device(): strain = arrived[:2 * wide]  4.24 us
    concatenate x1, local copies, waits for them, and re-layouts, on_device(): strain_wide = jnp.concatenate([before, strain, after], axis=2)  4.17 us
    ppermute x1, starting transfers between devices, on_device(): above = lax.ppermute(second[C_DEV - REACH:], 'chan', ring_up)  4.09 us
    unnamed x45, local copies, waits for them, and re-layouts  2.41 us
  transfers between devices with their start and end apart: 5, of which 2 were waited for; matrix products, arithmetic and copies ran while one was open for 21% of the time, Pallas kernels for 0%

profile of v4, /device:TPU:1, one launch (start us, length us, event | category | flops | bytes accessed | tf_op | source)
XLA Modules:
  0.0 99.6 jit_solution(12486317211121357233)
XLA Ops:
  0.0 0.7 compare_select_fusion
  0.7 0.7 compare_and_fusion.3
  1.4 1.0 pad_slice_fusion.2
  5.1 1.0 copy.76
  6.1 1.5 %reshape.312 = bf16[64,2,656]{2,1,0:T(2,128)(2,1)} reshape(bf16[64,4,8,41]{3,2,1,0:T(8,128)(2,1)S(1)} %bitcast.79) | data formatting | bytes 335872
  7.6 13.0 %all-to-all-start = ((bf16[64,2,656]{2,1,0:T(2,128)(2,1)}), bf16[64,2,656]{2,1,0:T(2,128)(2,1)S(1)}, u32[]{:S(2)}, u32[]{:S(2)}) async-start(bf16[64,2,656]{2,1,0:T(2,128)(2,1)} %reshape.312), calls=%async_computation | async-start | bytes 393216 | tf_op jit(solution)/shard_map/all_to_all | solution.py:205
  23.8 0.8 copy.84.b_ref
  25.5 0.7 copy.83.w_ref
  27.5 0.7 copy.86.w_ref
  28.4 0.9 reshape.276.w_ref
  30.8 0.8 copy.92.w_ref
  32.5 0.8 add_convert_fusion.m_ref
  33.3 0.7 and_convert_fusion.1
  34.0 0.8 reshape.313
  35.6 1.3 %collective-permute-start.1 = (bf16[40,4,8]{0,2,1:T(8,128)(2,1)S(1)}, bf16[40,4,8]{0,2,1:T(8,128)(2,1)}, u32[]{:S(2)}, u32[]{:S(2)}) collective-permute-start(bf16[40,4,8]{0,2,1:T(8,128)(2,1)S(1)} %slice.85), channel_id=1, source_target_pairs={{1,0},{2,1},{3,2},{5,4},{6,5},{7,6},{9,8},{10,9},{11,10},{13,12},{... | collective-permute-start | bytes 7688 | tf_op jit(solution)/shard_map/ppermute | solution.py:214
  36.9 4.6 %collective-permute-start = (bf16[40,4,7]{0,2,1:T(8,128)(2,1)}, bf16[40,4,7]{0,2,1:T(8,128)(2,1)}, u32[]{:S(2)}, u32[]{:S(2)}) collective-permute-start(bf16[40,4,7]{0,2,1:T(8,128)(2,1)} %slice.84), channel_id=1, source_target_pairs={{0,1},{1,2},{2,3},{4,5},{5,6},{6,7},{8,9},{9,10},{10,11},{12,13},{... | collective-permute-start | bytes 6728 | tf_op jit(solution)/shard_map/ppermute | solution.py:213
  43.5 4.2 %copy.79 = bf16[1,40,4,64,8]{4,3,2,1,0:T(8,128)(2,1)S(1)} copy(bf16[1,40,4,64,8]{1,4,2,3,0:T(8,128)(2,1)S(1)} %bitcast.78) | data formatting | bytes 327680 | tf_op jit(solution)/shard_map/slice | solution.py:209
  47.6 4.2 %concatenate.27 = bf16[2,80,512]{2,1,0:T(8,128)(2,1)S(1)} reshape(bf16[1,40,4,64,8]{4,3,2,1,0:T(8,128)(2,1)S(1)} %copy.79) | data formatting | bytes 327680 | tf_op jit(solution)/shard_map/concatenate | solution.py:215
  51.8 0.8 copy.78
  52.7 0.8 copy.80
  53.5 0.8 pad_maximum_fusion.3.x_ref
  54.3 6.2 %shard_map.181.x_ref = bf16[2,14,64,524]{3,2,1,0:T(8,128)(2,1)} custom-call(bf16[2,80,527]{2,1,0:T(8,128)(2,1)} %pad_maximum_fusion.3.x_ref, bf16[256,28]{1,0:T(8,128)(2,1)} %copy.83.w_ref, f32[144,1]{1,0:T(8,128)} %copy.84.b_ref, f32[2,14,4,524]{3,2,1,0:T(4,128)} %add_convert_fusion.m_ref), custom_call_target="tpu_custom_call" | custom-call | tf_op jit(solution)/shard_map/pallas_call | solution.py:86
  61.1 7.2 %shard_map.182 = bf16[2,8,32,522]{3,2,1,0:T(8,128)(2,1)} custom-call(bf16[2,14,64,524]{3,2,1,0:T(8,128)(2,1)} %shard_map.181.x_ref, bf16[96,448]{1,0:T(8,128)(2,1)} %copy.86.w_ref, f32[144,1]{1,0:T(8,128)} %copy.84.b_ref, f32[2,8,1,522]{3,2,1,0:T(1,128)} %broadcast_in_dim.125.m_ref), custom_call_target="tpu_custom_call" | custom-call | tf_op jit(solution)/shard_map/pallas_call | solution.py:86
  68.3 1.2 %slice_convert_fusion = (f32[1,8,32,522]{3,2,1,0:T(8,128)S(1)}, f32[8,32,522]{2,1,0:T(8,128)S(1)}, bf16[1,8,32,522]{3,2,1,0:T(8,128)(2,1)S(1)}) fusion(bf16[2,8,32,522]{3,2,1,0:T(8,128)(2,1)} %shard_map.182), kind=kLoop, calls=%fused_computation.19 | loop fusion | flops 133632 | bytes 1870848 | tf_op jit(solution)/shard_map/convert_element_type | solution.py:233
  70.0 4.1 %collective-permute-start.2 = (bf16[6,32,522]{2,1,0:T(8,128)(2,1)S(1)}, bf16[6,32,522]{2,1,0:T(8,128)(2,1)S(1)}, u32[]{:S(2)}, u32[]{:S(2)}) collective-permute-start(bf16[6,32,522]{2,1,0:T(8,128)(2,1)S(1)} %get-tuple-element.20), channel_id=1, source_target_pairs={{0,4},{4,8},{8,12},{12,16},{16,20},{20,24},{24,28},{28,32},{32,36}... | collective-permute-start | bytes 601352 | tf_op jit(solution)/shard_map/ppermute | solution.py:237
  74.1 1.9 %collective-permute-start.3 = (bf16[6,32,522]{2,1,0:T(8,128)(2,1)S(1)}, bf16[6,32,522]{2,1,0:T(8,128)(2,1)S(1)}, u32[]{:S(2)}, u32[]{:S(2)}) collective-permute-start(bf16[6,32,522]{2,1,0:T(8,128)(2,1)S(1)} %get-tuple-element.21), channel_id=1, source_target_pairs={{4,0},{8,4},{12,8},{16,12},{20,16},{24,20},{28,24},{32,28},{36,32}... | collective-permute-start | bytes 601352 | tf_op jit(solution)/shard_map/ppermute | solution.py:238
  76.0 0.7 and_convert_fusion.m_ref
  77.2 4.4 %collective-permute-done.3 = bf16[6,32,522]{2,1,0:T(8,128)(2,1)S(1)} collective-permute-done((bf16[6,32,522]{2,1,0:T(8,128)(2,1)S(1)}, bf16[6,32,522]{2,1,0:T(8,128)(2,1)S(1)}, u32[]{:S(2)}, u32[]{:S(2)}) %collective-permute-start.3) | collective-permute-done | bytes 200480 | tf_op jit(solution)/shard_map/ppermute | solution.py:238
  81.6 1.0 %maximum_bitcast_fusion.x_ref = bf16[1,20,32,522]{3,2,1,0:T(8,128)(2,1)} fusion(bf16[6,32,522]{2,1,0:T(8,128)(2,1)S(1)} %collective-permute-done.3, bf16[8,32,522]{2,1,0:T(8,128)(2,1)S(1)} %multiply_convert_fusion, bf16[6,32,522]{2,1,0:T(8,128)(2,1)S(1)} %collective-permute-done.2), kind=kLoop, calls=%fused_computation.8 | loop fusion | flops 668160 | bytes 1336320 | tf_op jit(solution)/shard_map/broadcast_in_dim | solution.py:245
  82.6 10.2 %shard_map.183.x_ref = bf16[1,14,128,129]{3,2,1,0:T(8,128)(2,1)} custom-call(bf16[1,20,32,522]{3,2,1,0:T(8,128)(2,1)} %maximum_bitcast_fusion.x_ref, bf16[224,224]{1,0:T(8,128)(2,1)} %reshape.276.w_ref, f32[144,1]{1,0:T(8,128)} %copy.84.b_ref, f32[1,14,1,516]{3,2,1,0:T(1,128)} %and_convert_fusion.m_ref, bf16[128,128]{1,0:T(8,128)(2,1)} %constant.163.clone.rest_0_), custom_call_target="tpu_custom_call" | custom-call | tf_op jit(solution)/shard_map/pallas_call | solution.py:86
  93.5 4.5 %shard_map.184 = bf16[1,8,64,128]{3,2,1,0:T(8,128)(2,1)} custom-call(bf16[1,14,128,129]{3,2,1,0:T(8,128)(2,1)} %shard_map.183.x_ref, bf16[128,896]{1,0:T(8,128)(2,1)} %copy.92.w_ref, f32[144,1]{1,0:T(8,128)} %copy.84.b_ref, f32[1,8,1,128]{3,2,1,0:T(1,128)} %broadcast_in_dim.134.m_ref), custom_call_target="tpu_custom_call" | custom-call | tf_op jit(solution)/shard_map/pallas_call | solution.py:86
  97.9 1.6 %copy.94 = bf16[64,8,128]{2,1,0:T(8,128)(2,1)} copy(bf16[64,8,128]{2,0,1:T(8,128)(2,1)} %bitcast.84) | data formatting | bytes 262144 | tf_op jit(solution)/shard_map/transpose | solution.py:268
  (95 shorter events, 10.9 us)
Async XLA Ops:
  0.0 29.3 %copy-start = (bf16[64,32,7,7]{0,1,3,2:T(8,128)(2,1)S(1)}, bf16[64,32,7,7]{0,1,3,2:T(8,128)(2,1)}, u32[]{:S(2)}) copy-start(bf16[64,32,7,7]{0,1,3,2:T(8,128)(2,1)} %param.31) | copy-start | bytes 602116
  2.8 17.8 %copy-start.20 = (s32[64]{0:T(128)S(1)}, s32[64]{0:T(128)}, u32[]{:S(2)}) copy-start(s32[64]{0:T(128)} %param.22) | copy-start | bytes 772
  2.9 20.9 %copy-start.15 = (f32[64]{0:T(128)S(1)}, f32[64]{0:T(128)}, u32[]{:S(2)}) copy-start(f32[64]{0:T(128)} %param.32) | copy-start | bytes 772
  2.9 20.9 %copy-start.16 = (f32[32]{0:T(128)S(1)}, f32[32]{0:T(128)}, u32[]{:S(2)}) copy-start(f32[32]{0:T(128)} %param.30) | copy-start | bytes 388
  2.9 20.9 %copy-start.17 = (f32[32]{0:T(128)S(1)}, f32[32]{0:T(128)}, u32[]{:S(2)}) copy-start(f32[32]{0:T(128)} %param.27) | copy-start | bytes 388
  2.9 20.9 %copy-start.18 = (f32[16]{0:T(128)S(1)}, f32[16]{0:T(128)}, u32[]{:S(2)}) copy-start(f32[16]{0:T(128)} %param.25) | copy-start | bytes 196
  2.9 21.7 %copy-start.5 = (bf16[16,1,7,7]{0,3,2,1:T(8,128)(2,1)S(1)}, bf16[16,1,7,7]{0,3,2,1:T(8,128)(2,1)}, u32[]{:S(2)}) copy-start(bf16[16,1,7,7]{0,3,2,1:T(8,128)(2,1)} %param.24) | copy-start | bytes 4708
  2.9 21.7 %copy-start.14 = (s32[64]{0:T(128)S(1)}, s32[64]{0:T(128)}, u32[]{:S(2)}) copy-start(s32[64]{0:T(128)} %constant.202) | copy-start | bytes 772
  3.2 22.1 %copy-start.10 = (pred[4,4,4]{1,0,2:T(4,128)(4,1)S(1)}, pred[4,4,4]{1,0,2:T(4,128)(4,1)}, u32[]{:S(2)}) copy-start(pred[4,4,4]{1,0,2:T(4,128)(4,1)} %constant.172) | copy-start | bytes 196
  3.2 23.1 %copy-start.13 = (s32[12]{0:T(128)S(1)}, s32[12]{0:T(128)}, u32[]{:S(2)}) copy-start(s32[12]{0:T(128)} %constant.203) | copy-start | bytes 148
  3.2 23.1 %copy-start.1 = (bf16[32,16,7,7]{0,1,3,2:T(8,128)(2,1)S(1)}, bf16[32,16,7,7]{0,1,3,2:T(8,128)(2,1)}, u32[]{:S(2)}) copy-start(bf16[32,16,7,7]{0,1,3,2:T(8,128)(2,1)} %param.26) | copy-start | bytes 150532
  5.0 21.9 %copy-start.19 = (pred[3,4]{0,1:T(4,128)(4,1)S(1)}, pred[3,4]{0,1:T(4,128)(4,1)}, u32[]{:S(2)}) copy-start(pred[3,4]{0,1:T(4,128)(4,1)} %constant.181) | copy-start | bytes 40
  6.1 22.1 %copy-start.2 = (bf16[32,32,7,7]{1,0,3,2:T(8,128)(2,1)S(1)}, bf16[32,32,7,7]{1,0,3,2:T(8,128)(2,1)}, u32[]{:S(2)}) copy-start(bf16[32,32,7,7]{1,0,3,2:T(8,128)(2,1)} %param.29) | copy-start | bytes 301060
  7.6 26.4 %all-to-all-start = ((bf16[64,2,656]{2,1,0:T(2,128)(2,1)}), bf16[64,2,656]{2,1,0:T(2,128)(2,1)S(1)}, u32[]{:S(2)}, u32[]{:S(2)}) async-start(bf16[64,2,656]{2,1,0:T(2,128)(2,1)} %reshape.312), calls=%async_computation | async-start | bytes 393216 | tf_op jit(solution)/shard_map/all_to_all | solution.py:205
  25.5 3.8 %copy-start.12 = (s32[8]{0:T(128)S(1)}, s32[8]{0:T(128)}, u32[]{:S(2)}) copy-start(s32[8]{0:T(128)} %constant.204) | copy-start | bytes 100
  29.4 0.7 copy-start.11
  32.3 11.2 %copy-start.6 = (pred[14]{0:T(512)(128)(4,1)}, pred[14]{0:T(512)(128)(4,1)S(1)}, u32[]{:S(2)}) copy-start(pred[14]{0:T(512)(128)(4,1)S(1)} %get-tuple-element.28) | copy-start | bytes 46
  35.6 17.0 %collective-permute-start.1 = (bf16[40,4,8]{0,2,1:T(8,128)(2,1)S(1)}, bf16[40,4,8]{0,2,1:T(8,128)(2,1)}, u32[]{:S(2)}, u32[]{:S(2)}) collective-permute-start(bf16[40,4,8]{0,2,1:T(8,128)(2,1)S(1)} %slice.85), channel_id=1, source_target_pairs={{1,0},{2,1},{3,2},{5,4},{6,5},{7,6},{9,8},{10,9},{11,10},{13,12},{... | collective-permute-start | bytes 7688 | tf_op jit(solution)/shard_map/ppermute | solution.py:214
  36.9 14.9 %collective-permute-start = (bf16[40,4,7]{0,2,1:T(8,128)(2,1)}, bf16[40,4,7]{0,2,1:T(8,128)(2,1)}, u32[]{:S(2)}, u32[]{:S(2)}) collective-permute-start(bf16[40,4,7]{0,2,1:T(8,128)(2,1)} %slice.84), channel_id=1, source_target_pairs={{0,1},{1,2},{2,3},{4,5},{5,6},{6,7},{8,9},{9,10},{10,11},{12,13},{... | collective-permute-start | bytes 6728 | tf_op jit(solution)/shard_map/ppermute | solution.py:213
  61.1 8.5 %copy-start.4 = (bf16[7,32,32]{2,1,0:T(8,128)(2,1)S(1)}, bf16[7,32,32]{2,1,0:T(8,128)(2,1)}, u32[]{:S(2)}) copy-start(bf16[7,32,32]{2,1,0:T(8,128)(2,1)} %param.28) | copy-start | bytes 43012
  68.3 1.6 %copy-start.3 = (f32[8,522]{1,0:T(8,128)S(1)}, f32[8,522]{1,0:T(8,128)}, u32[]{:S(2)}) copy-start(f32[8,522]{1,0:T(8,128)} %and_convert_fusion.1) | copy-start | bytes 50116
  69.5 6.5 %copy-start.7 = (pred[14]{0:T(512)(128)(4,1)S(1)}, pred[14]{0:T(512)(128)(4,1)}, u32[]{:S(2)}) copy-start(pred[14]{0:T(512)(128)(4,1)} %copy-done.6) | copy-start | bytes 46
  69.5 6.5 %copy-start.8 = (pred[516]{0:T(1024)(128)(4,1)S(1)}, pred[516]{0:T(1024)(128)(4,1)}, u32[]{:S(2)}) copy-start(pred[516]{0:T(1024)(128)(4,1)} %get-tuple-element.31) | copy-start | bytes 1552
  69.5 6.5 %copy-start.9 = (pred[516]{0:T(1024)(128)(4,1)S(1)}, pred[516]{0:T(1024)(128)(4,1)}, u32[]{:S(2)}) copy-start(pred[516]{0:T(1024)(128)(4,1)} %get-tuple-element.32) | copy-start | bytes 1552
  70.0 7.2 %collective-permute-start.2 = (bf16[6,32,522]{2,1,0:T(8,128)(2,1)S(1)}, bf16[6,32,522]{2,1,0:T(8,128)(2,1)S(1)}, u32[]{:S(2)}, u32[]{:S(2)}) collective-permute-start(bf16[6,32,522]{2,1,0:T(8,128)(2,1)S(1)} %get-tuple-element.20), channel_id=1, source_target_pairs={{0,4},{4,8},{8,12},{12,16},{16,20},{20,24},{24,28},{28,32},{32,36}... | collective-permute-start | bytes 601352 | tf_op jit(solution)/shard_map/ppermute | solution.py:237
  74.1 7.5 %collective-permute-start.3 = (bf16[6,32,522]{2,1,0:T(8,128)(2,1)S(1)}, bf16[6,32,522]{2,1,0:T(8,128)(2,1)S(1)}, u32[]{:S(2)}, u32[]{:S(2)}) collective-permute-start(bf16[6,32,522]{2,1,0:T(8,128)(2,1)S(1)} %get-tuple-element.21), channel_id=1, source_target_pairs={{4,0},{8,4},{12,8},{16,12},{20,16},{24,20},{28,24},{32,28},{36,32}... | collective-permute-start | bytes 601352 | tf_op jit(solution)/shard_map/ppermute | solution.py:238

commit v5 on v3

--- a/solution.py
+++ b/solution.py
@@ -92,6 +92,28 @@
     )(*args)
 
 
+def strain_layout(raw, left, right, rows):
+    channels = raw.shape[1]
+    cols = raw.shape[0] // PH
+    n_out = WL + cols + WR
+
+    def kernel(raw_ref, l_ref, r_ref, o_ref):
+        ci = lax.broadcasted_iota(jnp.int32, (rows, channels), 1)
+        ri = lax.broadcasted_iota(jnp.int32, (rows, channels), 0)
+        nt = (((1,), (1,)), ((), ()))
+        pieces = ((l_ref, 0, left.shape[0] // PH, left.shape[0] // PH - WL), (raw_ref, WL, cols, 0), (r_ref, WL + cols, WR, 0))
+        for src, lo, n, skip in pieces:
+            acc = None
+            for q in range(PH):
+                e = (ri == ci * PH + q).astype(jnp.float32)
+                piece = src[pl.ds(q, n, stride=PH), :].astype(jnp.float32)
+                y = lax.dot_general(e, piece, nt, preferred_element_type=jnp.float32)
+                acc = y if acc is None else acc + y
+            o_ref[:, lo : lo + n - skip] = acc[:, skip:].astype(o_ref.dtype)
+
+    return pl.pallas_call(kernel, out_shape=jax.ShapeDtypeStruct((rows, n_out), jnp.bfloat16))(raw, left, right)
+
+
 def weights_stride1(w):
     fout, fin = w.shape[:2]
     return jnp.transpose(w, (3, 0, 2, 1)).reshape(7 * fout, 7 * fin)
@@ -205,16 +227,12 @@
     arrived = lax.all_to_all(outgoing, "chan", split_axis=0, concat_axis=0, tiled=True)
     mate_offset = arrived[:, 0, 2 * wide].astype(jnp.int32)[mate]
     times = blocks * times_here
-    cols = times // PH
-    strain = jnp.transpose(
-        arrived[:, :, : 2 * wide].reshape(blocks, times_here // PH, PH, 2 * wide), (3, 2, 0, 1)
-    ).reshape(2 * wide, PH, cols)
     tms = lax.axis_size("tm")
     up = [(i, i + 1) for i in range(tms - 1)]
     down = [(j, i) for i, j in up]
-    before = lax.ppermute(strain[:, :, cols - WL :], "tm", up)
-    after = lax.ppermute(strain[:, :, :WR], "tm", down)
-    strain_wide = jnp.concatenate([before, strain, after], axis=2)
+    before = lax.ppermute(arrived[blocks - 1], "tm", up)
+    after = lax.ppermute(arrived[0, : PH * WR], "tm", down)
+    strain_wide = strain_layout(arrived.reshape(times, -1), before, after, 2 * wide * PH)
 
     quarter = times // 4
     length = quarter + 2 * LEAD

time: 99 us -> 94.2 us (0.952)
  local copies, waits for them, and re-layouts: 21.8 us -> 16.3 us
  Pallas kernels: 28.1 us -> 30.3 us
  starting transfers between devices: 24.4 us -> 23 us
    concatenate x1 -> x0, local copies, waits for them, and re-layouts: 4.18 us -> none  [on_device(): strain_wide = jnp.concatenate([before, strain, after], axis=2)]
    pallas_call x0 -> x1, Pallas kernels: none -> 2.24 us  [strain_layout(): pl.pallas_call(kernel, out_shape=jax.ShapeDtypeStruct((rows, n_out), jnp....]
    transpose x3 -> x0, local copies, waits for them, and re-layouts: 2.04 us -> none  [the longest x2 1.54 us: on_device(): jnp.transpose(arrived[:, :, :2 * wide].reshape(blocks, times_here // PH,...]
    unnamed x36 -> x41, local copies, waits for them, and re-layouts: 3 us -> 2.97 us
  transfers between devices with their start and end apart: 5 -> 5, of which waited for: 3 -> 3; matrix products, arithmetic and copies ran while one was open for 17% -> 12% of each run, Pallas kernels for 0% -> 0%
where the time goes in v5:
time: 94.2 us; the launch traced here: 93.4 us
  Pallas kernels  30.3 us (32%)
  starting transfers between devices  23 us (24%)
  local copies, waits for them, and re-layouts  16.3 us (17%)
  waiting for transfers between devices  10.4 us (11%)
  other arithmetic  8.29 us (9%)
  between operations  4.92 us (5%)
    pallas_call x4, Pallas kernels, banded(): pl.pallas_call(kernel, grid=(windows,), in_specs=specs, out_specs=pl.Bloc...  28.1 us
    all_to_all x1, starting transfers between devices, on_device(): lax.all_to_all(outgoing, 'chan', split_axis=0, concat_axis=0, tiled=True)  13 us
    all_to_all x1, waiting for transfers between devices, on_device(): lax.all_to_all(outgoing, 'chan', split_axis=0, concat_axis=0, tiled=True)  5.53 us
    ppermute x1, waiting for transfers between devices, on_device(): below = lax.ppermute(second[:REACH], 'chan', ring_down)  4.4 us
    ppermute x1, starting transfers between devices, on_device(): above = lax.ppermute(second[C_DEV - REACH:], 'chan', ring_up)  3.6 us
    ppermute x1, starting transfers between devices, on_device(): before = lax.ppermute(arrived[blocks - 1], 'tm', up)  3.2 us
    unnamed x41, local copies, waits for them, and re-layouts  2.97 us
    pallas_call x1, Pallas kernels, strain_layout(): pl.pallas_call(kernel, out_shape=jax.ShapeDtypeStruct((rows, n_out), jnp....  2.24 us
  transfers between devices with their start and end apart: 5, of which 3 were waited for; matrix products, arithmetic and copies ran while one was open for 12% of the time, Pallas kernels for 0%

profile of v5, /device:TPU:1, one launch (start us, length us, event | category | flops | bytes accessed | tf_op | source)
XLA Modules:
  0.0 93.4 jit_solution(13133921331457995878)
XLA Ops:
  0.0 0.7 compare_select_fusion
  0.7 0.7 compare_and_fusion.3
  1.4 1.0 %pad_slice_fusion.2 = (bf16[32,512]{1,0:T(8,128)(2,1)S(1)}, bf16[32,512]{1,0:T(8,128)(2,1)S(1)}, bf16[32,512]{1,0:T(8,128)(2,1)S(1)}) fusion(bf16[32,512]{1,0:T(8,128)(2,1)} %param.21), kind=kLoop, calls=%fused_computation.33 | loop fusion | bytes 131072 | tf_op jit(solution)/shard_map/slice | solution.py:222
  4.8 0.7 gather_fusion
  6.3 1.5 %reshape.306 = bf16[64,2,656]{2,1,0:T(2,128)(2,1)} reshape(bf16[64,32,41]{2,1,0:T(8,128)(2,1)S(1)} %maximum_bitcast_fusion.1) | data formatting | bytes 335872
  7.8 13.0 %all-to-all-start = ((bf16[64,2,656]{2,1,0:T(2,128)(2,1)}), bf16[64,2,656]{2,1,0:T(2,128)(2,1)S(1)}, u32[]{:S(2)}, u32[]{:S(2)}) async-start(bf16[64,2,656]{2,1,0:T(2,128)(2,1)} %reshape.306), calls=%async_computation | async-start | bytes 393216 | tf_op jit(solution)/shard_map/all_to_all | solution.py:227
  22.3 0.8 add_convert_fusion.m_ref
  23.1 0.6 gather_fusion.1
  23.8 0.6 gather_fusion.2
  24.9 0.6 gather_fusion.3
  26.2 5.5 %all-to-all-done = bf16[64,2,656]{2,1,0:T(2,128)(2,1)S(1)} async-done(((bf16[64,2,656]{2,1,0:T(2,128)(2,1)}), bf16[64,2,656]{2,1,0:T(2,128)(2,1)S(1)}, u32[]{:S(2)}, u32[]{:S(2)}) %all-to-all-start) | async-done | bytes 167968 | tf_op jit(solution)/shard_map/all_to_all | solution.py:227
  31.7 0.8 reshape.307
  32.6 3.2 %collective-permute-start = (bf16[32,41]{1,0:T(8,128)(2,1)S(1)}, bf16[32,41]{1,0:T(8,128)(2,1)S(1)}, u32[]{:S(2)}, u32[]{:S(2)}) collective-permute-start(bf16[32,41]{1,0:T(8,128)(2,1)S(1)} %get-tuple-element.21), channel_id=1, source_target_pairs={{0,1},{1,2},{2,3},{4,5},{5,6},{6,7},{8,9},{9,10},{10,11},{12,13},{... | collective-permute-start | bytes 7880 | tf_op jit(solution)/shard_map/ppermute | solution.py:233
  35.8 1.3 %collective-permute-start.1 = (bf16[32,41]{1,0:T(8,128)(2,1)S(1)}, bf16[32,41]{1,0:T(8,128)(2,1)S(1)}, u32[]{:S(2)}, u32[]{:S(2)}) collective-permute-start(bf16[32,41]{1,0:T(8,128)(2,1)S(1)} %get-tuple-element.20), channel_id=1, source_target_pairs={{1,0},{2,1},{3,2},{5,4},{6,5},{7,6},{9,8},{10,9},{11,10},{13,12},{... | collective-permute-start | bytes 7880 | tf_op jit(solution)/shard_map/ppermute | solution.py:234
  38.3 0.7 copy.73.b_ref
  39.2 0.7 copy.72.w_ref
  40.2 0.7 copy.75.w_ref
  41.1 0.9 reshape.271.w_ref
  42.3 0.9 copy.80.w_ref
  46.4 2.2 %shard_map.181 = bf16[160,527]{1,0:T(8,128)(2,1)} custom-call(bf16[2048,41]{1,0:T(8,128)(2,1)} %bitcast.65, bf16[32,41]{1,0:T(8,128)(2,1)} %copy-done.6, bf16[32,41]{1,0:T(8,128)(2,1)} %copy-done.7), custom_call_target="tpu_custom_call" | custom-call | tf_op jit(solution)/shard_map/pallas_call | solution.py:114
  48.7 6.2 %shard_map.182.x_ref = bf16[2,14,64,524]{3,2,1,0:T(8,128)(2,1)} custom-call(bf16[2,80,527]{2,1,0:T(8,128)(2,1)} %bitcast.66, bf16[256,28]{1,0:T(8,128)(2,1)} %copy.72.w_ref, f32[144,1]{1,0:T(8,128)} %copy.73.b_ref, f32[2,14,4,524]{3,2,1,0:T(4,128)} %add_convert_fusion.m_ref), custom_call_target="tpu_custom_call" | custom-call | tf_op jit(solution)/shard_map/pallas_call | solution.py:86
  54.8 0.6 broadcast_in_dim.125.m_ref
  55.5 7.2 %shard_map.183 = bf16[2,8,32,522]{3,2,1,0:T(8,128)(2,1)} custom-call(bf16[2,14,64,524]{3,2,1,0:T(8,128)(2,1)} %shard_map.182.x_ref, bf16[96,448]{1,0:T(8,128)(2,1)} %copy.75.w_ref, f32[144,1]{1,0:T(8,128)} %copy.73.b_ref, f32[2,8,1,522]{3,2,1,0:T(1,128)} %broadcast_in_dim.125.m_ref), custom_call_target="tpu_custom_call" | custom-call | tf_op jit(solution)/shard_map/pallas_call | solution.py:86
  62.6 1.2 %slice_convert_fusion = (f32[1,8,32,522]{3,2,1,0:T(8,128)S(1)}, f32[8,32,522]{2,1,0:T(8,128)S(1)}, bf16[1,8,32,522]{3,2,1,0:T(8,128)(2,1)S(1)}) fusion(bf16[2,8,32,522]{3,2,1,0:T(8,128)(2,1)} %shard_map.183), kind=kLoop, calls=%fused_computation.17 | loop fusion | flops 133632 | bytes 1870848 | tf_op jit(solution)/shard_map/convert_element_type | solution.py:253
  64.3 3.6 %collective-permute-start.2 = (bf16[6,32,522]{2,1,0:T(8,128)(2,1)S(1)}, bf16[6,32,522]{2,1,0:T(8,128)(2,1)S(1)}, u32[]{:S(2)}, u32[]{:S(2)}) collective-permute-start(bf16[6,32,522]{2,1,0:T(8,128)(2,1)S(1)} %get-tuple-element.22), channel_id=1, source_target_pairs={{0,4},{4,8},{8,12},{12,16},{16,20},{20,24},{24,28},{28,32},{32,36}... | collective-permute-start | bytes 601352 | tf_op jit(solution)/shard_map/ppermute | solution.py:257
  67.9 1.9 %collective-permute-start.3 = (bf16[6,32,522]{2,1,0:T(8,128)(2,1)S(1)}, bf16[6,32,522]{2,1,0:T(8,128)(2,1)S(1)}, u32[]{:S(2)}, u32[]{:S(2)}) collective-permute-start(bf16[6,32,522]{2,1,0:T(8,128)(2,1)S(1)} %get-tuple-element.23), channel_id=1, source_target_pairs={{4,0},{8,4},{12,8},{16,12},{20,16},{24,20},{28,24},{32,28},{36,32}... | collective-permute-start | bytes 601352 | tf_op jit(solution)/shard_map/ppermute | solution.py:258
  69.8 0.7 and_convert_fusion.m_ref
  71.0 4.4 %collective-permute-done.3 = bf16[6,32,522]{2,1,0:T(8,128)(2,1)S(1)} collective-permute-done((bf16[6,32,522]{2,1,0:T(8,128)(2,1)S(1)}, bf16[6,32,522]{2,1,0:T(8,128)(2,1)S(1)}, u32[]{:S(2)}, u32[]{:S(2)}) %collective-permute-start.3) | collective-permute-done | bytes 200480 | tf_op jit(solution)/shard_map/ppermute | solution.py:258
  75.4 1.0 %maximum_bitcast_fusion.x_ref = bf16[1,20,32,522]{3,2,1,0:T(8,128)(2,1)} fusion(bf16[6,32,522]{2,1,0:T(8,128)(2,1)S(1)} %collective-permute-done.3, bf16[8,32,522]{2,1,0:T(8,128)(2,1)S(1)} %multiply_convert_fusion, bf16[6,32,522]{2,1,0:T(8,128)(2,1)S(1)} %collective-permute-done.2), kind=kLoop, calls=%fused_computation.8 | loop fusion | flops 668160 | bytes 1336320 | tf_op jit(solution)/shard_map/broadcast_in_dim | solution.py:265
  76.4 10.2 %shard_map.184.x_ref = bf16[1,14,128,129]{3,2,1,0:T(8,128)(2,1)} custom-call(bf16[1,20,32,522]{3,2,1,0:T(8,128)(2,1)} %maximum_bitcast_fusion.x_ref, bf16[224,224]{1,0:T(8,128)(2,1)} %reshape.271.w_ref, f32[144,1]{1,0:T(8,128)} %copy.73.b_ref, f32[1,14,1,516]{3,2,1,0:T(1,128)} %and_convert_fusion.m_ref, bf16[128,128]{1,0:T(8,128)(2,1)} %constant.160.clone.rest_0_), custom_call_target="tpu_custom_call" | custom-call | tf_op jit(solution)/shard_map/pallas_call | solution.py:86
  87.3 4.5 %shard_map.185 = bf16[1,8,64,128]{3,2,1,0:T(8,128)(2,1)} custom-call(bf16[1,14,128,129]{3,2,1,0:T(8,128)(2,1)} %shard_map.184.x_ref, bf16[128,896]{1,0:T(8,128)(2,1)} %copy.80.w_ref, f32[144,1]{1,0:T(8,128)} %copy.73.b_ref, f32[1,8,1,128]{3,2,1,0:T(1,128)} %broadcast_in_dim.134.m_ref), custom_call_target="tpu_custom_call" | custom-call | tf_op jit(solution)/shard_map/pallas_call | solution.py:86
  91.7 1.6 %copy.82 = bf16[64,8,128]{2,1,0:T(8,128)(2,1)} copy(bf16[64,8,128]{2,0,1:T(8,128)(2,1)} %bitcast.70) | data formatting | bytes 262144 | tf_op jit(solution)/shard_map/transpose | solution.py:288
  (82 shorter events, 8.1 us)
Async XLA Ops:
  0.0 24.8 %copy-start = (bf16[64,32,7,7]{0,1,3,2:T(8,128)(2,1)S(1)}, bf16[64,32,7,7]{0,1,3,2:T(8,128)(2,1)}, u32[]{:S(2)}) copy-start(bf16[64,32,7,7]{0,1,3,2:T(8,128)(2,1)} %param.31) | copy-start | bytes 602116
  5.4 15.4 %copy-start.18 = (s32[64]{0:T(128)S(1)}, s32[64]{0:T(128)}, u32[]{:S(2)}) copy-start(s32[64]{0:T(128)} %param.22) | copy-start | bytes 772
  5.4 16.5 %copy-start.5 = (bf16[16,1,7,7]{0,3,2,1:T(8,128)(2,1)S(1)}, bf16[16,1,7,7]{0,3,2,1:T(8,128)(2,1)}, u32[]{:S(2)}) copy-start(bf16[16,1,7,7]{0,3,2,1:T(8,128)(2,1)} %param.24) | copy-start | bytes 4708
  5.4 16.6 %copy-start.12 = (s32[64]{0:T(128)S(1)}, s32[64]{0:T(128)}, u32[]{:S(2)}) copy-start(s32[64]{0:T(128)} %constant.199) | copy-start | bytes 772
  5.5 16.6 %copy-start.11 = (s32[12]{0:T(128)S(1)}, s32[12]{0:T(128)}, u32[]{:S(2)}) copy-start(s32[12]{0:T(128)} %constant.200) | copy-start | bytes 148
  5.5 16.6 %copy-start.10 = (s32[8]{0:T(128)S(1)}, s32[8]{0:T(128)}, u32[]{:S(2)}) copy-start(s32[8]{0:T(128)} %constant.201) | copy-start | bytes 100
  5.6 18.1 %copy-start.8 = (pred[4,4,4]{1,0,2:T(4,128)(4,1)S(1)}, pred[4,4,4]{1,0,2:T(4,128)(4,1)}, u32[]{:S(2)}) copy-start(pred[4,4,4]{1,0,2:T(4,128)(4,1)} %constant.169) | copy-start | bytes 196
  5.6 18.2 %copy-start.1 = (bf16[32,16,7,7]{0,1,3,2:T(8,128)(2,1)S(1)}, bf16[32,16,7,7]{0,1,3,2:T(8,128)(2,1)}, u32[]{:S(2)}) copy-start(bf16[32,16,7,7]{0,1,3,2:T(8,128)(2,1)} %param.26) | copy-start | bytes 150532
  6.3 18.2 %copy-start.17 = (pred[3,4]{0,1:T(4,128)(4,1)S(1)}, pred[3,4]{0,1:T(4,128)(4,1)}, u32[]{:S(2)}) copy-start(pred[3,4]{0,1:T(4,128)(4,1)} %constant.178) | copy-start | bytes 40
  7.8 23.9 %all-to-all-start = ((bf16[64,2,656]{2,1,0:T(2,128)(2,1)}), bf16[64,2,656]{2,1,0:T(2,128)(2,1)S(1)}, u32[]{:S(2)}, u32[]{:S(2)}) async-start(bf16[64,2,656]{2,1,0:T(2,128)(2,1)} %reshape.306), calls=%async_computation | async-start | bytes 393216 | tf_op jit(solution)/shard_map/all_to_all | solution.py:227
  24.8 0.8 copy-start.9
  24.8 12.2 %copy-start.13 = (f32[64]{0:T(128)S(1)}, f32[64]{0:T(128)}, u32[]{:S(2)}) copy-start(f32[64]{0:T(128)} %param.32) | copy-start | bytes 772
  24.8 12.2 %copy-start.14 = (f32[32]{0:T(128)S(1)}, f32[32]{0:T(128)}, u32[]{:S(2)}) copy-start(f32[32]{0:T(128)} %param.30) | copy-start | bytes 388
  24.8 12.2 %copy-start.15 = (f32[32]{0:T(128)S(1)}, f32[32]{0:T(128)}, u32[]{:S(2)}) copy-start(f32[32]{0:T(128)} %param.27) | copy-start | bytes 388
  24.9 12.2 %copy-start.16 = (f32[16]{0:T(128)S(1)}, f32[16]{0:T(128)}, u32[]{:S(2)}) copy-start(f32[16]{0:T(128)} %param.25) | copy-start | bytes 196
  25.5 15.4 %copy-start.3 = (bf16[32,32,7,7]{1,0,3,2:T(8,128)(2,1)S(1)}, bf16[32,32,7,7]{1,0,3,2:T(8,128)(2,1)}, u32[]{:S(2)}) copy-start(bf16[32,32,7,7]{1,0,3,2:T(8,128)(2,1)} %param.29) | copy-start | bytes 301060
  32.5 13.3 %copy-start.2 = (bf16[64,32,41]{2,1,0:T(8,128)(2,1)}, bf16[64,32,41]{2,1,0:T(8,128)(2,1)S(1)}, u32[]{:S(2)}) copy-start(bf16[64,32,41]{2,1,0:T(8,128)(2,1)S(1)} %reshape.307) | copy-start | bytes 503812
  32.6 13.2 %collective-permute-start = (bf16[32,41]{1,0:T(8,128)(2,1)S(1)}, bf16[32,41]{1,0:T(8,128)(2,1)S(1)}, u32[]{:S(2)}, u32[]{:S(2)}) collective-permute-start(bf16[32,41]{1,0:T(8,128)(2,1)S(1)} %get-tuple-element.21), channel_id=1, source_target_pairs={{0,1},{1,2},{2,3},{4,5},{5,6},{6,7},{8,9},{9,10},{10,11},{12,13},{... | collective-permute-start | bytes 7880 | tf_op jit(solution)/shard_map/ppermute | solution.py:233
  35.8 10.0 %collective-permute-start.1 = (bf16[32,41]{1,0:T(8,128)(2,1)S(1)}, bf16[32,41]{1,0:T(8,128)(2,1)S(1)}, u32[]{:S(2)}, u32[]{:S(2)}) collective-permute-start(bf16[32,41]{1,0:T(8,128)(2,1)S(1)} %get-tuple-element.20), channel_id=1, source_target_pairs={{1,0},{2,1},{3,2},{5,4},{6,5},{7,6},{9,8},{10,9},{11,10},{13,12},{... | collective-permute-start | bytes 7880 | tf_op jit(solution)/shard_map/ppermute | solution.py:234
  45.8 0.6 copy-start.6
  45.8 0.6 copy-start.7
  62.6 1.3 %copy-start.4 = (bf16[7,32,32]{2,1,0:T(8,128)(2,1)S(1)}, bf16[7,32,32]{2,1,0:T(8,128)(2,1)}, u32[]{:S(2)}) copy-start(bf16[7,32,32]{2,1,0:T(8,128)(2,1)} %param.28) | copy-start | bytes 43012
  64.3 6.7 %collective-permute-start.2 = (bf16[6,32,522]{2,1,0:T(8,128)(2,1)S(1)}, bf16[6,32,522]{2,1,0:T(8,128)(2,1)S(1)}, u32[]{:S(2)}, u32[]{:S(2)}) collective-permute-start(bf16[6,32,522]{2,1,0:T(8,128)(2,1)S(1)} %get-tuple-element.22), channel_id=1, source_target_pairs={{0,4},{4,8},{8,12},{12,16},{16,20},{20,24},{24,28},{28,32},{32,36}... | collective-permute-start | bytes 601352 | tf_op jit(solution)/shard_map/ppermute | solution.py:257
  67.9 7.5 %collective-permute-start.3 = (bf16[6,32,522]{2,1,0:T(8,128)(2,1)S(1)}, bf16[6,32,522]{2,1,0:T(8,128)(2,1)S(1)}, u32[]{:S(2)}, u32[]{:S(2)}) collective-permute-start(bf16[6,32,522]{2,1,0:T(8,128)(2,1)S(1)} %get-tuple-element.23), channel_id=1, source_target_pairs={{4,0},{8,4},{12,8},{16,12},{20,16},{24,20},{28,24},{32,28},{36,32}... | collective-permute-start | bytes 601352 | tf_op jit(solution)/shard_map/ppermute | solution.py:258

commit v6 on v5

--- a/solution.py
+++ b/solution.py
@@ -39,7 +39,7 @@
             if flat:
                 xs = x_ref[r * row_step : r * row_step + k_all, :]
             else:
-                xs = x_ref[pl.ds(r, 7), :, :].reshape(k_all, n_in)
+                xs = x_ref[r : r + 7, :, :].reshape(k_all, n_in)
             z = jnp.dot(w_ref[...], xs, preferred_element_type=jnp.float32)
             m_row = m_ref[r]
             for g in range(groups):
@@ -66,11 +66,8 @@
                         ].astype(jnp.bfloat16)
             return carry
 
-        if flat:
-            for r in range(r_out):
-                row(r, 0)
-        else:
-            lax.fori_loop(0, r_out, row, 0)
+        for r in range(r_out):
+            row(r, 0)
 
     def per_window(a):
         return pl.BlockSpec((None,) + a.shape[1:], lambda w, n=a.ndim - 1: (w,) + (0,) * n)

time: 94.2 us -> 86.4 us (0.917)
  Pallas kernels: 30.3 us -> 22.5 us
    pallas_call x4, Pallas kernels: 28.1 us -> 20.2 us  [banded(): pl.pallas_call(kernel, grid=(windows,), in_specs=specs, out_specs=pl.Bloc...]
  transfers between devices with their start and end apart: 5 -> 5, of which waited for: 3 -> 3; matrix products, arithmetic and copies ran while one was open for 12% -> 13% of each run, Pallas kernels for 0% -> 0%
where the time goes in v6:
time: 86.4 us; the launch traced here: 85.6 us
  starting transfers between devices  23.2 us (27%)
  Pallas kernels  22.5 us (26%)
  local copies, waits for them, and re-layouts  16.3 us (19%)
  waiting for transfers between devices  10.2 us (12%)
  other arithmetic  8.29 us (10%)
  between operations  4.92 us (6%)
    pallas_call x4, Pallas kernels, banded(): pl.pallas_call(kernel, grid=(windows,), in_specs=specs, out_specs=pl.Bloc...  20.2 us
    all_to_all x1, starting transfers between devices, on_device(): lax.all_to_all(outgoing, 'chan', split_axis=0, concat_axis=0, tiled=True)  13 us
    all_to_all x1, waiting for transfers between devices, on_device(): lax.all_to_all(outgoing, 'chan', split_axis=0, concat_axis=0, tiled=True)  5.53 us
    ppermute x1, waiting for transfers between devices, on_device(): below = lax.ppermute(second[:REACH], 'chan', ring_down)  4.4 us
    ppermute x1, starting transfers between devices, on_device(): above = lax.ppermute(second[C_DEV - REACH:], 'chan', ring_up)  3.61 us
    ppermute x1, starting transfers between devices, on_device(): before = lax.ppermute(arrived[blocks - 1], 'tm', up)  3.2 us
    unnamed x41, local copies, waits for them, and re-layouts  2.97 us
    pallas_call x1, Pallas kernels, strain_layout(): pl.pallas_call(kernel, out_shape=jax.ShapeDtypeStruct((rows, n_out), jnp....  2.24 us
  transfers between devices with their start and end apart: 5, of which 3 were waited for; matrix products, arithmetic and copies ran while one was open for 13% of the time, Pallas kernels for 0%

profile of v6, /device:TPU:1, one launch (start us, length us, event | category | flops | bytes accessed | tf_op | source)
XLA Modules:
  0.0 85.6 jit_solution(12209749240504555466)
XLA Ops:
  0.0 0.7 compare_select_fusion
  0.7 0.7 compare_and_fusion.3
  1.4 1.0 %pad_slice_fusion.2 = (bf16[32,512]{1,0:T(8,128)(2,1)S(1)}, bf16[32,512]{1,0:T(8,128)(2,1)S(1)}, bf16[32,512]{1,0:T(8,128)(2,1)S(1)}) fusion(bf16[32,512]{1,0:T(8,128)(2,1)} %param.21), kind=kLoop, calls=%fused_computation.33 | loop fusion | bytes 131072 | tf_op jit(solution)/shard_map/slice | solution.py:219
  4.8 0.7 gather_fusion
  6.3 1.5 %reshape.306 = bf16[64,2,656]{2,1,0:T(2,128)(2,1)} reshape(bf16[64,32,41]{2,1,0:T(8,128)(2,1)S(1)} %maximum_bitcast_fusion.1) | data formatting | bytes 335872
  7.8 13.0 %all-to-all-start = ((bf16[64,2,656]{2,1,0:T(2,128)(2,1)}), bf16[64,2,656]{2,1,0:T(2,128)(2,1)S(1)}, u32[]{:S(2)}, u32[]{:S(2)}) async-start(bf16[64,2,656]{2,1,0:T(2,128)(2,1)} %reshape.306), calls=%async_computation | async-start | bytes 393216 | tf_op jit(solution)/shard_map/all_to_all | solution.py:224
  22.3 0.8 add_convert_fusion.m_ref
  23.1 0.6 gather_fusion.1
  23.8 0.6 gather_fusion.2
  24.9 0.6 gather_fusion.3
  26.2 5.5 %all-to-all-done = bf16[64,2,656]{2,1,0:T(2,128)(2,1)S(1)} async-done(((bf16[64,2,656]{2,1,0:T(2,128)(2,1)}), bf16[64,2,656]{2,1,0:T(2,128)(2,1)S(1)}, u32[]{:S(2)}, u32[]{:S(2)}) %all-to-all-start) | async-done | bytes 167968 | tf_op jit(solution)/shard_map/all_to_all | solution.py:224
  31.7 0.8 reshape.307
  32.6 3.2 %collective-permute-start = (bf16[32,41]{1,0:T(8,128)(2,1)S(1)}, bf16[32,41]{1,0:T(8,128)(2,1)S(1)}, u32[]{:S(2)}, u32[]{:S(2)}) collective-permute-start(bf16[32,41]{1,0:T(8,128)(2,1)S(1)} %get-tuple-element.21), channel_id=1, source_target_pairs={{0,1},{1,2},{2,3},{4,5},{5,6},{6,7},{8,9},{9,10},{10,11},{12,13},{... | collective-permute-start | bytes 7880 | tf_op jit(solution)/shard_map/ppermute | solution.py:230
  35.8 1.3 %collective-permute-start.1 = (bf16[32,41]{1,0:T(8,128)(2,1)S(1)}, bf16[32,41]{1,0:T(8,128)(2,1)S(1)}, u32[]{:S(2)}, u32[]{:S(2)}) collective-permute-start(bf16[32,41]{1,0:T(8,128)(2,1)S(1)} %get-tuple-element.20), channel_id=1, source_target_pairs={{1,0},{2,1},{3,2},{5,4},{6,5},{7,6},{9,8},{10,9},{11,10},{13,12},{... | collective-permute-start | bytes 7880 | tf_op jit(solution)/shard_map/ppermute | solution.py:231
  38.3 0.7 copy.73.b_ref
  39.2 0.7 copy.72.w_ref
  40.2 0.7 copy.75.w_ref
  41.1 0.9 %reshape.271.w_ref = bf16[224,224]{1,0:T(8,128)(2,1)} reshape(bf16[7,32,7,32]{3,2,1,0:T(8,128)(2,1)S(1)} %copy.77) | data formatting | bytes 200704 | tf_op jit(solution)/shard_map/reshape | solution.py:116
  42.3 0.9 copy.80.w_ref
  46.4 2.2 %shard_map.181 = bf16[160,527]{1,0:T(8,128)(2,1)} custom-call(bf16[2048,41]{1,0:T(8,128)(2,1)} %bitcast.65, bf16[32,41]{1,0:T(8,128)(2,1)} %copy-done.6, bf16[32,41]{1,0:T(8,128)(2,1)} %copy-done.7), custom_call_target="tpu_custom_call" | custom-call | tf_op jit(solution)/shard_map/pallas_call | solution.py:111
  48.7 6.2 %shard_map.182.x_ref = bf16[2,14,64,524]{3,2,1,0:T(8,128)(2,1)} custom-call(bf16[2,80,527]{2,1,0:T(8,128)(2,1)} %bitcast.66, bf16[256,28]{1,0:T(8,128)(2,1)} %copy.72.w_ref, f32[144,1]{1,0:T(8,128)} %copy.73.b_ref, f32[2,14,4,524]{3,2,1,0:T(4,128)} %add_convert_fusion.m_ref), custom_call_target="tpu_custom_call" | custom-call | tf_op jit(solution)/shard_map/pallas_call | solution.py:83
  54.8 0.6 broadcast_in_dim.125.m_ref
  55.5 4.0 %shard_map.183 = bf16[2,8,32,522]{3,2,1,0:T(8,128)(2,1)} custom-call(bf16[2,14,64,524]{3,2,1,0:T(8,128)(2,1)} %shard_map.182.x_ref, bf16[96,448]{1,0:T(8,128)(2,1)} %copy.75.w_ref, f32[144,1]{1,0:T(8,128)} %copy.73.b_ref, f32[2,8,1,522]{3,2,1,0:T(1,128)} %broadcast_in_dim.125.m_ref), custom_call_target="tpu_custom_call" | custom-call | tf_op jit(solution)/shard_map/pallas_call | solution.py:83
  59.5 1.2 %slice_convert_fusion = (f32[1,8,32,522]{3,2,1,0:T(8,128)S(1)}, f32[8,32,522]{2,1,0:T(8,128)S(1)}, bf16[1,8,32,522]{3,2,1,0:T(8,128)(2,1)S(1)}) fusion(bf16[2,8,32,522]{3,2,1,0:T(8,128)(2,1)} %shard_map.183), kind=kLoop, calls=%fused_computation.17 | loop fusion | flops 133632 | bytes 1870848 | tf_op jit(solution)/shard_map/convert_element_type | solution.py:250
  61.1 3.6 %collective-permute-start.2 = (bf16[6,32,522]{2,1,0:T(8,128)(2,1)S(1)}, bf16[6,32,522]{2,1,0:T(8,128)(2,1)S(1)}, u32[]{:S(2)}, u32[]{:S(2)}) collective-permute-start(bf16[6,32,522]{2,1,0:T(8,128)(2,1)S(1)} %get-tuple-element.22), channel_id=1, source_target_pairs={{0,4},{4,8},{8,12},{12,16},{16,20},{20,24},{24,28},{28,32},{32,36}... | collective-permute-start | bytes 601352 | tf_op jit(solution)/shard_map/ppermute | solution.py:254
  64.8 2.1 %collective-permute-start.3 = (bf16[6,32,522]{2,1,0:T(8,128)(2,1)S(1)}, bf16[6,32,522]{2,1,0:T(8,128)(2,1)S(1)}, u32[]{:S(2)}, u32[]{:S(2)}) collective-permute-start(bf16[6,32,522]{2,1,0:T(8,128)(2,1)S(1)} %get-tuple-element.23), channel_id=1, source_target_pairs={{4,0},{8,4},{12,8},{16,12},{20,16},{24,20},{28,24},{32,28},{36,32}... | collective-permute-start | bytes 601352 | tf_op jit(solution)/shard_map/ppermute | solution.py:255
  66.9 0.7 and_convert_fusion.m_ref
  67.9 4.4 %collective-permute-done.3 = bf16[6,32,522]{2,1,0:T(8,128)(2,1)S(1)} collective-permute-done((bf16[6,32,522]{2,1,0:T(8,128)(2,1)S(1)}, bf16[6,32,522]{2,1,0:T(8,128)(2,1)S(1)}, u32[]{:S(2)}, u32[]{:S(2)}) %collective-permute-start.3) | collective-permute-done | bytes 200480 | tf_op jit(solution)/shard_map/ppermute | solution.py:255
  72.3 1.0 %maximum_bitcast_fusion.x_ref = bf16[1,20,32,522]{3,2,1,0:T(8,128)(2,1)} fusion(bf16[6,32,522]{2,1,0:T(8,128)(2,1)S(1)} %collective-permute-done.3, bf16[8,32,522]{2,1,0:T(8,128)(2,1)S(1)} %multiply_convert_fusion, bf16[6,32,522]{2,1,0:T(8,128)(2,1)S(1)} %collective-permute-done.2), kind=kLoop, calls=%fused_computation.8 | loop fusion | flops 668160 | bytes 1336320 | tf_op jit(solution)/shard_map/broadcast_in_dim | solution.py:262
  73.3 7.2 %shard_map.184.x_ref = bf16[1,14,128,129]{3,2,1,0:T(8,128)(2,1)} custom-call(bf16[1,20,32,522]{3,2,1,0:T(8,128)(2,1)} %maximum_bitcast_fusion.x_ref, bf16[224,224]{1,0:T(8,128)(2,1)} %reshape.271.w_ref, f32[144,1]{1,0:T(8,128)} %copy.73.b_ref, f32[1,14,1,516]{3,2,1,0:T(1,128)} %and_convert_fusion.m_ref, bf16[128,128]{1,0:T(8,128)(2,1)} %constant.160.clone.rest_0_), custom_call_target="tpu_custom_call" | custom-call | tf_op jit(solution)/shard_map/pallas_call | solution.py:83
  81.1 2.8 %shard_map.185 = bf16[1,8,64,128]{3,2,1,0:T(8,128)(2,1)} custom-call(bf16[1,14,128,129]{3,2,1,0:T(8,128)(2,1)} %shard_map.184.x_ref, bf16[128,896]{1,0:T(8,128)(2,1)} %copy.80.w_ref, f32[144,1]{1,0:T(8,128)} %copy.73.b_ref, f32[1,8,1,128]{3,2,1,0:T(1,128)} %broadcast_in_dim.134.m_ref), custom_call_target="tpu_custom_call" | custom-call | tf_op jit(solution)/shard_map/pallas_call | solution.py:83
  83.9 1.6 %copy.82 = bf16[64,8,128]{2,1,0:T(8,128)(2,1)} copy(bf16[64,8,128]{2,0,1:T(8,128)(2,1)} %bitcast.70) | data formatting | bytes 262144 | tf_op jit(solution)/shard_map/transpose | solution.py:285
  (82 shorter events, 7.9 us)
Async XLA Ops:
  0.0 24.8 %copy-start = (bf16[64,32,7,7]{0,1,3,2:T(8,128)(2,1)S(1)}, bf16[64,32,7,7]{0,1,3,2:T(8,128)(2,1)}, u32[]{:S(2)}) copy-start(bf16[64,32,7,7]{0,1,3,2:T(8,128)(2,1)} %param.31) | copy-start | bytes 602116
  5.4 15.4 %copy-start.18 = (s32[64]{0:T(128)S(1)}, s32[64]{0:T(128)}, u32[]{:S(2)}) copy-start(s32[64]{0:T(128)} %param.22) | copy-start | bytes 772
  5.4 16.5 %copy-start.5 = (bf16[16,1,7,7]{0,3,2,1:T(8,128)(2,1)S(1)}, bf16[16,1,7,7]{0,3,2,1:T(8,128)(2,1)}, u32[]{:S(2)}) copy-start(bf16[16,1,7,7]{0,3,2,1:T(8,128)(2,1)} %param.24) | copy-start | bytes 4708
  5.4 16.6 %copy-start.12 = (s32[64]{0:T(128)S(1)}, s32[64]{0:T(128)}, u32[]{:S(2)}) copy-start(s32[64]{0:T(128)} %constant.199) | copy-start | bytes 772
  5.5 16.6 %copy-start.11 = (s32[12]{0:T(128)S(1)}, s32[12]{0:T(128)}, u32[]{:S(2)}) copy-start(s32[12]{0:T(128)} %constant.200) | copy-start | bytes 148
  5.5 16.6 %copy-start.10 = (s32[8]{0:T(128)S(1)}, s32[8]{0:T(128)}, u32[]{:S(2)}) copy-start(s32[8]{0:T(128)} %constant.201) | copy-start | bytes 100
  5.6 18.1 %copy-start.8 = (pred[4,4,4]{1,0,2:T(4,128)(4,1)S(1)}, pred[4,4,4]{1,0,2:T(4,128)(4,1)}, u32[]{:S(2)}) copy-start(pred[4,4,4]{1,0,2:T(4,128)(4,1)} %constant.169) | copy-start | bytes 196
  5.6 18.2 %copy-start.1 = (bf16[32,16,7,7]{0,1,3,2:T(8,128)(2,1)S(1)}, bf16[32,16,7,7]{0,1,3,2:T(8,128)(2,1)}, u32[]{:S(2)}) copy-start(bf16[32,16,7,7]{0,1,3,2:T(8,128)(2,1)} %param.26) | copy-start | bytes 150532
  6.3 18.2 %copy-start.17 = (pred[3,4]{0,1:T(4,128)(4,1)S(1)}, pred[3,4]{0,1:T(4,128)(4,1)}, u32[]{:S(2)}) copy-start(pred[3,4]{0,1:T(4,128)(4,1)} %constant.178) | copy-start | bytes 40
  7.8 23.9 %all-to-all-start = ((bf16[64,2,656]{2,1,0:T(2,128)(2,1)}), bf16[64,2,656]{2,1,0:T(2,128)(2,1)S(1)}, u32[]{:S(2)}, u32[]{:S(2)}) async-start(bf16[64,2,656]{2,1,0:T(2,128)(2,1)} %reshape.306), calls=%async_computation | async-start | bytes 393216 | tf_op jit(solution)/shard_map/all_to_all | solution.py:224
  24.8 0.8 copy-start.9
  24.8 12.2 %copy-start.13 = (f32[64]{0:T(128)S(1)}, f32[64]{0:T(128)}, u32[]{:S(2)}) copy-start(f32[64]{0:T(128)} %param.32) | copy-start | bytes 772
  24.8 12.2 %copy-start.14 = (f32[32]{0:T(128)S(1)}, f32[32]{0:T(128)}, u32[]{:S(2)}) copy-start(f32[32]{0:T(128)} %param.30) | copy-start | bytes 388
  24.8 12.2 %copy-start.15 = (f32[32]{0:T(128)S(1)}, f32[32]{0:T(128)}, u32[]{:S(2)}) copy-start(f32[32]{0:T(128)} %param.27) | copy-start | bytes 388
  24.9 12.2 %copy-start.16 = (f32[16]{0:T(128)S(1)}, f32[16]{0:T(128)}, u32[]{:S(2)}) copy-start(f32[16]{0:T(128)} %param.25) | copy-start | bytes 196
  25.5 15.4 %copy-start.3 = (bf16[32,32,7,7]{1,0,3,2:T(8,128)(2,1)S(1)}, bf16[32,32,7,7]{1,0,3,2:T(8,128)(2,1)}, u32[]{:S(2)}) copy-start(bf16[32,32,7,7]{1,0,3,2:T(8,128)(2,1)} %param.29) | copy-start | bytes 301060
  32.5 13.3 %copy-start.2 = (bf16[64,32,41]{2,1,0:T(8,128)(2,1)}, bf16[64,32,41]{2,1,0:T(8,128)(2,1)S(1)}, u32[]{:S(2)}) copy-start(bf16[64,32,41]{2,1,0:T(8,128)(2,1)S(1)} %reshape.307) | copy-start | bytes 503812
  32.6 13.2 %collective-permute-start = (bf16[32,41]{1,0:T(8,128)(2,1)S(1)}, bf16[32,41]{1,0:T(8,128)(2,1)S(1)}, u32[]{:S(2)}, u32[]{:S(2)}) collective-permute-start(bf16[32,41]{1,0:T(8,128)(2,1)S(1)} %get-tuple-element.21), channel_id=1, source_target_pairs={{0,1},{1,2},{2,3},{4,5},{5,6},{6,7},{8,9},{9,10},{10,11},{12,13},{... | collective-permute-start | bytes 7880 | tf_op jit(solution)/shard_map/ppermute | solution.py:230
  35.8 10.0 %collective-permute-start.1 = (bf16[32,41]{1,0:T(8,128)(2,1)S(1)}, bf16[32,41]{1,0:T(8,128)(2,1)S(1)}, u32[]{:S(2)}, u32[]{:S(2)}) collective-permute-start(bf16[32,41]{1,0:T(8,128)(2,1)S(1)} %get-tuple-element.20), channel_id=1, source_target_pairs={{1,0},{2,1},{3,2},{5,4},{6,5},{7,6},{9,8},{10,9},{11,10},{13,12},{... | collective-permute-start | bytes 7880 | tf_op jit(solution)/shard_map/ppermute | solution.py:231
  45.8 0.6 copy-start.6
  45.8 0.6 copy-start.7
  59.5 1.3 %copy-start.4 = (bf16[7,32,32]{2,1,0:T(8,128)(2,1)S(1)}, bf16[7,32,32]{2,1,0:T(8,128)(2,1)}, u32[]{:S(2)}) copy-start(bf16[7,32,32]{2,1,0:T(8,128)(2,1)} %param.28) | copy-start | bytes 43012
  61.1 6.7 %collective-permute-start.2 = (bf16[6,32,522]{2,1,0:T(8,128)(2,1)S(1)}, bf16[6,32,522]{2,1,0:T(8,128)(2,1)S(1)}, u32[]{:S(2)}, u32[]{:S(2)}) collective-permute-start(bf16[6,32,522]{2,1,0:T(8,128)(2,1)S(1)} %get-tuple-element.22), channel_id=1, source_target_pairs={{0,4},{4,8},{8,12},{12,16},{16,20},{20,24},{24,28},{28,32},{32,36}... | collective-permute-start | bytes 601352 | tf_op jit(solution)/shard_map/ppermute | solution.py:254
  64.8 7.5 %collective-permute-start.3 = (bf16[6,32,522]{2,1,0:T(8,128)(2,1)S(1)}, bf16[6,32,522]{2,1,0:T(8,128)(2,1)S(1)}, u32[]{:S(2)}, u32[]{:S(2)}) collective-permute-start(bf16[6,32,522]{2,1,0:T(8,128)(2,1)S(1)} %get-tuple-element.23), channel_id=1, source_target_pairs={{4,0},{8,4},{12,8},{16,12},{20,16},{24,20},{28,24},{32,28},{36,32}... | collective-permute-start | bytes 601352 | tf_op jit(solution)/shard_map/ppermute | solution.py:255

commit v7 on v6

--- a/solution.py
+++ b/solution.py
@@ -173,7 +173,7 @@
     )
     first = banded(
         strain_wide.reshape(n_win, wide * PH, n_s),
-        weights_first(first_weight),
+        first_weight,
         biases,
         0,
         first_mask,
@@ -184,7 +184,7 @@
     )
     return banded(
         first,
-        weights_stride4(second_weight, 3, 2),
+        second_weight,
         biases,
         16,
         jnp.ones((n_win, C_DEV, 1, length), jnp.float32),
@@ -222,6 +222,17 @@
     both = jnp.concatenate([windows, jnp.take(windows, partners, axis=1), tag], axis=2)
     outgoing = jnp.transpose(both, (1, 0, 2))
     arrived = lax.all_to_all(outgoing, "chan", split_axis=0, concat_axis=0, tiled=True)
+    biases = jnp.concatenate([first_bias, second_bias, third_bias, fourth_bias]).reshape(-1, 1)
+    prepared = (
+        weights_first(first_weight),
+        weights_stride4(second_weight, 3, 2),
+        weights_stride1(third_weight),
+        weights_stride4(fourth_weight, 2, 0),
+        biases,
+    )
+    arrived, (first_weight, second_weight, third_weight, fourth_weight, biases) = lax.optimization_barrier(
+        (arrived, prepared)
+    )
     mate_offset = arrived[:, 0, 2 * wide].astype(jnp.int32)[mate]
     times = blocks * times_here
     tms = lax.axis_size("tm")
@@ -233,7 +244,6 @@
 
     quarter = times // 4
     length = quarter + 2 * LEAD
-    biases = jnp.concatenate([first_bias, second_bias, third_bias, fourth_bias]).reshape(-1, 1)
     lower = lower_layers(
         strain_wide.reshape(2, wide, PH, -1), (me, mate), first_weight, biases, second_weight, times, length
     )
@@ -260,7 +270,7 @@
     third_mask = edge_mask(wide - 6, 1, n_t, 3 - REACH, lambda p, j: (j - (LEAD - 3), quarter), me)
     third = banded(
         second_wide[None],
-        weights_stride1(third_weight),
+        third_weight,
         biases,
         48,
         third_mask[None],
@@ -273,7 +283,7 @@
     )
     features = banded(
         third,
-        weights_stride4(fourth_weight, 2, 0),
+        fourth_weight,
         biases,
         80,
         jnp.ones((1, C_DEV, 1, quarter // 4), jnp.float32),

time: 86.4 us -> 83.6 us (0.968)
  waiting for transfers between devices: 10.2 us -> 7.51 us
    optimization_barrier x0 -> x5, local copies, waits for them, and re-layouts: none -> 3.85 us  [on_device(): lax.optimization_barrier((arrived, prepared))]
    all_to_all x1, waiting for transfers between devices: 5.53 us -> 3.64 us  [on_device(): lax.all_to_all(outgoing, 'chan', split_axis=0, concat_axis=0, tiled=True)]
    reshape x4 -> x2, local copies, waits for them, and re-layouts: 2.05 us -> 0.45 us  [weights_stride4(): jnp.transpose(taps, (3, 0, 2, 4, 1)).reshape(shifts * fout, 7 * PH * fin)]
    unnamed x41 -> x40, local copies, waits for them, and re-layouts: 2.97 us -> 2.18 us
  transfers between devices with their start and end apart: 5 -> 5, of which waited for: 3 -> 2; matrix products, arithmetic and copies ran while one was open for 13% -> 13% of each run, Pallas kernels for 0% -> 0%
where the time goes in v7:
time: 83.6 us; the launch traced here: 82.7 us
  starting transfers between devices  23.2 us (28%)
  Pallas kernels  22.4 us (27%)
  local copies, waits for them, and re-layouts  16.3 us (19%)
  other arithmetic  8.28 us (10%)
  waiting for transfers between devices  7.51 us (9%)
  between operations  4.81 us (6%)
    pallas_call x4, Pallas kernels, banded(): pl.pallas_call(kernel, grid=(windows,), in_specs=specs, out_specs=pl.Bloc...  20.2 us
    all_to_all x1, starting transfers between devices, on_device(): lax.all_to_all(outgoing, 'chan', split_axis=0, concat_axis=0, tiled=True)  13 us
    ppermute x1, waiting for transfers between devices, on_device(): below = lax.ppermute(second[:REACH], 'chan', ring_down)  3.86 us
    optimization_barrier x5, local copies, waits for them, and re-layouts, on_device(): lax.optimization_barrier((arrived, prepared))  3.85 us
    all_to_all x1, waiting for transfers between devices, on_device(): lax.all_to_all(outgoing, 'chan', split_axis=0, concat_axis=0, tiled=True)  3.64 us
    ppermute x1, starting transfers between devices, on_device(): above = lax.ppermute(second[C_DEV - REACH:], 'chan', ring_up)  3.6 us
    ppermute x1, starting transfers between devices, on_device(): before = lax.ppermute(arrived[blocks - 1], 'tm', up)  3.2 us
    pallas_call x1, Pallas kernels, strain_layout(): pl.pallas_call(kernel, out_shape=jax.ShapeDtypeStruct((rows, n_out), jnp....  2.24 us
  transfers between devices with their start and end apart: 5, of which 2 were waited for; matrix products, arithmetic and copies ran while one was open for 13% of the time, Pallas kernels for 0%

profile of v7, /device:TPU:1, one launch (start us, length us, event | category | flops | bytes accessed | tf_op | source)
XLA Modules:
  0.0 82.7 jit_solution(13794136750497580790)
XLA Ops:
  0.0 0.7 compare_select_fusion
  0.7 0.7 compare_and_fusion.3
  1.4 1.0 %pad_slice_fusion.2 = (bf16[32,512]{1,0:T(8,128)(2,1)S(1)}, bf16[32,512]{1,0:T(8,128)(2,1)S(1)}, bf16[32,512]{1,0:T(8,128)(2,1)S(1)}) fusion(bf16[32,512]{1,0:T(8,128)(2,1)} %param.21), kind=kLoop, calls=%fused_computation.33 | loop fusion | bytes 131072 | tf_op jit(solution)/shard_map/slice | solution.py:219
  4.8 0.7 gather_fusion
  6.2 1.5 %reshape.306 = bf16[64,2,656]{2,1,0:T(2,128)(2,1)} reshape(bf16[64,32,41]{2,1,0:T(8,128)(2,1)S(1)} %maximum_bitcast_fusion.1) | data formatting | bytes 335872
  7.7 13.0 %all-to-all-start = ((bf16[64,2,656]{2,1,0:T(2,128)(2,1)}), bf16[64,2,656]{2,1,0:T(2,128)(2,1)S(1)}, u32[]{:S(2)}, u32[]{:S(2)}) async-start(bf16[64,2,656]{2,1,0:T(2,128)(2,1)} %reshape.306), calls=%async_computation | async-start | bytes 393216 | tf_op jit(solution)/shard_map/all_to_all | solution.py:224
  21.3 0.6 gather_fusion.3
  22.9 0.6 gather_fusion.2
  24.4 0.9 %reshape.269.w_ref = bf16[224,224]{1,0:T(8,128)(2,1)} reshape(bf16[7,32,7,32]{3,2,1,0:T(8,128)(2,1)S(1)} %copy.73) | data formatting | bytes 200704 | tf_op jit(solution)/shard_map/reshape | solution.py:116
  25.3 0.6 gather_fusion.1
  27.0 0.8 add_convert_fusion.m_ref
  28.0 3.6 %all-to-all-done = bf16[64,2,656]{2,1,0:T(2,128)(2,1)S(1)} async-done(((bf16[64,2,656]{2,1,0:T(2,128)(2,1)}), bf16[64,2,656]{2,1,0:T(2,128)(2,1)S(1)}, u32[]{:S(2)}, u32[]{:S(2)}) %all-to-all-start) | async-done | bytes 167968 | tf_op jit(solution)/shard_map/all_to_all | solution.py:224
  31.6 0.8 reshape.307
  32.5 3.2 %collective-permute-start = (bf16[32,41]{1,0:T(8,128)(2,1)S(1)}, bf16[32,41]{1,0:T(8,128)(2,1)S(1)}, u32[]{:S(2)}, u32[]{:S(2)}) collective-permute-start(bf16[32,41]{1,0:T(8,128)(2,1)S(1)} %get-tuple-element.33), channel_id=1, source_target_pairs={{0,1},{1,2},{2,3},{4,5},{5,6},{6,7},{8,9},{9,10},{10,11},{12,13},{... | collective-permute-start | bytes 7880 | tf_op jit(solution)/shard_map/ppermute | solution.py:241
  35.7 1.3 %collective-permute-start.1 = (bf16[32,41]{1,0:T(8,128)(2,1)S(1)}, bf16[32,41]{1,0:T(8,128)(2,1)S(1)}, u32[]{:S(2)}, u32[]{:S(2)}) collective-permute-start(bf16[32,41]{1,0:T(8,128)(2,1)S(1)} %get-tuple-element.32), channel_id=1, source_target_pairs={{1,0},{2,1},{3,2},{5,4},{6,5},{7,6},{9,8},{10,9},{11,10},{13,12},{... | collective-permute-start | bytes 7880 | tf_op jit(solution)/shard_map/ppermute | solution.py:242
  40.8 0.7 copy.76.b_ref
  41.5 0.7 copy.75.w_ref
  42.2 0.7 copy.77.w_ref
  43.6 2.2 %shard_map.181 = bf16[160,527]{1,0:T(8,128)(2,1)} custom-call(bf16[2048,41]{1,0:T(8,128)(2,1)} %bitcast.65, bf16[32,41]{1,0:T(8,128)(2,1)} %copy-done.6, bf16[32,41]{1,0:T(8,128)(2,1)} %copy-done.7), custom_call_target="tpu_custom_call" | custom-call | tf_op jit(solution)/shard_map/pallas_call | solution.py:111
  45.8 6.2 %shard_map.182.x_ref = bf16[2,14,64,524]{3,2,1,0:T(8,128)(2,1)} custom-call(bf16[2,80,527]{2,1,0:T(8,128)(2,1)} %bitcast.66, bf16[256,28]{1,0:T(8,128)(2,1)} %copy.75.w_ref, f32[144,1]{1,0:T(8,128)} %copy.76.b_ref, f32[2,14,4,524]{3,2,1,0:T(4,128)} %add_convert_fusion.m_ref), custom_call_target="tpu_custom_call" | custom-call | tf_op jit(solution)/shard_map/pallas_call | solution.py:83
  52.0 0.6 broadcast_in_dim.132.m_ref
  52.6 4.0 %shard_map.183 = bf16[2,8,32,522]{3,2,1,0:T(8,128)(2,1)} custom-call(bf16[2,14,64,524]{3,2,1,0:T(8,128)(2,1)} %shard_map.182.x_ref, bf16[96,448]{1,0:T(8,128)(2,1)} %copy.77.w_ref, f32[144,1]{1,0:T(8,128)} %copy.76.b_ref, f32[2,8,1,522]{3,2,1,0:T(1,128)} %broadcast_in_dim.132.m_ref), custom_call_target="tpu_custom_call" | custom-call | tf_op jit(solution)/shard_map/pallas_call | solution.py:83
  56.6 1.2 %slice_convert_fusion = (f32[1,8,32,522]{3,2,1,0:T(8,128)S(1)}, f32[8,32,522]{2,1,0:T(8,128)S(1)}, bf16[1,8,32,522]{3,2,1,0:T(8,128)(2,1)S(1)}) fusion(bf16[2,8,32,522]{3,2,1,0:T(8,128)(2,1)} %shard_map.183), kind=kLoop, calls=%fused_computation.17 | loop fusion | flops 133632 | bytes 1870848 | tf_op jit(solution)/shard_map/convert_element_type | solution.py:260
  58.3 3.6 %collective-permute-start.2 = (bf16[6,32,522]{2,1,0:T(8,128)(2,1)S(1)}, bf16[6,32,522]{2,1,0:T(8,128)(2,1)S(1)}, u32[]{:S(2)}, u32[]{:S(2)}) collective-permute-start(bf16[6,32,522]{2,1,0:T(8,128)(2,1)S(1)} %get-tuple-element.34), channel_id=1, source_target_pairs={{0,4},{4,8},{8,12},{12,16},{16,20},{20,24},{24,28},{28,32},{32,36}... | collective-permute-start | bytes 601352 | tf_op jit(solution)/shard_map/ppermute | solution.py:264
  61.9 2.1 %collective-permute-start.3 = (bf16[6,32,522]{2,1,0:T(8,128)(2,1)S(1)}, bf16[6,32,522]{2,1,0:T(8,128)(2,1)S(1)}, u32[]{:S(2)}, u32[]{:S(2)}) collective-permute-start(bf16[6,32,522]{2,1,0:T(8,128)(2,1)S(1)} %get-tuple-element.35), channel_id=1, source_target_pairs={{4,0},{8,4},{12,8},{16,12},{20,16},{24,20},{28,24},{32,28},{36,32}... | collective-permute-start | bytes 601352 | tf_op jit(solution)/shard_map/ppermute | solution.py:265
  64.0 0.7 and_convert_fusion.m_ref
  64.7 0.8 %copy.80.w_ref = bf16[128,896]{1,0:T(8,128)(2,1)} copy(bf16[128,896]{0,1:T(8,128)(2,1)S(1)} %reshape.270) | data formatting | bytes 458752 | tf_op jit(solution)/shard_map/optimization_barrier | solution.py:233
  65.6 3.9 %collective-permute-done.3 = bf16[6,32,522]{2,1,0:T(8,128)(2,1)S(1)} collective-permute-done((bf16[6,32,522]{2,1,0:T(8,128)(2,1)S(1)}, bf16[6,32,522]{2,1,0:T(8,128)(2,1)S(1)}, u32[]{:S(2)}, u32[]{:S(2)}) %collective-permute-start.3) | collective-permute-done | bytes 200480 | tf_op jit(solution)/shard_map/ppermute | solution.py:265
  69.4 1.0 %maximum_bitcast_fusion.x_ref = bf16[1,20,32,522]{3,2,1,0:T(8,128)(2,1)} fusion(bf16[6,32,522]{2,1,0:T(8,128)(2,1)S(1)} %collective-permute-done.3, bf16[8,32,522]{2,1,0:T(8,128)(2,1)S(1)} %multiply_convert_fusion, bf16[6,32,522]{2,1,0:T(8,128)(2,1)S(1)} %collective-permute-done.2), kind=kLoop, calls=%fused_computation.8 | loop fusion | flops 668160 | bytes 1336320 | tf_op jit(solution)/shard_map/broadcast_in_dim | solution.py:272
  70.5 7.2 %shard_map.184.x_ref = bf16[1,14,128,129]{3,2,1,0:T(8,128)(2,1)} custom-call(bf16[1,20,32,522]{3,2,1,0:T(8,128)(2,1)} %maximum_bitcast_fusion.x_ref, bf16[224,224]{1,0:T(8,128)(2,1)} %reshape.269.w_ref, f32[144,1]{1,0:T(8,128)} %copy.76.b_ref, f32[1,14,1,516]{3,2,1,0:T(1,128)} %and_convert_fusion.m_ref, bf16[128,128]{1,0:T(8,128)(2,1)} %constant.162.clone.rest_0_), custom_call_target="tpu_custom_call" | custom-call | tf_op jit(solution)/shard_map/pallas_call | solution.py:83
  78.3 2.8 %shard_map.185 = bf16[1,8,64,128]{3,2,1,0:T(8,128)(2,1)} custom-call(bf16[1,14,128,129]{3,2,1,0:T(8,128)(2,1)} %shard_map.184.x_ref, bf16[128,896]{1,0:T(8,128)(2,1)} %copy.80.w_ref, f32[144,1]{1,0:T(8,128)} %copy.76.b_ref, f32[1,8,1,128]{3,2,1,0:T(1,128)} %broadcast_in_dim.134.m_ref), custom_call_target="tpu_custom_call" | custom-call | tf_op jit(solution)/shard_map/pallas_call | solution.py:83
  81.1 1.6 %copy.82 = bf16[64,8,128]{2,1,0:T(8,128)(2,1)} copy(bf16[64,8,128]{2,0,1:T(8,128)(2,1)} %bitcast.70) | data formatting | bytes 262144 | tf_op jit(solution)/shard_map/transpose | solution.py:295
  (82 shorter events, 7.6 us)
Async XLA Ops:
  0.0 21.3 %copy-start = (bf16[64,32,7,7]{0,1,3,2:T(8,128)(2,1)S(1)}, bf16[64,32,7,7]{0,1,3,2:T(8,128)(2,1)}, u32[]{:S(2)}) copy-start(bf16[64,32,7,7]{0,1,3,2:T(8,128)(2,1)} %param.31) | copy-start | bytes 602116
  5.4 15.3 %copy-start.18 = (s32[64]{0:T(128)S(1)}, s32[64]{0:T(128)}, u32[]{:S(2)}) copy-start(s32[64]{0:T(128)} %param.22) | copy-start | bytes 772
  5.4 15.9 %copy-start.12 = (s32[8]{0:T(128)S(1)}, s32[8]{0:T(128)}, u32[]{:S(2)}) copy-start(s32[8]{0:T(128)} %constant.201) | copy-start | bytes 100
  7.7 23.9 %all-to-all-start = ((bf16[64,2,656]{2,1,0:T(2,128)(2,1)}), bf16[64,2,656]{2,1,0:T(2,128)(2,1)S(1)}, u32[]{:S(2)}, u32[]{:S(2)}) async-start(bf16[64,2,656]{2,1,0:T(2,128)(2,1)} %reshape.306), calls=%async_computation | async-start | bytes 393216 | tf_op jit(solution)/shard_map/all_to_all | solution.py:224
  21.3 0.7 copy-start.9
  21.3 1.5 %copy-start.11 = (s32[12]{0:T(128)S(1)}, s32[12]{0:T(128)}, u32[]{:S(2)}) copy-start(s32[12]{0:T(128)} %constant.200) | copy-start | bytes 148
  22.0 0.9 %copy-start.1 = (bf16[32,16,7,7]{0,1,3,2:T(8,128)(2,1)S(1)}, bf16[32,16,7,7]{0,1,3,2:T(8,128)(2,1)}, u32[]{:S(2)}) copy-start(bf16[32,16,7,7]{0,1,3,2:T(8,128)(2,1)} %param.26) | copy-start | bytes 150532
  22.0 1.6 %copy-start.17 = (pred[3,4]{0,1:T(4,128)(4,1)S(1)}, pred[3,4]{0,1:T(4,128)(4,1)}, u32[]{:S(2)}) copy-start(pred[3,4]{0,1:T(4,128)(4,1)} %constant.178) | copy-start | bytes 40
  22.6 1.6 %copy-start.3 = (bf16[32,32,7,7]{1,0,3,2:T(8,128)(2,1)S(1)}, bf16[32,32,7,7]{1,0,3,2:T(8,128)(2,1)}, u32[]{:S(2)}) copy-start(bf16[32,32,7,7]{1,0,3,2:T(8,128)(2,1)} %param.29) | copy-start | bytes 301060
  22.9 2.4 %copy-start.5 = (bf16[16,1,7,7]{0,3,2,1:T(8,128)(2,1)S(1)}, bf16[16,1,7,7]{0,3,2,1:T(8,128)(2,1)}, u32[]{:S(2)}) copy-start(bf16[16,1,7,7]{0,3,2,1:T(8,128)(2,1)} %param.24) | copy-start | bytes 4708
  22.9 2.4 %copy-start.10 = (s32[64]{0:T(128)S(1)}, s32[64]{0:T(128)}, u32[]{:S(2)}) copy-start(s32[64]{0:T(128)} %constant.199) | copy-start | bytes 772
  22.9 3.0 %copy-start.8 = (pred[4,4,4]{1,0,2:T(4,128)(4,1)S(1)}, pred[4,4,4]{1,0,2:T(4,128)(4,1)}, u32[]{:S(2)}) copy-start(pred[4,4,4]{1,0,2:T(4,128)(4,1)} %constant.169) | copy-start | bytes 196
  23.5 4.3 %copy-start.13 = (f32[64]{0:T(128)S(1)}, f32[64]{0:T(128)}, u32[]{:S(2)}) copy-start(f32[64]{0:T(128)} %param.32) | copy-start | bytes 772
  23.5 4.3 %copy-start.14 = (f32[32]{0:T(128)S(1)}, f32[32]{0:T(128)}, u32[]{:S(2)}) copy-start(f32[32]{0:T(128)} %param.30) | copy-start | bytes 388
  23.6 4.2 %copy-start.15 = (f32[32]{0:T(128)S(1)}, f32[32]{0:T(128)}, u32[]{:S(2)}) copy-start(f32[32]{0:T(128)} %param.27) | copy-start | bytes 388
  23.6 4.2 %copy-start.16 = (f32[16]{0:T(128)S(1)}, f32[16]{0:T(128)}, u32[]{:S(2)}) copy-start(f32[16]{0:T(128)} %param.25) | copy-start | bytes 196
  32.4 10.6 %copy-start.2 = (bf16[64,32,41]{2,1,0:T(8,128)(2,1)}, bf16[64,32,41]{2,1,0:T(8,128)(2,1)S(1)}, u32[]{:S(2)}) copy-start(bf16[64,32,41]{2,1,0:T(8,128)(2,1)S(1)} %reshape.307) | copy-start | bytes 503812
  32.5 10.5 %collective-permute-start = (bf16[32,41]{1,0:T(8,128)(2,1)S(1)}, bf16[32,41]{1,0:T(8,128)(2,1)S(1)}, u32[]{:S(2)}, u32[]{:S(2)}) collective-permute-start(bf16[32,41]{1,0:T(8,128)(2,1)S(1)} %get-tuple-element.33), channel_id=1, source_target_pairs={{0,1},{1,2},{2,3},{4,5},{5,6},{6,7},{8,9},{9,10},{10,11},{12,13},{... | collective-permute-start | bytes 7880 | tf_op jit(solution)/shard_map/ppermute | solution.py:241
  35.7 7.3 %collective-permute-start.1 = (bf16[32,41]{1,0:T(8,128)(2,1)S(1)}, bf16[32,41]{1,0:T(8,128)(2,1)S(1)}, u32[]{:S(2)}, u32[]{:S(2)}) collective-permute-start(bf16[32,41]{1,0:T(8,128)(2,1)S(1)} %get-tuple-element.32), channel_id=1, source_target_pairs={{1,0},{2,1},{3,2},{5,4},{6,5},{7,6},{9,8},{10,9},{11,10},{13,12},{... | collective-permute-start | bytes 7880 | tf_op jit(solution)/shard_map/ppermute | solution.py:242
  43.0 0.6 copy-start.6
  43.0 0.6 copy-start.7
  56.6 1.3 %copy-start.4 = (bf16[7,32,32]{2,1,0:T(8,128)(2,1)S(1)}, bf16[7,32,32]{2,1,0:T(8,128)(2,1)}, u32[]{:S(2)}) copy-start(bf16[7,32,32]{2,1,0:T(8,128)(2,1)} %param.28) | copy-start | bytes 43012
  58.3 7.3 %collective-permute-start.2 = (bf16[6,32,522]{2,1,0:T(8,128)(2,1)S(1)}, bf16[6,32,522]{2,1,0:T(8,128)(2,1)S(1)}, u32[]{:S(2)}, u32[]{:S(2)}) collective-permute-start(bf16[6,32,522]{2,1,0:T(8,128)(2,1)S(1)} %get-tuple-element.34), channel_id=1, source_target_pairs={{0,4},{4,8},{8,12},{12,16},{16,20},{20,24},{24,28},{28,32},{32,36}... | collective-permute-start | bytes 601352 | tf_op jit(solution)/shard_map/ppermute | solution.py:264
  61.9 7.5 %collective-permute-start.3 = (bf16[6,32,522]{2,1,0:T(8,128)(2,1)S(1)}, bf16[6,32,522]{2,1,0:T(8,128)(2,1)S(1)}, u32[]{:S(2)}, u32[]{:S(2)}) collective-permute-start(bf16[6,32,522]{2,1,0:T(8,128)(2,1)S(1)} %get-tuple-element.35), channel_id=1, source_target_pairs={{4,0},{8,4},{12,8},{16,12},{20,16},{24,20},{28,24},{32,28},{36,32}... | collective-permute-start | bytes 601352 | tf_op jit(solution)/shard_map/ppermute | solution.py:265

commit v8 on v7

--- a/solution.py
+++ b/solution.py
@@ -28,7 +28,11 @@
     else:
         out_shape = (windows, r_out, PH * fout, n_sel)
 
-    def kernel(x_ref, w_ref, b_ref, m_ref, *rest):
+    def kernel(x_ref, w_ref, b_ref, *rest):
+        if mask is None:
+            m_ref, rest = None, rest
+        else:
+            m_ref, rest = rest[0], rest[1:]
         if select is None:
             (o_ref,) = rest
         else:
@@ -41,7 +45,7 @@
             else:
                 xs = x_ref[r : r + 7, :, :].reshape(k_all, n_in)
             z = jnp.dot(w_ref[...], xs, preferred_element_type=jnp.float32)
-            m_row = m_ref[r]
+            m_row = None if m_ref is None else m_ref[r]
             for g in range(groups):
                 base = g * shifts * fout
                 acc = z[base : base + fout, 0:n_out]
@@ -50,7 +54,9 @@
                 acc = acc + b_val
                 if relu:
                     acc = jnp.maximum(acc, 0.0)
-                acc = (acc * m_row[g : g + 1, :]).astype(jnp.bfloat16)
+                if m_row is not None:
+                    acc = acc * m_row[g : g + 1, :]
+                acc = acc.astype(jnp.bfloat16)
                 if select is None:
                     o_ref[r, g * fout : (g + 1) * fout, :] = acc
                     continue
@@ -75,8 +81,11 @@
     def whole(a):
         return pl.BlockSpec(a.shape, lambda w, n=a.ndim: (0,) * n)
 
-    args = [x, w_all, bias, mask]
-    specs = [per_window(x), whole(w_all), whole(bias), per_window(mask)]
+    args = [x, w_all, bias]
+    specs = [per_window(x), whole(w_all), whole(bias)]
+    if mask is not None:
+        args.append(mask)
+        specs.append(per_window(mask))
     if select is not None:
         args.append(select)
         specs.append(whole(select))
@@ -187,7 +196,7 @@
         second_weight,
         biases,
         16,
-        jnp.ones((n_win, C_DEV, 1, length), jnp.float32),
+        None,
         groups=1,
         shifts=3,
         n_out=length,
@@ -219,7 +228,7 @@
         [padded[:, k * C_DEV : k * C_DEV + nc].reshape(times_here, blocks, C_DEV) for k in range(3)], axis=2
     )[:, :, :wide]
     tag = jnp.zeros((times_here, blocks, 1), recorded.dtype).at[0].set(offsets[0].astype(recorded.dtype))
-    both = jnp.concatenate([windows, jnp.take(windows, partners, axis=1), tag], axis=2)
+    both = jnp.concatenate([windows, jnp.take(windows, partners, axis=1, mode="clip"), tag], axis=2)
     outgoing = jnp.transpose(both, (1, 0, 2))
     arrived = lax.all_to_all(outgoing, "chan", split_axis=0, concat_axis=0, tiled=True)
     biases = jnp.concatenate([first_bias, second_bias, third_bias, fourth_bias]).reshape(-1, 1)
@@ -230,9 +239,16 @@
         weights_stride4(fourth_weight, 2, 0),
         biases,
     )
-    arrived, (first_weight, second_weight, third_weight, fourth_weight, biases) = lax.optimization_barrier(
-        (arrived, prepared)
-    )
+    quarter = blocks * times_here // 4
+    length = quarter + 2 * LEAD
+    n_t = length - 6
+    masks = (
+        edge_mask(C_DEV, 1, length, 0, lambda p, j: (j - LEAD, quarter), me),
+        edge_mask(wide - 6, 1, n_t, 3 - REACH, lambda p, j: (j - (LEAD - 3), quarter), me),
+    )
+    arrived, prepared, masks = lax.optimization_barrier((arrived, prepared, masks))
+    first_weight, second_weight, third_weight, fourth_weight, biases = prepared
+    second_mask, third_mask = masks
     mate_offset = arrived[:, 0, 2 * wide].astype(jnp.int32)[mate]
     times = blocks * times_here
     tms = lax.axis_size("tm")
@@ -256,7 +272,6 @@
     extra = lax.dynamic_update_slice(
         jnp.zeros((C_DEV, F2, length), jnp.float32), coupling, (own_offset - 3, 0, 0)
     )
-    second_mask = edge_mask(C_DEV, 1, length, 0, lambda p, j: (j - LEAD, quarter), me)
     second = (jnp.maximum(pre_second.astype(jnp.float32) + extra, 0.0) * second_mask).astype(jnp.bfloat16)
 
     ring_up = [(i, i + 1) for i in range(blocks - 1)]
@@ -267,7 +282,6 @@
 
     n_t = length - 6
     n_sel = quarter // 4 + 1
-    third_mask = edge_mask(wide - 6, 1, n_t, 3 - REACH, lambda p, j: (j - (LEAD - 3), quarter), me)
     third = banded(
         second_wide[None],
         third_weight,
@@ -286,7 +300,7 @@
         fourth_weight,
         biases,
         80,
-        jnp.ones((1, C_DEV, 1, quarter // 4), jnp.float32),
+        None,
         groups=1,
         shifts=2,
         n_out=quarter // 4,

time: 83.6 us -> 83.2 us (level)
  local copies, waits for them, and re-layouts: 16.3 us -> 15.1 us
  starting transfers between devices: 23.2 us -> 24.3 us
  other arithmetic: 8.28 us -> 7.37 us
    broadcast_in_dim x2 -> x0, local copies, waits for them, and re-layouts: 1.23 us -> none  [the longest x1 0.64 us: lower_layers(): jnp.ones((n_win, C_DEV, 1, length), jnp.float32)]
    select_n x2 -> x0, other arithmetic: 0.85 us -> none  [on_device(): jnp.take(windows, partners, axis=1)]
  transfers between devices with their start and end apart: 5 -> 5, of which waited for: 2 -> 3; matrix products, arithmetic and copies ran while one was open for 13% -> 13% of each run, Pallas kernels for 0% -> 0%
where the time goes in v8:
time: 83.2 us; the launch traced here: 82.7 us
  starting transfers between devices  24.3 us (29%)
  Pallas kernels  22.4 us (27%)
  local copies, waits for them, and re-layouts  15.1 us (18%)
  waiting for transfers between devices  8.15 us (10%)
  other arithmetic  7.37 us (9%)
  between operations  5.17 us (6%)
    pallas_call x4, Pallas kernels, banded(): pl.pallas_call(kernel, grid=(windows,), in_specs=specs, out_specs=pl.Bloc...  20.2 us
    all_to_all x1, starting transfers between devices, on_device(): lax.all_to_all(outgoing, 'chan', split_axis=0, concat_axis=0, tiled=True)  13 us
    ppermute x1, waiting for transfers between devices, on_device(): below = lax.ppermute(second[:REACH], 'chan', ring_down)  4.4 us
    ppermute x1, starting transfers between devices, on_device(): before = lax.ppermute(arrived[blocks - 1], 'tm', up)  3.99 us
    ppermute x1, starting transfers between devices, on_device(): above = lax.ppermute(second[C_DEV - REACH:], 'chan', ring_up)  3.9 us
    optimization_barrier x5, local copies, waits for them, and re-layouts, on_device(): lax.optimization_barrier((arrived, prepared, masks))  3.85 us
    all_to_all x1, waiting for transfers between devices, on_device(): lax.all_to_all(outgoing, 'chan', split_axis=0, concat_axis=0, tiled=True)  3.56 us
    pallas_call x1, Pallas kernels, strain_layout(): pl.pallas_call(kernel, out_shape=jax.ShapeDtypeStruct((rows, n_out), jnp....  2.24 us
  transfers between devices with their start and end apart: 5, of which 3 were waited for; matrix products, arithmetic and copies ran while one was open for 13% of the time, Pallas kernels for 0%

profile of v8, /device:TPU:1, one launch (start us, length us, event | category | flops | bytes accessed | tf_op | source)
XLA Modules:
  0.0 82.7 jit_solution(16067801343197566362)
XLA Ops:
  0.7 0.7 pad_clamp_fusion.3
  1.4 1.0 %pad_slice_fusion.2 = (bf16[32,512]{1,0:T(8,128)(2,1)S(1)}, bf16[32,512]{1,0:T(8,128)(2,1)S(1)}, bf16[32,512]{1,0:T(8,128)(2,1)S(1)}) fusion(bf16[32,512]{1,0:T(8,128)(2,1)} %param.21), kind=kLoop, calls=%fused_computation.32 | loop fusion | bytes 131072 | tf_op jit(solution)/shard_map/slice | solution.py:228
  4.2 0.7 gather_fusion
  5.5 1.5 %reshape.318 = bf16[64,2,656]{2,1,0:T(2,128)(2,1)} reshape(bf16[64,32,41]{2,1,0:T(8,128)(2,1)S(1)} %maximum_bitcast_fusion.1) | data formatting | bytes 335872
  7.0 13.0 %all-to-all-start = ((bf16[64,2,656]{2,1,0:T(2,128)(2,1)}), bf16[64,2,656]{2,1,0:T(2,128)(2,1)S(1)}, u32[]{:S(2)}, u32[]{:S(2)}) async-start(bf16[64,2,656]{2,1,0:T(2,128)(2,1)} %reshape.318), calls=%async_computation | async-start | bytes 393216 | tf_op jit(solution)/shard_map/all_to_all | solution.py:233
  20.0 0.7 dynamic_slice.11
  21.5 0.6 gather_fusion.1
  22.4 0.6 gather_fusion.2
  23.6 0.6 gather_fusion.3
  25.3 0.9 %reshape.281.w_ref = bf16[224,224]{1,0:T(8,128)(2,1)} reshape(bf16[7,32,7,32]{3,2,1,0:T(8,128)(2,1)S(1)} %copy.73) | data formatting | bytes 200704 | tf_op jit(solution)/shard_map/reshape | solution.py:125
  26.4 0.7 and_convert_fusion
  27.3 3.6 %all-to-all-done = bf16[64,2,656]{2,1,0:T(2,128)(2,1)S(1)} async-done(((bf16[64,2,656]{2,1,0:T(2,128)(2,1)}), bf16[64,2,656]{2,1,0:T(2,128)(2,1)S(1)}, u32[]{:S(2)}, u32[]{:S(2)}) %all-to-all-start) | async-done | bytes 167968 | tf_op jit(solution)/shard_map/all_to_all | solution.py:233
  30.9 0.8 reshape.319
  31.7 1.3 %collective-permute-start.1 = (bf16[32,41]{1,0:T(8,128)(2,1)S(1)}, bf16[32,41]{1,0:T(8,128)(2,1)S(1)}, u32[]{:S(2)}, u32[]{:S(2)}) collective-permute-start(bf16[32,41]{1,0:T(8,128)(2,1)S(1)} %get-tuple-element.36), channel_id=1, source_target_pairs={{1,0},{2,1},{3,2},{5,4},{6,5},{7,6},{9,8},{10,9},{11,10},{13,12},{... | collective-permute-start | bytes 7880 | tf_op jit(solution)/shard_map/ppermute | solution.py:258
  33.0 4.0 %collective-permute-start = (bf16[32,41]{1,0:T(8,128)(2,1)S(1)}, bf16[32,41]{1,0:T(8,128)(2,1)S(1)}, u32[]{:S(2)}, u32[]{:S(2)}) collective-permute-start(bf16[32,41]{1,0:T(8,128)(2,1)S(1)} %get-tuple-element.37), channel_id=1, source_target_pairs={{0,1},{1,2},{2,3},{4,5},{5,6},{6,7},{8,9},{9,10},{10,11},{12,13},{... | collective-permute-start | bytes 7880 | tf_op jit(solution)/shard_map/ppermute | solution.py:257
  37.0 0.8 add_convert_fusion.rest_0_
  41.7 0.7 copy.75.w_ref
  42.4 0.7 copy.76.b_ref
  43.1 0.7 copy.77.w_ref
  43.9 0.6 copy-done.6
  44.5 2.2 %shard_map.181 = bf16[160,527]{1,0:T(8,128)(2,1)} custom-call(bf16[2048,41]{1,0:T(8,128)(2,1)} %bitcast.66, bf16[32,41]{1,0:T(8,128)(2,1)} %copy-done.7, bf16[32,41]{1,0:T(8,128)(2,1)} %copy-done.6), custom_call_target="tpu_custom_call" | custom-call | tf_op jit(solution)/shard_map/pallas_call | solution.py:120
  46.7 6.2 %shard_map.182.x_ref = bf16[2,14,64,524]{3,2,1,0:T(8,128)(2,1)} custom-call(bf16[2,80,527]{2,1,0:T(8,128)(2,1)} %bitcast.68, bf16[256,28]{1,0:T(8,128)(2,1)} %copy.75.w_ref, f32[144,1]{1,0:T(8,128)} %copy.76.b_ref, f32[2,14,4,524]{3,2,1,0:T(4,128)} %add_convert_fusion.rest_0_), custom_call_target="tpu_custom_call" | custom-call | tf_op jit(solution)/shard_map/pallas_call | solution.py:92
  52.9 4.0 %shard_map.183 = bf16[2,8,32,522]{3,2,1,0:T(8,128)(2,1)} custom-call(bf16[2,14,64,524]{3,2,1,0:T(8,128)(2,1)} %shard_map.182.x_ref, bf16[96,448]{1,0:T(8,128)(2,1)} %copy.77.w_ref, f32[144,1]{1,0:T(8,128)} %copy.76.b_ref), custom_call_target="tpu_custom_call" | custom-call | tf_op jit(solution)/shard_map/pallas_call | solution.py:92
  56.9 1.2 %slice_convert_fusion = (f32[1,8,32,522]{3,2,1,0:T(8,128)S(1)}, f32[8,32,522]{2,1,0:T(8,128)S(1)}, bf16[1,8,32,522]{3,2,1,0:T(8,128)(2,1)S(1)}) fusion(bf16[2,8,32,522]{3,2,1,0:T(8,128)(2,1)} %shard_map.183), kind=kLoop, calls=%fused_computation.16 | loop fusion | flops 133632 | bytes 1870848 | tf_op jit(solution)/shard_map/convert_element_type | solution.py:275
  58.6 3.9 %collective-permute-start.2 = (bf16[6,32,522]{2,1,0:T(8,128)(2,1)S(1)}, bf16[6,32,522]{2,1,0:T(8,128)(2,1)S(1)}, u32[]{:S(2)}, u32[]{:S(2)}) collective-permute-start(bf16[6,32,522]{2,1,0:T(8,128)(2,1)S(1)} %get-tuple-element.38), channel_id=1, source_target_pairs={{0,4},{4,8},{8,12},{12,16},{16,20},{20,24},{24,28},{28,32},{32,36}... | collective-permute-start | bytes 601352 | tf_op jit(solution)/shard_map/ppermute | solution.py:279
  62.5 2.1 %collective-permute-start.3 = (bf16[6,32,522]{2,1,0:T(8,128)(2,1)S(1)}, bf16[6,32,522]{2,1,0:T(8,128)(2,1)S(1)}, u32[]{:S(2)}, u32[]{:S(2)}) collective-permute-start(bf16[6,32,522]{2,1,0:T(8,128)(2,1)S(1)} %get-tuple-element.39), channel_id=1, source_target_pairs={{4,0},{8,4},{12,8},{16,12},{20,16},{24,20},{28,24},{32,28},{36,32}... | collective-permute-start | bytes 601352 | tf_op jit(solution)/shard_map/ppermute | solution.py:280
  64.6 0.8 %copy.80.w_ref = bf16[128,896]{1,0:T(8,128)(2,1)} copy(bf16[128,896]{0,1:T(8,128)(2,1)S(1)} %reshape.282) | data formatting | bytes 458752 | tf_op jit(solution)/shard_map/optimization_barrier | solution.py:249
  65.6 4.4 %collective-permute-done.3 = bf16[6,32,522]{2,1,0:T(8,128)(2,1)S(1)} collective-permute-done((bf16[6,32,522]{2,1,0:T(8,128)(2,1)S(1)}, bf16[6,32,522]{2,1,0:T(8,128)(2,1)S(1)}, u32[]{:S(2)}, u32[]{:S(2)}) %collective-permute-start.3) | collective-permute-done | bytes 200480 | tf_op jit(solution)/shard_map/ppermute | solution.py:280
  70.0 1.0 %maximum_bitcast_fusion.x_ref = bf16[1,20,32,522]{3,2,1,0:T(8,128)(2,1)} fusion(bf16[6,32,522]{2,1,0:T(8,128)(2,1)S(1)} %collective-permute-done.3, bf16[8,32,522]{2,1,0:T(8,128)(2,1)S(1)} %multiply_convert_fusion, bf16[6,32,522]{2,1,0:T(8,128)(2,1)S(1)} %collective-permute-done.2), kind=kLoop, calls=%fused_computation.8 | loop fusion | flops 668160 | bytes 1336320 | tf_op jit(solution)/shard_map/broadcast_in_dim | solution.py:286
  71.0 7.2 %shard_map.184.x_ref = bf16[1,14,128,129]{3,2,1,0:T(8,128)(2,1)} custom-call(bf16[1,20,32,522]{3,2,1,0:T(8,128)(2,1)} %maximum_bitcast_fusion.x_ref, bf16[224,224]{1,0:T(8,128)(2,1)} %reshape.281.w_ref, f32[144,1]{1,0:T(8,128)} %copy.76.b_ref, f32[1,14,1,516]{3,2,1,0:T(1,128)} %bitcast.76, bf16[128,128]{1,0:T(8,128)(2,1)} %constant.146.clone.rest_1_), custom_call_target="tpu_custom_call" | custom-call | tf_op jit(solution)/shard_map/pallas_call | solution.py:92
  78.3 2.8 %shard_map.185 = bf16[1,8,64,128]{3,2,1,0:T(8,128)(2,1)} custom-call(bf16[1,14,128,129]{3,2,1,0:T(8,128)(2,1)} %shard_map.184.x_ref, bf16[128,896]{1,0:T(8,128)(2,1)} %copy.80.w_ref, f32[144,1]{1,0:T(8,128)} %copy.76.b_ref), custom_call_target="tpu_custom_call" | custom-call | tf_op jit(solution)/shard_map/pallas_call | solution.py:92
  81.0 1.6 %copy.82 = bf16[64,8,128]{2,1,0:T(8,128)(2,1)} copy(bf16[64,8,128]{2,0,1:T(8,128)(2,1)} %bitcast.72) | data formatting | bytes 262144 | tf_op jit(solution)/shard_map/transpose | solution.py:309
  (78 shorter events, 5.8 us)
Async XLA Ops:
  0.0 23.6 %copy-start = (bf16[64,32,7,7]{0,1,3,2:T(8,128)(2,1)S(1)}, bf16[64,32,7,7]{0,1,3,2:T(8,128)(2,1)}, u32[]{:S(2)}) copy-start(bf16[64,32,7,7]{0,1,3,2:T(8,128)(2,1)} %param.31) | copy-start | bytes 602116
  4.1 15.9 %copy-start.10 = (s32[64]{0:T(128)S(1)}, s32[64]{0:T(128)}, u32[]{:S(2)}) copy-start(s32[64]{0:T(128)} %param.22) | copy-start | bytes 772
  4.1 17.3 %copy-start.13 = (s32[64]{0:T(128)S(1)}, s32[64]{0:T(128)}, u32[]{:S(2)}) copy-start(s32[64]{0:T(128)} %constant.183) | copy-start | bytes 772
  4.1 17.3 %copy-start.12 = (s32[12]{0:T(128)S(1)}, s32[12]{0:T(128)}, u32[]{:S(2)}) copy-start(s32[12]{0:T(128)} %constant.184) | copy-start | bytes 148
  4.1 17.3 %copy-start.11 = (s32[8]{0:T(128)S(1)}, s32[8]{0:T(128)}, u32[]{:S(2)}) copy-start(s32[8]{0:T(128)} %constant.185) | copy-start | bytes 100
  4.1 17.3 %copy-start.5 = (bf16[16,1,7,7]{0,3,2,1:T(8,128)(2,1)S(1)}, bf16[16,1,7,7]{0,3,2,1:T(8,128)(2,1)}, u32[]{:S(2)}) copy-start(bf16[16,1,7,7]{0,3,2,1:T(8,128)(2,1)} %param.24) | copy-start | bytes 4708
  4.2 18.0 %copy-start.8 = (pred[4,4,4]{1,0,2:T(4,128)(4,1)S(1)}, pred[4,4,4]{1,0,2:T(4,128)(4,1)}, u32[]{:S(2)}) copy-start(pred[4,4,4]{1,0,2:T(4,128)(4,1)} %constant.153) | copy-start | bytes 196
  4.8 17.6 %copy-start.1 = (bf16[32,16,7,7]{0,1,3,2:T(8,128)(2,1)S(1)}, bf16[32,16,7,7]{0,1,3,2:T(8,128)(2,1)}, u32[]{:S(2)}) copy-start(bf16[32,16,7,7]{0,1,3,2:T(8,128)(2,1)} %param.26) | copy-start | bytes 150532
  5.5 17.5 %copy-start.18 = (pred[3,4]{0,1:T(4,128)(4,1)S(1)}, pred[3,4]{0,1:T(4,128)(4,1)}, u32[]{:S(2)}) copy-start(pred[3,4]{0,1:T(4,128)(4,1)} %constant.162) | copy-start | bytes 40
  7.0 23.9 %all-to-all-start = ((bf16[64,2,656]{2,1,0:T(2,128)(2,1)}), bf16[64,2,656]{2,1,0:T(2,128)(2,1)S(1)}, u32[]{:S(2)}, u32[]{:S(2)}) async-start(bf16[64,2,656]{2,1,0:T(2,128)(2,1)} %reshape.318), calls=%async_computation | async-start | bytes 393216 | tf_op jit(solution)/shard_map/all_to_all | solution.py:233
  23.6 0.7 copy-start.9
  23.6 1.5 %copy-start.3 = (bf16[32,32,7,7]{1,0,3,2:T(8,128)(2,1)S(1)}, bf16[32,32,7,7]{1,0,3,2:T(8,128)(2,1)}, u32[]{:S(2)}) copy-start(bf16[32,32,7,7]{1,0,3,2:T(8,128)(2,1)} %param.29) | copy-start | bytes 301060
  24.3 2.8 %copy-start.14 = (f32[64]{0:T(128)S(1)}, f32[64]{0:T(128)}, u32[]{:S(2)}) copy-start(f32[64]{0:T(128)} %param.32) | copy-start | bytes 772
  24.3 2.8 %copy-start.15 = (f32[32]{0:T(128)S(1)}, f32[32]{0:T(128)}, u32[]{:S(2)}) copy-start(f32[32]{0:T(128)} %param.30) | copy-start | bytes 388
  24.3 2.8 %copy-start.16 = (f32[32]{0:T(128)S(1)}, f32[32]{0:T(128)}, u32[]{:S(2)}) copy-start(f32[32]{0:T(128)} %param.27) | copy-start | bytes 388
  24.3 2.8 %copy-start.17 = (f32[16]{0:T(128)S(1)}, f32[16]{0:T(128)}, u32[]{:S(2)}) copy-start(f32[16]{0:T(128)} %param.25) | copy-start | bytes 196
  31.7 12.2 %copy-start.2 = (bf16[64,32,41]{2,1,0:T(8,128)(2,1)}, bf16[64,32,41]{2,1,0:T(8,128)(2,1)S(1)}, u32[]{:S(2)}) copy-start(bf16[64,32,41]{2,1,0:T(8,128)(2,1)S(1)} %reshape.319) | copy-start | bytes 503812
  31.7 12.1 %collective-permute-start.1 = (bf16[32,41]{1,0:T(8,128)(2,1)S(1)}, bf16[32,41]{1,0:T(8,128)(2,1)S(1)}, u32[]{:S(2)}, u32[]{:S(2)}) collective-permute-start(bf16[32,41]{1,0:T(8,128)(2,1)S(1)} %get-tuple-element.36), channel_id=1, source_target_pairs={{1,0},{2,1},{3,2},{5,4},{6,5},{7,6},{9,8},{10,9},{11,10},{13,12},{... | collective-permute-start | bytes 7880 | tf_op jit(solution)/shard_map/ppermute | solution.py:258
  33.0 10.8 %collective-permute-start = (bf16[32,41]{1,0:T(8,128)(2,1)S(1)}, bf16[32,41]{1,0:T(8,128)(2,1)S(1)}, u32[]{:S(2)}, u32[]{:S(2)}) collective-permute-start(bf16[32,41]{1,0:T(8,128)(2,1)S(1)} %get-tuple-element.37), channel_id=1, source_target_pairs={{0,1},{1,2},{2,3},{4,5},{5,6},{6,7},{8,9},{9,10},{10,11},{12,13},{... | collective-permute-start | bytes 7880 | tf_op jit(solution)/shard_map/ppermute | solution.py:257
  43.9 0.6 copy-start.6
  43.9 0.6 copy-start.7
  56.9 1.3 %copy-start.4 = (bf16[7,32,32]{2,1,0:T(8,128)(2,1)S(1)}, bf16[7,32,32]{2,1,0:T(8,128)(2,1)}, u32[]{:S(2)}) copy-start(bf16[7,32,32]{2,1,0:T(8,128)(2,1)} %param.28) | copy-start | bytes 43012
  58.6 7.0 %collective-permute-start.2 = (bf16[6,32,522]{2,1,0:T(8,128)(2,1)S(1)}, bf16[6,32,522]{2,1,0:T(8,128)(2,1)S(1)}, u32[]{:S(2)}, u32[]{:S(2)}) collective-permute-start(bf16[6,32,522]{2,1,0:T(8,128)(2,1)S(1)} %get-tuple-element.38), channel_id=1, source_target_pairs={{0,4},{4,8},{8,12},{12,16},{16,20},{20,24},{24,28},{28,32},{32,36}... | collective-permute-start | bytes 601352 | tf_op jit(solution)/shard_map/ppermute | solution.py:279
  62.5 7.5 %collective-permute-start.3 = (bf16[6,32,522]{2,1,0:T(8,128)(2,1)S(1)}, bf16[6,32,522]{2,1,0:T(8,128)(2,1)S(1)}, u32[]{:S(2)}, u32[]{:S(2)}) collective-permute-start(bf16[6,32,522]{2,1,0:T(8,128)(2,1)S(1)} %get-tuple-element.39), channel_id=1, source_target_pairs={{4,0},{8,4},{12,8},{16,12},{20,16},{24,20},{28,24},{32,28},{36,32}... | collective-permute-start | bytes 601352 | tf_op jit(solution)/shard_map/ppermute | solution.py:280

commit v9 on v8

--- a/solution.py
+++ b/solution.py
@@ -15,7 +15,7 @@
 LANE_BLOCK = 256
 
 
-def banded(x, w_all, bias, b_row, mask, *, groups, shifts, n_out, relu, select=None, n_sel=0):
+def banded(x, w_all, bias, b_row, mask, *, groups, shifts, n_out, relu, select=None, n_sel=0, rows_inner=False):
     windows = x.shape[0]
     flat = x.ndim == 3
     k_all = w_all.shape[1]
@@ -23,7 +23,9 @@
     r_out = (x.shape[1] // row_step if flat else x.shape[1]) - 6
     n_in = x.shape[-1]
     fout = w_all.shape[0] // (groups * shifts)
-    if select is None:
+    if rows_inner:
+        out_shape = (windows, groups * fout, r_out, n_out)
+    elif select is None:
         out_shape = (windows, r_out, groups * fout, n_out)
     else:
         out_shape = (windows, r_out, PH * fout, n_sel)
@@ -57,6 +59,9 @@
                 if m_row is not None:
                     acc = acc * m_row[g : g + 1, :]
                 acc = acc.astype(jnp.bfloat16)
+                if rows_inner:
+                    o_ref[g * fout : (g + 1) * fout, r : r + 1, :] = acc[:, None, :]
+                    continue
                 if select is None:
                     o_ref[r, g * fout : (g + 1) * fout, :] = acc
                     continue
@@ -305,8 +310,9 @@
         shifts=2,
         n_out=quarter // 4,
         relu=True,
-    )
-    return jnp.transpose(features[0], (1, 0, 2))
+        rows_inner=True,
+    )
+    return features[0]
 
 
 def solution(mesh):

time: 83.2 us -> 81.7 us (0.982)
  local copies, waits for them, and re-layouts: 15.1 us -> 13.5 us
    transpose x1 -> x0, local copies, waits for them, and re-layouts: 1.65 us -> none  [on_device(): return jnp.transpose(features[0], (1, 0, 2))]
where the time goes in v9:
time: 81.7 us; the launch traced here: 81.2 us
  starting transfers between devices  24.3 us (30%)
  Pallas kernels  22.5 us (28%)
  local copies, waits for them, and re-layouts  13.5 us (17%)
  waiting for transfers between devices  8.15 us (10%)
  other arithmetic  7.37 us (9%)
  between operations  5.16 us (6%)
    pallas_call x4, Pallas kernels, banded(): pl.pallas_call(kernel, grid=(windows,), in_specs=specs, out_specs=pl.Bloc...  20.3 us
    all_to_all x1, starting transfers between devices, on_device(): lax.all_to_all(outgoing, 'chan', split_axis=0, concat_axis=0, tiled=True)  13 us
    ppermute x1, waiting for transfers between devices, on_device(): below = lax.ppermute(second[:REACH], 'chan', ring_down)  4.4 us
    ppermute x1, starting transfers between devices, on_device(): before = lax.ppermute(arrived[blocks - 1], 'tm', up)  3.99 us
    ppermute x1, starting transfers between devices, on_device(): above = lax.ppermute(second[C_DEV - REACH:], 'chan', ring_up)  3.9 us
    optimization_barrier x5, local copies, waits for them, and re-layouts, on_device(): lax.optimization_barrier((arrived, prepared, masks))  3.85 us
    all_to_all x1, waiting for transfers between devices, on_device(): lax.all_to_all(outgoing, 'chan', split_axis=0, concat_axis=0, tiled=True)  3.56 us
    pallas_call x1, Pallas kernels, strain_layout(): pl.pallas_call(kernel, out_shape=jax.ShapeDtypeStruct((rows, n_out), jnp....  2.24 us
  transfers between devices with their start and end apart: 5, of which 3 were waited for; matrix products, arithmetic and copies ran while one was open for 13% of the time, Pallas kernels for 0%

profile of v9, /device:TPU:1, one launch (start us, length us, event | category | flops | bytes accessed | tf_op | source)
XLA Modules:
  0.0 81.2 jit_solution(12694565304060560483)
XLA Ops:
  0.7 0.7 pad_clamp_fusion.3
  1.4 1.0 %pad_slice_fusion.2 = (bf16[32,512]{1,0:T(8,128)(2,1)S(1)}, bf16[32,512]{1,0:T(8,128)(2,1)S(1)}, bf16[32,512]{1,0:T(8,128)(2,1)S(1)}) fusion(bf16[32,512]{1,0:T(8,128)(2,1)} %param.21), kind=kLoop, calls=%fused_computation.32 | loop fusion | bytes 131072 | tf_op jit(solution)/shard_map/slice | solution.py:233
  4.2 0.7 gather_fusion
  5.5 1.5 %reshape.318 = bf16[64,2,656]{2,1,0:T(2,128)(2,1)} reshape(bf16[64,32,41]{2,1,0:T(8,128)(2,1)S(1)} %maximum_bitcast_fusion.1) | data formatting | bytes 335872
  7.0 13.0 %all-to-all-start = ((bf16[64,2,656]{2,1,0:T(2,128)(2,1)}), bf16[64,2,656]{2,1,0:T(2,128)(2,1)S(1)}, u32[]{:S(2)}, u32[]{:S(2)}) async-start(bf16[64,2,656]{2,1,0:T(2,128)(2,1)} %reshape.318), calls=%async_computation | async-start | bytes 393216 | tf_op jit(solution)/shard_map/all_to_all | solution.py:238
  20.0 0.7 dynamic_slice.11
  21.5 0.6 gather_fusion.1
  22.4 0.6 gather_fusion.2
  23.6 0.6 gather_fusion.3
  24.3 0.6 fusion.2
  25.3 0.9 %reshape.281.w_ref = bf16[224,224]{1,0:T(8,128)(2,1)} reshape(bf16[7,32,7,32]{3,2,1,0:T(8,128)(2,1)S(1)} %copy.70) | data formatting | bytes 200704 | tf_op jit(solution)/shard_map/reshape | solution.py:130
  26.4 0.7 and_convert_fusion
  27.3 3.6 %all-to-all-done = bf16[64,2,656]{2,1,0:T(2,128)(2,1)S(1)} async-done(((bf16[64,2,656]{2,1,0:T(2,128)(2,1)}), bf16[64,2,656]{2,1,0:T(2,128)(2,1)S(1)}, u32[]{:S(2)}, u32[]{:S(2)}) %all-to-all-start) | async-done | bytes 167968 | tf_op jit(solution)/shard_map/all_to_all | solution.py:238
  30.9 0.8 %reshape.319 = bf16[64,32,41]{2,1,0:T(8,128)(2,1)S(1)} reshape(bf16[64,2,656]{2,1,0:T(2,128)(2,1)S(1)} %all-to-all-done) | data formatting | bytes 335872 | tf_op jit(solution)/shard_map/optimization_barrier | solution.py:254
  31.7 1.3 %collective-permute-start.1 = (bf16[32,41]{1,0:T(8,128)(2,1)S(1)}, bf16[32,41]{1,0:T(8,128)(2,1)S(1)}, u32[]{:S(2)}, u32[]{:S(2)}) collective-permute-start(bf16[32,41]{1,0:T(8,128)(2,1)S(1)} %get-tuple-element.36), channel_id=1, source_target_pairs={{1,0},{2,1},{3,2},{5,4},{6,5},{7,6},{9,8},{10,9},{11,10},{13,12},{... | collective-permute-start | bytes 7880 | tf_op jit(solution)/shard_map/ppermute | solution.py:263
  33.0 4.0 %collective-permute-start = (bf16[32,41]{1,0:T(8,128)(2,1)S(1)}, bf16[32,41]{1,0:T(8,128)(2,1)S(1)}, u32[]{:S(2)}, u32[]{:S(2)}) collective-permute-start(bf16[32,41]{1,0:T(8,128)(2,1)S(1)} %get-tuple-element.37), channel_id=1, source_target_pairs={{0,1},{1,2},{2,3},{4,5},{5,6},{6,7},{8,9},{9,10},{10,11},{12,13},{... | collective-permute-start | bytes 7880 | tf_op jit(solution)/shard_map/ppermute | solution.py:262
  37.0 0.8 add_convert_fusion.rest_0_
  41.7 0.7 copy.72.w_ref
  42.4 0.7 copy.73.b_ref
  43.1 0.7 copy.74.w_ref
  43.9 0.6 copy-done.6
  44.5 2.2 %shard_map.181 = bf16[160,527]{1,0:T(8,128)(2,1)} custom-call(bf16[2048,41]{1,0:T(8,128)(2,1)} %bitcast.64, bf16[32,41]{1,0:T(8,128)(2,1)} %copy-done.7, bf16[32,41]{1,0:T(8,128)(2,1)} %copy-done.6), custom_call_target="tpu_custom_call" | custom-call | tf_op jit(solution)/shard_map/pallas_call | solution.py:125
  46.7 6.2 %shard_map.182.x_ref = bf16[2,14,64,524]{3,2,1,0:T(8,128)(2,1)} custom-call(bf16[2,80,527]{2,1,0:T(8,128)(2,1)} %bitcast.66, bf16[256,28]{1,0:T(8,128)(2,1)} %copy.72.w_ref, f32[144,1]{1,0:T(8,128)} %copy.73.b_ref, f32[2,14,4,524]{3,2,1,0:T(4,128)} %add_convert_fusion.rest_0_), custom_call_target="tpu_custom_call" | custom-call | tf_op jit(solution)/shard_map/pallas_call | solution.py:97
  52.9 4.0 %shard_map.183 = bf16[2,8,32,522]{3,2,1,0:T(8,128)(2,1)} custom-call(bf16[2,14,64,524]{3,2,1,0:T(8,128)(2,1)} %shard_map.182.x_ref, bf16[96,448]{1,0:T(8,128)(2,1)} %copy.74.w_ref, f32[144,1]{1,0:T(8,128)} %copy.73.b_ref), custom_call_target="tpu_custom_call" | custom-call | tf_op jit(solution)/shard_map/pallas_call | solution.py:97
  56.9 1.2 %slice_convert_fusion = (f32[1,8,32,522]{3,2,1,0:T(8,128)S(1)}, f32[8,32,522]{2,1,0:T(8,128)S(1)}, bf16[1,8,32,522]{3,2,1,0:T(8,128)(2,1)S(1)}) fusion(bf16[2,8,32,522]{3,2,1,0:T(8,128)(2,1)} %shard_map.183), kind=kLoop, calls=%fused_computation.16 | loop fusion | flops 133632 | bytes 1870848 | tf_op jit(solution)/shard_map/convert_element_type | solution.py:280
  58.6 3.9 %collective-permute-start.2 = (bf16[6,32,522]{2,1,0:T(8,128)(2,1)S(1)}, bf16[6,32,522]{2,1,0:T(8,128)(2,1)S(1)}, u32[]{:S(2)}, u32[]{:S(2)}) collective-permute-start(bf16[6,32,522]{2,1,0:T(8,128)(2,1)S(1)} %get-tuple-element.38), channel_id=1, source_target_pairs={{0,4},{4,8},{8,12},{12,16},{16,20},{20,24},{24,28},{28,32},{32,36}... | collective-permute-start | bytes 601352 | tf_op jit(solution)/shard_map/ppermute | solution.py:284
  62.5 2.1 %collective-permute-start.3 = (bf16[6,32,522]{2,1,0:T(8,128)(2,1)S(1)}, bf16[6,32,522]{2,1,0:T(8,128)(2,1)S(1)}, u32[]{:S(2)}, u32[]{:S(2)}) collective-permute-start(bf16[6,32,522]{2,1,0:T(8,128)(2,1)S(1)} %get-tuple-element.39), channel_id=1, source_target_pairs={{4,0},{8,4},{12,8},{16,12},{20,16},{24,20},{28,24},{32,28},{36,32}... | collective-permute-start | bytes 601352 | tf_op jit(solution)/shard_map/ppermute | solution.py:285
  64.6 0.8 %copy.77.w_ref = bf16[128,896]{1,0:T(8,128)(2,1)} copy(bf16[128,896]{0,1:T(8,128)(2,1)S(1)} %reshape.282) | data formatting | bytes 458752 | tf_op jit(solution)/shard_map/optimization_barrier | solution.py:254
  65.6 4.4 %collective-permute-done.3 = bf16[6,32,522]{2,1,0:T(8,128)(2,1)S(1)} collective-permute-done((bf16[6,32,522]{2,1,0:T(8,128)(2,1)S(1)}, bf16[6,32,522]{2,1,0:T(8,128)(2,1)S(1)}, u32[]{:S(2)}, u32[]{:S(2)}) %collective-permute-start.3) | collective-permute-done | bytes 200480 | tf_op jit(solution)/shard_map/ppermute | solution.py:285
  70.0 1.0 %maximum_bitcast_fusion.x_ref = bf16[1,20,32,522]{3,2,1,0:T(8,128)(2,1)} fusion(bf16[6,32,522]{2,1,0:T(8,128)(2,1)S(1)} %collective-permute-done.3, bf16[8,32,522]{2,1,0:T(8,128)(2,1)S(1)} %multiply_convert_fusion, bf16[6,32,522]{2,1,0:T(8,128)(2,1)S(1)} %collective-permute-done.2), kind=kLoop, calls=%fused_computation.8 | loop fusion | flops 668160 | bytes 1336320 | tf_op jit(solution)/shard_map/broadcast_in_dim | solution.py:291
  71.0 7.2 %shard_map.184.x_ref = bf16[1,14,128,129]{3,2,1,0:T(8,128)(2,1)} custom-call(bf16[1,20,32,522]{3,2,1,0:T(8,128)(2,1)} %maximum_bitcast_fusion.x_ref, bf16[224,224]{1,0:T(8,128)(2,1)} %reshape.281.w_ref, f32[144,1]{1,0:T(8,128)} %copy.73.b_ref, f32[1,14,1,516]{3,2,1,0:T(1,128)} %bitcast.73, bf16[128,128]{1,0:T(8,128)(2,1)} %constant.146.clone.rest_1_), custom_call_target="tpu_custom_call" | custom-call | tf_op jit(solution)/shard_map/pallas_call | solution.py:97
  78.3 2.9 %shard_map.185 = bf16[1,64,8,128]{3,2,1,0:T(8,128)(2,1)} custom-call(bf16[1,14,128,129]{3,2,1,0:T(8,128)(2,1)} %shard_map.184.x_ref, bf16[128,896]{1,0:T(8,128)(2,1)} %copy.77.w_ref, f32[144,1]{1,0:T(8,128)} %copy.73.b_ref), custom_call_target="tpu_custom_call" | custom-call | tf_op jit(solution)/shard_map/pallas_call | solution.py:97
  (77 shorter events, 5.3 us)
Async XLA Ops:
  0.0 23.6 %copy-start = (bf16[64,32,7,7]{0,1,3,2:T(8,128)(2,1)S(1)}, bf16[64,32,7,7]{0,1,3,2:T(8,128)(2,1)}, u32[]{:S(2)}) copy-start(bf16[64,32,7,7]{0,1,3,2:T(8,128)(2,1)} %param.31) | copy-start | bytes 602116
  4.1 15.9 %copy-start.10 = (s32[64]{0:T(128)S(1)}, s32[64]{0:T(128)}, u32[]{:S(2)}) copy-start(s32[64]{0:T(128)} %param.22) | copy-start | bytes 772
  4.1 17.3 %copy-start.13 = (s32[64]{0:T(128)S(1)}, s32[64]{0:T(128)}, u32[]{:S(2)}) copy-start(s32[64]{0:T(128)} %constant.183) | copy-start | bytes 772
  4.1 17.3 %copy-start.12 = (s32[12]{0:T(128)S(1)}, s32[12]{0:T(128)}, u32[]{:S(2)}) copy-start(s32[12]{0:T(128)} %constant.184) | copy-start | bytes 148
  4.1 17.3 %copy-start.11 = (s32[8]{0:T(128)S(1)}, s32[8]{0:T(128)}, u32[]{:S(2)}) copy-start(s32[8]{0:T(128)} %constant.185) | copy-start | bytes 100
  4.1 17.3 %copy-start.5 = (bf16[16,1,7,7]{0,3,2,1:T(8,128)(2,1)S(1)}, bf16[16,1,7,7]{0,3,2,1:T(8,128)(2,1)}, u32[]{:S(2)}) copy-start(bf16[16,1,7,7]{0,3,2,1:T(8,128)(2,1)} %param.24) | copy-start | bytes 4708
  4.2 18.0 %copy-start.8 = (pred[4,4,4]{1,0,2:T(4,128)(4,1)S(1)}, pred[4,4,4]{1,0,2:T(4,128)(4,1)}, u32[]{:S(2)}) copy-start(pred[4,4,4]{1,0,2:T(4,128)(4,1)} %constant.153) | copy-start | bytes 196
  4.8 17.6 %copy-start.1 = (bf16[32,16,7,7]{0,1,3,2:T(8,128)(2,1)S(1)}, bf16[32,16,7,7]{0,1,3,2:T(8,128)(2,1)}, u32[]{:S(2)}) copy-start(bf16[32,16,7,7]{0,1,3,2:T(8,128)(2,1)} %param.26) | copy-start | bytes 150532
  5.5 17.5 %copy-start.18 = (pred[3,4]{0,1:T(4,128)(4,1)S(1)}, pred[3,4]{0,1:T(4,128)(4,1)}, u32[]{:S(2)}) copy-start(pred[3,4]{0,1:T(4,128)(4,1)} %constant.162) | copy-start | bytes 40
  7.0 23.9 %all-to-all-start = ((bf16[64,2,656]{2,1,0:T(2,128)(2,1)}), bf16[64,2,656]{2,1,0:T(2,128)(2,1)S(1)}, u32[]{:S(2)}, u32[]{:S(2)}) async-start(bf16[64,2,656]{2,1,0:T(2,128)(2,1)} %reshape.318), calls=%async_computation | async-start | bytes 393216 | tf_op jit(solution)/shard_map/all_to_all | solution.py:238
  23.6 0.7 copy-start.9
  23.6 1.5 %copy-start.3 = (bf16[32,32,7,7]{1,0,3,2:T(8,128)(2,1)S(1)}, bf16[32,32,7,7]{1,0,3,2:T(8,128)(2,1)}, u32[]{:S(2)}) copy-start(bf16[32,32,7,7]{1,0,3,2:T(8,128)(2,1)} %param.29) | copy-start | bytes 301060
  24.3 2.8 %copy-start.14 = (f32[64]{0:T(128)S(1)}, f32[64]{0:T(128)}, u32[]{:S(2)}) copy-start(f32[64]{0:T(128)} %param.32) | copy-start | bytes 772
  24.3 2.8 %copy-start.15 = (f32[32]{0:T(128)S(1)}, f32[32]{0:T(128)}, u32[]{:S(2)}) copy-start(f32[32]{0:T(128)} %param.30) | copy-start | bytes 388
  24.3 2.8 %copy-start.16 = (f32[32]{0:T(128)S(1)}, f32[32]{0:T(128)}, u32[]{:S(2)}) copy-start(f32[32]{0:T(128)} %param.27) | copy-start | bytes 388
  24.3 2.8 %copy-start.17 = (f32[16]{0:T(128)S(1)}, f32[16]{0:T(128)}, u32[]{:S(2)}) copy-start(f32[16]{0:T(128)} %param.25) | copy-start | bytes 196
  31.7 12.2 %copy-start.2 = (bf16[64,32,41]{2,1,0:T(8,128)(2,1)}, bf16[64,32,41]{2,1,0:T(8,128)(2,1)S(1)}, u32[]{:S(2)}) copy-start(bf16[64,32,41]{2,1,0:T(8,128)(2,1)S(1)} %reshape.319) | copy-start | bytes 503812
  31.7 12.1 %collective-permute-start.1 = (bf16[32,41]{1,0:T(8,128)(2,1)S(1)}, bf16[32,41]{1,0:T(8,128)(2,1)S(1)}, u32[]{:S(2)}, u32[]{:S(2)}) collective-permute-start(bf16[32,41]{1,0:T(8,128)(2,1)S(1)} %get-tuple-element.36), channel_id=1, source_target_pairs={{1,0},{2,1},{3,2},{5,4},{6,5},{7,6},{9,8},{10,9},{11,10},{13,12},{... | collective-permute-start | bytes 7880 | tf_op jit(solution)/shard_map/ppermute | solution.py:263
  33.0 10.8 %collective-permute-start = (bf16[32,41]{1,0:T(8,128)(2,1)S(1)}, bf16[32,41]{1,0:T(8,128)(2,1)S(1)}, u32[]{:S(2)}, u32[]{:S(2)}) collective-permute-start(bf16[32,41]{1,0:T(8,128)(2,1)S(1)} %get-tuple-element.37), channel_id=1, source_target_pairs={{0,1},{1,2},{2,3},{4,5},{5,6},{6,7},{8,9},{9,10},{10,11},{12,13},{... | collective-permute-start | bytes 7880 | tf_op jit(solution)/shard_map/ppermute | solution.py:262
  43.9 0.6 copy-start.6
  43.9 0.6 copy-start.7
  56.9 1.3 %copy-start.4 = (bf16[7,32,32]{2,1,0:T(8,128)(2,1)S(1)}, bf16[7,32,32]{2,1,0:T(8,128)(2,1)}, u32[]{:S(2)}) copy-start(bf16[7,32,32]{2,1,0:T(8,128)(2,1)} %param.28) | copy-start | bytes 43012
  58.6 7.0 %collective-permute-start.2 = (bf16[6,32,522]{2,1,0:T(8,128)(2,1)S(1)}, bf16[6,32,522]{2,1,0:T(8,128)(2,1)S(1)}, u32[]{:S(2)}, u32[]{:S(2)}) collective-permute-start(bf16[6,32,522]{2,1,0:T(8,128)(2,1)S(1)} %get-tuple-element.38), channel_id=1, source_target_pairs={{0,4},{4,8},{8,12},{12,16},{16,20},{20,24},{24,28},{28,32},{32,36}... | collective-permute-start | bytes 601352 | tf_op jit(solution)/shard_map/ppermute | solution.py:284
  62.5 7.5 %collective-permute-start.3 = (bf16[6,32,522]{2,1,0:T(8,128)(2,1)S(1)}, bf16[6,32,522]{2,1,0:T(8,128)(2,1)S(1)}, u32[]{:S(2)}, u32[]{:S(2)}) collective-permute-start(bf16[6,32,522]{2,1,0:T(8,128)(2,1)S(1)} %get-tuple-element.39), channel_id=1, source_target_pairs={{4,0},{8,4},{12,8},{16,12},{20,16},{24,20},{28,24},{32,28},{36,32}... | collective-permute-start | bytes 601352 | tf_op jit(solution)/shard_map/ppermute | solution.py:285

commit v10 on v9

--- a/solution.py
+++ b/solution.py
@@ -103,26 +103,36 @@
     )(*args)
 
 
-def strain_layout(raw, left, right, rows):
-    channels = raw.shape[1]
-    cols = raw.shape[0] // PH
+def strain_layout(arrived, rows):
+    blocks, span, channels = arrived.shape
+    here = span // 3
+    per = here // PH
+    cols = blocks * per
     n_out = WL + cols + WR
 
-    def kernel(raw_ref, l_ref, r_ref, o_ref):
+    def kernel(a_ref, o_ref):
         ci = lax.broadcasted_iota(jnp.int32, (rows, channels), 1)
         ri = lax.broadcasted_iota(jnp.int32, (rows, channels), 0)
         nt = (((1,), (1,)), ((), ()))
-        pieces = ((l_ref, 0, left.shape[0] // PH, left.shape[0] // PH - WL), (raw_ref, WL, cols, 0), (r_ref, WL + cols, WR, 0))
-        for src, lo, n, skip in pieces:
+        picks = (
+            (lambda q: a_ref[blocks - 1, pl.ds(here + q, per, stride=PH), :], 0, per - WL),
+            (lambda q: a_ref[:, pl.ds(q, per, stride=PH), :].astype(jnp.float32).reshape(cols, channels), WL, 0),
+            (lambda q: a_ref[0, pl.ds(2 * here + q, per, stride=PH), :], WL + cols, per - WR),
+        )
+        for take, lo, skip in picks:
             acc = None
             for q in range(PH):
                 e = (ri == ci * PH + q).astype(jnp.float32)
-                piece = src[pl.ds(q, n, stride=PH), :].astype(jnp.float32)
+                piece = take(q).astype(jnp.float32)
                 y = lax.dot_general(e, piece, nt, preferred_element_type=jnp.float32)
                 acc = y if acc is None else acc + y
-            o_ref[:, lo : lo + n - skip] = acc[:, skip:].astype(o_ref.dtype)
-
-    return pl.pallas_call(kernel, out_shape=jax.ShapeDtypeStruct((rows, n_out), jnp.bfloat16))(raw, left, right)
+            width = acc.shape[1] - skip
+            if lo == 0:
+                o_ref[:, 0:width] = acc[:, skip:].astype(o_ref.dtype)
+            else:
+                o_ref[:, lo : lo + width] = acc[:, :width].astype(o_ref.dtype)
+
+    return pl.pallas_call(kernel, out_shape=jax.ShapeDtypeStruct((rows, n_out), jnp.bfloat16))(arrived)
 
 
 def weights_stride1(w):
@@ -228,11 +238,15 @@
     mate = partners[me]
     times_here, nc = recorded.shape
     wide = C_DEV + 2 * REACH
-    padded = jnp.pad(recorded, ((0, 0), (REACH, 3 * C_DEV - REACH)))
+    tms = lax.axis_size("tm")
+    up = [(i, i + 1) for i in range(tms - 1)]
+    down = [(j, i) for i, j in up]
+    spread = jnp.concatenate([recorded, lax.ppermute(recorded, "tm", up), lax.ppermute(recorded, "tm", down)])
+    padded = jnp.pad(spread, ((0, 0), (REACH, 3 * C_DEV - REACH)))
     windows = jnp.concatenate(
-        [padded[:, k * C_DEV : k * C_DEV + nc].reshape(times_here, blocks, C_DEV) for k in range(3)], axis=2
+        [padded[:, k * C_DEV : k * C_DEV + nc].reshape(3 * times_here, blocks, C_DEV) for k in range(3)], axis=2
     )[:, :, :wide]
-    tag = jnp.zeros((times_here, blocks, 1), recorded.dtype).at[0].set(offsets[0].astype(recorded.dtype))
+    tag = jnp.zeros((3 * times_here, blocks, 1), recorded.dtype).at[0].set(offsets[0].astype(recorded.dtype))
     both = jnp.concatenate([windows, jnp.take(windows, partners, axis=1, mode="clip"), tag], axis=2)
     outgoing = jnp.transpose(both, (1, 0, 2))
     arrived = lax.all_to_all(outgoing, "chan", split_axis=0, concat_axis=0, tiled=True)
@@ -256,12 +270,7 @@
     second_mask, third_mask = masks
     mate_offset = arrived[:, 0, 2 * wide].astype(jnp.int32)[mate]
     times = blocks * times_here
-    tms = lax.axis_size("tm")
-    up = [(i, i + 1) for i in range(tms - 1)]
-    down = [(j, i) for i, j in up]
-    before = lax.ppermute(arrived[blocks - 1], "tm", up)
-    after = lax.ppermute(arrived[0, : PH * WR], "tm", down)
-    strain_wide = strain_layout(arrived.reshape(times, -1), before, after, 2 * wide * PH)
+    strain_wide = strain_layout(arrived, 2 * wide * PH)
 
     quarter = times // 4
     length = quarter + 2 * LEAD

time: 81.7 us -> 101 us (1.24)
  waiting for transfers between devices: 8.15 us -> 25.7 us
  other arithmetic: 7.37 us -> 10.5 us
  local copies, waits for them, and re-layouts: 13.5 us -> 12.4 us
    all_to_all x1, waiting for transfers between devices: 3.56 us -> 21.2 us  [on_device(): lax.all_to_all(outgoing, 'chan', split_axis=0, concat_axis=0, tiled=True)]
    slice x4 -> x0, local copies, waits for them, and re-layouts: 1.32 us -> none  [on_device(): padded[:, k * C_DEV:k * C_DEV + nc].reshape(times_here, blocks, C_DEV)]
    gather x2, other arithmetic: 0.01 us -> 1.32 us  [weights_stride4(): jnp.take(w, np.clip(b, 0, 6).reshape(-1), axis=3)]
    unnamed x40 -> x22, local copies, waits for them, and re-layouts: 2.16 us -> 1.71 us
where the time goes in v10:
time: 101 us
  waiting for transfers between devices  25.7 us (25%)
  starting transfers between devices  24.2 us (24%)
  Pallas kernels  22.9 us (23%)
  local copies, waits for them, and re-layouts  12.4 us (12%)
  other arithmetic  10.5 us (10%)
  between operations  4.72 us (5%)
    all_to_all x1, waiting for transfers between devices, on_device(): lax.all_to_all(outgoing, 'chan', split_axis=0, concat_axis=0, tiled=True)  21.2 us
    pallas_call x4, Pallas kernels, banded(): pl.pallas_call(kernel, grid=(windows,), in_specs=specs, out_specs=pl.Bloc...  20.3 us
    all_to_all x1, starting transfers between devices, on_device(): lax.all_to_all(outgoing, 'chan', split_axis=0, concat_axis=0, tiled=True)  12.9 us
    optimization_barrier x5, local copies, waits for them, and re-layouts, on_device(): lax.optimization_barrier((arrived, prepared, masks))  4.76 us
    ppermute x1, starting transfers between devices, on_device(): lax.ppermute(recorded, 'tm', up)  4.65 us
    ppermute x1, waiting for transfers between devices, on_device(): below = lax.ppermute(second[:REACH], 'chan', ring_down)  4.4 us
    ppermute x1, starting transfers between devices, on_device(): above = lax.ppermute(second[C_DEV - REACH:], 'chan', ring_up)  3.26 us
    pallas_call x1, Pallas kernels, strain_layout(): pl.pallas_call(kernel, out_shape=jax.ShapeDtypeStruct((rows, n_out), jnp....  2.61 us
  transfers between devices with their start and end apart: 5, of which 3 were waited for; matrix products, arithmetic and copies ran while one was open for 13% of the time, Pallas kernels for 0%

profile of v10, /device:TPU:1, one launch (start us, length us, event | category | flops | bytes accessed | tf_op | source)
XLA Modules:
  0.0 100.7 jit_solution(8685344313612527964)
XLA Ops:
  0.0 0.9 copy.63
  0.9 1.3 %collective-permute-start.1 = (bf16[32,512]{0,1:T(8,128)(2,1)S(1)}, bf16[32,512]{0,1:T(8,128)(2,1)S(1)}, u32[]{:S(2)}, u32[]{:S(2)}) collective-permute-start(bf16[32,512]{0,1:T(8,128)(2,1)S(1)} %copy.63), channel_id=1, source_target_pairs={{1,0},{2,1},{3,2},{5,4},{6,5},{7,6},{9,8},{10,9},{11,10},{13,12},{... | collective-permute-start | bytes 98312 | tf_op jit(solution)/shard_map/ppermute | solution.py:244
  2.2 4.7 %collective-permute-start = (bf16[32,512]{0,1:T(8,128)(2,1)S(1)}, bf16[32,512]{0,1:T(8,128)(2,1)S(1)}, u32[]{:S(2)}, u32[]{:S(2)}) collective-permute-start(bf16[32,512]{0,1:T(8,128)(2,1)S(1)} %copy.63), channel_id=1, source_target_pairs={{0,1},{1,2},{2,3},{4,5},{5,6},{6,7},{8,9},{9,10},{10,11},{12,13},{... | collective-permute-start | bytes 98312 | tf_op jit(solution)/shard_map/ppermute | solution.py:244
  7.0 0.7 pad_clamp_fusion.2
  7.6 0.7 pad_clamp_fusion.1
  8.3 0.7 pad_clamp_fusion
  9.0 0.7 pad_clamp_fusion.3
  9.6 0.7 copy.85
  11.0 0.8 fusion.15
  11.8 1.5 %gather_fusion.2 = bf16[12,32,16,7]{1,2,3,0:T(8,128)(2,1)S(1)} fusion(bf16[32,16,7,7]{0,1,3,2:T(8,128)(2,1)} %param.26, s32[1024]{0:T(1024)S(1)} %pad_clamp_fusion.1), kind=kCustom, calls=%fused_computation.2 | custom fusion | bytes 172080 | tf_op jit(solution)/shard_map/jit(_take)/gather | solution.py:149
  19.1 0.9 reshape.278.w_ref
  21.0 0.7 gather_fusion
  21.7 1.2 %maximum_bitcast_fusion.1 = bf16[64,96,41]{1,2,0:T(8,128)(2,1)} fusion(bf16[96,64,1]{0,2,1:T(2,128)(2,1)S(1)} %scatter.8, bf16[96,64,20]{0,2,1:T(8,128)(2,1)S(1)} %bitcast.61, bf16[96,64,20]{0,2,1:T(8,128)(2,1)S(1)} %pad_maximum_fusion), kind=kLoop, calls=%fused_computation.9 | loop fusion | flops 1511424 | bytes 1007616 | tf_op jit(solution)/shard_map/transpose | solution.py:251
  22.9 12.9 %all-to-all-start = ((bf16[64,96,41]{1,2,0:T(8,128)(2,1)}), bf16[64,96,41]{1,2,0:T(8,128)(2,1)S(1)}, u32[]{:S(2)}, u32[]{:S(2)}) async-start(bf16[64,96,41]{1,2,0:T(8,128)(2,1)} %maximum_bitcast_fusion.1), calls=%async_computation | async-start | bytes 1572864 | tf_op jit(solution)/shard_map/all_to_all | solution.py:252
  36.0 0.8 add_convert_fusion.rest_0_
  36.8 0.7 and_convert_fusion
  37.5 21.2 %all-to-all-done = bf16[64,96,41]{1,2,0:T(8,128)(2,1)S(1)} async-done(((bf16[64,96,41]{1,2,0:T(8,128)(2,1)}), bf16[64,96,41]{1,2,0:T(8,128)(2,1)S(1)}, u32[]{:S(2)}, u32[]{:S(2)}) %all-to-all-start) | async-done | bytes 503840 | tf_op jit(solution)/shard_map/all_to_all | solution.py:252
  58.7 1.7 %copy.69.a_ref = bf16[64,96,41]{2,1,0:T(8,128)(2,1)} copy(bf16[64,96,41]{1,2,0:T(8,128)(2,1)S(1)} %all-to-all-done) | data formatting | bytes 1007616 | tf_op jit(solution)/shard_map/optimization_barrier | solution.py:268
  62.0 0.7 copy.70.w_ref
  62.8 0.7 copy.71.b_ref
  63.5 0.7 copy.72.w_ref
  64.3 2.6 %shard_map.181 = bf16[160,527]{1,0:T(8,128)(2,1)} custom-call(bf16[64,96,41]{2,1,0:T(8,128)(2,1)} %copy.69.a_ref), custom_call_target="tpu_custom_call" | custom-call | tf_op jit(solution)/shard_map/pallas_call | solution.py:135
  66.9 6.2 %shard_map.182.x_ref = bf16[2,14,64,524]{3,2,1,0:T(8,128)(2,1)} custom-call(bf16[2,80,527]{2,1,0:T(8,128)(2,1)} %bitcast.63, bf16[256,28]{1,0:T(8,128)(2,1)} %copy.70.w_ref, f32[144,1]{1,0:T(8,128)} %copy.71.b_ref, f32[2,14,4,524]{3,2,1,0:T(4,128)} %add_convert_fusion.rest_0_), custom_call_target="tpu_custom_call" | custom-call | tf_op jit(solution)/shard_map/pallas_call | solution.py:97
  73.0 4.0 %shard_map.183 = bf16[2,8,32,522]{3,2,1,0:T(8,128)(2,1)} custom-call(bf16[2,14,64,524]{3,2,1,0:T(8,128)(2,1)} %shard_map.182.x_ref, bf16[96,448]{1,0:T(8,128)(2,1)} %copy.72.w_ref, f32[144,1]{1,0:T(8,128)} %copy.71.b_ref), custom_call_target="tpu_custom_call" | custom-call | tf_op jit(solution)/shard_map/pallas_call | solution.py:97
  77.1 1.2 %slice_convert_fusion = (f32[1,8,32,522]{3,2,1,0:T(8,128)S(1)}, f32[8,32,522]{2,1,0:T(8,128)S(1)}, bf16[1,8,32,522]{3,2,1,0:T(8,128)(2,1)S(1)}) fusion(bf16[2,8,32,522]{3,2,1,0:T(8,128)(2,1)} %shard_map.183), kind=kLoop, calls=%fused_computation.18 | loop fusion | flops 133632 | bytes 1870848 | tf_op jit(solution)/shard_map/convert_element_type | solution.py:289
  78.7 3.3 %collective-permute-start.2 = (bf16[6,32,522]{2,1,0:T(8,128)(2,1)S(1)}, bf16[6,32,522]{2,1,0:T(8,128)(2,1)S(1)}, u32[]{:S(2)}, u32[]{:S(2)}) collective-permute-start(bf16[6,32,522]{2,1,0:T(8,128)(2,1)S(1)} %get-tuple-element.36), channel_id=1, source_target_pairs={{0,4},{4,8},{8,12},{12,16},{16,20},{20,24},{24,28},{28,32},{32,36}... | collective-permute-start | bytes 601352 | tf_op jit(solution)/shard_map/ppermute | solution.py:293
  82.0 2.1 %collective-permute-start.3 = (bf16[6,32,522]{2,1,0:T(8,128)(2,1)S(1)}, bf16[6,32,522]{2,1,0:T(8,128)(2,1)S(1)}, u32[]{:S(2)}, u32[]{:S(2)}) collective-permute-start(bf16[6,32,522]{2,1,0:T(8,128)(2,1)S(1)} %get-tuple-element.37), channel_id=1, source_target_pairs={{4,0},{8,4},{12,8},{16,12},{20,16},{24,20},{28,24},{32,28},{36,32}... | collective-permute-start | bytes 601352 | tf_op jit(solution)/shard_map/ppermute | solution.py:294
  84.1 0.9 copy.75.w_ref
  85.1 4.4 %collective-permute-done.3 = bf16[6,32,522]{2,1,0:T(8,128)(2,1)S(1)} collective-permute-done((bf16[6,32,522]{2,1,0:T(8,128)(2,1)S(1)}, bf16[6,32,522]{2,1,0:T(8,128)(2,1)S(1)}, u32[]{:S(2)}, u32[]{:S(2)}) %collective-permute-start.3) | collective-permute-done | bytes 200480 | tf_op jit(solution)/shard_map/ppermute | solution.py:294
  89.5 1.1 %maximum_bitcast_fusion.x_ref = bf16[1,20,32,522]{3,2,1,0:T(8,128)(2,1)} fusion(bf16[6,32,522]{2,1,0:T(8,128)(2,1)S(1)} %collective-permute-done.3, bf16[8,32,522]{2,1,0:T(8,128)(2,1)S(1)} %multiply_convert_fusion, bf16[6,32,522]{2,1,0:T(8,128)(2,1)S(1)} %collective-permute-done.2), kind=kLoop, calls=%fused_computation.8 | loop fusion | flops 668160 | bytes 1336320 | tf_op jit(solution)/shard_map/broadcast_in_dim | solution.py:300
  90.6 7.2 %shard_map.184.x_ref = bf16[1,14,128,129]{3,2,1,0:T(8,128)(2,1)} custom-call(bf16[1,20,32,522]{3,2,1,0:T(8,128)(2,1)} %maximum_bitcast_fusion.x_ref, bf16[224,224]{1,0:T(8,128)(2,1)} %reshape.278.w_ref, f32[144,1]{1,0:T(8,128)} %copy.71.b_ref, f32[1,14,1,516]{3,2,1,0:T(1,128)} %bitcast.67, bf16[128,128]{1,0:T(8,128)(2,1)} %constant.146.clone.rest_1_), custom_call_target="tpu_custom_call" | custom-call | tf_op jit(solution)/shard_map/pallas_call | solution.py:97
  97.8 2.9 %shard_map.185 = bf16[1,64,8,128]{3,2,1,0:T(8,128)(2,1)} custom-call(bf16[1,14,128,129]{3,2,1,0:T(8,128)(2,1)} %shard_map.184.x_ref, bf16[128,896]{1,0:T(8,128)(2,1)} %copy.75.w_ref, f32[144,1]{1,0:T(8,128)} %copy.71.b_ref), custom_call_target="tpu_custom_call" | custom-call | tf_op jit(solution)/shard_map/pallas_call | solution.py:97
  (53 shorter events, 5.3 us)
Async XLA Ops:
  0.0 13.7 %copy-start = (bf16[64,32,7,7]{0,1,3,2:T(8,128)(2,1)S(1)}, bf16[64,32,7,7]{0,1,3,2:T(8,128)(2,1)}, u32[]{:S(2)}) copy-start(bf16[64,32,7,7]{0,1,3,2:T(8,128)(2,1)} %param.31) | copy-start | bytes 602116
  0.0 13.3 %copy-start.9 = (pred[3,4]{0,1:T(4,128)(4,1)S(1)}, pred[3,4]{0,1:T(4,128)(4,1)}, u32[]{:S(2)}) copy-start(pred[3,4]{0,1:T(4,128)(4,1)} %constant.162) | copy-start | bytes 40
  0.9 19.7 %collective-permute-start.1 = (bf16[32,512]{0,1:T(8,128)(2,1)S(1)}, bf16[32,512]{0,1:T(8,128)(2,1)S(1)}, u32[]{:S(2)}, u32[]{:S(2)}) collective-permute-start(bf16[32,512]{0,1:T(8,128)(2,1)S(1)} %copy.63), channel_id=1, source_target_pairs={{1,0},{2,1},{3,2},{5,4},{6,5},{7,6},{9,8},{10,9},{11,10},{13,12},{... | collective-permute-start | bytes 98312 | tf_op jit(solution)/shard_map/ppermute | solution.py:244
  2.2 18.4 %collective-permute-start = (bf16[32,512]{0,1:T(8,128)(2,1)S(1)}, bf16[32,512]{0,1:T(8,128)(2,1)S(1)}, u32[]{:S(2)}, u32[]{:S(2)}) collective-permute-start(bf16[32,512]{0,1:T(8,128)(2,1)S(1)} %copy.63), channel_id=1, source_target_pairs={{0,1},{1,2},{2,3},{4,5},{5,6},{6,7},{8,9},{9,10},{10,11},{12,13},{... | collective-permute-start | bytes 98312 | tf_op jit(solution)/shard_map/ppermute | solution.py:244
  13.7 0.7 copy-start.3
  13.7 1.3 %copy-start.5 = (f32[64]{0:T(128)S(1)}, f32[64]{0:T(128)}, u32[]{:S(2)}) copy-start(f32[64]{0:T(128)} %param.32) | copy-start | bytes 772
  13.7 1.3 %copy-start.6 = (f32[32]{0:T(128)S(1)}, f32[32]{0:T(128)}, u32[]{:S(2)}) copy-start(f32[32]{0:T(128)} %param.30) | copy-start | bytes 388
  13.7 1.3 %copy-start.7 = (f32[32]{0:T(128)S(1)}, f32[32]{0:T(128)}, u32[]{:S(2)}) copy-start(f32[32]{0:T(128)} %param.27) | copy-start | bytes 388
  13.7 1.3 %copy-start.8 = (f32[16]{0:T(128)S(1)}, f32[16]{0:T(128)}, u32[]{:S(2)}) copy-start(f32[16]{0:T(128)} %param.25) | copy-start | bytes 196
  13.7 1.4 %copy-start.4 = (s32[64]{0:T(128)S(1)}, s32[64]{0:T(128)}, u32[]{:S(2)}) copy-start(s32[64]{0:T(128)} %param.22) | copy-start | bytes 772
  14.4 4.5 %copy-start.1 = (bf16[32,32,7,7]{1,0,3,2:T(8,128)(2,1)S(1)}, bf16[32,32,7,7]{1,0,3,2:T(8,128)(2,1)}, u32[]{:S(2)}) copy-start(bf16[32,32,7,7]{1,0,3,2:T(8,128)(2,1)} %param.29) | copy-start | bytes 301060
  22.9 35.8 %all-to-all-start = ((bf16[64,96,41]{1,2,0:T(8,128)(2,1)}), bf16[64,96,41]{1,2,0:T(8,128)(2,1)S(1)}, u32[]{:S(2)}, u32[]{:S(2)}) async-start(bf16[64,96,41]{1,2,0:T(8,128)(2,1)} %maximum_bitcast_fusion.1), calls=%async_computation | async-start | bytes 1572864 | tf_op jit(solution)/shard_map/all_to_all | solution.py:252
  77.1 1.3 %copy-start.2 = (bf16[7,32,32]{2,1,0:T(8,128)(2,1)S(1)}, bf16[7,32,32]{2,1,0:T(8,128)(2,1)}, u32[]{:S(2)}) copy-start(bf16[7,32,32]{2,1,0:T(8,128)(2,1)} %param.28) | copy-start | bytes 43012
  78.7 6.4 %collective-permute-start.2 = (bf16[6,32,522]{2,1,0:T(8,128)(2,1)S(1)}, bf16[6,32,522]{2,1,0:T(8,128)(2,1)S(1)}, u32[]{:S(2)}, u32[]{:S(2)}) collective-permute-start(bf16[6,32,522]{2,1,0:T(8,128)(2,1)S(1)} %get-tuple-element.36), channel_id=1, source_target_pairs={{0,4},{4,8},{8,12},{12,16},{16,20},{20,24},{24,28},{28,32},{32,36}... | collective-permute-start | bytes 601352 | tf_op jit(solution)/shard_map/ppermute | solution.py:293
  82.0 7.5 %collective-permute-start.3 = (bf16[6,32,522]{2,1,0:T(8,128)(2,1)S(1)}, bf16[6,32,522]{2,1,0:T(8,128)(2,1)S(1)}, u32[]{:S(2)}, u32[]{:S(2)}) collective-permute-start(bf16[6,32,522]{2,1,0:T(8,128)(2,1)S(1)} %get-tuple-element.37), channel_id=1, source_target_pairs={{4,0},{8,4},{12,8},{16,12},{20,16},{24,20},{28,24},{32,28},{36,32}... | collective-permute-start | bytes 601352 | tf_op jit(solution)/shard_map/ppermute | solution.py:294

commit v11 on v9

--- a/solution.py
+++ b/solution.py
@@ -125,6 +125,16 @@
     return pl.pallas_call(kernel, out_shape=jax.ShapeDtypeStruct((rows, n_out), jnp.bfloat16))(raw, left, right)
 
 
+def settled(arrays):
+    n = len(arrays)
+
+    def kernel(*refs):
+        for src_ref, dst_ref in zip(refs[:n], refs[n:]):
+            dst_ref[...] = src_ref[...]
+
+    return pl.pallas_call(kernel, out_shape=tuple(jax.ShapeDtypeStruct(a.shape, a.dtype) for a in arrays))(*arrays)
+
+
 def weights_stride1(w):
     fout, fin = w.shape[:2]
     return jnp.transpose(w, (3, 0, 2, 1)).reshape(7 * fout, 7 * fin)
@@ -251,6 +261,7 @@
         edge_mask(C_DEV, 1, length, 0, lambda p, j: (j - LEAD, quarter), me),
         edge_mask(wide - 6, 1, n_t, 3 - REACH, lambda p, j: (j - (LEAD - 3), quarter), me),
     )
+    prepared = settled(prepared)
     arrived, prepared, masks = lax.optimization_barrier((arrived, prepared, masks))
     first_weight, second_weight, third_weight, fourth_weight, biases = prepared
     second_mask, third_mask = masks

time: 81.7 us -> 81.2 us (level)
  waiting for transfers between devices: 8.15 us -> 5.41 us
  Pallas kernels: 22.5 us -> 24.5 us
    all_to_all x1, waiting for transfers between devices: 3.56 us -> 0.01 us  [on_device(): lax.all_to_all(outgoing, 'chan', split_axis=0, concat_axis=0, tiled=True)]
    optimization_barrier x5 -> x1, local copies, waits for them, and re-layouts: 3.85 us -> 0.82 us  [on_device(): lax.optimization_barrier((arrived, prepared, masks))]
    pallas_call x0 -> x1, Pallas kernels: none -> 1.95 us  [settled(): pl.pallas_call(kernel, out_shape=tuple((jax.ShapeDtypeStruct(a.shape, a.d...]
    reshape x2 -> x4, local copies, waits for them, and re-layouts: 0.46 us -> 2.06 us  [weights_stride4(): jnp.transpose(taps, (3, 0, 2, 4, 1)).reshape(shifts * fout, 7 * PH * fin)]
    ppermute x1, waiting for transfers between devices: 0.18 us -> 1.01 us  [on_device(): above = lax.ppermute(second[C_DEV - REACH:], 'chan', ring_up)]
  transfers between devices with their start and end apart: 5 -> 5, of which waited for: 3 -> 2; matrix products, arithmetic and copies ran while one was open for 13% -> 13% of each run, Pallas kernels for 0% -> 2%
where the time goes in v11:
time: 81.2 us; the launch traced here: 80.2 us
  Pallas kernels  24.5 us (30%)
  starting transfers between devices  24.4 us (30%)
  local copies, waits for them, and re-layouts  13.4 us (17%)
  other arithmetic  7.35 us (9%)
  waiting for transfers between devices  5.41 us (7%)
  between operations  4.85 us (6%)
    pallas_call x4, Pallas kernels, banded(): pl.pallas_call(kernel, grid=(windows,), in_specs=specs, out_specs=pl.Bloc...  20.3 us
    all_to_all x1, starting transfers between devices, on_device(): lax.all_to_all(outgoing, 'chan', split_axis=0, concat_axis=0, tiled=True)  13 us
    ppermute x1, waiting for transfers between devices, on_device(): below = lax.ppermute(second[:REACH], 'chan', ring_down)  4.4 us
    ppermute x1, starting transfers between devices, on_device(): above = lax.ppermute(second[C_DEV - REACH:], 'chan', ring_up)  4.08 us
    ppermute x1, starting transfers between devices, on_device(): before = lax.ppermute(arrived[blocks - 1], 'tm', up)  3.99 us
    pallas_call x1, Pallas kernels, strain_layout(): pl.pallas_call(kernel, out_shape=jax.ShapeDtypeStruct((rows, n_out), jnp....  2.24 us
    unnamed x40, local copies, waits for them, and re-layouts  2.15 us
    ppermute x1, starting transfers between devices, on_device(): below = lax.ppermute(second[:REACH], 'chan', ring_down)  2.1 us
  transfers between devices with their start and end apart: 5, of which 2 were waited for; matrix products, arithmetic and copies ran while one was open for 13% of the time, Pallas kernels for 2%

profile of v11, /device:TPU:1, one launch (start us, length us, event | category | flops | bytes accessed | tf_op | source)
XLA Modules:
  0.0 80.2 jit_solution(10300563509192364526)
XLA Ops:
  0.7 0.7 pad_clamp_fusion.3
  1.4 1.0 %pad_slice_fusion.2 = (bf16[32,512]{1,0:T(8,128)(2,1)S(1)}, bf16[32,512]{1,0:T(8,128)(2,1)S(1)}, bf16[32,512]{1,0:T(8,128)(2,1)S(1)}) fusion(bf16[32,512]{1,0:T(8,128)(2,1)} %param.21), kind=kLoop, calls=%fused_computation.32 | loop fusion | bytes 131072 | tf_op jit(solution)/shard_map/slice | solution.py:243
  4.2 0.7 gather_fusion
  5.5 1.5 %reshape.318 = bf16[64,2,656]{2,1,0:T(2,128)(2,1)} reshape(bf16[64,32,41]{2,1,0:T(8,128)(2,1)S(1)} %maximum_bitcast_fusion.1) | data formatting | bytes 335872
  7.0 13.0 %all-to-all-start = ((bf16[64,2,656]{2,1,0:T(2,128)(2,1)}), bf16[64,2,656]{2,1,0:T(2,128)(2,1)S(1)}, u32[]{:S(2)}, u32[]{:S(2)}) async-start(bf16[64,2,656]{2,1,0:T(2,128)(2,1)} %reshape.318), calls=%async_computation | async-start | bytes 393216 | tf_op jit(solution)/shard_map/all_to_all | solution.py:248
  20.1 0.6 dynamic_slice.11
  21.5 0.8 copy.69.refs_4_
  22.2 0.6 gather_fusion.1
  23.1 0.7 copy.66.refs_0_
  23.9 0.6 gather_fusion.2
  25.0 0.8 copy.67.refs_1_
  25.8 0.6 gather_fusion.3
  27.3 0.8 %copy.68.refs_3_ = bf16[128,896]{1,0:T(8,128)(2,1)} copy(bf16[128,896]{0,1:T(8,128)(2,1)S(1)} %reshape.282) | data formatting | bytes 458752 | tf_op jit(solution)/shard_map/reshape | solution.py:151
  28.3 0.9 %reshape.281.refs_2_ = bf16[224,224]{1,0:T(8,128)(2,1)} reshape(bf16[7,32,7,32]{3,2,1,0:T(8,128)(2,1)S(1)} %copy.64) | data formatting | bytes 200704 | tf_op jit(solution)/shard_map/reshape | solution.py:140
  29.3 0.7 and_convert_fusion
  30.0 2.0 %shard_map.181 = (bf16[256,28]{1,0:T(8,128)(2,1)}, bf16[96,448]{1,0:T(8,128)(2,1)}, bf16[224,224]{1,0:T(8,128)(2,1)}, bf16[128,896]{1,0:T(8,128)(2,1)}, f32[144,1]{1,0:T(8,128)}) custom-call(bf16[256,28]{1,0:T(8,128)(2,1)} %copy.66.refs_0_, bf16[96,448]{1,0:T(8,128)(2,1)} %copy.67.refs_1_, bf16[224,224]{1,0:T(8,128)(2,1)} %reshape.281.refs_2_, ...), custom_call_target="tpu_custom_call" | custom-call | tf_op jit(solution)/shard_map/pallas_call | solution.py:135
  32.2 0.8 %reshape.319 = bf16[64,32,41]{2,1,0:T(8,128)(2,1)S(1)} reshape(bf16[64,2,656]{2,1,0:T(2,128)(2,1)S(1)} %all-to-all-done) | data formatting | bytes 335872 | tf_op jit(solution)/shard_map/optimization_barrier | solution.py:265
  33.0 1.3 %collective-permute-start.1 = (bf16[32,41]{1,0:T(8,128)(2,1)S(1)}, bf16[32,41]{1,0:T(8,128)(2,1)S(1)}, u32[]{:S(2)}, u32[]{:S(2)}) collective-permute-start(bf16[32,41]{1,0:T(8,128)(2,1)S(1)} %get-tuple-element.46), channel_id=1, source_target_pairs={{1,0},{2,1},{3,2},{5,4},{6,5},{7,6},{9,8},{10,9},{11,10},{13,12},{... | collective-permute-start | bytes 7880 | tf_op jit(solution)/shard_map/ppermute | solution.py:274
  34.3 4.0 %collective-permute-start = (bf16[32,41]{1,0:T(8,128)(2,1)S(1)}, bf16[32,41]{1,0:T(8,128)(2,1)S(1)}, u32[]{:S(2)}, u32[]{:S(2)}) collective-permute-start(bf16[32,41]{1,0:T(8,128)(2,1)S(1)} %get-tuple-element.47), channel_id=1, source_target_pairs={{0,1},{1,2},{2,3},{4,5},{5,6},{6,7},{8,9},{9,10},{10,11},{12,13},{... | collective-permute-start | bytes 7880 | tf_op jit(solution)/shard_map/ppermute | solution.py:273
  38.3 0.8 %add_convert_fusion.rest_0_ = f32[2,14,4,524]{3,2,1,0:T(4,128)} fusion(pred[1,14,4,524]{3,2,1,0:T(4,128)(4,1)S(1)} %get-tuple-element.54, pred[1,14,4,524]{3,2,1,0:T(4,128)(4,1)S(1)} %get-tuple-element.53), kind=kLoop, calls=%fused_computation.18 | loop fusion | flops 117376 | bytes 293440 | tf_op jit(solution)/shard_map/stack | solution.py:192
  42.8 0.6 copy-done.6
  43.4 2.2 %shard_map.182 = bf16[160,527]{1,0:T(8,128)(2,1)} custom-call(bf16[2048,41]{1,0:T(8,128)(2,1)} %bitcast.64, bf16[32,41]{1,0:T(8,128)(2,1)} %copy-done.7, bf16[32,41]{1,0:T(8,128)(2,1)} %copy-done.6), custom_call_target="tpu_custom_call" | custom-call | tf_op jit(solution)/shard_map/pallas_call | solution.py:125
  45.6 6.2 %shard_map.183.x_ref = bf16[2,14,64,524]{3,2,1,0:T(8,128)(2,1)} custom-call(bf16[2,80,527]{2,1,0:T(8,128)(2,1)} %bitcast.66, bf16[256,28]{1,0:T(8,128)(2,1)} %get-tuple-element.36.w_ref, f32[144,1]{1,0:T(8,128)} %get-tuple-element.37.b_ref, f32[2,14,4,524]{3,2,1,0:T(4,128)} %add_convert_fusion.rest_0_), custom_call_target="tpu_custom_call" | custom-call | tf_op jit(solution)/shard_map/pallas_call | solution.py:97
  51.8 4.0 %shard_map.184 = bf16[2,8,32,522]{3,2,1,0:T(8,128)(2,1)} custom-call(bf16[2,14,64,524]{3,2,1,0:T(8,128)(2,1)} %shard_map.183.x_ref, bf16[96,448]{1,0:T(8,128)(2,1)} %get-tuple-element.38.w_ref, f32[144,1]{1,0:T(8,128)} %get-tuple-element.37.b_ref), custom_call_target="tpu_custom_call" | custom-call | tf_op jit(solution)/shard_map/pallas_call | solution.py:97
  55.8 1.2 %slice_convert_fusion = (f32[1,8,32,522]{3,2,1,0:T(8,128)S(1)}, f32[8,32,522]{2,1,0:T(8,128)S(1)}, bf16[1,8,32,522]{3,2,1,0:T(8,128)(2,1)S(1)}) fusion(bf16[2,8,32,522]{3,2,1,0:T(8,128)(2,1)} %shard_map.184), kind=kLoop, calls=%fused_computation.16 | loop fusion | flops 133632 | bytes 1870848 | tf_op jit(solution)/shard_map/convert_element_type | solution.py:291
  57.5 4.1 %collective-permute-start.2 = (bf16[6,32,522]{2,1,0:T(8,128)(2,1)S(1)}, bf16[6,32,522]{2,1,0:T(8,128)(2,1)S(1)}, u32[]{:S(2)}, u32[]{:S(2)}) collective-permute-start(bf16[6,32,522]{2,1,0:T(8,128)(2,1)S(1)} %get-tuple-element.48), channel_id=1, source_target_pairs={{0,4},{4,8},{8,12},{12,16},{16,20},{20,24},{24,28},{28,32},{32,36}... | collective-permute-start | bytes 601352 | tf_op jit(solution)/shard_map/ppermute | solution.py:295
  61.6 2.1 %collective-permute-start.3 = (bf16[6,32,522]{2,1,0:T(8,128)(2,1)S(1)}, bf16[6,32,522]{2,1,0:T(8,128)(2,1)S(1)}, u32[]{:S(2)}, u32[]{:S(2)}) collective-permute-start(bf16[6,32,522]{2,1,0:T(8,128)(2,1)S(1)} %get-tuple-element.49), channel_id=1, source_target_pairs={{4,0},{8,4},{12,8},{16,12},{20,16},{24,20},{28,24},{32,28},{36,32}... | collective-permute-start | bytes 601352 | tf_op jit(solution)/shard_map/ppermute | solution.py:296
  63.7 1.0 %collective-permute-done.2 = bf16[6,32,522]{2,1,0:T(8,128)(2,1)S(1)} collective-permute-done((bf16[6,32,522]{2,1,0:T(8,128)(2,1)S(1)}, bf16[6,32,522]{2,1,0:T(8,128)(2,1)S(1)}, u32[]{:S(2)}, u32[]{:S(2)}) %collective-permute-start.2) | collective-permute-done | bytes 200480 | tf_op jit(solution)/shard_map/ppermute | solution.py:295
  64.7 4.4 %collective-permute-done.3 = bf16[6,32,522]{2,1,0:T(8,128)(2,1)S(1)} collective-permute-done((bf16[6,32,522]{2,1,0:T(8,128)(2,1)S(1)}, bf16[6,32,522]{2,1,0:T(8,128)(2,1)S(1)}, u32[]{:S(2)}, u32[]{:S(2)}) %collective-permute-start.3) | collective-permute-done | bytes 200480 | tf_op jit(solution)/shard_map/ppermute | solution.py:296
  69.1 1.0 %maximum_bitcast_fusion.x_ref = bf16[1,20,32,522]{3,2,1,0:T(8,128)(2,1)} fusion(bf16[6,32,522]{2,1,0:T(8,128)(2,1)S(1)} %collective-permute-done.3, bf16[8,32,522]{2,1,0:T(8,128)(2,1)S(1)} %multiply_convert_fusion, bf16[6,32,522]{2,1,0:T(8,128)(2,1)S(1)} %collective-permute-done.2), kind=kLoop, calls=%fused_computation.8 | loop fusion | flops 668160 | bytes 1336320 | tf_op jit(solution)/shard_map/broadcast_in_dim | solution.py:302
  70.1 7.2 %shard_map.185.x_ref = bf16[1,14,128,129]{3,2,1,0:T(8,128)(2,1)} custom-call(bf16[1,20,32,522]{3,2,1,0:T(8,128)(2,1)} %maximum_bitcast_fusion.x_ref, bf16[224,224]{1,0:T(8,128)(2,1)} %get-tuple-element.40.w_ref, f32[144,1]{1,0:T(8,128)} %get-tuple-element.37.b_ref, f32[1,14,1,516]{3,2,1,0:T(1,128)} %bitcast.73, bf16[128,128]{1,0:T(8,128)(2,1)} %constant.146.clone.rest_1_), custom_call_target="tpu_custom_call" | custom-call | tf_op jit(solution)/shard_map/pallas_call | solution.py:97
  77.3 2.9 %shard_map.186 = bf16[1,64,8,128]{3,2,1,0:T(8,128)(2,1)} custom-call(bf16[1,14,128,129]{3,2,1,0:T(8,128)(2,1)} %shard_map.185.x_ref, bf16[128,896]{1,0:T(8,128)(2,1)} %get-tuple-element.42.w_ref, f32[144,1]{1,0:T(8,128)} %get-tuple-element.37.b_ref), custom_call_target="tpu_custom_call" | custom-call | tf_op jit(solution)/shard_map/pallas_call | solution.py:97
  (78 shorter events, 5.7 us)
Async XLA Ops:
  0.0 25.8 %copy-start = (bf16[64,32,7,7]{0,1,3,2:T(8,128)(2,1)S(1)}, bf16[64,32,7,7]{0,1,3,2:T(8,128)(2,1)}, u32[]{:S(2)}) copy-start(bf16[64,32,7,7]{0,1,3,2:T(8,128)(2,1)} %param.31) | copy-start | bytes 602116
  4.1 16.0 %copy-start.10 = (s32[64]{0:T(128)S(1)}, s32[64]{0:T(128)}, u32[]{:S(2)}) copy-start(s32[64]{0:T(128)} %param.22) | copy-start | bytes 772
  4.1 17.1 %copy-start.13 = (s32[64]{0:T(128)S(1)}, s32[64]{0:T(128)}, u32[]{:S(2)}) copy-start(s32[64]{0:T(128)} %constant.183) | copy-start | bytes 772
  4.1 17.1 %copy-start.12 = (s32[12]{0:T(128)S(1)}, s32[12]{0:T(128)}, u32[]{:S(2)}) copy-start(s32[12]{0:T(128)} %constant.184) | copy-start | bytes 148
  4.1 17.2 %copy-start.11 = (s32[8]{0:T(128)S(1)}, s32[8]{0:T(128)}, u32[]{:S(2)}) copy-start(s32[8]{0:T(128)} %constant.185) | copy-start | bytes 100
  4.1 17.2 %copy-start.5 = (bf16[16,1,7,7]{0,3,2,1:T(8,128)(2,1)S(1)}, bf16[16,1,7,7]{0,3,2,1:T(8,128)(2,1)}, u32[]{:S(2)}) copy-start(bf16[16,1,7,7]{0,3,2,1:T(8,128)(2,1)} %param.24) | copy-start | bytes 4708
  4.2 17.2 %copy-start.14 = (f32[64]{0:T(128)S(1)}, f32[64]{0:T(128)}, u32[]{:S(2)}) copy-start(f32[64]{0:T(128)} %param.32) | copy-start | bytes 772
  4.2 17.2 %copy-start.15 = (f32[32]{0:T(128)S(1)}, f32[32]{0:T(128)}, u32[]{:S(2)}) copy-start(f32[32]{0:T(128)} %param.30) | copy-start | bytes 388
  4.2 17.2 %copy-start.16 = (f32[32]{0:T(128)S(1)}, f32[32]{0:T(128)}, u32[]{:S(2)}) copy-start(f32[32]{0:T(128)} %param.27) | copy-start | bytes 388
  4.2 17.2 %copy-start.17 = (f32[16]{0:T(128)S(1)}, f32[16]{0:T(128)}, u32[]{:S(2)}) copy-start(f32[16]{0:T(128)} %param.25) | copy-start | bytes 196
  4.2 18.6 %copy-start.8 = (pred[4,4,4]{1,0,2:T(4,128)(4,1)S(1)}, pred[4,4,4]{1,0,2:T(4,128)(4,1)}, u32[]{:S(2)}) copy-start(pred[4,4,4]{1,0,2:T(4,128)(4,1)} %constant.153) | copy-start | bytes 196
  4.9 19.0 %copy-start.1 = (bf16[32,16,7,7]{0,1,3,2:T(8,128)(2,1)S(1)}, bf16[32,16,7,7]{0,1,3,2:T(8,128)(2,1)}, u32[]{:S(2)}) copy-start(bf16[32,16,7,7]{0,1,3,2:T(8,128)(2,1)} %param.26) | copy-start | bytes 150532
  5.5 18.9 %copy-start.18 = (pred[3,4]{0,1:T(4,128)(4,1)S(1)}, pred[3,4]{0,1:T(4,128)(4,1)}, u32[]{:S(2)}) copy-start(pred[3,4]{0,1:T(4,128)(4,1)} %constant.162) | copy-start | bytes 40
  7.0 25.1 %all-to-all-start = ((bf16[64,2,656]{2,1,0:T(2,128)(2,1)}), bf16[64,2,656]{2,1,0:T(2,128)(2,1)S(1)}, u32[]{:S(2)}, u32[]{:S(2)}) async-start(bf16[64,2,656]{2,1,0:T(2,128)(2,1)} %reshape.318), calls=%async_computation | async-start | bytes 393216 | tf_op jit(solution)/shard_map/all_to_all | solution.py:248
  25.8 0.7 copy-start.9
  26.5 1.7 %copy-start.3 = (bf16[32,32,7,7]{1,0,3,2:T(8,128)(2,1)S(1)}, bf16[32,32,7,7]{1,0,3,2:T(8,128)(2,1)}, u32[]{:S(2)}) copy-start(bf16[32,32,7,7]{1,0,3,2:T(8,128)(2,1)} %param.29) | copy-start | bytes 301060
  33.0 9.8 %copy-start.2 = (bf16[64,32,41]{2,1,0:T(8,128)(2,1)}, bf16[64,32,41]{2,1,0:T(8,128)(2,1)S(1)}, u32[]{:S(2)}) copy-start(bf16[64,32,41]{2,1,0:T(8,128)(2,1)S(1)} %reshape.319) | copy-start | bytes 503812
  33.0 9.7 %collective-permute-start.1 = (bf16[32,41]{1,0:T(8,128)(2,1)S(1)}, bf16[32,41]{1,0:T(8,128)(2,1)S(1)}, u32[]{:S(2)}, u32[]{:S(2)}) collective-permute-start(bf16[32,41]{1,0:T(8,128)(2,1)S(1)} %get-tuple-element.46), channel_id=1, source_target_pairs={{1,0},{2,1},{3,2},{5,4},{6,5},{7,6},{9,8},{10,9},{11,10},{13,12},{... | collective-permute-start | bytes 7880 | tf_op jit(solution)/shard_map/ppermute | solution.py:274
  34.3 8.4 %collective-permute-start = (bf16[32,41]{1,0:T(8,128)(2,1)S(1)}, bf16[32,41]{1,0:T(8,128)(2,1)S(1)}, u32[]{:S(2)}, u32[]{:S(2)}) collective-permute-start(bf16[32,41]{1,0:T(8,128)(2,1)S(1)} %get-tuple-element.47), channel_id=1, source_target_pairs={{0,1},{1,2},{2,3},{4,5},{5,6},{6,7},{8,9},{9,10},{10,11},{12,13},{... | collective-permute-start | bytes 7880 | tf_op jit(solution)/shard_map/ppermute | solution.py:273
  42.7 0.6 copy-start.6
  42.8 0.6 copy-start.7
  55.8 1.3 %copy-start.4 = (bf16[7,32,32]{2,1,0:T(8,128)(2,1)S(1)}, bf16[7,32,32]{2,1,0:T(8,128)(2,1)}, u32[]{:S(2)}) copy-start(bf16[7,32,32]{2,1,0:T(8,128)(2,1)} %param.28) | copy-start | bytes 43012
  57.5 7.2 %collective-permute-start.2 = (bf16[6,32,522]{2,1,0:T(8,128)(2,1)S(1)}, bf16[6,32,522]{2,1,0:T(8,128)(2,1)S(1)}, u32[]{:S(2)}, u32[]{:S(2)}) collective-permute-start(bf16[6,32,522]{2,1,0:T(8,128)(2,1)S(1)} %get-tuple-element.48), channel_id=1, source_target_pairs={{0,4},{4,8},{8,12},{12,16},{16,20},{20,24},{24,28},{28,32},{32,36}... | collective-permute-start | bytes 601352 | tf_op jit(solution)/shard_map/ppermute | solution.py:295
  61.6 7.5 %collective-permute-start.3 = (bf16[6,32,522]{2,1,0:T(8,128)(2,1)S(1)}, bf16[6,32,522]{2,1,0:T(8,128)(2,1)S(1)}, u32[]{:S(2)}, u32[]{:S(2)}) collective-permute-start(bf16[6,32,522]{2,1,0:T(8,128)(2,1)S(1)} %get-tuple-element.49), channel_id=1, source_target_pairs={{4,0},{8,4},{12,8},{16,12},{20,16},{24,20},{28,24},{32,28},{36,32}... | collective-permute-start | bytes 601352 | tf_op jit(solution)/shard_map/ppermute | solution.py:296

commit v12 on v11

--- a/solution.py
+++ b/solution.py
@@ -185,16 +185,10 @@
     return ok.astype(jnp.float32)
 
 
-def lower_layers(strain_wide, blocks_of, first_weight, biases, second_weight, times, length):
+def lower_layers(strain_wide, first_mask, first_weight, biases, second_weight, length):
     wide = C_DEV + 2 * REACH
     n_win, n_s = strain_wide.shape[0], strain_wide.shape[-1]
     n_f = n_s - 3
-    first_mask = jnp.stack(
-        [
-            edge_mask(wide - 6, PH, n_f, 3 - REACH, lambda p, v: (PH * (v - (WL - 1)) + p, times), b)
-            for b in blocks_of
-        ]
-    )
     first = banded(
         strain_wide.reshape(n_win, wide * PH, n_s),
         first_weight,
@@ -257,14 +251,17 @@
     quarter = blocks * times_here // 4
     length = quarter + 2 * LEAD
     n_t = length - 6
+    n_f = WL + blocks * times_here // PH + WR - 3
+    first_time = lambda p, v: (PH * (v - (WL - 1)) + p, blocks * times_here)
     masks = (
+        jnp.stack([edge_mask(wide - 6, PH, n_f, 3 - REACH, first_time, b) for b in (me, mate)]),
         edge_mask(C_DEV, 1, length, 0, lambda p, j: (j - LEAD, quarter), me),
         edge_mask(wide - 6, 1, n_t, 3 - REACH, lambda p, j: (j - (LEAD - 3), quarter), me),
     )
     prepared = settled(prepared)
     arrived, prepared, masks = lax.optimization_barrier((arrived, prepared, masks))
     first_weight, second_weight, third_weight, fourth_weight, biases = prepared
-    second_mask, third_mask = masks
+    first_mask, second_mask, third_mask = masks
     mate_offset = arrived[:, 0, 2 * wide].astype(jnp.int32)[mate]
     times = blocks * times_here
     tms = lax.axis_size("tm")
@@ -277,7 +274,7 @@
     quarter = times // 4
     length = quarter + 2 * LEAD
     lower = lower_layers(
-        strain_wide.reshape(2, wide, PH, -1), (me, mate), first_weight, biases, second_weight, times, length
+        strain_wide.reshape(2, wide, PH, -1), first_mask, first_weight, biases, second_weight, length
     )
     pre_second, mate_second = lower[0], lower[1]
 

time: 81.2 us -> 81.4 us (level)
  no operation moved by 1% of the time
where the time goes in v12:
time: 81.4 us; the launch traced here: 80.4 us
  Pallas kernels  24.5 us (30%)
  starting transfers between devices  24.4 us (30%)
  local copies, waits for them, and re-layouts  13.5 us (17%)
  other arithmetic  7.32 us (9%)
  waiting for transfers between devices  5.41 us (7%)
  between operations  4.93 us (6%)
    pallas_call x4, Pallas kernels, banded(): pl.pallas_call(kernel, grid=(windows,), in_specs=specs, out_specs=pl.Bloc...  20.4 us
    all_to_all x1, starting transfers between devices, on_device(): lax.all_to_all(outgoing, 'chan', split_axis=0, concat_axis=0, tiled=True)  13 us
    ppermute x1, waiting for transfers between devices, on_device(): below = lax.ppermute(second[:REACH], 'chan', ring_down)  4.4 us
    ppermute x1, starting transfers between devices, on_device(): above = lax.ppermute(second[C_DEV - REACH:], 'chan', ring_up)  4.09 us
    ppermute x1, starting transfers between devices, on_device(): before = lax.ppermute(arrived[blocks - 1], 'tm', up)  3.99 us
    pallas_call x1, Pallas kernels, strain_layout(): pl.pallas_call(kernel, out_shape=jax.ShapeDtypeStruct((rows, n_out), jnp....  2.24 us
    unnamed x40, local copies, waits for them, and re-layouts  2.15 us
    ppermute x1, starting transfers between devices, on_device(): below = lax.ppermute(second[:REACH], 'chan', ring_down)  2.1 us
  transfers between devices with their start and end apart: 5, of which 2 were waited for; matrix products, arithmetic and copies ran while one was open for 13% of the time, Pallas kernels for 2%

profile of v12, /device:TPU:1, one launch (start us, length us, event | category | flops | bytes accessed | tf_op | source)
XLA Modules:
  0.0 80.4 jit_solution(18163302902100509961)
XLA Ops:
  0.7 0.7 pad_clamp_fusion.3
  1.4 1.0 %pad_slice_fusion.2 = (bf16[32,512]{1,0:T(8,128)(2,1)S(1)}, bf16[32,512]{1,0:T(8,128)(2,1)S(1)}, bf16[32,512]{1,0:T(8,128)(2,1)S(1)}) fusion(bf16[32,512]{1,0:T(8,128)(2,1)} %param.21), kind=kLoop, calls=%fused_computation.32 | loop fusion | bytes 131072 | tf_op jit(solution)/shard_map/slice | solution.py:237
  4.2 0.7 gather_fusion
  5.5 1.5 %reshape.318 = bf16[64,2,656]{2,1,0:T(2,128)(2,1)} reshape(bf16[64,32,41]{2,1,0:T(8,128)(2,1)S(1)} %maximum_bitcast_fusion.1) | data formatting | bytes 335872
  7.0 13.0 %all-to-all-start = ((bf16[64,2,656]{2,1,0:T(2,128)(2,1)}), bf16[64,2,656]{2,1,0:T(2,128)(2,1)S(1)}, u32[]{:S(2)}, u32[]{:S(2)}) async-start(bf16[64,2,656]{2,1,0:T(2,128)(2,1)} %reshape.318), calls=%async_computation | async-start | bytes 393216 | tf_op jit(solution)/shard_map/all_to_all | solution.py:242
  20.1 0.7 dynamic_slice.11
  21.6 0.7 copy.69.refs_4_
  22.3 0.6 gather_fusion.1
  23.2 0.7 copy.66.refs_0_
  24.0 0.6 gather_fusion.2
  25.2 0.7 copy.67.refs_1_
  25.9 0.6 gather_fusion.3
  27.4 0.9 %copy.68.refs_3_ = bf16[128,896]{1,0:T(8,128)(2,1)} copy(bf16[128,896]{0,1:T(8,128)(2,1)S(1)} %reshape.282) | data formatting | bytes 458752 | tf_op jit(solution)/shard_map/reshape | solution.py:151
  28.4 0.9 %reshape.281.refs_2_ = bf16[224,224]{1,0:T(8,128)(2,1)} reshape(bf16[7,32,7,32]{3,2,1,0:T(8,128)(2,1)S(1)} %copy.64) | data formatting | bytes 200704 | tf_op jit(solution)/shard_map/reshape | solution.py:140
  29.5 0.8 %add_convert_fusion.rest_0_ = f32[2,14,4,524]{3,2,1,0:T(4,128)} fusion(pred[1,14,4,524]{3,2,1,0:T(4,128)(4,1)S(1)} %get-tuple-element.56, pred[1,14,4,524]{3,2,1,0:T(4,128)(4,1)S(1)} %get-tuple-element.55), kind=kLoop, calls=%fused_computation.18 | loop fusion | flops 117376 | bytes 293440 | tf_op jit(solution)/shard_map/stack | solution.py:257
  30.4 2.0 %shard_map.181 = (bf16[256,28]{1,0:T(8,128)(2,1)}, bf16[96,448]{1,0:T(8,128)(2,1)}, bf16[224,224]{1,0:T(8,128)(2,1)}, bf16[128,896]{1,0:T(8,128)(2,1)}, f32[144,1]{1,0:T(8,128)}) custom-call(bf16[256,28]{1,0:T(8,128)(2,1)} %copy.66.refs_0_, bf16[96,448]{1,0:T(8,128)(2,1)} %copy.67.refs_1_, bf16[224,224]{1,0:T(8,128)(2,1)} %reshape.281.refs_2_, ...), custom_call_target="tpu_custom_call" | custom-call | tf_op jit(solution)/shard_map/pallas_call | solution.py:135
  32.4 0.7 and_convert_fusion
  33.1 0.8 %reshape.319 = bf16[64,32,41]{2,1,0:T(8,128)(2,1)S(1)} reshape(bf16[64,2,656]{2,1,0:T(2,128)(2,1)S(1)} %all-to-all-done) | data formatting | bytes 335872 | tf_op jit(solution)/shard_map/optimization_barrier | solution.py:262
  34.0 1.3 %collective-permute-start.1 = (bf16[32,41]{1,0:T(8,128)(2,1)S(1)}, bf16[32,41]{1,0:T(8,128)(2,1)S(1)}, u32[]{:S(2)}, u32[]{:S(2)}) collective-permute-start(bf16[32,41]{1,0:T(8,128)(2,1)S(1)} %get-tuple-element.48), channel_id=1, source_target_pairs={{1,0},{2,1},{3,2},{5,4},{6,5},{7,6},{9,8},{10,9},{11,10},{13,12},{... | collective-permute-start | bytes 7880 | tf_op jit(solution)/shard_map/ppermute | solution.py:271
  35.3 4.0 %collective-permute-start = (bf16[32,41]{1,0:T(8,128)(2,1)S(1)}, bf16[32,41]{1,0:T(8,128)(2,1)S(1)}, u32[]{:S(2)}, u32[]{:S(2)}) collective-permute-start(bf16[32,41]{1,0:T(8,128)(2,1)S(1)} %get-tuple-element.49), channel_id=1, source_target_pairs={{0,1},{1,2},{2,3},{4,5},{5,6},{6,7},{8,9},{9,10},{10,11},{12,13},{... | collective-permute-start | bytes 7880 | tf_op jit(solution)/shard_map/ppermute | solution.py:270
  42.9 0.6 copy-done.6
  43.5 2.2 %shard_map.182 = bf16[160,527]{1,0:T(8,128)(2,1)} custom-call(bf16[2048,41]{1,0:T(8,128)(2,1)} %bitcast.64, bf16[32,41]{1,0:T(8,128)(2,1)} %copy-done.7, bf16[32,41]{1,0:T(8,128)(2,1)} %copy-done.6), custom_call_target="tpu_custom_call" | custom-call | tf_op jit(solution)/shard_map/pallas_call | solution.py:125
  45.7 6.2 %shard_map.183.x_ref = bf16[2,14,64,524]{3,2,1,0:T(8,128)(2,1)} custom-call(bf16[2,80,527]{2,1,0:T(8,128)(2,1)} %bitcast.66, bf16[256,28]{1,0:T(8,128)(2,1)} %get-tuple-element.37.w_ref, f32[144,1]{1,0:T(8,128)} %get-tuple-element.38.b_ref, f32[2,14,4,524]{3,2,1,0:T(4,128)} %add_convert_fusion.rest_0_), custom_call_target="tpu_custom_call" | custom-call | tf_op jit(solution)/shard_map/pallas_call | solution.py:97
  51.9 4.0 %shard_map.184 = bf16[2,8,32,522]{3,2,1,0:T(8,128)(2,1)} custom-call(bf16[2,14,64,524]{3,2,1,0:T(8,128)(2,1)} %shard_map.183.x_ref, bf16[96,448]{1,0:T(8,128)(2,1)} %get-tuple-element.40.w_ref, f32[144,1]{1,0:T(8,128)} %get-tuple-element.38.b_ref), custom_call_target="tpu_custom_call" | custom-call | tf_op jit(solution)/shard_map/pallas_call | solution.py:97
  55.9 1.2 %slice_convert_fusion = (f32[1,8,32,522]{3,2,1,0:T(8,128)S(1)}, f32[8,32,522]{2,1,0:T(8,128)S(1)}, bf16[1,8,32,522]{3,2,1,0:T(8,128)(2,1)S(1)}) fusion(bf16[2,8,32,522]{3,2,1,0:T(8,128)(2,1)} %shard_map.184), kind=kLoop, calls=%fused_computation.16 | loop fusion | flops 133632 | bytes 1870848 | tf_op jit(solution)/shard_map/convert_element_type | solution.py:288
  57.6 4.1 %collective-permute-start.2 = (bf16[6,32,522]{2,1,0:T(8,128)(2,1)S(1)}, bf16[6,32,522]{2,1,0:T(8,128)(2,1)S(1)}, u32[]{:S(2)}, u32[]{:S(2)}) collective-permute-start(bf16[6,32,522]{2,1,0:T(8,128)(2,1)S(1)} %get-tuple-element.50), channel_id=1, source_target_pairs={{0,4},{4,8},{8,12},{12,16},{16,20},{20,24},{24,28},{28,32},{32,36}... | collective-permute-start | bytes 601352 | tf_op jit(solution)/shard_map/ppermute | solution.py:292
  61.7 2.1 %collective-permute-start.3 = (bf16[6,32,522]{2,1,0:T(8,128)(2,1)S(1)}, bf16[6,32,522]{2,1,0:T(8,128)(2,1)S(1)}, u32[]{:S(2)}, u32[]{:S(2)}) collective-permute-start(bf16[6,32,522]{2,1,0:T(8,128)(2,1)S(1)} %get-tuple-element.51), channel_id=1, source_target_pairs={{4,0},{8,4},{12,8},{16,12},{20,16},{24,20},{28,24},{32,28},{36,32}... | collective-permute-start | bytes 601352 | tf_op jit(solution)/shard_map/ppermute | solution.py:293
  63.8 1.0 %collective-permute-done.2 = bf16[6,32,522]{2,1,0:T(8,128)(2,1)S(1)} collective-permute-done((bf16[6,32,522]{2,1,0:T(8,128)(2,1)S(1)}, bf16[6,32,522]{2,1,0:T(8,128)(2,1)S(1)}, u32[]{:S(2)}, u32[]{:S(2)}) %collective-permute-start.2) | collective-permute-done | bytes 200480 | tf_op jit(solution)/shard_map/ppermute | solution.py:292
  64.8 4.4 %collective-permute-done.3 = bf16[6,32,522]{2,1,0:T(8,128)(2,1)S(1)} collective-permute-done((bf16[6,32,522]{2,1,0:T(8,128)(2,1)S(1)}, bf16[6,32,522]{2,1,0:T(8,128)(2,1)S(1)}, u32[]{:S(2)}, u32[]{:S(2)}) %collective-permute-start.3) | collective-permute-done | bytes 200480 | tf_op jit(solution)/shard_map/ppermute | solution.py:293
  69.2 1.0 %maximum_bitcast_fusion.x_ref = bf16[1,20,32,522]{3,2,1,0:T(8,128)(2,1)} fusion(bf16[6,32,522]{2,1,0:T(8,128)(2,1)S(1)} %collective-permute-done.3, bf16[8,32,522]{2,1,0:T(8,128)(2,1)S(1)} %multiply_convert_fusion, bf16[6,32,522]{2,1,0:T(8,128)(2,1)S(1)} %collective-permute-done.2), kind=kLoop, calls=%fused_computation.8 | loop fusion | flops 668160 | bytes 1336320 | tf_op jit(solution)/shard_map/broadcast_in_dim | solution.py:299
  70.2 7.2 %shard_map.185.x_ref = bf16[1,14,128,129]{3,2,1,0:T(8,128)(2,1)} custom-call(bf16[1,20,32,522]{3,2,1,0:T(8,128)(2,1)} %maximum_bitcast_fusion.x_ref, bf16[224,224]{1,0:T(8,128)(2,1)} %get-tuple-element.42.w_ref, f32[144,1]{1,0:T(8,128)} %get-tuple-element.38.b_ref, f32[1,14,1,516]{3,2,1,0:T(1,128)} %bitcast.73, bf16[128,128]{1,0:T(8,128)(2,1)} %constant.146.clone.rest_1_), custom_call_target="tpu_custom_call" | custom-call | tf_op jit(solution)/shard_map/pallas_call | solution.py:97
  77.5 2.9 %shard_map.186 = bf16[1,64,8,128]{3,2,1,0:T(8,128)(2,1)} custom-call(bf16[1,14,128,129]{3,2,1,0:T(8,128)(2,1)} %shard_map.185.x_ref, bf16[128,896]{1,0:T(8,128)(2,1)} %get-tuple-element.44.w_ref, f32[144,1]{1,0:T(8,128)} %get-tuple-element.38.b_ref), custom_call_target="tpu_custom_call" | custom-call | tf_op jit(solution)/shard_map/pallas_call | solution.py:97
  (78 shorter events, 5.6 us)
Async XLA Ops:
  0.0 25.9 %copy-start = (bf16[64,32,7,7]{0,1,3,2:T(8,128)(2,1)S(1)}, bf16[64,32,7,7]{0,1,3,2:T(8,128)(2,1)}, u32[]{:S(2)}) copy-start(bf16[64,32,7,7]{0,1,3,2:T(8,128)(2,1)} %param.31) | copy-start | bytes 602116
  4.1 16.0 %copy-start.10 = (s32[64]{0:T(128)S(1)}, s32[64]{0:T(128)}, u32[]{:S(2)}) copy-start(s32[64]{0:T(128)} %param.22) | copy-start | bytes 772
  4.1 17.3 %copy-start.13 = (s32[64]{0:T(128)S(1)}, s32[64]{0:T(128)}, u32[]{:S(2)}) copy-start(s32[64]{0:T(128)} %constant.183) | copy-start | bytes 772
  4.1 17.3 %copy-start.12 = (s32[12]{0:T(128)S(1)}, s32[12]{0:T(128)}, u32[]{:S(2)}) copy-start(s32[12]{0:T(128)} %constant.184) | copy-start | bytes 148
  4.1 17.3 %copy-start.11 = (s32[8]{0:T(128)S(1)}, s32[8]{0:T(128)}, u32[]{:S(2)}) copy-start(s32[8]{0:T(128)} %constant.185) | copy-start | bytes 100
  4.1 17.3 %copy-start.5 = (bf16[16,1,7,7]{0,3,2,1:T(8,128)(2,1)S(1)}, bf16[16,1,7,7]{0,3,2,1:T(8,128)(2,1)}, u32[]{:S(2)}) copy-start(bf16[16,1,7,7]{0,3,2,1:T(8,128)(2,1)} %param.24) | copy-start | bytes 4708
  4.2 17.3 %copy-start.14 = (f32[64]{0:T(128)S(1)}, f32[64]{0:T(128)}, u32[]{:S(2)}) copy-start(f32[64]{0:T(128)} %param.32) | copy-start | bytes 772
  4.2 17.3 %copy-start.15 = (f32[32]{0:T(128)S(1)}, f32[32]{0:T(128)}, u32[]{:S(2)}) copy-start(f32[32]{0:T(128)} %param.30) | copy-start | bytes 388
  4.2 17.3 %copy-start.16 = (f32[32]{0:T(128)S(1)}, f32[32]{0:T(128)}, u32[]{:S(2)}) copy-start(f32[32]{0:T(128)} %param.27) | copy-start | bytes 388
  4.2 17.3 %copy-start.17 = (f32[16]{0:T(128)S(1)}, f32[16]{0:T(128)}, u32[]{:S(2)}) copy-start(f32[16]{0:T(128)} %param.25) | copy-start | bytes 196
  4.2 18.7 %copy-start.8 = (pred[4,4,4]{1,0,2:T(4,128)(4,1)S(1)}, pred[4,4,4]{1,0,2:T(4,128)(4,1)}, u32[]{:S(2)}) copy-start(pred[4,4,4]{1,0,2:T(4,128)(4,1)} %constant.153) | copy-start | bytes 196
  4.9 19.1 %copy-start.1 = (bf16[32,16,7,7]{0,1,3,2:T(8,128)(2,1)S(1)}, bf16[32,16,7,7]{0,1,3,2:T(8,128)(2,1)}, u32[]{:S(2)}) copy-start(bf16[32,16,7,7]{0,1,3,2:T(8,128)(2,1)} %param.26) | copy-start | bytes 150532
  5.5 19.1 %copy-start.18 = (pred[3,4]{0,1:T(4,128)(4,1)S(1)}, pred[3,4]{0,1:T(4,128)(4,1)}, u32[]{:S(2)}) copy-start(pred[3,4]{0,1:T(4,128)(4,1)} %constant.162) | copy-start | bytes 40
  7.0 26.1 %all-to-all-start = ((bf16[64,2,656]{2,1,0:T(2,128)(2,1)}), bf16[64,2,656]{2,1,0:T(2,128)(2,1)S(1)}, u32[]{:S(2)}, u32[]{:S(2)}) async-start(bf16[64,2,656]{2,1,0:T(2,128)(2,1)} %reshape.318), calls=%async_computation | async-start | bytes 393216 | tf_op jit(solution)/shard_map/all_to_all | solution.py:242
  25.9 0.7 copy-start.9
  26.6 1.7 %copy-start.3 = (bf16[32,32,7,7]{1,0,3,2:T(8,128)(2,1)S(1)}, bf16[32,32,7,7]{1,0,3,2:T(8,128)(2,1)}, u32[]{:S(2)}) copy-start(bf16[32,32,7,7]{1,0,3,2:T(8,128)(2,1)} %param.29) | copy-start | bytes 301060
  33.9 9.0 %copy-start.2 = (bf16[64,32,41]{2,1,0:T(8,128)(2,1)}, bf16[64,32,41]{2,1,0:T(8,128)(2,1)S(1)}, u32[]{:S(2)}) copy-start(bf16[64,32,41]{2,1,0:T(8,128)(2,1)S(1)} %reshape.319) | copy-start | bytes 503812
  34.0 8.9 %collective-permute-start.1 = (bf16[32,41]{1,0:T(8,128)(2,1)S(1)}, bf16[32,41]{1,0:T(8,128)(2,1)S(1)}, u32[]{:S(2)}, u32[]{:S(2)}) collective-permute-start(bf16[32,41]{1,0:T(8,128)(2,1)S(1)} %get-tuple-element.48), channel_id=1, source_target_pairs={{1,0},{2,1},{3,2},{5,4},{6,5},{7,6},{9,8},{10,9},{11,10},{13,12},{... | collective-permute-start | bytes 7880 | tf_op jit(solution)/shard_map/ppermute | solution.py:271
  35.3 7.6 %collective-permute-start = (bf16[32,41]{1,0:T(8,128)(2,1)S(1)}, bf16[32,41]{1,0:T(8,128)(2,1)S(1)}, u32[]{:S(2)}, u32[]{:S(2)}) collective-permute-start(bf16[32,41]{1,0:T(8,128)(2,1)S(1)} %get-tuple-element.49), channel_id=1, source_target_pairs={{0,1},{1,2},{2,3},{4,5},{5,6},{6,7},{8,9},{9,10},{10,11},{12,13},{... | collective-permute-start | bytes 7880 | tf_op jit(solution)/shard_map/ppermute | solution.py:270
  42.9 0.6 copy-start.6
  42.9 0.6 copy-start.7
  55.9 1.3 %copy-start.4 = (bf16[7,32,32]{2,1,0:T(8,128)(2,1)S(1)}, bf16[7,32,32]{2,1,0:T(8,128)(2,1)}, u32[]{:S(2)}) copy-start(bf16[7,32,32]{2,1,0:T(8,128)(2,1)} %param.28) | copy-start | bytes 43012
  57.6 7.2 %collective-permute-start.2 = (bf16[6,32,522]{2,1,0:T(8,128)(2,1)S(1)}, bf16[6,32,522]{2,1,0:T(8,128)(2,1)S(1)}, u32[]{:S(2)}, u32[]{:S(2)}) collective-permute-start(bf16[6,32,522]{2,1,0:T(8,128)(2,1)S(1)} %get-tuple-element.50), channel_id=1, source_target_pairs={{0,4},{4,8},{8,12},{12,16},{16,20},{20,24},{24,28},{28,32},{32,36}... | collective-permute-start | bytes 601352 | tf_op jit(solution)/shard_map/ppermute | solution.py:292
  61.7 7.5 %collective-permute-start.3 = (bf16[6,32,522]{2,1,0:T(8,128)(2,1)S(1)}, bf16[6,32,522]{2,1,0:T(8,128)(2,1)S(1)}, u32[]{:S(2)}, u32[]{:S(2)}) collective-permute-start(bf16[6,32,522]{2,1,0:T(8,128)(2,1)S(1)} %get-tuple-element.51), channel_id=1, source_target_pairs={{4,0},{8,4},{12,8},{16,12},{20,16},{24,20},{28,24},{32,28},{36,32}... | collective-permute-start | bytes 601352 | tf_op jit(solution)/shard_map/ppermute | solution.py:293

commit v13 on v12

--- a/solution.py
+++ b/solution.py
@@ -142,25 +142,14 @@
 
 def weights_stride4(w, shifts, lag):
     fout, fin = w.shape[:2]
-    s = np.arange(shifts)[:, None]
-    p = np.arange(PH)[None, :]
-    b = 4 * s + p - lag
-    ok = (b >= 0) & (b <= 6)
-    taps = jnp.take(w, np.clip(b, 0, 6).reshape(-1), axis=3).reshape(fout, fin, 7, shifts, PH)
-    taps = jnp.where(ok[None, None, None], taps, jnp.zeros((), w.dtype))
+    taps = jnp.pad(w, ((0, 0), (0, 0), (0, 0), (lag, shifts * PH - 7 - lag))).reshape(fout, fin, 7, shifts, PH)
     return jnp.transpose(taps, (3, 0, 2, 4, 1)).reshape(shifts * fout, 7 * PH * fin)
 
 
 def weights_first(w):
     fout = w.shape[0]
-    p = np.arange(PH)[:, None, None]
-    dd = np.arange(4)[None, :, None]
-    q = np.arange(PH)[None, None, :]
-    b = 4 * (dd - 1) + q - p + 3
-    ok = (b >= 0) & (b <= 6)
-    taps = jnp.take(w[:, 0], np.clip(b, 0, 6).reshape(-1), axis=2).reshape(fout, 7, PH, 4, PH)
-    taps = jnp.where(ok[None, None], taps, jnp.zeros((), w.dtype))
-    return jnp.transpose(taps, (2, 3, 0, 1, 4)).reshape(PH * 4 * fout, 7 * PH)
+    per_p = [jnp.pad(w[:, 0], ((0, 0), (0, 0), (p + 1, 8 - p))).reshape(fout, 7, 4, PH) for p in range(PH)]
+    return jnp.transpose(jnp.stack(per_p), (0, 3, 1, 2, 4)).reshape(PH * 4 * fout, 7 * PH)
 
 
 def phase_select():

time: 81.4 us -> 79.7 us (0.979)
  local copies, waits for them, and re-layouts: 13.5 us -> 12.5 us
    gather x3 -> x0, local copies, waits for them, and re-layouts: 1.87 us -> none  [the longest x2 1.24 us: weights_stride4(): jnp.take(w, np.clip(b, 0, 6).reshape(-1), axis=3)]
    transpose x3 -> x1, other arithmetic: 1 us -> 0.12 us  [weights_first(): jnp.transpose(jnp.stack(per_p), (0, 3, 1, 2, 4))]
    reshape x2 -> x4, local copies, waits for them, and re-layouts: 0.88 us -> 1.67 us  [the longest x2 0.89 us: weights_first(): jnp.transpose(jnp.stack(per_p), (0, 3, 1, 2, 4))]
    unnamed x40 -> x27, local copies, waits for them, and re-layouts: 2.15 us -> 2.09 us
  transfers between devices with their start and end apart: 5 -> 5, of which waited for: 2 -> 2; matrix products, arithmetic and copies ran while one was open for 13% -> 12% of each run, Pallas kernels for 2% -> 2%
where the time goes in v13:
time: 79.7 us; the launch traced here: 78.7 us
  Pallas kernels  24.6 us (31%)
  starting transfers between devices  24.4 us (31%)
  local copies, waits for them, and re-layouts  12.5 us (16%)
  other arithmetic  6.56 us (8%)
  waiting for transfers between devices  5.41 us (7%)
  between operations  5.04 us (6%)
    pallas_call x4, Pallas kernels, banded(): pl.pallas_call(kernel, grid=(windows,), in_specs=specs, out_specs=pl.Bloc...  20.4 us
    all_to_all x1, starting transfers between devices, on_device(): lax.all_to_all(outgoing, 'chan', split_axis=0, concat_axis=0, tiled=True)  13 us
    ppermute x1, waiting for transfers between devices, on_device(): below = lax.ppermute(second[:REACH], 'chan', ring_down)  4.4 us
    ppermute x1, starting transfers between devices, on_device(): above = lax.ppermute(second[C_DEV - REACH:], 'chan', ring_up)  4.09 us
    ppermute x1, starting transfers between devices, on_device(): before = lax.ppermute(arrived[blocks - 1], 'tm', up)  3.99 us
    pallas_call x1, Pallas kernels, strain_layout(): pl.pallas_call(kernel, out_shape=jax.ShapeDtypeStruct((rows, n_out), jnp....  2.25 us
    ppermute x1, starting transfers between devices, on_device(): below = lax.ppermute(second[:REACH], 'chan', ring_down)  2.1 us
    unnamed x27, local copies, waits for them, and re-layouts  2.09 us
  transfers between devices with their start and end apart: 5, of which 2 were waited for; matrix products, arithmetic and copies ran while one was open for 12% of the time, Pallas kernels for 2%

profile of v13, /device:TPU:1, one launch (start us, length us, event | category | flops | bytes accessed | tf_op | source)
XLA Modules:
  0.0 78.7 jit_solution(12525150336030033982)
XLA Ops:
  0.7 0.7 pad_clamp_fusion
  1.3 1.0 %pad_slice_fusion.2 = (bf16[32,512]{1,0:T(8,128)(2,1)S(1)}, bf16[32,512]{1,0:T(8,128)(2,1)S(1)}, bf16[32,512]{1,0:T(8,128)(2,1)S(1)}) fusion(bf16[32,512]{1,0:T(8,128)(2,1)} %param.15), kind=kLoop, calls=%fused_computation.26 | loop fusion | bytes 131072 | tf_op jit(solution)/shard_map/slice | solution.py:226
  3.6 0.5 pad_maximum_fusion
  4.1 0.7 gather_fusion
  4.9 0.5 maximum_bitcast_fusion.1
  5.4 1.4 %reshape.275 = bf16[64,2,656]{2,1,0:T(2,128)(2,1)} reshape(bf16[64,32,41]{2,1,0:T(8,128)(2,1)S(1)} %maximum_bitcast_fusion.1) | data formatting | bytes 335872
  6.9 13.0 %all-to-all-start = ((bf16[64,2,656]{2,1,0:T(2,128)(2,1)}), bf16[64,2,656]{2,1,0:T(2,128)(2,1)S(1)}, u32[]{:S(2)}, u32[]{:S(2)}) async-start(bf16[64,2,656]{2,1,0:T(2,128)(2,1)} %reshape.275), calls=%async_computation | async-start | bytes 393216 | tf_op jit(solution)/shard_map/all_to_all | solution.py:231
  20.0 0.6 dynamic_slice.11
  21.3 0.7 copy.72.refs_4_
  22.5 0.7 copy.69.refs_0_
  23.8 0.7 copy.70.refs_1_
  24.7 0.9 %reshape.261.refs_2_ = bf16[224,224]{1,0:T(8,128)(2,1)} reshape(bf16[7,32,7,32]{3,2,1,0:T(8,128)(2,1)S(1)} %copy.67) | data formatting | bytes 200704 | tf_op jit(solution)/shard_map/reshape | solution.py:140
  26.5 0.8 %copy.71.refs_3_ = bf16[128,896]{1,0:T(8,128)(2,1)} copy(bf16[128,896]{0,1:T(8,128)(2,1)S(1)} %reshape.263) | data formatting | bytes 458752 | tf_op jit(solution)/shard_map/reshape | solution.py:146
  27.5 0.8 %add_convert_fusion.rest_0_ = f32[2,14,4,524]{3,2,1,0:T(4,128)} fusion(pred[1,14,4,524]{3,2,1,0:T(4,128)(4,1)S(1)} %get-tuple-element.60, pred[1,14,4,524]{3,2,1,0:T(4,128)(4,1)S(1)} %get-tuple-element.59), kind=kLoop, calls=%fused_computation.13 | loop fusion | flops 117376 | bytes 293440 | tf_op jit(solution)/shard_map/stack | solution.py:246
  28.4 1.9 %shard_map.127 = (bf16[256,28]{1,0:T(8,128)(2,1)}, bf16[96,448]{1,0:T(8,128)(2,1)}, bf16[224,224]{1,0:T(8,128)(2,1)}, bf16[128,896]{1,0:T(8,128)(2,1)}, f32[144,1]{1,0:T(8,128)}) custom-call(bf16[256,28]{1,0:T(8,128)(2,1)} %copy.69.refs_0_, bf16[96,448]{1,0:T(8,128)(2,1)} %copy.70.refs_1_, bf16[224,224]{1,0:T(8,128)(2,1)} %reshape.261.refs_2_, ...), custom_call_target="tpu_custom_call" | custom-call | tf_op jit(solution)/shard_map/pallas_call | solution.py:135
  30.3 0.7 and_convert_fusion
  31.0 0.8 %reshape.276 = bf16[64,32,41]{2,1,0:T(8,128)(2,1)S(1)} reshape(bf16[64,2,656]{2,1,0:T(2,128)(2,1)S(1)} %all-to-all-done) | data formatting | bytes 335872 | tf_op jit(solution)/shard_map/optimization_barrier | solution.py:251
  31.9 1.3 %collective-permute-start.1 = (bf16[32,41]{1,0:T(8,128)(2,1)S(1)}, bf16[32,41]{1,0:T(8,128)(2,1)S(1)}, u32[]{:S(2)}, u32[]{:S(2)}) collective-permute-start(bf16[32,41]{1,0:T(8,128)(2,1)S(1)} %get-tuple-element.48), channel_id=1, source_target_pairs={{1,0},{2,1},{3,2},{5,4},{6,5},{7,6},{9,8},{10,9},{11,10},{13,12},{... | collective-permute-start | bytes 7880 | tf_op jit(solution)/shard_map/ppermute | solution.py:260
  33.2 4.0 %collective-permute-start = (bf16[32,41]{1,0:T(8,128)(2,1)S(1)}, bf16[32,41]{1,0:T(8,128)(2,1)S(1)}, u32[]{:S(2)}, u32[]{:S(2)}) collective-permute-start(bf16[32,41]{1,0:T(8,128)(2,1)S(1)} %get-tuple-element.49), channel_id=1, source_target_pairs={{0,1},{1,2},{2,3},{4,5},{5,6},{6,7},{8,9},{9,10},{10,11},{12,13},{... | collective-permute-start | bytes 7880 | tf_op jit(solution)/shard_map/ppermute | solution.py:259
  39.2 0.6 fusion.17
  41.2 0.6 copy-done.6
  41.8 2.3 %shard_map.128 = bf16[160,527]{1,0:T(8,128)(2,1)} custom-call(bf16[2048,41]{1,0:T(8,128)(2,1)} %bitcast.59, bf16[32,41]{1,0:T(8,128)(2,1)} %copy-done.7, bf16[32,41]{1,0:T(8,128)(2,1)} %copy-done.6), custom_call_target="tpu_custom_call" | custom-call | tf_op jit(solution)/shard_map/pallas_call | solution.py:125
  44.0 6.2 %shard_map.129.x_ref = bf16[2,14,64,524]{3,2,1,0:T(8,128)(2,1)} custom-call(bf16[2,80,527]{2,1,0:T(8,128)(2,1)} %bitcast.65, bf16[256,28]{1,0:T(8,128)(2,1)} %get-tuple-element.37.w_ref, f32[144,1]{1,0:T(8,128)} %get-tuple-element.38.b_ref, f32[2,14,4,524]{3,2,1,0:T(4,128)} %add_convert_fusion.rest_0_), custom_call_target="tpu_custom_call" | custom-call | tf_op jit(solution)/shard_map/pallas_call | solution.py:97
  50.2 4.1 %shard_map.130 = bf16[2,8,32,522]{3,2,1,0:T(8,128)(2,1)} custom-call(bf16[2,14,64,524]{3,2,1,0:T(8,128)(2,1)} %shard_map.129.x_ref, bf16[96,448]{1,0:T(8,128)(2,1)} %get-tuple-element.40.w_ref, f32[144,1]{1,0:T(8,128)} %get-tuple-element.38.b_ref), custom_call_target="tpu_custom_call" | custom-call | tf_op jit(solution)/shard_map/pallas_call | solution.py:97
  54.3 1.2 %slice_convert_fusion = (f32[1,8,32,522]{3,2,1,0:T(8,128)S(1)}, f32[8,32,522]{2,1,0:T(8,128)S(1)}, bf16[1,8,32,522]{3,2,1,0:T(8,128)(2,1)S(1)}) fusion(bf16[2,8,32,522]{3,2,1,0:T(8,128)(2,1)} %shard_map.130), kind=kLoop, calls=%fused_computation.11 | loop fusion | flops 133632 | bytes 1870848 | tf_op jit(solution)/shard_map/convert_element_type | solution.py:277
  55.9 4.1 %collective-permute-start.2 = (bf16[6,32,522]{2,1,0:T(8,128)(2,1)S(1)}, bf16[6,32,522]{2,1,0:T(8,128)(2,1)S(1)}, u32[]{:S(2)}, u32[]{:S(2)}) collective-permute-start(bf16[6,32,522]{2,1,0:T(8,128)(2,1)S(1)} %get-tuple-element.50), channel_id=1, source_target_pairs={{0,4},{4,8},{8,12},{12,16},{16,20},{20,24},{24,28},{28,32},{32,36}... | collective-permute-start | bytes 601352 | tf_op jit(solution)/shard_map/ppermute | solution.py:281
  60.0 2.1 %collective-permute-start.3 = (bf16[6,32,522]{2,1,0:T(8,128)(2,1)S(1)}, bf16[6,32,522]{2,1,0:T(8,128)(2,1)S(1)}, u32[]{:S(2)}, u32[]{:S(2)}) collective-permute-start(bf16[6,32,522]{2,1,0:T(8,128)(2,1)S(1)} %get-tuple-element.51), channel_id=1, source_target_pairs={{4,0},{8,4},{12,8},{16,12},{20,16},{24,20},{28,24},{32,28},{36,32}... | collective-permute-start | bytes 601352 | tf_op jit(solution)/shard_map/ppermute | solution.py:282
  62.1 1.0 %collective-permute-done.2 = bf16[6,32,522]{2,1,0:T(8,128)(2,1)S(1)} collective-permute-done((bf16[6,32,522]{2,1,0:T(8,128)(2,1)S(1)}, bf16[6,32,522]{2,1,0:T(8,128)(2,1)S(1)}, u32[]{:S(2)}, u32[]{:S(2)}) %collective-permute-start.2) | collective-permute-done | bytes 200480 | tf_op jit(solution)/shard_map/ppermute | solution.py:281
  63.1 4.4 %collective-permute-done.3 = bf16[6,32,522]{2,1,0:T(8,128)(2,1)S(1)} collective-permute-done((bf16[6,32,522]{2,1,0:T(8,128)(2,1)S(1)}, bf16[6,32,522]{2,1,0:T(8,128)(2,1)S(1)}, u32[]{:S(2)}, u32[]{:S(2)}) %collective-permute-start.3) | collective-permute-done | bytes 200480 | tf_op jit(solution)/shard_map/ppermute | solution.py:282
  67.5 1.1 %maximum_bitcast_fusion.x_ref = bf16[1,20,32,522]{3,2,1,0:T(8,128)(2,1)} fusion(bf16[6,32,522]{2,1,0:T(8,128)(2,1)S(1)} %collective-permute-done.3, bf16[8,32,522]{2,1,0:T(8,128)(2,1)S(1)} %multiply_convert_fusion, bf16[6,32,522]{2,1,0:T(8,128)(2,1)S(1)} %collective-permute-done.2), kind=kLoop, calls=%fused_computation.4 | loop fusion | flops 668160 | bytes 1336320 | tf_op jit(solution)/shard_map/broadcast_in_dim | solution.py:288
  68.6 7.2 %shard_map.131.x_ref = bf16[1,14,128,129]{3,2,1,0:T(8,128)(2,1)} custom-call(bf16[1,20,32,522]{3,2,1,0:T(8,128)(2,1)} %maximum_bitcast_fusion.x_ref, bf16[224,224]{1,0:T(8,128)(2,1)} %get-tuple-element.42.w_ref, f32[144,1]{1,0:T(8,128)} %get-tuple-element.38.b_ref, f32[1,14,1,516]{3,2,1,0:T(1,128)} %bitcast.70, bf16[128,128]{1,0:T(8,128)(2,1)} %constant.88.clone.rest_1_), custom_call_target="tpu_custom_call" | custom-call | tf_op jit(solution)/shard_map/pallas_call | solution.py:97
  75.8 2.9 %shard_map.132 = bf16[1,64,8,128]{3,2,1,0:T(8,128)(2,1)} custom-call(bf16[1,14,128,129]{3,2,1,0:T(8,128)(2,1)} %shard_map.131.x_ref, bf16[128,896]{1,0:T(8,128)(2,1)} %get-tuple-element.44.w_ref, f32[144,1]{1,0:T(8,128)} %get-tuple-element.38.b_ref), custom_call_target="tpu_custom_call" | custom-call | tf_op jit(solution)/shard_map/pallas_call | solution.py:97
  (66 shorter events, 4.2 us)
Async XLA Ops:
  0.0 55.5 %copy-start = (bf16[7,32,32]{2,1,0:T(8,128)(2,1)S(1)}, bf16[7,32,32]{2,1,0:T(8,128)(2,1)}, u32[]{:S(2)}) copy-start(bf16[7,32,32]{2,1,0:T(8,128)(2,1)} %param.22) | copy-start | bytes 43012
  4.1 15.9 %copy-start.8 = (s32[64]{0:T(128)S(1)}, s32[64]{0:T(128)}, u32[]{:S(2)}) copy-start(s32[64]{0:T(128)} %param.16) | copy-start | bytes 772
  4.1 17.1 %copy-start.9 = (f32[64]{0:T(128)S(1)}, f32[64]{0:T(128)}, u32[]{:S(2)}) copy-start(f32[64]{0:T(128)} %param.26) | copy-start | bytes 772
  4.1 17.1 %copy-start.10 = (f32[32]{0:T(128)S(1)}, f32[32]{0:T(128)}, u32[]{:S(2)}) copy-start(f32[32]{0:T(128)} %param.24) | copy-start | bytes 388
  4.1 17.1 %copy-start.11 = (f32[32]{0:T(128)S(1)}, f32[32]{0:T(128)}, u32[]{:S(2)}) copy-start(f32[32]{0:T(128)} %param.21) | copy-start | bytes 388
  4.1 17.1 %copy-start.12 = (f32[16]{0:T(128)S(1)}, f32[16]{0:T(128)}, u32[]{:S(2)}) copy-start(f32[16]{0:T(128)} %param.19) | copy-start | bytes 196
  4.1 18.0 %copy-start.5 = (bf16[16,1,7,7]{0,3,2,1:T(8,128)(2,1)S(1)}, bf16[16,1,7,7]{0,3,2,1:T(8,128)(2,1)}, u32[]{:S(2)}) copy-start(bf16[16,1,7,7]{0,3,2,1:T(8,128)(2,1)} %param.18) | copy-start | bytes 4708
  4.8 18.4 %copy-start.4 = (bf16[32,16,7,7]{0,1,3,2:T(8,128)(2,1)S(1)}, bf16[32,16,7,7]{0,1,3,2:T(8,128)(2,1)}, u32[]{:S(2)}) copy-start(bf16[32,16,7,7]{0,1,3,2:T(8,128)(2,1)} %param.20) | copy-start | bytes 150532
  5.4 19.1 %copy-start.3 = (bf16[32,32,7,7]{1,0,3,2:T(8,128)(2,1)S(1)}, bf16[32,32,7,7]{1,0,3,2:T(8,128)(2,1)}, u32[]{:S(2)}) copy-start(bf16[32,32,7,7]{1,0,3,2:T(8,128)(2,1)} %param.23) | copy-start | bytes 301060
  6.9 24.1 %all-to-all-start = ((bf16[64,2,656]{2,1,0:T(2,128)(2,1)}), bf16[64,2,656]{2,1,0:T(2,128)(2,1)S(1)}, u32[]{:S(2)}, u32[]{:S(2)}) async-start(bf16[64,2,656]{2,1,0:T(2,128)(2,1)} %reshape.275), calls=%async_computation | async-start | bytes 393216 | tf_op jit(solution)/shard_map/all_to_all | solution.py:231
  19.9 5.8 %copy-start.2 = (bf16[64,32,7,7]{0,1,3,2:T(8,128)(2,1)S(1)}, bf16[64,32,7,7]{0,1,3,2:T(8,128)(2,1)}, u32[]{:S(2)}) copy-start(bf16[64,32,7,7]{0,1,3,2:T(8,128)(2,1)} %param.25) | copy-start | bytes 602116
  31.9 9.3 %copy-start.1 = (bf16[64,32,41]{2,1,0:T(8,128)(2,1)}, bf16[64,32,41]{2,1,0:T(8,128)(2,1)S(1)}, u32[]{:S(2)}) copy-start(bf16[64,32,41]{2,1,0:T(8,128)(2,1)S(1)} %reshape.276) | copy-start | bytes 503812
  31.9 9.3 %collective-permute-start.1 = (bf16[32,41]{1,0:T(8,128)(2,1)S(1)}, bf16[32,41]{1,0:T(8,128)(2,1)S(1)}, u32[]{:S(2)}, u32[]{:S(2)}) collective-permute-start(bf16[32,41]{1,0:T(8,128)(2,1)S(1)} %get-tuple-element.48), channel_id=1, source_target_pairs={{1,0},{2,1},{3,2},{5,4},{6,5},{7,6},{9,8},{10,9},{11,10},{13,12},{... | collective-permute-start | bytes 7880 | tf_op jit(solution)/shard_map/ppermute | solution.py:260
  33.2 8.0 %collective-permute-start = (bf16[32,41]{1,0:T(8,128)(2,1)S(1)}, bf16[32,41]{1,0:T(8,128)(2,1)S(1)}, u32[]{:S(2)}, u32[]{:S(2)}) collective-permute-start(bf16[32,41]{1,0:T(8,128)(2,1)S(1)} %get-tuple-element.49), channel_id=1, source_target_pairs={{0,1},{1,2},{2,3},{4,5},{5,6},{6,7},{8,9},{9,10},{10,11},{12,13},{... | collective-permute-start | bytes 7880 | tf_op jit(solution)/shard_map/ppermute | solution.py:259
  41.2 0.6 copy-start.6
  41.2 0.6 copy-start.7
  55.9 7.2 %collective-permute-start.2 = (bf16[6,32,522]{2,1,0:T(8,128)(2,1)S(1)}, bf16[6,32,522]{2,1,0:T(8,128)(2,1)S(1)}, u32[]{:S(2)}, u32[]{:S(2)}) collective-permute-start(bf16[6,32,522]{2,1,0:T(8,128)(2,1)S(1)} %get-tuple-element.50), channel_id=1, source_target_pairs={{0,4},{4,8},{8,12},{12,16},{16,20},{20,24},{24,28},{28,32},{32,36}... | collective-permute-start | bytes 601352 | tf_op jit(solution)/shard_map/ppermute | solution.py:281
  60.0 7.5 %collective-permute-start.3 = (bf16[6,32,522]{2,1,0:T(8,128)(2,1)S(1)}, bf16[6,32,522]{2,1,0:T(8,128)(2,1)S(1)}, u32[]{:S(2)}, u32[]{:S(2)}) collective-permute-start(bf16[6,32,522]{2,1,0:T(8,128)(2,1)S(1)} %get-tuple-element.51), channel_id=1, source_target_pairs={{4,0},{8,4},{12,8},{16,12},{20,16},{24,20},{28,24},{32,28},{36,32}... | collective-permute-start | bytes 601352 | tf_op jit(solution)/shard_map/ppermute | solution.py:282

commit v14 on v13

--- a/solution.py
+++ b/solution.py
@@ -116,7 +116,7 @@
         for src, lo, n, skip in pieces:
             acc = None
             for q in range(PH):
-                e = (ri == ci * PH + q).astype(jnp.float32)
+                e = (ri == ci * PH + q + PH * (ci // (rows // (2 * PH) - 1))).astype(jnp.float32)
                 piece = src[pl.ds(q, n, stride=PH), :].astype(jnp.float32)
                 y = lax.dot_general(e, piece, nt, preferred_element_type=jnp.float32)
                 acc = y if acc is None else acc + y
@@ -135,6 +135,39 @@
     return pl.pallas_call(kernel, out_shape=tuple(jax.ShapeDtypeStruct(a.shape, a.dtype) for a in arrays))(*arrays)
 
 
+def first_layer(x, w_all, bias, mask):
+    windows, rows_in, n_in = x.shape
+    n_out = n_in - 3
+    r_out = rows_in // PH - 7
+    fout = w_all.shape[0] // PH
+
+    def kernel(x_ref, w_ref, b_ref, m_ref, o_ref):
+        b_val = b_ref[0 : PH * fout, :]
+        for r in range(r_out):
+            base = x_ref[PH * r : PH * r + 8 * PH, :]
+            xs = jnp.concatenate([base[:, d : d + n_out] for d in range(4)], axis=0)
+            acc = jnp.dot(w_ref[...], xs, preferred_element_type=jnp.float32) + b_val
+            acc = jnp.maximum(acc, 0.0)
+            m_row = m_ref[r]
+            for p in range(PH):
+                o_ref[r, p * fout : (p + 1) * fout, :] = (acc[p * fout : (p + 1) * fout] * m_row[p : p + 1, :]).astype(
+                    jnp.bfloat16
+                )
+
+    return pl.pallas_call(
+        kernel,
+        grid=(windows,),
+        in_specs=[
+            pl.BlockSpec((None, rows_in, n_in), lambda w: (w, 0, 0)),
+            pl.BlockSpec(w_all.shape, lambda w: (0, 0)),
+            pl.BlockSpec(bias.shape, lambda w: (0, 0)),
+            pl.BlockSpec((None,) + mask.shape[1:], lambda w: (w, 0, 0, 0)),
+        ],
+        out_specs=pl.BlockSpec((None, r_out, PH * fout, n_out), lambda w: (w, 0, 0, 0)),
+        out_shape=jax.ShapeDtypeStruct((windows, r_out, PH * fout, n_out), jnp.bfloat16),
+    )(x, w_all, bias, mask)
+
+
 def weights_stride1(w):
     fout, fin = w.shape[:2]
     return jnp.transpose(w, (3, 0, 2, 1)).reshape(7 * fout, 7 * fin)
@@ -148,8 +181,8 @@
 
 def weights_first(w):
     fout = w.shape[0]
-    per_p = [jnp.pad(w[:, 0], ((0, 0), (0, 0), (p + 1, 8 - p))).reshape(fout, 7, 4, PH) for p in range(PH)]
-    return jnp.transpose(jnp.stack(per_p), (0, 3, 1, 2, 4)).reshape(PH * 4 * fout, 7 * PH)
+    per_p = [jnp.pad(w[:, 0], ((0, 0), (0, 1), (p + 1, 8 - p))).reshape(fout, 8, 4, PH) for p in range(PH)]
+    return jnp.transpose(jnp.stack(per_p), (0, 1, 3, 2, 4)).reshape(PH * fout, 4 * 8 * PH)
 
 
 def phase_select():
@@ -178,22 +211,12 @@
     wide = C_DEV + 2 * REACH
     n_win, n_s = strain_wide.shape[0], strain_wide.shape[-1]
     n_f = n_s - 3
-    first = banded(
-        strain_wide.reshape(n_win, wide * PH, n_s),
-        first_weight,
-        biases,
-        0,
-        first_mask,
-        groups=PH,
-        shifts=4,
-        n_out=n_f,
-        relu=True,
-    )
+    first = first_layer(strain_wide, first_weight, biases, first_mask)
     return banded(
         first,
         second_weight,
         biases,
-        16,
+        64,
         None,
         groups=1,
         shifts=3,
@@ -229,7 +252,7 @@
     both = jnp.concatenate([windows, jnp.take(windows, partners, axis=1, mode="clip"), tag], axis=2)
     outgoing = jnp.transpose(both, (1, 0, 2))
     arrived = lax.all_to_all(outgoing, "chan", split_axis=0, concat_axis=0, tiled=True)
-    biases = jnp.concatenate([first_bias, second_bias, third_bias, fourth_bias]).reshape(-1, 1)
+    biases = jnp.concatenate([jnp.tile(first_bias, PH), second_bias, third_bias, fourth_bias]).reshape(-1, 1)
     prepared = (
         weights_first(first_weight),
         weights_stride4(second_weight, 3, 2),
@@ -258,12 +281,12 @@
     down = [(j, i) for i, j in up]
     before = lax.ppermute(arrived[blocks - 1], "tm", up)
     after = lax.ppermute(arrived[0, : PH * WR], "tm", down)
-    strain_wide = strain_layout(arrived.reshape(times, -1), before, after, 2 * wide * PH)
+    strain_wide = strain_layout(arrived.reshape(times, -1), before, after, 2 * (wide + 1) * PH)
 
     quarter = times // 4
     length = quarter + 2 * LEAD
     lower = lower_layers(
-        strain_wide.reshape(2, wide, PH, -1), first_mask, first_weight, biases, second_weight, length
+        strain_wide.reshape(2, (wide + 1) * PH, -1), first_mask, first_weight, biases, second_weight, length
     )
     pre_second, mate_second = lower[0], lower[1]
 
@@ -288,7 +311,7 @@
         second_wide[None],
         third_weight,
         biases,
-        48,
+        96,
         third_mask[None],
         groups=1,
         shifts=7,
@@ -301,7 +324,7 @@
         third,
         fourth_weight,
         biases,
-        80,
+        128,
         None,
         groups=1,
         shifts=2,

time: 79.7 us -> 79.7 us (level)
  Pallas kernels: 24.6 us -> 22.5 us
  local copies, waits for them, and re-layouts: 12.5 us -> 14.4 us
    pallas_call x4 -> x3, Pallas kernels: 20.4 us -> 14.2 us  [banded(): pl.pallas_call(kernel, grid=(windows,), in_specs=specs, out_specs=pl.Bloc...]
    pallas_call x0 -> x1, Pallas kernels: none -> 4.01 us  [first_layer(): pl.pallas_call(kernel, grid=(windows,), in_specs=[pl.BlockSpec((None, row...]
    reshape x3 -> x4, local copies, waits for them, and re-layouts: 1.63 us -> 3.26 us  [the longest x1 1.67 us: on_device(): strain_wide.reshape(2, (wide + 1) * PH, -1)]
where the time goes in v14:
time: 79.7 us; the launch traced here: 78.7 us
  starting transfers between devices  24.5 us (31%)
  Pallas kernels  22.5 us (28%)
  local copies, waits for them, and re-layouts  14.4 us (18%)
  other arithmetic  6.73 us (8%)
  waiting for transfers between devices  5.41 us (7%)
  between operations  4.99 us (6%)
    pallas_call x3, Pallas kernels, banded(): pl.pallas_call(kernel, grid=(windows,), in_specs=specs, out_specs=pl.Bloc...  14.2 us
    all_to_all x1, starting transfers between devices, on_device(): lax.all_to_all(outgoing, 'chan', split_axis=0, concat_axis=0, tiled=True)  13 us
    ppermute x1, waiting for transfers between devices, on_device(): below = lax.ppermute(second[:REACH], 'chan', ring_down)  4.4 us
    ppermute x1, starting transfers between devices, on_device(): above = lax.ppermute(second[C_DEV - REACH:], 'chan', ring_up)  4.1 us
    pallas_call x1, Pallas kernels, first_layer(): pl.pallas_call(kernel, grid=(windows,), in_specs=[pl.BlockSpec((None, row...  4.01 us
    ppermute x1, starting transfers between devices, on_device(): before = lax.ppermute(arrived[blocks - 1], 'tm', up)  3.99 us
    pallas_call x1, Pallas kernels, strain_layout(): pl.pallas_call(kernel, out_shape=jax.ShapeDtypeStruct((rows, n_out), jnp....  2.32 us
    unnamed x27, local copies, waits for them, and re-layouts  2.1 us
  transfers between devices with their start and end apart: 5, of which 2 were waited for; matrix products, arithmetic and copies ran while one was open for 12% of the time, Pallas kernels for 2%

profile of v14, /device:TPU:1, one launch (start us, length us, event | category | flops | bytes accessed | tf_op | source)
XLA Modules:
  0.0 78.7 jit_solution(4069445292971697594)
XLA Ops:
  0.7 0.7 pad_clamp_fusion
  1.3 1.0 %pad_slice_fusion.2 = (bf16[32,512]{1,0:T(8,128)(2,1)S(1)}, bf16[32,512]{1,0:T(8,128)(2,1)S(1)}, bf16[32,512]{1,0:T(8,128)(2,1)S(1)}) fusion(bf16[32,512]{1,0:T(8,128)(2,1)} %param.15), kind=kLoop, calls=%fused_computation.26 | loop fusion | bytes 131072 | tf_op jit(solution)/shard_map/slice | solution.py:249
  3.6 0.5 pad_maximum_fusion
  4.1 0.7 gather_fusion
  5.4 1.4 %reshape.280 = bf16[64,2,656]{2,1,0:T(2,128)(2,1)} reshape(bf16[64,32,41]{2,1,0:T(8,128)(2,1)S(1)} %maximum_bitcast_fusion.1) | data formatting | bytes 335872
  6.9 13.0 %all-to-all-start = ((bf16[64,2,656]{2,1,0:T(2,128)(2,1)}), bf16[64,2,656]{2,1,0:T(2,128)(2,1)S(1)}, u32[]{:S(2)}, u32[]{:S(2)}) async-start(bf16[64,2,656]{2,1,0:T(2,128)(2,1)} %reshape.280), calls=%async_computation | async-start | bytes 393216 | tf_op jit(solution)/shard_map/all_to_all | solution.py:254
  19.9 0.7 dynamic_slice.11
  21.5 0.8 copy.72.refs_4_
  23.1 0.7 copy.69.refs_0_
  24.3 0.7 copy.70.refs_1_
  25.3 0.9 %reshape.265.refs_2_ = bf16[224,224]{1,0:T(8,128)(2,1)} reshape(bf16[7,32,7,32]{3,2,1,0:T(8,128)(2,1)S(1)} %copy.67) | data formatting | bytes 200704 | tf_op jit(solution)/shard_map/reshape | solution.py:173
  27.0 0.8 %copy.71.refs_3_ = bf16[128,896]{1,0:T(8,128)(2,1)} copy(bf16[128,896]{0,1:T(8,128)(2,1)S(1)} %reshape.267) | data formatting | bytes 458752 | tf_op jit(solution)/shard_map/reshape | solution.py:179
  28.0 0.8 %add_convert_fusion.m_ref = f32[2,14,4,524]{3,2,1,0:T(4,128)} fusion(pred[1,14,4,524]{3,2,1,0:T(4,128)(4,1)S(1)} %get-tuple-element.60, pred[1,14,4,524]{3,2,1,0:T(4,128)(4,1)S(1)} %get-tuple-element.59), kind=kLoop, calls=%fused_computation.13 | loop fusion | flops 117376 | bytes 293440 | tf_op jit(solution)/shard_map/stack | solution.py:269
  28.9 2.0 %shard_map.127 = (bf16[64,128]{1,0:T(8,128)(2,1)}, bf16[96,448]{1,0:T(8,128)(2,1)}, bf16[224,224]{1,0:T(8,128)(2,1)}, bf16[128,896]{1,0:T(8,128)(2,1)}, f32[192,1]{1,0:T(8,128)}) custom-call(bf16[64,128]{1,0:T(8,128)(2,1)} %copy.69.refs_0_, bf16[96,448]{1,0:T(8,128)(2,1)} %copy.70.refs_1_, bf16[224,224]{1,0:T(8,128)(2,1)} %reshape.265.refs_2_, ...), custom_call_target="tpu_custom_call" | custom-call | tf_op jit(solution)/shard_map/pallas_call | solution.py:135
  30.9 0.7 and_convert_fusion
  31.6 0.8 %reshape.281 = bf16[64,32,41]{2,1,0:T(8,128)(2,1)S(1)} reshape(bf16[64,2,656]{2,1,0:T(2,128)(2,1)S(1)} %all-to-all-done) | data formatting | bytes 335872 | tf_op jit(solution)/shard_map/optimization_barrier | solution.py:274
  32.5 1.3 %collective-permute-start.1 = (bf16[32,41]{1,0:T(8,128)(2,1)S(1)}, bf16[32,41]{1,0:T(8,128)(2,1)S(1)}, u32[]{:S(2)}, u32[]{:S(2)}) collective-permute-start(bf16[32,41]{1,0:T(8,128)(2,1)S(1)} %get-tuple-element.48), channel_id=1, source_target_pairs={{1,0},{2,1},{3,2},{5,4},{6,5},{7,6},{9,8},{10,9},{11,10},{13,12},{... | collective-permute-start | bytes 7880 | tf_op jit(solution)/shard_map/ppermute | solution.py:283
  33.8 4.0 %collective-permute-start = (bf16[32,41]{1,0:T(8,128)(2,1)S(1)}, bf16[32,41]{1,0:T(8,128)(2,1)S(1)}, u32[]{:S(2)}, u32[]{:S(2)}) collective-permute-start(bf16[32,41]{1,0:T(8,128)(2,1)S(1)} %get-tuple-element.49), channel_id=1, source_target_pairs={{0,1},{1,2},{2,3},{4,5},{5,6},{6,7},{8,9},{9,10},{10,11},{12,13},{... | collective-permute-start | bytes 7880 | tf_op jit(solution)/shard_map/ppermute | solution.py:282
  39.9 0.5 fusion.17
  41.6 0.5 copy-done.6
  42.2 2.3 %shard_map.128 = bf16[168,527]{1,0:T(8,128)(2,1)} custom-call(bf16[2048,41]{1,0:T(8,128)(2,1)} %bitcast.58, bf16[32,41]{1,0:T(8,128)(2,1)} %copy-done.7, bf16[32,41]{1,0:T(8,128)(2,1)} %copy-done.6), custom_call_target="tpu_custom_call" | custom-call | tf_op jit(solution)/shard_map/pallas_call | solution.py:125
  44.5 1.7 %reshape.270.x_ref = bf16[2,84,527]{2,1,0:T(8,128)(2,1)} reshape(bf16[168,527]{1,0:T(8,128)(2,1)} %shard_map.128) | data formatting | bytes 354144 | tf_op jit(solution)/shard_map/reshape | solution.py:289
  46.2 4.0 %shard_map.129.x_ref = bf16[2,14,64,524]{3,2,1,0:T(8,128)(2,1)} custom-call(bf16[2,84,527]{2,1,0:T(8,128)(2,1)} %reshape.270.x_ref, bf16[64,128]{1,0:T(8,128)(2,1)} %get-tuple-element.37.w_ref, f32[192,1]{1,0:T(8,128)} %get-tuple-element.38.b_ref, f32[2,14,4,524]{3,2,1,0:T(4,128)} %add_convert_fusion.m_ref), custom_call_target="tpu_custom_call" | custom-call | tf_op jit(solution)/shard_map/pallas_call | solution.py:157
  50.2 4.1 %shard_map.130 = bf16[2,8,32,522]{3,2,1,0:T(8,128)(2,1)} custom-call(bf16[2,14,64,524]{3,2,1,0:T(8,128)(2,1)} %shard_map.129.x_ref, bf16[96,448]{1,0:T(8,128)(2,1)} %get-tuple-element.40.w_ref, f32[192,1]{1,0:T(8,128)} %get-tuple-element.38.b_ref), custom_call_target="tpu_custom_call" | custom-call | tf_op jit(solution)/shard_map/pallas_call | solution.py:97
  54.2 1.2 %slice_convert_fusion = (f32[1,8,32,522]{3,2,1,0:T(8,128)S(1)}, f32[8,32,522]{2,1,0:T(8,128)S(1)}, bf16[1,8,32,522]{3,2,1,0:T(8,128)(2,1)S(1)}) fusion(bf16[2,8,32,522]{3,2,1,0:T(8,128)(2,1)} %shard_map.130), kind=kLoop, calls=%fused_computation.11 | loop fusion | flops 133632 | bytes 1870848 | tf_op jit(solution)/shard_map/convert_element_type | solution.py:300
  55.9 4.1 %collective-permute-start.2 = (bf16[6,32,522]{2,1,0:T(8,128)(2,1)S(1)}, bf16[6,32,522]{2,1,0:T(8,128)(2,1)S(1)}, u32[]{:S(2)}, u32[]{:S(2)}) collective-permute-start(bf16[6,32,522]{2,1,0:T(8,128)(2,1)S(1)} %get-tuple-element.50), channel_id=1, source_target_pairs={{0,4},{4,8},{8,12},{12,16},{16,20},{20,24},{24,28},{28,32},{32,36}... | collective-permute-start | bytes 601352 | tf_op jit(solution)/shard_map/ppermute | solution.py:304
  60.0 2.1 %collective-permute-start.3 = (bf16[6,32,522]{2,1,0:T(8,128)(2,1)S(1)}, bf16[6,32,522]{2,1,0:T(8,128)(2,1)S(1)}, u32[]{:S(2)}, u32[]{:S(2)}) collective-permute-start(bf16[6,32,522]{2,1,0:T(8,128)(2,1)S(1)} %get-tuple-element.51), channel_id=1, source_target_pairs={{4,0},{8,4},{12,8},{16,12},{20,16},{24,20},{28,24},{32,28},{36,32}... | collective-permute-start | bytes 601352 | tf_op jit(solution)/shard_map/ppermute | solution.py:305
  62.1 1.0 %collective-permute-done.2 = bf16[6,32,522]{2,1,0:T(8,128)(2,1)S(1)} collective-permute-done((bf16[6,32,522]{2,1,0:T(8,128)(2,1)S(1)}, bf16[6,32,522]{2,1,0:T(8,128)(2,1)S(1)}, u32[]{:S(2)}, u32[]{:S(2)}) %collective-permute-start.2) | collective-permute-done | bytes 200480 | tf_op jit(solution)/shard_map/ppermute | solution.py:304
  63.1 4.4 %collective-permute-done.3 = bf16[6,32,522]{2,1,0:T(8,128)(2,1)S(1)} collective-permute-done((bf16[6,32,522]{2,1,0:T(8,128)(2,1)S(1)}, bf16[6,32,522]{2,1,0:T(8,128)(2,1)S(1)}, u32[]{:S(2)}, u32[]{:S(2)}) %collective-permute-start.3) | collective-permute-done | bytes 200480 | tf_op jit(solution)/shard_map/ppermute | solution.py:305
  67.5 1.1 %maximum_bitcast_fusion.x_ref = bf16[1,20,32,522]{3,2,1,0:T(8,128)(2,1)} fusion(bf16[6,32,522]{2,1,0:T(8,128)(2,1)S(1)} %collective-permute-done.3, bf16[8,32,522]{2,1,0:T(8,128)(2,1)S(1)} %multiply_convert_fusion, bf16[6,32,522]{2,1,0:T(8,128)(2,1)S(1)} %collective-permute-done.2), kind=kLoop, calls=%fused_computation.4 | loop fusion | flops 668160 | bytes 1336320 | tf_op jit(solution)/shard_map/broadcast_in_dim | solution.py:311
  68.6 7.2 %shard_map.131.x_ref = bf16[1,14,128,129]{3,2,1,0:T(8,128)(2,1)} custom-call(bf16[1,20,32,522]{3,2,1,0:T(8,128)(2,1)} %maximum_bitcast_fusion.x_ref, bf16[224,224]{1,0:T(8,128)(2,1)} %get-tuple-element.42.w_ref, f32[192,1]{1,0:T(8,128)} %get-tuple-element.38.b_ref, f32[1,14,1,516]{3,2,1,0:T(1,128)} %bitcast.68, bf16[128,128]{1,0:T(8,128)(2,1)} %constant.88.clone.rest_1_), custom_call_target="tpu_custom_call" | custom-call | tf_op jit(solution)/shard_map/pallas_call | solution.py:97
  75.8 2.9 %shard_map.132 = bf16[1,64,8,128]{3,2,1,0:T(8,128)(2,1)} custom-call(bf16[1,14,128,129]{3,2,1,0:T(8,128)(2,1)} %shard_map.131.x_ref, bf16[128,896]{1,0:T(8,128)(2,1)} %get-tuple-element.44.w_ref, f32[192,1]{1,0:T(8,128)} %get-tuple-element.38.b_ref), custom_call_target="tpu_custom_call" | custom-call | tf_op jit(solution)/shard_map/pallas_call | solution.py:97
  (69 shorter events, 5.2 us)
Async XLA Ops:
  0.0 55.5 %copy-start = (bf16[7,32,32]{2,1,0:T(8,128)(2,1)S(1)}, bf16[7,32,32]{2,1,0:T(8,128)(2,1)}, u32[]{:S(2)}) copy-start(bf16[7,32,32]{2,1,0:T(8,128)(2,1)} %param.22) | copy-start | bytes 43012
  4.1 15.9 %copy-start.8 = (s32[64]{0:T(128)S(1)}, s32[64]{0:T(128)}, u32[]{:S(2)}) copy-start(s32[64]{0:T(128)} %param.16) | copy-start | bytes 772
  4.1 17.2 %copy-start.9 = (f32[16]{0:T(128)S(1)}, f32[16]{0:T(128)}, u32[]{:S(2)}) copy-start(f32[16]{0:T(128)} %param.19) | copy-start | bytes 196
  4.1 17.3 %copy-start.10 = (f32[64]{0:T(128)S(1)}, f32[64]{0:T(128)}, u32[]{:S(2)}) copy-start(f32[64]{0:T(128)} %param.26) | copy-start | bytes 772
  4.1 17.3 %copy-start.11 = (f32[32]{0:T(128)S(1)}, f32[32]{0:T(128)}, u32[]{:S(2)}) copy-start(f32[32]{0:T(128)} %param.24) | copy-start | bytes 388
  4.1 17.3 %copy-start.12 = (f32[32]{0:T(128)S(1)}, f32[32]{0:T(128)}, u32[]{:S(2)}) copy-start(f32[32]{0:T(128)} %param.21) | copy-start | bytes 388
  4.1 18.1 %copy-start.5 = (bf16[16,1,7,7]{0,3,2,1:T(8,128)(2,1)S(1)}, bf16[16,1,7,7]{0,3,2,1:T(8,128)(2,1)}, u32[]{:S(2)}) copy-start(bf16[16,1,7,7]{0,3,2,1:T(8,128)(2,1)} %param.18) | copy-start | bytes 4708
  4.9 18.8 %copy-start.4 = (bf16[32,16,7,7]{0,1,3,2:T(8,128)(2,1)S(1)}, bf16[32,16,7,7]{0,1,3,2:T(8,128)(2,1)}, u32[]{:S(2)}) copy-start(bf16[32,16,7,7]{0,1,3,2:T(8,128)(2,1)} %param.20) | copy-start | bytes 150532
  5.4 19.6 %copy-start.3 = (bf16[32,32,7,7]{1,0,3,2:T(8,128)(2,1)S(1)}, bf16[32,32,7,7]{1,0,3,2:T(8,128)(2,1)}, u32[]{:S(2)}) copy-start(bf16[32,32,7,7]{1,0,3,2:T(8,128)(2,1)} %param.23) | copy-start | bytes 301060
  6.9 24.7 %all-to-all-start = ((bf16[64,2,656]{2,1,0:T(2,128)(2,1)}), bf16[64,2,656]{2,1,0:T(2,128)(2,1)S(1)}, u32[]{:S(2)}, u32[]{:S(2)}) async-start(bf16[64,2,656]{2,1,0:T(2,128)(2,1)} %reshape.280), calls=%async_computation | async-start | bytes 393216 | tf_op jit(solution)/shard_map/all_to_all | solution.py:254
  22.3 3.9 %copy-start.2 = (bf16[64,32,7,7]{0,1,3,2:T(8,128)(2,1)S(1)}, bf16[64,32,7,7]{0,1,3,2:T(8,128)(2,1)}, u32[]{:S(2)}) copy-start(bf16[64,32,7,7]{0,1,3,2:T(8,128)(2,1)} %param.25) | copy-start | bytes 602116
  32.4 9.1 %copy-start.1 = (bf16[64,32,41]{2,1,0:T(8,128)(2,1)}, bf16[64,32,41]{2,1,0:T(8,128)(2,1)S(1)}, u32[]{:S(2)}) copy-start(bf16[64,32,41]{2,1,0:T(8,128)(2,1)S(1)} %reshape.281) | copy-start | bytes 503812
  32.5 9.1 %collective-permute-start.1 = (bf16[32,41]{1,0:T(8,128)(2,1)S(1)}, bf16[32,41]{1,0:T(8,128)(2,1)S(1)}, u32[]{:S(2)}, u32[]{:S(2)}) collective-permute-start(bf16[32,41]{1,0:T(8,128)(2,1)S(1)} %get-tuple-element.48), channel_id=1, source_target_pairs={{1,0},{2,1},{3,2},{5,4},{6,5},{7,6},{9,8},{10,9},{11,10},{13,12},{... | collective-permute-start | bytes 7880 | tf_op jit(solution)/shard_map/ppermute | solution.py:283
  33.8 7.8 %collective-permute-start = (bf16[32,41]{1,0:T(8,128)(2,1)S(1)}, bf16[32,41]{1,0:T(8,128)(2,1)S(1)}, u32[]{:S(2)}, u32[]{:S(2)}) collective-permute-start(bf16[32,41]{1,0:T(8,128)(2,1)S(1)} %get-tuple-element.49), channel_id=1, source_target_pairs={{0,1},{1,2},{2,3},{4,5},{5,6},{6,7},{8,9},{9,10},{10,11},{12,13},{... | collective-permute-start | bytes 7880 | tf_op jit(solution)/shard_map/ppermute | solution.py:282
  41.5 0.6 copy-start.6
  41.6 0.6 copy-start.7
  55.9 7.2 %collective-permute-start.2 = (bf16[6,32,522]{2,1,0:T(8,128)(2,1)S(1)}, bf16[6,32,522]{2,1,0:T(8,128)(2,1)S(1)}, u32[]{:S(2)}, u32[]{:S(2)}) collective-permute-start(bf16[6,32,522]{2,1,0:T(8,128)(2,1)S(1)} %get-tuple-element.50), channel_id=1, source_target_pairs={{0,4},{4,8},{8,12},{12,16},{16,20},{20,24},{24,28},{28,32},{32,36}... | collective-permute-start | bytes 601352 | tf_op jit(solution)/shard_map/ppermute | solution.py:304
  60.0 7.5 %collective-permute-start.3 = (bf16[6,32,522]{2,1,0:T(8,128)(2,1)S(1)}, bf16[6,32,522]{2,1,0:T(8,128)(2,1)S(1)}, u32[]{:S(2)}, u32[]{:S(2)}) collective-permute-start(bf16[6,32,522]{2,1,0:T(8,128)(2,1)S(1)} %get-tuple-element.51), channel_id=1, source_target_pairs={{4,0},{8,4},{12,8},{16,12},{20,16},{24,20},{28,24},{32,28},{36,32}... | collective-permute-start | bytes 601352 | tf_op jit(solution)/shard_map/ppermute | solution.py:305

commit v15 on v14

--- a/solution.py
+++ b/solution.py
@@ -13,6 +13,8 @@
 WR = 8
 LEAD = 5
 LANE_BLOCK = 256
+WIN_ROWS = (C_DEV + 2 * REACH) * PH
+WIN_PAD = 96
 
 
 def banded(x, w_all, bias, b_row, mask, *, groups, shifts, n_out, relu, select=None, n_sel=0, rows_inner=False):
@@ -116,7 +118,7 @@
         for src, lo, n, skip in pieces:
             acc = None
             for q in range(PH):
-                e = (ri == ci * PH + q + PH * (ci // (rows // (2 * PH) - 1))).astype(jnp.float32)
+                e = (ri == ci * PH + q + (rows // 2 - WIN_ROWS) * (ci // (WIN_ROWS // PH))).astype(jnp.float32)
                 piece = src[pl.ds(q, n, stride=PH), :].astype(jnp.float32)
                 y = lax.dot_general(e, piece, nt, preferred_element_type=jnp.float32)
                 acc = y if acc is None else acc + y
@@ -138,7 +140,7 @@
 def first_layer(x, w_all, bias, mask):
     windows, rows_in, n_in = x.shape
     n_out = n_in - 3
-    r_out = rows_in // PH - 7
+    r_out = WIN_ROWS // PH - 6
     fout = w_all.shape[0] // PH
 
     def kernel(x_ref, w_ref, b_ref, m_ref, o_ref):
@@ -281,12 +283,12 @@
     down = [(j, i) for i, j in up]
     before = lax.ppermute(arrived[blocks - 1], "tm", up)
     after = lax.ppermute(arrived[0, : PH * WR], "tm", down)
-    strain_wide = strain_layout(arrived.reshape(times, -1), before, after, 2 * (wide + 1) * PH)
+    strain_wide = strain_layout(arrived.reshape(times, -1), before, after, 2 * WIN_PAD)
 
     quarter = times // 4
     length = quarter + 2 * LEAD
     lower = lower_layers(
-        strain_wide.reshape(2, (wide + 1) * PH, -1), first_mask, first_weight, biases, second_weight, length
+        strain_wide.reshape(2, WIN_PAD, -1), first_mask, first_weight, biases, second_weight, length
     )
     pre_second, mate_second = lower[0], lower[1]
 

time: 79.7 us -> 78 us (0.979)
  local copies, waits for them, and re-layouts: 14.4 us -> 12.7 us
    reshape x1 -> x0, local copies, waits for them, and re-layouts: 1.67 us -> none  [on_device(): strain_wide.reshape(2, (wide + 1) * PH, -1)]
  transfers between devices with their start and end apart: 5 -> 5, of which waited for: 2 -> 2; matrix products, arithmetic and copies ran while one was open for 12% -> 12% of each run, Pallas kernels for 2% -> 3%
where the time goes in v15:
time: 78 us; the launch traced here: 77 us
  starting transfers between devices  24.4 us (31%)
  Pallas kernels  22.5 us (29%)
  local copies, waits for them, and re-layouts  12.7 us (16%)
  other arithmetic  6.73 us (9%)
  waiting for transfers between devices  5.41 us (7%)
  between operations  4.99 us (6%)
    pallas_call x3, Pallas kernels, banded(): pl.pallas_call(kernel, grid=(windows,), in_specs=specs, out_specs=pl.Bloc...  14.2 us
    all_to_all x1, starting transfers between devices, on_device(): lax.all_to_all(outgoing, 'chan', split_axis=0, concat_axis=0, tiled=True)  13 us
    ppermute x1, waiting for transfers between devices, on_device(): below = lax.ppermute(second[:REACH], 'chan', ring_down)  4.4 us
    ppermute x1, starting transfers between devices, on_device(): above = lax.ppermute(second[C_DEV - REACH:], 'chan', ring_up)  4.09 us
    pallas_call x1, Pallas kernels, first_layer(): pl.pallas_call(kernel, grid=(windows,), in_specs=[pl.BlockSpec((None, row...  4.01 us
    ppermute x1, starting transfers between devices, on_device(): before = lax.ppermute(arrived[blocks - 1], 'tm', up)  3.99 us
    pallas_call x1, Pallas kernels, strain_layout(): pl.pallas_call(kernel, out_shape=jax.ShapeDtypeStruct((rows, n_out), jnp....  2.3 us
    unnamed x27, local copies, waits for them, and re-layouts  2.1 us
  transfers between devices with their start and end apart: 5, of which 2 were waited for; matrix products, arithmetic and copies ran while one was open for 12% of the time, Pallas kernels for 3%

profile of v15, /device:TPU:1, one launch (start us, length us, event | category | flops | bytes accessed | tf_op | source)
XLA Modules:
  0.0 77.0 jit_solution(14922544619391859313)
XLA Ops:
  0.7 0.7 pad_clamp_fusion
  1.3 1.0 %pad_slice_fusion.2 = (bf16[32,512]{1,0:T(8,128)(2,1)S(1)}, bf16[32,512]{1,0:T(8,128)(2,1)S(1)}, bf16[32,512]{1,0:T(8,128)(2,1)S(1)}) fusion(bf16[32,512]{1,0:T(8,128)(2,1)} %param.15), kind=kLoop, calls=%fused_computation.26 | loop fusion | bytes 131072 | tf_op jit(solution)/shard_map/slice | solution.py:251
  3.6 0.5 pad_maximum_fusion
  4.1 0.7 gather_fusion
  4.9 0.5 maximum_bitcast_fusion.1
  5.5 1.4 %reshape.280 = bf16[64,2,656]{2,1,0:T(2,128)(2,1)} reshape(bf16[64,32,41]{2,1,0:T(8,128)(2,1)S(1)} %maximum_bitcast_fusion.1) | data formatting | bytes 335872
  6.9 13.0 %all-to-all-start = ((bf16[64,2,656]{2,1,0:T(2,128)(2,1)}), bf16[64,2,656]{2,1,0:T(2,128)(2,1)S(1)}, u32[]{:S(2)}, u32[]{:S(2)}) async-start(bf16[64,2,656]{2,1,0:T(2,128)(2,1)} %reshape.280), calls=%async_computation | async-start | bytes 393216 | tf_op jit(solution)/shard_map/all_to_all | solution.py:256
  19.9 0.7 dynamic_slice.11
  21.5 0.8 %copy.72.refs_4_ = f32[192,1]{1,0:T(8,128)} copy(f32[192,1]{0,1:T(1,128)S(1)} %bitcast.77) | data formatting | bytes 1536 | tf_op jit(solution)/shard_map/reshape | solution.py:257
  23.1 0.7 copy.69.refs_0_
  24.3 0.7 copy.70.refs_1_
  25.3 0.9 %reshape.265.refs_2_ = bf16[224,224]{1,0:T(8,128)(2,1)} reshape(bf16[7,32,7,32]{3,2,1,0:T(8,128)(2,1)S(1)} %copy.67) | data formatting | bytes 200704 | tf_op jit(solution)/shard_map/reshape | solution.py:175
  27.0 0.8 %copy.71.refs_3_ = bf16[128,896]{1,0:T(8,128)(2,1)} copy(bf16[128,896]{0,1:T(8,128)(2,1)S(1)} %reshape.267) | data formatting | bytes 458752 | tf_op jit(solution)/shard_map/reshape | solution.py:181
  28.0 0.8 %add_convert_fusion.m_ref = f32[2,14,4,524]{3,2,1,0:T(4,128)} fusion(pred[1,14,4,524]{3,2,1,0:T(4,128)(4,1)S(1)} %get-tuple-element.60, pred[1,14,4,524]{3,2,1,0:T(4,128)(4,1)S(1)} %get-tuple-element.59), kind=kLoop, calls=%fused_computation.13 | loop fusion | flops 117376 | bytes 293440 | tf_op jit(solution)/shard_map/stack | solution.py:271
  28.9 2.0 %shard_map.127 = (bf16[64,128]{1,0:T(8,128)(2,1)}, bf16[96,448]{1,0:T(8,128)(2,1)}, bf16[224,224]{1,0:T(8,128)(2,1)}, bf16[128,896]{1,0:T(8,128)(2,1)}, f32[192,1]{1,0:T(8,128)}) custom-call(bf16[64,128]{1,0:T(8,128)(2,1)} %copy.69.refs_0_, bf16[96,448]{1,0:T(8,128)(2,1)} %copy.70.refs_1_, bf16[224,224]{1,0:T(8,128)(2,1)} %reshape.265.refs_2_, ...), custom_call_target="tpu_custom_call" | custom-call | tf_op jit(solution)/shard_map/pallas_call | solution.py:137
  30.9 0.7 and_convert_fusion
  31.6 0.8 %reshape.281 = bf16[64,32,41]{2,1,0:T(8,128)(2,1)S(1)} reshape(bf16[64,2,656]{2,1,0:T(2,128)(2,1)S(1)} %all-to-all-done) | data formatting | bytes 335872 | tf_op jit(solution)/shard_map/optimization_barrier | solution.py:276
  32.5 1.3 %collective-permute-start.1 = (bf16[32,41]{1,0:T(8,128)(2,1)S(1)}, bf16[32,41]{1,0:T(8,128)(2,1)S(1)}, u32[]{:S(2)}, u32[]{:S(2)}) collective-permute-start(bf16[32,41]{1,0:T(8,128)(2,1)S(1)} %get-tuple-element.48), channel_id=1, source_target_pairs={{1,0},{2,1},{3,2},{5,4},{6,5},{7,6},{9,8},{10,9},{11,10},{13,12},{... | collective-permute-start | bytes 7880 | tf_op jit(solution)/shard_map/ppermute | solution.py:285
  33.8 4.0 %collective-permute-start = (bf16[32,41]{1,0:T(8,128)(2,1)S(1)}, bf16[32,41]{1,0:T(8,128)(2,1)S(1)}, u32[]{:S(2)}, u32[]{:S(2)}) collective-permute-start(bf16[32,41]{1,0:T(8,128)(2,1)S(1)} %get-tuple-element.49), channel_id=1, source_target_pairs={{0,1},{1,2},{2,3},{4,5},{5,6},{6,7},{8,9},{9,10},{10,11},{12,13},{... | collective-permute-start | bytes 7880 | tf_op jit(solution)/shard_map/ppermute | solution.py:284
  39.9 0.5 fusion.17
  41.6 0.6 copy-done.6
  42.2 2.3 %shard_map.128 = bf16[192,527]{1,0:T(8,128)(2,1)} custom-call(bf16[2048,41]{1,0:T(8,128)(2,1)} %bitcast.59, bf16[32,41]{1,0:T(8,128)(2,1)} %copy-done.7, bf16[32,41]{1,0:T(8,128)(2,1)} %copy-done.6), custom_call_target="tpu_custom_call" | custom-call | tf_op jit(solution)/shard_map/pallas_call | solution.py:127
  44.5 4.0 %shard_map.129.x_ref = bf16[2,14,64,524]{3,2,1,0:T(8,128)(2,1)} custom-call(bf16[2,96,527]{2,1,0:T(8,128)(2,1)} %bitcast.65, bf16[64,128]{1,0:T(8,128)(2,1)} %get-tuple-element.37.w_ref, f32[192,1]{1,0:T(8,128)} %get-tuple-element.38.b_ref, f32[2,14,4,524]{3,2,1,0:T(4,128)} %add_convert_fusion.m_ref), custom_call_target="tpu_custom_call" | custom-call | tf_op jit(solution)/shard_map/pallas_call | solution.py:159
  48.5 4.1 %shard_map.130 = bf16[2,8,32,522]{3,2,1,0:T(8,128)(2,1)} custom-call(bf16[2,14,64,524]{3,2,1,0:T(8,128)(2,1)} %shard_map.129.x_ref, bf16[96,448]{1,0:T(8,128)(2,1)} %get-tuple-element.40.w_ref, f32[192,1]{1,0:T(8,128)} %get-tuple-element.38.b_ref), custom_call_target="tpu_custom_call" | custom-call | tf_op jit(solution)/shard_map/pallas_call | solution.py:99
  52.5 1.2 %slice_convert_fusion = (f32[1,8,32,522]{3,2,1,0:T(8,128)S(1)}, f32[8,32,522]{2,1,0:T(8,128)S(1)}, bf16[1,8,32,522]{3,2,1,0:T(8,128)(2,1)S(1)}) fusion(bf16[2,8,32,522]{3,2,1,0:T(8,128)(2,1)} %shard_map.130), kind=kLoop, calls=%fused_computation.11 | loop fusion | flops 133632 | bytes 1870848 | tf_op jit(solution)/shard_map/convert_element_type | solution.py:302
  54.2 4.1 %collective-permute-start.2 = (bf16[6,32,522]{2,1,0:T(8,128)(2,1)S(1)}, bf16[6,32,522]{2,1,0:T(8,128)(2,1)S(1)}, u32[]{:S(2)}, u32[]{:S(2)}) collective-permute-start(bf16[6,32,522]{2,1,0:T(8,128)(2,1)S(1)} %get-tuple-element.50), channel_id=1, source_target_pairs={{0,4},{4,8},{8,12},{12,16},{16,20},{20,24},{24,28},{28,32},{32,36}... | collective-permute-start | bytes 601352 | tf_op jit(solution)/shard_map/ppermute | solution.py:306
  58.3 2.1 %collective-permute-start.3 = (bf16[6,32,522]{2,1,0:T(8,128)(2,1)S(1)}, bf16[6,32,522]{2,1,0:T(8,128)(2,1)S(1)}, u32[]{:S(2)}, u32[]{:S(2)}) collective-permute-start(bf16[6,32,522]{2,1,0:T(8,128)(2,1)S(1)} %get-tuple-element.51), channel_id=1, source_target_pairs={{4,0},{8,4},{12,8},{16,12},{20,16},{24,20},{28,24},{32,28},{36,32}... | collective-permute-start | bytes 601352 | tf_op jit(solution)/shard_map/ppermute | solution.py:307
  60.4 1.0 %collective-permute-done.2 = bf16[6,32,522]{2,1,0:T(8,128)(2,1)S(1)} collective-permute-done((bf16[6,32,522]{2,1,0:T(8,128)(2,1)S(1)}, bf16[6,32,522]{2,1,0:T(8,128)(2,1)S(1)}, u32[]{:S(2)}, u32[]{:S(2)}) %collective-permute-start.2) | collective-permute-done | bytes 200480 | tf_op jit(solution)/shard_map/ppermute | solution.py:306
  61.4 4.4 %collective-permute-done.3 = bf16[6,32,522]{2,1,0:T(8,128)(2,1)S(1)} collective-permute-done((bf16[6,32,522]{2,1,0:T(8,128)(2,1)S(1)}, bf16[6,32,522]{2,1,0:T(8,128)(2,1)S(1)}, u32[]{:S(2)}, u32[]{:S(2)}) %collective-permute-start.3) | collective-permute-done | bytes 200480 | tf_op jit(solution)/shard_map/ppermute | solution.py:307
  65.8 1.1 %maximum_bitcast_fusion.x_ref = bf16[1,20,32,522]{3,2,1,0:T(8,128)(2,1)} fusion(bf16[6,32,522]{2,1,0:T(8,128)(2,1)S(1)} %collective-permute-done.3, bf16[8,32,522]{2,1,0:T(8,128)(2,1)S(1)} %multiply_convert_fusion, bf16[6,32,522]{2,1,0:T(8,128)(2,1)S(1)} %collective-permute-done.2), kind=kLoop, calls=%fused_computation.4 | loop fusion | flops 668160 | bytes 1336320 | tf_op jit(solution)/shard_map/broadcast_in_dim | solution.py:313
  66.9 7.2 %shard_map.131.x_ref = bf16[1,14,128,129]{3,2,1,0:T(8,128)(2,1)} custom-call(bf16[1,20,32,522]{3,2,1,0:T(8,128)(2,1)} %maximum_bitcast_fusion.x_ref, bf16[224,224]{1,0:T(8,128)(2,1)} %get-tuple-element.42.w_ref, f32[192,1]{1,0:T(8,128)} %get-tuple-element.38.b_ref, f32[1,14,1,516]{3,2,1,0:T(1,128)} %bitcast.70, bf16[128,128]{1,0:T(8,128)(2,1)} %constant.88.clone.rest_1_), custom_call_target="tpu_custom_call" | custom-call | tf_op jit(solution)/shard_map/pallas_call | solution.py:99
  74.1 2.9 %shard_map.132 = bf16[1,64,8,128]{3,2,1,0:T(8,128)(2,1)} custom-call(bf16[1,14,128,129]{3,2,1,0:T(8,128)(2,1)} %shard_map.131.x_ref, bf16[128,896]{1,0:T(8,128)(2,1)} %get-tuple-element.44.w_ref, f32[192,1]{1,0:T(8,128)} %get-tuple-element.38.b_ref), custom_call_target="tpu_custom_call" | custom-call | tf_op jit(solution)/shard_map/pallas_call | solution.py:99
  (68 shorter events, 4.7 us)
Async XLA Ops:
  0.0 53.8 %copy-start = (bf16[7,32,32]{2,1,0:T(8,128)(2,1)S(1)}, bf16[7,32,32]{2,1,0:T(8,128)(2,1)}, u32[]{:S(2)}) copy-start(bf16[7,32,32]{2,1,0:T(8,128)(2,1)} %param.22) | copy-start | bytes 43012
  4.1 15.9 %copy-start.8 = (s32[64]{0:T(128)S(1)}, s32[64]{0:T(128)}, u32[]{:S(2)}) copy-start(s32[64]{0:T(128)} %param.16) | copy-start | bytes 772
  4.1 17.2 %copy-start.9 = (f32[16]{0:T(128)S(1)}, f32[16]{0:T(128)}, u32[]{:S(2)}) copy-start(f32[16]{0:T(128)} %param.19) | copy-start | bytes 196
  4.1 17.3 %copy-start.10 = (f32[64]{0:T(128)S(1)}, f32[64]{0:T(128)}, u32[]{:S(2)}) copy-start(f32[64]{0:T(128)} %param.26) | copy-start | bytes 772
  4.1 17.3 %copy-start.11 = (f32[32]{0:T(128)S(1)}, f32[32]{0:T(128)}, u32[]{:S(2)}) copy-start(f32[32]{0:T(128)} %param.24) | copy-start | bytes 388
  4.1 17.3 %copy-start.12 = (f32[32]{0:T(128)S(1)}, f32[32]{0:T(128)}, u32[]{:S(2)}) copy-start(f32[32]{0:T(128)} %param.21) | copy-start | bytes 388
  4.1 18.1 %copy-start.5 = (bf16[16,1,7,7]{0,3,2,1:T(8,128)(2,1)S(1)}, bf16[16,1,7,7]{0,3,2,1:T(8,128)(2,1)}, u32[]{:S(2)}) copy-start(bf16[16,1,7,7]{0,3,2,1:T(8,128)(2,1)} %param.18) | copy-start | bytes 4708
  4.9 18.8 %copy-start.4 = (bf16[32,16,7,7]{0,1,3,2:T(8,128)(2,1)S(1)}, bf16[32,16,7,7]{0,1,3,2:T(8,128)(2,1)}, u32[]{:S(2)}) copy-start(bf16[32,16,7,7]{0,1,3,2:T(8,128)(2,1)} %param.20) | copy-start | bytes 150532
  5.4 19.6 %copy-start.3 = (bf16[32,32,7,7]{1,0,3,2:T(8,128)(2,1)S(1)}, bf16[32,32,7,7]{1,0,3,2:T(8,128)(2,1)}, u32[]{:S(2)}) copy-start(bf16[32,32,7,7]{1,0,3,2:T(8,128)(2,1)} %param.23) | copy-start | bytes 301060
  6.9 24.7 %all-to-all-start = ((bf16[64,2,656]{2,1,0:T(2,128)(2,1)}), bf16[64,2,656]{2,1,0:T(2,128)(2,1)S(1)}, u32[]{:S(2)}, u32[]{:S(2)}) async-start(bf16[64,2,656]{2,1,0:T(2,128)(2,1)} %reshape.280), calls=%async_computation | async-start | bytes 393216 | tf_op jit(solution)/shard_map/all_to_all | solution.py:256
  22.3 3.9 %copy-start.2 = (bf16[64,32,7,7]{0,1,3,2:T(8,128)(2,1)S(1)}, bf16[64,32,7,7]{0,1,3,2:T(8,128)(2,1)}, u32[]{:S(2)}) copy-start(bf16[64,32,7,7]{0,1,3,2:T(8,128)(2,1)} %param.25) | copy-start | bytes 602116
  32.4 9.1 %copy-start.1 = (bf16[64,32,41]{2,1,0:T(8,128)(2,1)}, bf16[64,32,41]{2,1,0:T(8,128)(2,1)S(1)}, u32[]{:S(2)}) copy-start(bf16[64,32,41]{2,1,0:T(8,128)(2,1)S(1)} %reshape.281) | copy-start | bytes 503812
  32.5 9.1 %collective-permute-start.1 = (bf16[32,41]{1,0:T(8,128)(2,1)S(1)}, bf16[32,41]{1,0:T(8,128)(2,1)S(1)}, u32[]{:S(2)}, u32[]{:S(2)}) collective-permute-start(bf16[32,41]{1,0:T(8,128)(2,1)S(1)} %get-tuple-element.48), channel_id=1, source_target_pairs={{1,0},{2,1},{3,2},{5,4},{6,5},{7,6},{9,8},{10,9},{11,10},{13,12},{... | collective-permute-start | bytes 7880 | tf_op jit(solution)/shard_map/ppermute | solution.py:285
  33.8 7.8 %collective-permute-start = (bf16[32,41]{1,0:T(8,128)(2,1)S(1)}, bf16[32,41]{1,0:T(8,128)(2,1)S(1)}, u32[]{:S(2)}, u32[]{:S(2)}) collective-permute-start(bf16[32,41]{1,0:T(8,128)(2,1)S(1)} %get-tuple-element.49), channel_id=1, source_target_pairs={{0,1},{1,2},{2,3},{4,5},{5,6},{6,7},{8,9},{9,10},{10,11},{12,13},{... | collective-permute-start | bytes 7880 | tf_op jit(solution)/shard_map/ppermute | solution.py:284
  41.5 0.6 copy-start.6
  41.6 0.6 copy-start.7
  54.2 7.2 %collective-permute-start.2 = (bf16[6,32,522]{2,1,0:T(8,128)(2,1)S(1)}, bf16[6,32,522]{2,1,0:T(8,128)(2,1)S(1)}, u32[]{:S(2)}, u32[]{:S(2)}) collective-permute-start(bf16[6,32,522]{2,1,0:T(8,128)(2,1)S(1)} %get-tuple-element.50), channel_id=1, source_target_pairs={{0,4},{4,8},{8,12},{12,16},{16,20},{20,24},{24,28},{28,32},{32,36}... | collective-permute-start | bytes 601352 | tf_op jit(solution)/shard_map/ppermute | solution.py:306
  58.3 7.5 %collective-permute-start.3 = (bf16[6,32,522]{2,1,0:T(8,128)(2,1)S(1)}, bf16[6,32,522]{2,1,0:T(8,128)(2,1)S(1)}, u32[]{:S(2)}, u32[]{:S(2)}) collective-permute-start(bf16[6,32,522]{2,1,0:T(8,128)(2,1)S(1)} %get-tuple-element.51), channel_id=1, source_target_pairs={{4,0},{8,4},{12,8},{16,12},{20,16},{24,20},{28,24},{32,28},{36,32}... | collective-permute-start | bytes 601352 | tf_op jit(solution)/shard_map/ppermute | solution.py:307

commit v16 on v15

--- a/solution.py
+++ b/solution.py
@@ -281,8 +281,8 @@
     tms = lax.axis_size("tm")
     up = [(i, i + 1) for i in range(tms - 1)]
     down = [(j, i) for i, j in up]
+    after = lax.ppermute(arrived[0, : PH * WR], "tm", down)
     before = lax.ppermute(arrived[blocks - 1], "tm", up)
-    after = lax.ppermute(arrived[0, : PH * WR], "tm", down)
     strain_wide = strain_layout(arrived.reshape(times, -1), before, after, 2 * WIN_PAD)
 
     quarter = times // 4

time: 78 us -> 78 us (level)
  no operation moved by 1% of the time
where the time goes in v16:
time: 78 us; the launch traced here: 77 us
  starting transfers between devices  24.5 us (31%)
  Pallas kernels  22.5 us (29%)
  local copies, waits for them, and re-layouts  12.7 us (16%)
  other arithmetic  6.73 us (9%)
  waiting for transfers between devices  5.41 us (7%)
  between operations  4.98 us (6%)
    pallas_call x3, Pallas kernels, banded(): pl.pallas_call(kernel, grid=(windows,), in_specs=specs, out_specs=pl.Bloc...  14.2 us
    all_to_all x1, starting transfers between devices, on_device(): lax.all_to_all(outgoing, 'chan', split_axis=0, concat_axis=0, tiled=True)  13 us
    ppermute x1, waiting for transfers between devices, on_device(): below = lax.ppermute(second[:REACH], 'chan', ring_down)  4.4 us
    ppermute x1, starting transfers between devices, on_device(): above = lax.ppermute(second[C_DEV - REACH:], 'chan', ring_up)  4.1 us
    pallas_call x1, Pallas kernels, first_layer(): pl.pallas_call(kernel, grid=(windows,), in_specs=[pl.BlockSpec((None, row...  4.01 us
    ppermute x1, starting transfers between devices, on_device(): before = lax.ppermute(arrived[blocks - 1], 'tm', up)  3.99 us
    pallas_call x1, Pallas kernels, strain_layout(): pl.pallas_call(kernel, out_shape=jax.ShapeDtypeStruct((rows, n_out), jnp....  2.3 us
    unnamed x27, local copies, waits for them, and re-layouts  2.1 us
  transfers between devices with their start and end apart: 5, of which 2 were waited for; matrix products, arithmetic and copies ran while one was open for 12% of the time, Pallas kernels for 3%

profile of v16, /device:TPU:1, one launch (start us, length us, event | category | flops | bytes accessed | tf_op | source)
XLA Modules:
  0.0 77.0 jit_solution(14922544619391859313)
XLA Ops:
  0.7 0.7 pad_clamp_fusion
  1.3 1.0 %pad_slice_fusion.2 = (bf16[32,512]{1,0:T(8,128)(2,1)S(1)}, bf16[32,512]{1,0:T(8,128)(2,1)S(1)}, bf16[32,512]{1,0:T(8,128)(2,1)S(1)}) fusion(bf16[32,512]{1,0:T(8,128)(2,1)} %param.15), kind=kLoop, calls=%fused_computation.26 | loop fusion | bytes 131072 | tf_op jit(solution)/shard_map/slice | solution.py:251
  3.6 0.5 pad_maximum_fusion
  4.1 0.7 gather_fusion
  4.9 0.5 maximum_bitcast_fusion.1
  5.4 1.4 %reshape.280 = bf16[64,2,656]{2,1,0:T(2,128)(2,1)} reshape(bf16[64,32,41]{2,1,0:T(8,128)(2,1)S(1)} %maximum_bitcast_fusion.1) | data formatting | bytes 335872
  6.9 13.0 %all-to-all-start = ((bf16[64,2,656]{2,1,0:T(2,128)(2,1)}), bf16[64,2,656]{2,1,0:T(2,128)(2,1)S(1)}, u32[]{:S(2)}, u32[]{:S(2)}) async-start(bf16[64,2,656]{2,1,0:T(2,128)(2,1)} %reshape.280), calls=%async_computation | async-start | bytes 393216 | tf_op jit(solution)/shard_map/all_to_all | solution.py:256
  19.9 0.7 dynamic_slice.11
  21.5 0.8 %copy.72.refs_4_ = f32[192,1]{1,0:T(8,128)} copy(f32[192,1]{0,1:T(1,128)S(1)} %bitcast.77) | data formatting | bytes 1536 | tf_op jit(solution)/shard_map/reshape | solution.py:257
  23.1 0.7 copy.69.refs_0_
  24.3 0.7 copy.70.refs_1_
  25.3 0.9 %reshape.265.refs_2_ = bf16[224,224]{1,0:T(8,128)(2,1)} reshape(bf16[7,32,7,32]{3,2,1,0:T(8,128)(2,1)S(1)} %copy.67) | data formatting | bytes 200704 | tf_op jit(solution)/shard_map/reshape | solution.py:175
  27.0 0.8 %copy.71.refs_3_ = bf16[128,896]{1,0:T(8,128)(2,1)} copy(bf16[128,896]{0,1:T(8,128)(2,1)S(1)} %reshape.267) | data formatting | bytes 458752 | tf_op jit(solution)/shard_map/reshape | solution.py:181
  28.0 0.8 %add_convert_fusion.m_ref = f32[2,14,4,524]{3,2,1,0:T(4,128)} fusion(pred[1,14,4,524]{3,2,1,0:T(4,128)(4,1)S(1)} %get-tuple-element.60, pred[1,14,4,524]{3,2,1,0:T(4,128)(4,1)S(1)} %get-tuple-element.59), kind=kLoop, calls=%fused_computation.13 | loop fusion | flops 117376 | bytes 293440 | tf_op jit(solution)/shard_map/stack | solution.py:271
  28.9 2.0 %shard_map.127 = (bf16[64,128]{1,0:T(8,128)(2,1)}, bf16[96,448]{1,0:T(8,128)(2,1)}, bf16[224,224]{1,0:T(8,128)(2,1)}, bf16[128,896]{1,0:T(8,128)(2,1)}, f32[192,1]{1,0:T(8,128)}) custom-call(bf16[64,128]{1,0:T(8,128)(2,1)} %copy.69.refs_0_, bf16[96,448]{1,0:T(8,128)(2,1)} %copy.70.refs_1_, bf16[224,224]{1,0:T(8,128)(2,1)} %reshape.265.refs_2_, ...), custom_call_target="tpu_custom_call" | custom-call | tf_op jit(solution)/shard_map/pallas_call | solution.py:137
  30.9 0.7 and_convert_fusion
  31.6 0.8 %reshape.281 = bf16[64,32,41]{2,1,0:T(8,128)(2,1)S(1)} reshape(bf16[64,2,656]{2,1,0:T(2,128)(2,1)S(1)} %all-to-all-done) | data formatting | bytes 335872 | tf_op jit(solution)/shard_map/optimization_barrier | solution.py:276
  32.5 1.3 %collective-permute-start.1 = (bf16[32,41]{1,0:T(8,128)(2,1)S(1)}, bf16[32,41]{1,0:T(8,128)(2,1)S(1)}, u32[]{:S(2)}, u32[]{:S(2)}) collective-permute-start(bf16[32,41]{1,0:T(8,128)(2,1)S(1)} %get-tuple-element.48), channel_id=1, source_target_pairs={{1,0},{2,1},{3,2},{5,4},{6,5},{7,6},{9,8},{10,9},{11,10},{13,12},{... | collective-permute-start | bytes 7880 | tf_op jit(solution)/shard_map/ppermute | solution.py:284
  33.8 4.0 %collective-permute-start = (bf16[32,41]{1,0:T(8,128)(2,1)S(1)}, bf16[32,41]{1,0:T(8,128)(2,1)S(1)}, u32[]{:S(2)}, u32[]{:S(2)}) collective-permute-start(bf16[32,41]{1,0:T(8,128)(2,1)S(1)} %get-tuple-element.49), channel_id=1, source_target_pairs={{0,1},{1,2},{2,3},{4,5},{5,6},{6,7},{8,9},{9,10},{10,11},{12,13},{... | collective-permute-start | bytes 7880 | tf_op jit(solution)/shard_map/ppermute | solution.py:285
  39.9 0.5 fusion.17
  41.6 0.6 copy-done.6
  42.2 2.3 %shard_map.128 = bf16[192,527]{1,0:T(8,128)(2,1)} custom-call(bf16[2048,41]{1,0:T(8,128)(2,1)} %bitcast.59, bf16[32,41]{1,0:T(8,128)(2,1)} %copy-done.7, bf16[32,41]{1,0:T(8,128)(2,1)} %copy-done.6), custom_call_target="tpu_custom_call" | custom-call | tf_op jit(solution)/shard_map/pallas_call | solution.py:127
  44.5 4.0 %shard_map.129.x_ref = bf16[2,14,64,524]{3,2,1,0:T(8,128)(2,1)} custom-call(bf16[2,96,527]{2,1,0:T(8,128)(2,1)} %bitcast.65, bf16[64,128]{1,0:T(8,128)(2,1)} %get-tuple-element.37.w_ref, f32[192,1]{1,0:T(8,128)} %get-tuple-element.38.b_ref, f32[2,14,4,524]{3,2,1,0:T(4,128)} %add_convert_fusion.m_ref), custom_call_target="tpu_custom_call" | custom-call | tf_op jit(solution)/shard_map/pallas_call | solution.py:159
  48.5 4.1 %shard_map.130 = bf16[2,8,32,522]{3,2,1,0:T(8,128)(2,1)} custom-call(bf16[2,14,64,524]{3,2,1,0:T(8,128)(2,1)} %shard_map.129.x_ref, bf16[96,448]{1,0:T(8,128)(2,1)} %get-tuple-element.40.w_ref, f32[192,1]{1,0:T(8,128)} %get-tuple-element.38.b_ref), custom_call_target="tpu_custom_call" | custom-call | tf_op jit(solution)/shard_map/pallas_call | solution.py:99
  52.5 1.2 %slice_convert_fusion = (f32[1,8,32,522]{3,2,1,0:T(8,128)S(1)}, f32[8,32,522]{2,1,0:T(8,128)S(1)}, bf16[1,8,32,522]{3,2,1,0:T(8,128)(2,1)S(1)}) fusion(bf16[2,8,32,522]{3,2,1,0:T(8,128)(2,1)} %shard_map.130), kind=kLoop, calls=%fused_computation.11 | loop fusion | flops 133632 | bytes 1870848 | tf_op jit(solution)/shard_map/convert_element_type | solution.py:302
  54.2 4.1 %collective-permute-start.2 = (bf16[6,32,522]{2,1,0:T(8,128)(2,1)S(1)}, bf16[6,32,522]{2,1,0:T(8,128)(2,1)S(1)}, u32[]{:S(2)}, u32[]{:S(2)}) collective-permute-start(bf16[6,32,522]{2,1,0:T(8,128)(2,1)S(1)} %get-tuple-element.50), channel_id=1, source_target_pairs={{0,4},{4,8},{8,12},{12,16},{16,20},{20,24},{24,28},{28,32},{32,36}... | collective-permute-start | bytes 601352 | tf_op jit(solution)/shard_map/ppermute | solution.py:306
  58.3 2.1 %collective-permute-start.3 = (bf16[6,32,522]{2,1,0:T(8,128)(2,1)S(1)}, bf16[6,32,522]{2,1,0:T(8,128)(2,1)S(1)}, u32[]{:S(2)}, u32[]{:S(2)}) collective-permute-start(bf16[6,32,522]{2,1,0:T(8,128)(2,1)S(1)} %get-tuple-element.51), channel_id=1, source_target_pairs={{4,0},{8,4},{12,8},{16,12},{20,16},{24,20},{28,24},{32,28},{36,32}... | collective-permute-start | bytes 601352 | tf_op jit(solution)/shard_map/ppermute | solution.py:307
  60.4 1.0 %collective-permute-done.2 = bf16[6,32,522]{2,1,0:T(8,128)(2,1)S(1)} collective-permute-done((bf16[6,32,522]{2,1,0:T(8,128)(2,1)S(1)}, bf16[6,32,522]{2,1,0:T(8,128)(2,1)S(1)}, u32[]{:S(2)}, u32[]{:S(2)}) %collective-permute-start.2) | collective-permute-done | bytes 200480 | tf_op jit(solution)/shard_map/ppermute | solution.py:306
  61.4 4.4 %collective-permute-done.3 = bf16[6,32,522]{2,1,0:T(8,128)(2,1)S(1)} collective-permute-done((bf16[6,32,522]{2,1,0:T(8,128)(2,1)S(1)}, bf16[6,32,522]{2,1,0:T(8,128)(2,1)S(1)}, u32[]{:S(2)}, u32[]{:S(2)}) %collective-permute-start.3) | collective-permute-done | bytes 200480 | tf_op jit(solution)/shard_map/ppermute | solution.py:307
  65.8 1.1 %maximum_bitcast_fusion.x_ref = bf16[1,20,32,522]{3,2,1,0:T(8,128)(2,1)} fusion(bf16[6,32,522]{2,1,0:T(8,128)(2,1)S(1)} %collective-permute-done.3, bf16[8,32,522]{2,1,0:T(8,128)(2,1)S(1)} %multiply_convert_fusion, bf16[6,32,522]{2,1,0:T(8,128)(2,1)S(1)} %collective-permute-done.2), kind=kLoop, calls=%fused_computation.4 | loop fusion | flops 668160 | bytes 1336320 | tf_op jit(solution)/shard_map/broadcast_in_dim | solution.py:313
  66.9 7.2 %shard_map.131.x_ref = bf16[1,14,128,129]{3,2,1,0:T(8,128)(2,1)} custom-call(bf16[1,20,32,522]{3,2,1,0:T(8,128)(2,1)} %maximum_bitcast_fusion.x_ref, bf16[224,224]{1,0:T(8,128)(2,1)} %get-tuple-element.42.w_ref, f32[192,1]{1,0:T(8,128)} %get-tuple-element.38.b_ref, f32[1,14,1,516]{3,2,1,0:T(1,128)} %bitcast.70, bf16[128,128]{1,0:T(8,128)(2,1)} %constant.88.clone.rest_1_), custom_call_target="tpu_custom_call" | custom-call | tf_op jit(solution)/shard_map/pallas_call | solution.py:99
  74.1 2.9 %shard_map.132 = bf16[1,64,8,128]{3,2,1,0:T(8,128)(2,1)} custom-call(bf16[1,14,128,129]{3,2,1,0:T(8,128)(2,1)} %shard_map.131.x_ref, bf16[128,896]{1,0:T(8,128)(2,1)} %get-tuple-element.44.w_ref, f32[192,1]{1,0:T(8,128)} %get-tuple-element.38.b_ref), custom_call_target="tpu_custom_call" | custom-call | tf_op jit(solution)/shard_map/pallas_call | solution.py:99
  (68 shorter events, 4.7 us)
Async XLA Ops:
  0.0 53.8 %copy-start = (bf16[7,32,32]{2,1,0:T(8,128)(2,1)S(1)}, bf16[7,32,32]{2,1,0:T(8,128)(2,1)}, u32[]{:S(2)}) copy-start(bf16[7,32,32]{2,1,0:T(8,128)(2,1)} %param.22) | copy-start | bytes 43012
  4.1 15.9 %copy-start.8 = (s32[64]{0:T(128)S(1)}, s32[64]{0:T(128)}, u32[]{:S(2)}) copy-start(s32[64]{0:T(128)} %param.16) | copy-start | bytes 772
  4.1 17.2 %copy-start.9 = (f32[16]{0:T(128)S(1)}, f32[16]{0:T(128)}, u32[]{:S(2)}) copy-start(f32[16]{0:T(128)} %param.19) | copy-start | bytes 196
  4.1 17.3 %copy-start.10 = (f32[64]{0:T(128)S(1)}, f32[64]{0:T(128)}, u32[]{:S(2)}) copy-start(f32[64]{0:T(128)} %param.26) | copy-start | bytes 772
  4.1 17.3 %copy-start.11 = (f32[32]{0:T(128)S(1)}, f32[32]{0:T(128)}, u32[]{:S(2)}) copy-start(f32[32]{0:T(128)} %param.24) | copy-start | bytes 388
  4.1 17.3 %copy-start.12 = (f32[32]{0:T(128)S(1)}, f32[32]{0:T(128)}, u32[]{:S(2)}) copy-start(f32[32]{0:T(128)} %param.21) | copy-start | bytes 388
  4.1 18.1 %copy-start.5 = (bf16[16,1,7,7]{0,3,2,1:T(8,128)(2,1)S(1)}, bf16[16,1,7,7]{0,3,2,1:T(8,128)(2,1)}, u32[]{:S(2)}) copy-start(bf16[16,1,7,7]{0,3,2,1:T(8,128)(2,1)} %param.18) | copy-start | bytes 4708
  4.9 18.8 %copy-start.4 = (bf16[32,16,7,7]{0,1,3,2:T(8,128)(2,1)S(1)}, bf16[32,16,7,7]{0,1,3,2:T(8,128)(2,1)}, u32[]{:S(2)}) copy-start(bf16[32,16,7,7]{0,1,3,2:T(8,128)(2,1)} %param.20) | copy-start | bytes 150532
  5.4 19.6 %copy-start.3 = (bf16[32,32,7,7]{1,0,3,2:T(8,128)(2,1)S(1)}, bf16[32,32,7,7]{1,0,3,2:T(8,128)(2,1)}, u32[]{:S(2)}) copy-start(bf16[32,32,7,7]{1,0,3,2:T(8,128)(2,1)} %param.23) | copy-start | bytes 301060
  6.9 24.7 %all-to-all-start = ((bf16[64,2,656]{2,1,0:T(2,128)(2,1)}), bf16[64,2,656]{2,1,0:T(2,128)(2,1)S(1)}, u32[]{:S(2)}, u32[]{:S(2)}) async-start(bf16[64,2,656]{2,1,0:T(2,128)(2,1)} %reshape.280), calls=%async_computation | async-start | bytes 393216 | tf_op jit(solution)/shard_map/all_to_all | solution.py:256
  22.3 3.9 %copy-start.2 = (bf16[64,32,7,7]{0,1,3,2:T(8,128)(2,1)S(1)}, bf16[64,32,7,7]{0,1,3,2:T(8,128)(2,1)}, u32[]{:S(2)}) copy-start(bf16[64,32,7,7]{0,1,3,2:T(8,128)(2,1)} %param.25) | copy-start | bytes 602116
  32.4 9.1 %copy-start.1 = (bf16[64,32,41]{2,1,0:T(8,128)(2,1)}, bf16[64,32,41]{2,1,0:T(8,128)(2,1)S(1)}, u32[]{:S(2)}) copy-start(bf16[64,32,41]{2,1,0:T(8,128)(2,1)S(1)} %reshape.281) | copy-start | bytes 503812
  32.5 9.1 %collective-permute-start.1 = (bf16[32,41]{1,0:T(8,128)(2,1)S(1)}, bf16[32,41]{1,0:T(8,128)(2,1)S(1)}, u32[]{:S(2)}, u32[]{:S(2)}) collective-permute-start(bf16[32,41]{1,0:T(8,128)(2,1)S(1)} %get-tuple-element.48), channel_id=1, source_target_pairs={{1,0},{2,1},{3,2},{5,4},{6,5},{7,6},{9,8},{10,9},{11,10},{13,12},{... | collective-permute-start | bytes 7880 | tf_op jit(solution)/shard_map/ppermute | solution.py:284
  33.8 7.8 %collective-permute-start = (bf16[32,41]{1,0:T(8,128)(2,1)S(1)}, bf16[32,41]{1,0:T(8,128)(2,1)S(1)}, u32[]{:S(2)}, u32[]{:S(2)}) collective-permute-start(bf16[32,41]{1,0:T(8,128)(2,1)S(1)} %get-tuple-element.49), channel_id=1, source_target_pairs={{0,1},{1,2},{2,3},{4,5},{5,6},{6,7},{8,9},{9,10},{10,11},{12,13},{... | collective-permute-start | bytes 7880 | tf_op jit(solution)/shard_map/ppermute | solution.py:285
  41.5 0.6 copy-start.6
  41.6 0.6 copy-start.7
  54.2 7.2 %collective-permute-start.2 = (bf16[6,32,522]{2,1,0:T(8,128)(2,1)S(1)}, bf16[6,32,522]{2,1,0:T(8,128)(2,1)S(1)}, u32[]{:S(2)}, u32[]{:S(2)}) collective-permute-start(bf16[6,32,522]{2,1,0:T(8,128)(2,1)S(1)} %get-tuple-element.50), channel_id=1, source_target_pairs={{0,4},{4,8},{8,12},{12,16},{16,20},{20,24},{24,28},{28,32},{32,36}... | collective-permute-start | bytes 601352 | tf_op jit(solution)/shard_map/ppermute | solution.py:306
  58.3 7.5 %collective-permute-start.3 = (bf16[6,32,522]{2,1,0:T(8,128)(2,1)S(1)}, bf16[6,32,522]{2,1,0:T(8,128)(2,1)S(1)}, u32[]{:S(2)}, u32[]{:S(2)}) collective-permute-start(bf16[6,32,522]{2,1,0:T(8,128)(2,1)S(1)} %get-tuple-element.51), channel_id=1, source_target_pairs={{4,0},{8,4},{12,8},{16,12},{20,16},{24,20},{28,24},{32,28},{36,32}... | collective-permute-start | bytes 601352 | tf_op jit(solution)/shard_map/ppermute | solution.py:307
